TPU v7x, 128 devices: a whole 4x4x4 slice. The times are simulated.
128 devices in a mesh: row: 16 (over z, x), col: 8 (over y, core).
Axes of the slice: x: 4, y: 4, z: 4, core: 2. Of those that a mesh axis runs over, the one named last changes fastest.
Arguments:
- pixels: bfloat16 [256, 128, 768], P('row', 'col'), may hold values from -6 to 6
- conv_weight: bfloat16 [3, 3, 64, 128], replicated, may hold values from -0.25 to 0.25
- time_weight: bfloat16 [3, 16, 8, 8], replicated, may hold values from -1.25 to 1.25
- class_weight: bfloat16 [128, 20], replicated, may hold values from -0.5 to 0.5
- pixel_slot: int32 [256, 128], P('row', 'col'), may hold values from 0 to 63, as said below
- straddle_dir: int32 [16, 8, 32], P('row', 'col'), may hold values from 0 to 8, as said below
- straddle_slot: int32 [16, 8, 32], P('row', 'col'), may hold values from 0 to 31
- labels: int32 [16, 8, 32], P('row', 'col'), may hold values from 0 to 19
Outputs:
- input_grad: bfloat16 [256, 128, 768], P('row', 'col')
- conv_grad: float32 [3, 3, 64, 128], replicated
- time_grad: float32 [3, 16, 8, 8], replicated
- class_grad: float32 [128, 20], replicated
Inputs may be any that keep to these rules, and one draw needn't show every extreme that they name: `pixel_slot`: below 32 a pixel is in the tile's own parcel of that number, from 32 on in its straddling entry of that number minus 32. Every index of a tile's list is held by at least one pixel of that tile. The owner of entry e of tile (r, c) is tile (r + q // 3 - 1, c + q % 3 - 1) with q = straddle_dir[r, c, e]; q is never 4 and the owner lies within the scene.
All inputs are finite; a program needn't handle non-finite values.
Results may differ from a plain program's by a relative error of at most 0.012.
Values may be sent and summed in bfloat16 or wider, within the bound.
No kernel may reach another device: no remote copies, remote signals or barrier semaphores. Data moves between devices by JAX's collectives and lax.ppermute only.
A program may use at most 64 MiB of HBM per device.

v0:
```python
import jax
import jax.numpy as jnp
from jax import lax
from jax.sharding import PartitionSpec as P

DATES = 12
C_IN = 64
C_OUT = 128
GROUPS = 16
CLASSES = 20
P_OWN = 32
S_STR = 32
CPG = 8


EPSILON = 1e-05
PRECISE = lax.Precision.HIGHEST


def with_halo(cells, sides, width):
    for axis, dim in sides:
        count = lax.axis_size(axis)
        ends = count - 1
        head = lax.slice_in_dim(cells, 0, width, axis=dim)
        tail = lax.slice_in_dim(cells, cells.shape[dim] - width, cells.shape[dim], axis=dim)
        cells = jnp.concatenate(
            [
                lax.ppermute(tail, axis, [(i, (i + 1) % count) for i in range(ends)]),
                cells,
                lax.ppermute(head, axis, [((i + 1) % count, i) for i in range(ends)]),
            ],
            axis=dim,
        )
    return cells


def silu_slope(value):
    sig = jax.nn.sigmoid(value)
    return sig * (1.0 + value * (1.0 - sig))


def spatial_forward(padded, conv_weight, tile_rows, tile_cols):
    running_sum = None
    for row_tap in range(3):
        tap_patch = jnp.concatenate(
            [
                padded[row_tap : row_tap + tile_rows, col_tap : col_tap + tile_cols]
                for col_tap in range(3)
            ],
            axis=-1,
        )
        tap_term = jnp.dot(
            tap_patch,
            conv_weight[row_tap].reshape(3 * C_IN, C_OUT),
            preferred_element_type=jnp.float32,
        )
        running_sum = tap_term if running_sum is None else running_sum + tap_term
    return running_sum


def transposed_conv(padded_grad, conv_weight, out_rows, out_cols):
    input_sum = None
    for row_tap in range(3):
        grad_patch = jnp.concatenate(
            [
                padded_grad[
                    2 - row_tap : 2 - row_tap + out_rows, 2 - col_tap : 2 - col_tap + out_cols
                ]
                for col_tap in range(3)
            ],
            axis=-1,
        )
        flipped = jnp.concatenate([conv_weight[row_tap, col_tap].T for col_tap in range(3)], axis=0)
        tap_term = jnp.dot(grad_patch, flipped, preferred_element_type=jnp.float32)
        input_sum = tap_term if input_sum is None else input_sum + tap_term
    return input_sum


def block_weights(time_weight):
    group_eye = jnp.eye(GROUPS, dtype=jnp.bfloat16)
    return jnp.einsum("kgco,gh->kgcho", time_weight, group_eye).reshape(3, C_OUT, C_OUT)


def per_device(
    pixels, conv_weight, time_weight, class_weight, pixel_slot, straddle_dir, straddle_slot, labels
):
    tile_rows, tile_cols = (pixels.shape[0], pixels.shape[1])
    slot_count = P_OWN + S_STR
    padded_pixels = with_halo(pixels, (("row", 0), ("col", 1)), 1).reshape(
        tile_rows + 2, tile_cols + 2, DATES, C_IN
    )
    pre_act = spatial_forward(padded_pixels, conv_weight, tile_rows, tile_cols)
    hidden = jax.nn.silu(pre_act).astype(jnp.bfloat16)
    dense_time = block_weights(time_weight)
    padded_hidden = jnp.pad(hidden, ((0, 0), (0, 0), (1, 1), (0, 0)))
    mixed_time = None
    for time_tap in range(3):
        tap_term = jnp.dot(
            padded_hidden[:, :, time_tap : time_tap + DATES],
            dense_time[time_tap],
            preferred_element_type=jnp.float32,
        )
        mixed_time = tap_term if mixed_time is None else mixed_time + tap_term
    embedded = (
        jnp.mean(jax.nn.silu(mixed_time), axis=2)
        .astype(jnp.bfloat16)
        .reshape(tile_rows * tile_cols, C_OUT)
    )
    flat_slot = pixel_slot.reshape(tile_rows * tile_cols)
    membership = (jnp.arange(slot_count, dtype=jnp.int32)[:, None] == flat_slot[None, :]).astype(
        jnp.bfloat16
    )
    partial_value = jnp.dot(membership, embedded, preferred_element_type=jnp.float32)
    direction = straddle_dir.reshape(S_STR)
    owner_slot = straddle_slot.reshape(S_STR)
    own_slots = jnp.arange(P_OWN, dtype=jnp.int32)
    target = jnp.concatenate([4 * P_OWN + own_slots, direction * P_OWN + owner_slot])
    select = (jnp.arange(9 * P_OWN, dtype=jnp.int32)[:, None] == target[None, :]).astype(
        jnp.float32
    )
    outgoing = jnp.dot(select, partial_value, precision=PRECISE).reshape(3, 3, P_OWN, C_OUT)
    border = with_halo(outgoing.astype(jnp.bfloat16), (("row", 0), ("col", 1)), 1).astype(
        outgoing.dtype
    )
    parcel_sums = jnp.sum(border[0::2, 0::2], axis=(0, 1))
    centered = parcel_sums - jnp.mean(parcel_sums, axis=-1, keepdims=True)
    variance = jnp.mean(centered * centered, axis=-1, keepdims=True)
    inverse = lax.rsqrt(variance + EPSILON)
    normed = centered * inverse
    rounded = normed.astype(jnp.bfloat16)
    logits = jnp.dot(rounded, class_weight, preferred_element_type=jnp.float32)
    exp_logits = jnp.exp(logits)
    probability = exp_logits / jnp.sum(exp_logits, axis=-1, keepdims=True)
    label_hot = (
        labels.reshape(P_OWN)[:, None] == jnp.arange(CLASSES, dtype=jnp.int32)[None, :]
    ).astype(jnp.float32)
    parcel_total = P_OWN * lax.axis_size("row") * lax.axis_size("col")
    grad_logits = (probability - label_hot) / parcel_total
    class_term = jnp.dot(rounded.astype(jnp.float32).T, grad_logits, precision=PRECISE)
    class_grad = lax.psum(class_term, ("row", "col"))
    grad_normed = jnp.dot(grad_logits, class_weight.astype(jnp.float32).T, precision=PRECISE)
    parcel_grad = (
        inverse
        * (
            grad_normed
            - jnp.mean(grad_normed, axis=-1, keepdims=True)
            - normed * jnp.mean(grad_normed * normed, axis=-1, keepdims=True)
        )
    ).astype(jnp.bfloat16)
    beside_all = with_halo(
        parcel_grad.reshape(1, 1, P_OWN, C_OUT), (("row", 0), ("col", 1)), 1
    ).reshape(9 * P_OWN, C_OUT)
    picker = (target[:, None] == jnp.arange(9 * P_OWN, dtype=jnp.int32)[None, :]).astype(
        jnp.bfloat16
    )
    slot_grad = jnp.dot(picker, beside_all, preferred_element_type=jnp.float32).astype(jnp.bfloat16)
    pixel_grad = jnp.dot(membership.T, slot_grad, preferred_element_type=jnp.float32).reshape(
        tile_rows, tile_cols, C_OUT
    )
    grad_mixed = ((pixel_grad / DATES)[:, :, None, :] * silu_slope(mixed_time)).astype(jnp.bfloat16)
    group_eye = jnp.eye(GROUPS, dtype=jnp.float32)
    time_taps = []
    for time_tap in range(3):
        dense_grad = jnp.einsum(
            "ijtc,ijtd->cd",
            padded_hidden[:, :, time_tap : time_tap + DATES],
            grad_mixed,
            preferred_element_type=jnp.float32,
        )
        reshaped = dense_grad.reshape(GROUPS, CPG, GROUPS, CPG)
        time_taps.append(jnp.einsum("gchd,gh->gcd", reshaped, group_eye, precision=PRECISE))
    time_term = jnp.stack(time_taps)
    time_grad = lax.psum(time_term, ("row", "col"))
    padded_mixed = jnp.pad(grad_mixed, ((0, 0), (0, 0), (1, 1), (0, 0)))
    grad_hidden = None
    for time_tap in range(3):
        tap_term = jnp.dot(
            padded_mixed[:, :, 2 - time_tap : 2 - time_tap + DATES],
            dense_time[time_tap].T,
            preferred_element_type=jnp.float32,
        )
        grad_hidden = tap_term if grad_hidden is None else grad_hidden + tap_term
    grad_pre = (grad_hidden * silu_slope(pre_act)).astype(jnp.bfloat16)
    conv_rows = []
    for row_tap in range(3):
        tap_patch = jnp.concatenate(
            [
                padded_pixels[row_tap : row_tap + tile_rows, col_tap : col_tap + tile_cols]
                for col_tap in range(3)
            ],
            axis=-1,
        )
        conv_rows.append(
            jnp.einsum(
                "ijtc,ijtd->cd", tap_patch, grad_pre, preferred_element_type=jnp.float32
            ).reshape(3, C_IN, C_OUT)
        )
    conv_term = jnp.stack(conv_rows)
    padded_grad = with_halo(
        grad_pre.reshape(tile_rows, tile_cols, DATES * C_OUT), (("row", 0), ("col", 1)), 1
    ).reshape(tile_rows + 2, tile_cols + 2, DATES, C_OUT)
    input_sum = transposed_conv(padded_grad, conv_weight, tile_rows, tile_cols)
    input_grad = input_sum.astype(jnp.bfloat16).reshape(tile_rows, tile_cols, DATES * C_IN)
    conv_grad = lax.psum(conv_term, ("row", "col"))
    return (input_grad, conv_grad, time_grad, class_grad)


def solution(mesh):
    in_specs = (
        P("row", "col", None),
        P(),
        P(),
        P(),
        P("row", "col"),
        P("row", "col", None),
        P("row", "col", None),
        P("row", "col", None),
    )
    out_specs = (P("row", "col", None), P(), P(), P())
    return jax.shard_map(
        per_device, mesh=mesh, in_specs=in_specs, out_specs=out_specs, check_vma=False
    )
```

profile of v0, /device:TPU:1, one launch (start us, length us, event | category | flops | bytes accessed | tf_op | source)
XLA Modules:
  0.0 247.5 jit_solution(10021036725478528957)
XLA Ops:
  8.0 3.9 %collective-permute-start = (bf16[1,16,768]{2,1,0:T(8,128)(2,1)S(1)}, bf16[1,16,768]{2,1,0:T(8,128)(2,1)S(1)}, u32[]{:S(2)}, u32[]{:S(2)}) collective-permute-start(bf16[1,16,768]{2,1,0:T(8,128)(2,1)S(1)} %get-tuple-element.38), channel_id=1, source_target_pairs={{0,8},{8,16},{16,24},{24,32},{32,40},{40,48},{48,56},{56,64},{64,7... | collective-permute-start | bytes 73736 | tf_op jit(solution)/shard_map/ppermute | solution.py:28
  11.9 1.3 collective-permute-start.1
  16.6 5.2 %collective-permute-start.2 = (bf16[18,1,768]{2,1,0:T(2,128)(2,1)S(1)}, bf16[18,1,768]{2,1,0:T(2,128)(2,1)S(1)}, u32[]{:S(2)}, u32[]{:S(2)}) collective-permute-start(bf16[18,1,768]{2,1,0:T(2,128)(2,1)S(1)} %get-tuple-element.35), channel_id=1, source_target_pairs={{0,1},{1,2},{2,3},{3,4},{4,5},{5,6},{6,7},{8,9},{9,10},{10,11},{11... | collective-permute-start | bytes 82952 | tf_op jit(solution)/shard_map/ppermute | solution.py:28
  21.8 1.9 collective-permute-start.3
  25.4 1.9 collective-permute-done.3
  28.4 2.6 %fusion.81 = (bf16[16,16,12,64]{3,2,1,0:T(8,128)(2,1)S(1)}, bf16[16,16,12,64]{3,2,1,0:T(8,128)(2,1)S(1)}, bf16[16,16,12,64]{3,2,1,0:T(8,128)(2,1)S(1)}, bf16[16,...) fusion(bf16[18,18,12,64]{3,2,1,0:T(8,128)(2,1)S(1)} %reshape.91), kind=kLoop, calls=%fused_computation.148 | loop fusion | bytes 7077888 | tf_op jit(solution)/shard_map/slice | solution.py:47
  34.9 2.4 multiply_convert_fusion.2
  39.0 3.1 %collective-permute-start.4 = (bf16[1,3,32,128]{3,2,1,0:T(8,128)(2,1)S(1)}, bf16[1,3,32,128]{3,2,1,0:T(8,128)(2,1)S(1)}, u32[]{:S(2)}, u32[]{:S(2)}) collective-permute-start(bf16[1,3,32,128]{3,2,1,0:T(8,128)(2,1)S(1)} %bitcast.197), channel_id=1, source_target_pairs={{0,8},{8,16},{16,24},{24,32},{32,40},{40,48},{48,56},{56,64},{64,7... | collective-permute-start | bytes 73736 | tf_op jit(solution)/shard_map/ppermute | solution.py:28
  42.1 1.3 collective-permute-start.5
  43.5 3.3 %collective-permute-done.5 = bf16[1,3,32,128]{3,2,1,0:T(8,128)(2,1)S(1)} collective-permute-done((bf16[1,3,32,128]{3,2,1,0:T(8,128)(2,1)S(1)}, bf16[1,3,32,128]{3,2,1,0:T(8,128)(2,1)S(1)}, u32[]{:S(2)}, u32[]{:S(2)}) %collective-permute-start.5) | collective-permute-done | bytes 24608 | tf_op jit(solution)/shard_map/ppermute | solution.py:30
  46.7 3.3 %collective-permute-start.6 = (bf16[5,1,32,128]{3,2,1,0:T(8,128)(2,1)S(1)}, bf16[5,1,32,128]{3,2,1,0:T(8,128)(2,1)S(1)}, u32[]{:S(2)}, u32[]{:S(2)}) collective-permute-start(bf16[5,1,32,128]{3,2,1,0:T(8,128)(2,1)S(1)} %get-tuple-element.51), channel_id=1, source_target_pairs={{0,1},{1,2},{2,3},{3,4},{4,5},{5,6},{6,7},{8,9},{9,10},{10,11},{11... | collective-permute-start | bytes 122888 | tf_op jit(solution)/shard_map/ppermute | solution.py:28
  50.0 1.9 collective-permute-start.7
  52.6 2.8 %collective-permute-done.7 = bf16[5,1,32,128]{3,2,1,0:T(8,128)(2,1)S(1)} collective-permute-done((bf16[5,1,32,128]{3,2,1,0:T(8,128)(2,1)S(1)}, bf16[5,1,32,128]{3,2,1,0:T(8,128)(2,1)S(1)}, u32[]{:S(2)}, u32[]{:S(2)}) %collective-permute-start.7) | collective-permute-done | bytes 40992 | tf_op jit(solution)/shard_map/ppermute | solution.py:30
  56.4 4.8 %collective-permute-start.8 = (bf16[1,1,32,128]{3,2,1,0:T(8,128)(2,1)S(1)}, bf16[1,1,32,128]{3,2,1,0:T(8,128)(2,1)S(1)}, u32[]{:S(2)}, u32[]{:S(2)}) collective-permute-start(bf16[1,1,32,128]{3,2,1,0:T(8,128)(2,1)S(1)} %fusion.60), channel_id=1, source_target_pairs={{0,8},{8,16},{16,24},{24,32},{32,40},{40,48},{48,56},{56,64},{64,7... | collective-permute-start | bytes 24584 | tf_op jit(solution)/shard_map/ppermute | solution.py:28
  61.2 1.3 collective-permute-start.9
  62.5 3.4 %collective-permute-done.9 = bf16[1,1,32,128]{3,2,1,0:T(8,128)(2,1)S(1)} collective-permute-done((bf16[1,1,32,128]{3,2,1,0:T(8,128)(2,1)S(1)}, bf16[1,1,32,128]{3,2,1,0:T(8,128)(2,1)S(1)}, u32[]{:S(2)}, u32[]{:S(2)}) %collective-permute-start.9) | collective-permute-done | bytes 8224 | tf_op jit(solution)/shard_map/ppermute | solution.py:30
  65.8 3.0 %collective-permute-start.10 = (bf16[3,1,32,128]{3,2,1,0:T(8,128)(2,1)S(1)}, bf16[3,1,32,128]{3,2,1,0:T(8,128)(2,1)S(1)}, u32[]{:S(2)}, u32[]{:S(2)}) collective-permute-start(bf16[3,1,32,128]{3,2,1,0:T(8,128)(2,1)S(1)} %pad_maximum_fusion.18), channel_id=1, source_target_pairs={{0,1},{1,2},{2,3},{3,4},{4,5},{5,6},{6,7},{8,9},{9,10},{10,11},{11... | collective-permute-start | bytes 73736 | tf_op jit(solution)/shard_map/ppermute | solution.py:28
  68.9 2.1 collective-permute-start.11
  71.2 2.8 %collective-permute-done.11 = bf16[3,1,32,128]{3,2,1,0:T(8,128)(2,1)S(1)} collective-permute-done((bf16[3,1,32,128]{3,2,1,0:T(8,128)(2,1)S(1)}, bf16[3,1,32,128]{3,2,1,0:T(8,128)(2,1)S(1)}, u32[]{:S(2)}, u32[]{:S(2)}) %collective-permute-start.11) | collective-permute-done | bytes 24608 | tf_op jit(solution)/shard_map/ppermute | solution.py:30
  79.7 1.2 fusion.23
  81.3 1.2 fusion.21
  82.9 1.2 fusion.20
  87.3 5.1 %collective-permute-start.12 = (bf16[1,16,1536]{2,1,0:T(8,128)(2,1)S(1)}, bf16[1,16,1536]{2,1,0:T(8,128)(2,1)S(1)}, u32[]{:S(2)}, u32[]{:S(2)}) collective-permute-start(bf16[1,16,1536]{2,1,0:T(8,128)(2,1)S(1)} %bitcast.193), channel_id=1, source_target_pairs={{0,8},{8,16},{16,24},{24,32},{32,40},{40,48},{48,56},{56,64},{64,7... | collective-permute-start | bytes 147464 | tf_op jit(solution)/shard_map/ppermute | solution.py:28
  93.4 1.3 collective-permute-start.13
  94.8 3.7 %collective-permute-done.13 = bf16[1,16,1536]{2,1,0:T(8,128)(2,1)S(1)} collective-permute-done((bf16[1,16,1536]{2,1,0:T(8,128)(2,1)S(1)}, bf16[1,16,1536]{2,1,0:T(8,128)(2,1)S(1)}, u32[]{:S(2)}, u32[]{:S(2)}) %collective-permute-start.13) | collective-permute-done | bytes 49184 | tf_op jit(solution)/shard_map/ppermute | solution.py:30
  98.7 3.1 %collective-permute-start.14 = (bf16[18,1,1536]{2,1,0:T(2,128)(2,1)S(1)}, bf16[18,1,1536]{2,1,0:T(2,128)(2,1)S(1)}, u32[]{:S(2)}, u32[]{:S(2)}) collective-permute-start(bf16[18,1,1536]{2,1,0:T(2,128)(2,1)S(1)} %get-tuple-element.31), channel_id=1, source_target_pairs={{0,1},{1,2},{2,3},{3,4},{4,5},{5,6},{6,7},{8,9},{9,10},{10,11},{11... | collective-permute-start | bytes 165896 | tf_op jit(solution)/shard_map/ppermute | solution.py:28
  101.8 1.9 collective-permute-start.15
  103.7 69.4 %all-reduce.2 = (f32[3,16,8,8]{1,3,2,0:T(8,128)}, f32[128,20]{0,1:T(8,128)}) all-reduce(f32[3,16,8,8]{1,3,2,0:T(8,128)S(1)} %pad_maximum_fusion.13, f32[128,20]{0,1:T(8,128)S(1)} %fusion.63), channel_id=1, replica_groups=mesh['row'=16,'col'=8] {'row','col'}, use_global_device_ids=true, to_apply=%region_8.9 | all-reduce | flops 5632 | bytes 45056 | tf_op jit(solution)/shard_map/psum | solution.py:173
  174.5 2.8 %fusion.80 = (bf16[16,16,12,128]{3,2,1,0:T(8,128)(2,1)S(1)}, bf16[16,16,12,128]{3,2,1,0:T(8,128)(2,1)S(1)}, bf16[16,16,12,128]{3,2,1,0:T(8,128)(2,1)S(1)}, bf16[...) fusion(bf16[18,18,12,128]{3,2,1,0:T(8,128)(2,1)S(1)} %reshape.95), kind=kLoop, calls=%fused_computation.147 | loop fusion | bytes 14155776 | tf_op jit(solution)/shard_map/slice | solution.py:66
  182.2 1.4 reshape.96
  183.6 55.3 %all-reduce.5.cloned.1.call-done = f32[3,3,64,128]{3,2,1,0:T(8,128)} async-done(((f32[3,3,64,128]{3,2,1,0:T(8,128)}), f32[3,3,64,128]{3,2,1,0:T(8,128)}) %all-reduce.5.cloned.1.call-update) | async-done | bytes 294928 | tf_op jit(solution)/shard_map/psum | solution.py:204
  239.0 1.7 copy.92
  (169 shorter events, 31.0 us)
Async XLA Ops:
  7.2 48.6 %copy-start = (bf16[128,20]{0,1:T(8,128)(2,1)S(1)}, bf16[128,20]{0,1:T(8,128)(2,1)}, u32[]{:S(2)}) copy-start(bf16[128,20]{0,1:T(8,128)(2,1)} %param.11) | copy-start | bytes 15364
  7.2 231.8 %all-reduce.5.cloned.1.call-start = ((), (), s32[]{:S(2)}) async-start(), calls=%async_computation | async-start | bytes 589824 | tf_op jit(solution)/shard_map/psum | solution.py:204
  8.0 7.9 %collective-permute-start = (bf16[1,16,768]{2,1,0:T(8,128)(2,1)S(1)}, bf16[1,16,768]{2,1,0:T(8,128)(2,1)S(1)}, u32[]{:S(2)}, u32[]{:S(2)}) collective-permute-start(bf16[1,16,768]{2,1,0:T(8,128)(2,1)S(1)} %get-tuple-element.38), channel_id=1, source_target_pairs={{0,8},{8,16},{16,24},{24,32},{32,40},{40,48},{48,56},{56,64},{64,7... | collective-permute-start | bytes 73736 | tf_op jit(solution)/shard_map/ppermute | solution.py:28
  11.9 4.6 %collective-permute-start.1 = (bf16[1,16,768]{2,1,0:T(8,128)(2,1)S(1)}, bf16[1,16,768]{2,1,0:T(8,128)(2,1)S(1)}, u32[]{:S(2)}, u32[]{:S(2)}) collective-permute-start(bf16[1,16,768]{2,1,0:T(8,128)(2,1)S(1)} %get-tuple-element.37), channel_id=1, source_target_pairs={{8,0},{16,8},{24,16},{32,24},{40,32},{48,40},{56,48},{64,56},{72,6... | collective-permute-start | bytes 73736 | tf_op jit(solution)/shard_map/ppermute | solution.py:30
  15.9 9.4 %copy-start.27 = (s32[16,16]{1,0:T(8,128)S(1)}, s32[16,16]{1,0:T(8,128)}, u32[]{:S(2)}) copy-start(s32[16,16]{1,0:T(8,128)} %param.12) | copy-start | bytes 3076
  16.6 8.8 %collective-permute-start.2 = (bf16[18,1,768]{2,1,0:T(2,128)(2,1)S(1)}, bf16[18,1,768]{2,1,0:T(2,128)(2,1)S(1)}, u32[]{:S(2)}, u32[]{:S(2)}) collective-permute-start(bf16[18,1,768]{2,1,0:T(2,128)(2,1)S(1)} %get-tuple-element.35), channel_id=1, source_target_pairs={{0,1},{1,2},{2,3},{3,4},{4,5},{5,6},{6,7},{8,9},{9,10},{10,11},{11... | collective-permute-start | bytes 82952 | tf_op jit(solution)/shard_map/ppermute | solution.py:28
  21.8 5.5 %collective-permute-start.3 = (bf16[18,1,768]{2,1,0:T(2,128)(2,1)S(1)}, bf16[18,1,768]{2,1,0:T(2,128)(2,1)S(1)}, u32[]{:S(2)}, u32[]{:S(2)}) collective-permute-start(bf16[18,1,768]{2,1,0:T(2,128)(2,1)S(1)} %get-tuple-element.36), channel_id=1, source_target_pairs={{1,0},{2,1},{3,2},{4,3},{5,4},{6,5},{7,6},{9,8},{10,9},{11,10},{12... | collective-permute-start | bytes 82952 | tf_op jit(solution)/shard_map/ppermute | solution.py:30
  31.2 1.8 copy-start.2
  31.9 2.0 copy-start.12
  32.1 1.8 copy-start.14
  32.4 1.6 copy-start.18
  32.6 2.2 copy-start.8
  32.8 2.0 copy-start.10
  33.0 1.8 copy-start.16
  37.9 14.1 %copy-start.20 = (bf16[3,3,64,128]{3,2,1,0:T(8,128)(2,1)S(1)}, bf16[3,3,64,128]{3,2,1,0:T(8,128)(2,1)}, u32[]{:S(2)}) copy-start(bf16[3,3,64,128]{3,2,1,0:T(8,128)(2,1)} %param.9) | copy-start | bytes 442372
  38.6 17.4 %copy-start.30 = (s32[1,1,32]{2,1,0:T(1,128)S(1)}, s32[1,1,32]{2,1,0:T(1,128)}, u32[]{:S(2)}) copy-start(s32[1,1,32]{2,1,0:T(1,128)} %param.15) | copy-start | bytes 388
  39.0 4.4 %collective-permute-start.4 = (bf16[1,3,32,128]{3,2,1,0:T(8,128)(2,1)S(1)}, bf16[1,3,32,128]{3,2,1,0:T(8,128)(2,1)S(1)}, u32[]{:S(2)}, u32[]{:S(2)}) collective-permute-start(bf16[1,3,32,128]{3,2,1,0:T(8,128)(2,1)S(1)} %bitcast.197), channel_id=1, source_target_pairs={{0,8},{8,16},{16,24},{24,32},{32,40},{40,48},{48,56},{56,64},{64,7... | collective-permute-start | bytes 73736 | tf_op jit(solution)/shard_map/ppermute | solution.py:28
  42.1 4.6 %collective-permute-start.5 = (bf16[1,3,32,128]{3,2,1,0:T(8,128)(2,1)S(1)}, bf16[1,3,32,128]{3,2,1,0:T(8,128)(2,1)S(1)}, u32[]{:S(2)}, u32[]{:S(2)}) collective-permute-start(bf16[1,3,32,128]{3,2,1,0:T(8,128)(2,1)S(1)} %bitcast.196), channel_id=1, source_target_pairs={{8,0},{16,8},{24,16},{32,24},{40,32},{48,40},{56,48},{64,56},{72,6... | collective-permute-start | bytes 73736 | tf_op jit(solution)/shard_map/ppermute | solution.py:30
  46.7 5.9 %collective-permute-start.6 = (bf16[5,1,32,128]{3,2,1,0:T(8,128)(2,1)S(1)}, bf16[5,1,32,128]{3,2,1,0:T(8,128)(2,1)S(1)}, u32[]{:S(2)}, u32[]{:S(2)}) collective-permute-start(bf16[5,1,32,128]{3,2,1,0:T(8,128)(2,1)S(1)} %get-tuple-element.51), channel_id=1, source_target_pairs={{0,1},{1,2},{2,3},{3,4},{4,5},{5,6},{6,7},{8,9},{9,10},{10,11},{11... | collective-permute-start | bytes 122888 | tf_op jit(solution)/shard_map/ppermute | solution.py:28
  50.0 5.3 %collective-permute-start.7 = (bf16[5,1,32,128]{3,2,1,0:T(8,128)(2,1)S(1)}, bf16[5,1,32,128]{3,2,1,0:T(8,128)(2,1)S(1)}, u32[]{:S(2)}, u32[]{:S(2)}) collective-permute-start(bf16[5,1,32,128]{3,2,1,0:T(8,128)(2,1)S(1)} %get-tuple-element.52), channel_id=1, source_target_pairs={{1,0},{2,1},{3,2},{4,3},{5,4},{6,5},{7,6},{9,8},{10,9},{11,10},{12... | collective-permute-start | bytes 122888 | tf_op jit(solution)/shard_map/ppermute | solution.py:30
  56.4 6.1 %collective-permute-start.8 = (bf16[1,1,32,128]{3,2,1,0:T(8,128)(2,1)S(1)}, bf16[1,1,32,128]{3,2,1,0:T(8,128)(2,1)S(1)}, u32[]{:S(2)}, u32[]{:S(2)}) collective-permute-start(bf16[1,1,32,128]{3,2,1,0:T(8,128)(2,1)S(1)} %fusion.60), channel_id=1, source_target_pairs={{0,8},{8,16},{16,24},{24,32},{32,40},{40,48},{48,56},{56,64},{64,7... | collective-permute-start | bytes 24584 | tf_op jit(solution)/shard_map/ppermute | solution.py:28
  61.2 4.7 %collective-permute-start.9 = (bf16[1,1,32,128]{3,2,1,0:T(8,128)(2,1)S(1)}, bf16[1,1,32,128]{3,2,1,0:T(8,128)(2,1)S(1)}, u32[]{:S(2)}, u32[]{:S(2)}) collective-permute-start(bf16[1,1,32,128]{3,2,1,0:T(8,128)(2,1)S(1)} %fusion.60), channel_id=1, source_target_pairs={{8,0},{16,8},{24,16},{32,24},{40,32},{48,40},{56,48},{64,56},{72,6... | collective-permute-start | bytes 24584 | tf_op jit(solution)/shard_map/ppermute | solution.py:30
  65.8 5.4 %collective-permute-start.10 = (bf16[3,1,32,128]{3,2,1,0:T(8,128)(2,1)S(1)}, bf16[3,1,32,128]{3,2,1,0:T(8,128)(2,1)S(1)}, u32[]{:S(2)}, u32[]{:S(2)}) collective-permute-start(bf16[3,1,32,128]{3,2,1,0:T(8,128)(2,1)S(1)} %pad_maximum_fusion.18), channel_id=1, source_target_pairs={{0,1},{1,2},{2,3},{3,4},{4,5},{5,6},{6,7},{8,9},{9,10},{10,11},{11... | collective-permute-start | bytes 73736 | tf_op jit(solution)/shard_map/ppermute | solution.py:28
  68.9 5.1 %collective-permute-start.11 = (bf16[3,1,32,128]{3,2,1,0:T(8,128)(2,1)S(1)}, bf16[3,1,32,128]{3,2,1,0:T(8,128)(2,1)S(1)}, u32[]{:S(2)}, u32[]{:S(2)}) collective-permute-start(bf16[3,1,32,128]{3,2,1,0:T(8,128)(2,1)S(1)} %pad_maximum_fusion.18), channel_id=1, source_target_pairs={{1,0},{2,1},{3,2},{4,3},{5,4},{6,5},{7,6},{9,8},{10,9},{11,10},{12... | collective-permute-start | bytes 73736 | tf_op jit(solution)/shard_map/ppermute | solution.py:30
  78.1 1.6 copy-start.19
  79.7 1.6 copy-start.7
  81.3 1.6 copy-start.17
  87.3 7.4 %collective-permute-start.12 = (bf16[1,16,1536]{2,1,0:T(8,128)(2,1)S(1)}, bf16[1,16,1536]{2,1,0:T(8,128)(2,1)S(1)}, u32[]{:S(2)}, u32[]{:S(2)}) collective-permute-start(bf16[1,16,1536]{2,1,0:T(8,128)(2,1)S(1)} %bitcast.193), channel_id=1, source_target_pairs={{0,8},{8,16},{16,24},{24,32},{32,40},{40,48},{48,56},{56,64},{64,7... | collective-permute-start | bytes 147464 | tf_op jit(solution)/shard_map/ppermute | solution.py:28
  93.4 5.1 %collective-permute-start.13 = (bf16[1,16,1536]{2,1,0:T(8,128)(2,1)S(1)}, bf16[1,16,1536]{2,1,0:T(8,128)(2,1)S(1)}, u32[]{:S(2)}, u32[]{:S(2)}) collective-permute-start(bf16[1,16,1536]{2,1,0:T(8,128)(2,1)S(1)} %bitcast.194), channel_id=1, source_target_pairs={{8,0},{16,8},{24,16},{32,24},{40,32},{48,40},{56,48},{64,56},{72,6... | collective-permute-start | bytes 147464 | tf_op jit(solution)/shard_map/ppermute | solution.py:30
  98.7 74.4 %collective-permute-start.14 = (bf16[18,1,1536]{2,1,0:T(2,128)(2,1)S(1)}, bf16[18,1,1536]{2,1,0:T(2,128)(2,1)S(1)}, u32[]{:S(2)}, u32[]{:S(2)}) collective-permute-start(bf16[18,1,1536]{2,1,0:T(2,128)(2,1)S(1)} %get-tuple-element.31), channel_id=1, source_target_pairs={{0,1},{1,2},{2,3},{3,4},{4,5},{5,6},{6,7},{8,9},{9,10},{10,11},{11... | collective-permute-start | bytes 165896 | tf_op jit(solution)/shard_map/ppermute | solution.py:28
  101.8 71.3 %collective-permute-start.15 = (bf16[18,1,1536]{2,1,0:T(2,128)(2,1)S(1)}, bf16[18,1,1536]{2,1,0:T(2,128)(2,1)S(1)}, u32[]{:S(2)}, u32[]{:S(2)}) collective-permute-start(bf16[18,1,1536]{2,1,0:T(2,128)(2,1)S(1)} %get-tuple-element.32), channel_id=1, source_target_pairs={{1,0},{2,1},{3,2},{4,3},{5,4},{6,5},{7,6},{9,8},{10,9},{11,10},{12... | collective-permute-start | bytes 165896 | tf_op jit(solution)/shard_map/ppermute | solution.py:30
  181.2 59.5 %copy-start.1 = (bf16[128,20]{0,1:T(8,128)(2,1)S(1)}, bf16[128,20]{0,1:T(8,128)(2,1)}, u32[]{:S(2)}) copy-start(bf16[128,20]{0,1:T(8,128)(2,1)} %param.11) | copy-start | bytes 15364
  (17 other events, 18.1 us)
Sparse Core Ops, SparseCore 0:
  93.5 145.4 all-reduce.4
where the time goes:
time: 248 us; the launch traced here: 247 us
  waiting for transfers between devices  73.4 us (30%)
  blocking collectives  69.4 us (28%)
  starting transfers between devices  44.5 us (18%)
  local copies, waits for them, and re-layouts  25.2 us (10%)
  matrix products  17 us (7%)
  between operations  15 us (6%)
  other arithmetic  3.07 us (1%)
    psum x1, blocking collectives, per_device(): time_grad = lax.psum(time_term, ('row', 'col'))  69.4 us
    psum x1, waiting for transfers between devices, per_device(): conv_grad = lax.psum(conv_term, ('row', 'col'))  55.3 us
    ppermute x8, starting transfers between devices, with_halo(): lax.ppermute(tail, axis, [(i, (i + 1) % count) for i in range(ends)])  31.5 us
    ppermute x8, waiting for transfers between devices, with_halo(): lax.ppermute(head, axis, [((i + 1) % count, i) for i in range(ends)])  18 us
    ppermute x8, starting transfers between devices, with_halo(): lax.ppermute(head, axis, [((i + 1) % count, i) for i in range(ends)])  13 us
    unnamed x88, local copies, waits for them, and re-layouts  9.2 us
  transfers between devices with their start and end apart: 17, of which 8 were waited for; matrix products, arithmetic and copies ran while one was open for 6% of the time, Pallas kernels for 0%

commit v1 on v0

--- a/solution.py
+++ b/solution.py
@@ -32,6 +32,16 @@
             axis=dim,
         )
     return cells
+
+
+def butterfly_sum(flat):
+    for axis in ("col", "row"):
+        size = lax.axis_size(axis)
+        bit = 1
+        while bit < size:
+            flat = flat + lax.ppermute(flat, axis, [(i, i ^ bit) for i in range(size)])
+            bit *= 2
+    return flat
 
 
 def silu_slope(value):
@@ -137,7 +147,6 @@
     parcel_total = P_OWN * lax.axis_size("row") * lax.axis_size("col")
     grad_logits = (probability - label_hot) / parcel_total
     class_term = jnp.dot(rounded.astype(jnp.float32).T, grad_logits, precision=PRECISE)
-    class_grad = lax.psum(class_term, ("row", "col"))
     grad_normed = jnp.dot(grad_logits, class_weight.astype(jnp.float32).T, precision=PRECISE)
     parcel_grad = (
         inverse
@@ -170,7 +179,6 @@
         reshaped = dense_grad.reshape(GROUPS, CPG, GROUPS, CPG)
         time_taps.append(jnp.einsum("gchd,gh->gcd", reshaped, group_eye, precision=PRECISE))
     time_term = jnp.stack(time_taps)
-    time_grad = lax.psum(time_term, ("row", "col"))
     padded_mixed = jnp.pad(grad_mixed, ((0, 0), (0, 0), (1, 1), (0, 0)))
     grad_hidden = None
     for time_tap in range(3):
@@ -201,7 +209,13 @@
     ).reshape(tile_rows + 2, tile_cols + 2, DATES, C_OUT)
     input_sum = transposed_conv(padded_grad, conv_weight, tile_rows, tile_cols)
     input_grad = input_sum.astype(jnp.bfloat16).reshape(tile_rows, tile_cols, DATES * C_IN)
-    conv_grad = lax.psum(conv_term, ("row", "col"))
+    flat = butterfly_sum(
+        jnp.concatenate([conv_term.reshape(-1), time_term.reshape(-1), class_term.reshape(-1)])
+    )
+    conv_size, time_size = (conv_term.size, time_term.size)
+    conv_grad = flat[:conv_size].reshape(conv_term.shape)
+    time_grad = flat[conv_size : conv_size + time_size].reshape(time_term.shape)
+    class_grad = flat[conv_size + time_size :].reshape(class_term.shape)
     return (input_grad, conv_grad, time_grad, class_grad)
 
 

time: 248 us -> 151 us (0.61)
  the two profiles are of different devices: /device:TPU:1 before, /device:TPU:0 now
where the time goes in v1:
time: 151 us
  starting transfers between devices  71.4 us (47%)
  waiting for transfers between devices  32.3 us (21%)
  local copies, waits for them, and re-layouts  25.5 us (17%)
  matrix products  17.1 us (11%)
  other arithmetic  2.69 us (2%)
  between operations  1.63 us (1%)
    ppermute x7, starting transfers between devices, butterfly_sum(): flat = flat + lax.ppermute(flat, axis, [(i, i ^ bit) for i in range(size)])  32.5 us
    ppermute x8, starting transfers between devices, with_halo(): lax.ppermute(tail, axis, [(i, (i + 1) % count) for i in range(ends)])  28.6 us
    ppermute x7, waiting for transfers between devices, butterfly_sum(): flat = flat + lax.ppermute(flat, axis, [(i, i ^ bit) for i in range(size)])  20.4 us
    ppermute x8, starting transfers between devices, with_halo(): lax.ppermute(head, axis, [((i + 1) % count, i) for i in range(ends)])  10.3 us
    unnamed x79, local copies, waits for them, and re-layouts  9.2 us
    ppermute x8, waiting for transfers between devices, with_halo(): lax.ppermute(head, axis, [((i + 1) % count, i) for i in range(ends)])  8.49 us
    dot_general x3, matrix products, spatial_forward(): jnp.dot(tap_patch, conv_weight[row_tap].reshape(3 * C_IN, C_OUT), preferr...  4.1 us
    dot_general x3, matrix products, per_device(): jnp.einsum('ijtc,ijtd->cd', tap_patch, grad_pre, preferred_element_type=j...  3.57 us
  transfers between devices with their start and end apart: 23, of which 13 were waited for; matrix products, arithmetic and copies ran while one was open for 10% of the time, Pallas kernels for 0%

profile of v1, /device:TPU:0, one launch (start us, length us, event | category | flops | bytes accessed | tf_op | source)
XLA Modules:
  0.0 150.6 jit_solution(6136455541633932681)
XLA Ops:
  2.7 4.5 %collective-permute-start = (bf16[1,16,768]{2,1,0:T(8,128)(2,1)S(1)}, bf16[1,16,768]{2,1,0:T(8,128)(2,1)S(1)}, u32[]{:S(2)}, u32[]{:S(2)}) collective-permute-start(bf16[1,16,768]{2,1,0:T(8,128)(2,1)S(1)} %get-tuple-element.40), channel_id=1, source_target_pairs={{0,8},{8,16},{16,24},{24,32},{32,40},{40,48},{48,56},{56,64},{64,7... | collective-permute-start | bytes 73736 | tf_op jit(solution)/shard_map/ppermute | solution.py:28
  10.5 1.3 collective-permute-start.2
  11.8 1.3 collective-permute-start.3
  14.7 2.1 %collective-permute-done.3 = bf16[18,1,768]{2,1,0:T(2,128)(2,1)S(1)} collective-permute-done((bf16[18,1,768]{2,1,0:T(2,128)(2,1)S(1)}, bf16[18,1,768]{2,1,0:T(2,128)(2,1)S(1)}, u32[]{:S(2)}, u32[]{:S(2)}) %collective-permute-start.3) | collective-permute-done | bytes 27680 | tf_op jit(solution)/shard_map/ppermute | solution.py:30
  17.9 2.6 %fusion.82 = (bf16[16,16,12,64]{3,2,1,0:T(8,128)(2,1)S(1)}, bf16[16,16,12,64]{3,2,1,0:T(8,128)(2,1)S(1)}, bf16[16,16,12,64]{3,2,1,0:T(8,128)(2,1)S(1)}, bf16[16,...) fusion(bf16[18,18,12,64]{3,2,1,0:T(8,128)(2,1)S(1)} %reshape.115), kind=kLoop, calls=%fused_computation.150 | loop fusion | bytes 7077888 | tf_op jit(solution)/shard_map/slice | solution.py:57
  25.0 2.4 %multiply_convert_fusion.2 = (bf16[16,16,12,128]{3,1,2,0:T(8,128)(2,1)S(1)}, f32[16,16,12,128]{3,1,2,0:T(8,128)}) fusion(bf16[192,128,1,1]{1,0,3,2:T(8,128)(2,1)S(1)} %bitcast.200, bf16[16,16,12,64]{3,1,2,0:T(8,128)(2,1)S(1)} %copy.67, bf16[16,16,12,64]{3,1,2,0:T(8,128)(2,1)S(1)} %copy.66, bf16[16,16,12,64]{3,1,2,0:T(8,128)(2,1)S(1)} %copy.65, ...), kind=kOutput, calls=%fused_computation.28 | convolution fusion | flops 157286400 | bytes 6733824 | tf_op jit(solution)/shard_map/dot_general | solution.py:62
  29.1 1.3 collective-permute-start.5
  30.4 4.5 %collective-permute-start.4 = (bf16[1,3,32,128]{3,2,1,0:T(8,128)(2,1)S(1)}, bf16[1,3,32,128]{3,2,1,0:T(8,128)(2,1)S(1)}, u32[]{:S(2)}, u32[]{:S(2)}) collective-permute-start(bf16[1,3,32,128]{3,2,1,0:T(8,128)(2,1)S(1)} %bitcast.206), channel_id=1, source_target_pairs={{0,8},{8,16},{16,24},{24,32},{32,40},{40,48},{48,56},{56,64},{64,7... | collective-permute-start | bytes 73736 | tf_op jit(solution)/shard_map/ppermute | solution.py:28
  35.0 1.5 collective-permute-done.4
  36.5 3.6 %collective-permute-start.6 = (bf16[5,1,32,128]{3,2,1,0:T(8,128)(2,1)S(1)}, bf16[5,1,32,128]{3,2,1,0:T(8,128)(2,1)S(1)}, u32[]{:S(2)}, u32[]{:S(2)}) collective-permute-start(bf16[5,1,32,128]{3,2,1,0:T(8,128)(2,1)S(1)} %get-tuple-element.53), channel_id=1, source_target_pairs={{0,1},{1,2},{2,3},{3,4},{4,5},{5,6},{6,7},{8,9},{9,10},{10,11},{11... | collective-permute-start | bytes 122888 | tf_op jit(solution)/shard_map/ppermute | solution.py:28
  40.1 1.3 collective-permute-start.7
  41.4 2.4 %collective-permute-done.7 = bf16[5,1,32,128]{3,2,1,0:T(8,128)(2,1)S(1)} collective-permute-done((bf16[5,1,32,128]{3,2,1,0:T(8,128)(2,1)S(1)}, bf16[5,1,32,128]{3,2,1,0:T(8,128)(2,1)S(1)}, u32[]{:S(2)}, u32[]{:S(2)}) %collective-permute-start.7) | collective-permute-done | bytes 40992 | tf_op jit(solution)/shard_map/ppermute | solution.py:30
  46.2 4.8 %collective-permute-start.8 = (bf16[1,1,32,128]{3,2,1,0:T(8,128)(2,1)S(1)}, bf16[1,1,32,128]{3,2,1,0:T(8,128)(2,1)S(1)}, u32[]{:S(2)}, u32[]{:S(2)}) collective-permute-start(bf16[1,1,32,128]{3,2,1,0:T(8,128)(2,1)S(1)} %fusion.60), channel_id=1, source_target_pairs={{0,8},{8,16},{16,24},{24,32},{32,40},{40,48},{48,56},{56,64},{64,7... | collective-permute-start | bytes 24584 | tf_op jit(solution)/shard_map/ppermute | solution.py:28
  51.0 1.3 collective-permute-done.8
  53.6 4.6 %collective-permute-start.10 = (bf16[3,1,32,128]{3,2,1,0:T(8,128)(2,1)S(1)}, bf16[3,1,32,128]{3,2,1,0:T(8,128)(2,1)S(1)}, u32[]{:S(2)}, u32[]{:S(2)}) collective-permute-start(bf16[3,1,32,128]{3,2,1,0:T(8,128)(2,1)S(1)} %pad_maximum_fusion.19), channel_id=1, source_target_pairs={{0,1},{1,2},{2,3},{3,4},{4,5},{5,6},{6,7},{8,9},{9,10},{10,11},{11... | collective-permute-start | bytes 73736 | tf_op jit(solution)/shard_map/ppermute | solution.py:28
  72.3 1.9 %collective-permute-start.16 = (f32[79360]{0:T(1024)S(1)}, f32[79360]{0:T(1024)S(1)}, u32[]{:S(2)}, u32[]{:S(2)}) collective-permute-start(f32[79360]{0:T(1024)S(1)} %pad_maximum_fusion.5), channel_id=1, source_target_pairs={{0,1},{1,0},{2,3},{3,2},{4,5},{5,4},{6,7},{7,6},{8,9},{9,8},{10,11... | collective-permute-start | bytes 952328 | tf_op jit(solution)/shard_map/ppermute | solution.py:42
  74.2 3.9 %collective-permute-start.12 = (bf16[1,16,1536]{2,1,0:T(8,128)(2,1)S(1)}, bf16[1,16,1536]{2,1,0:T(8,128)(2,1)S(1)}, u32[]{:S(2)}, u32[]{:S(2)}) collective-permute-start(bf16[1,16,1536]{2,1,0:T(8,128)(2,1)S(1)} %bitcast.204), channel_id=1, source_target_pairs={{0,8},{8,16},{16,24},{24,32},{32,40},{40,48},{48,56},{56,64},{64,7... | collective-permute-start | bytes 147464 | tf_op jit(solution)/shard_map/ppermute | solution.py:28
  79.9 2.3 %collective-permute-start.17 = (f32[79360]{0:T(1024)S(1)}, f32[79360]{0:T(1024)S(1)}, u32[]{:S(2)}, u32[]{:S(2)}) collective-permute-start(f32[79360]{0:T(1024)S(1)} %fusion.78), channel_id=1, source_target_pairs={{0,2},{1,3},{2,0},{3,1},{4,6},{5,7},{6,4},{7,5},{8,10},{9,11},{10,... | collective-permute-start | bytes 952328 | tf_op jit(solution)/shard_map/ppermute | solution.py:42
  82.3 3.9 %collective-permute-done.13 = bf16[1,16,1536]{2,1,0:T(8,128)(2,1)S(1)} collective-permute-done((bf16[1,16,1536]{2,1,0:T(8,128)(2,1)S(1)}, bf16[1,16,1536]{2,1,0:T(8,128)(2,1)S(1)}, u32[]{:S(2)}, u32[]{:S(2)}) %collective-permute-start.13) | collective-permute-done | bytes 49184 | tf_op jit(solution)/shard_map/ppermute | solution.py:30
  86.2 3.5 %collective-permute-done.17 = f32[79360]{0:T(1024)S(1)} collective-permute-done((f32[79360]{0:T(1024)S(1)}, f32[79360]{0:T(1024)S(1)}, u32[]{:S(2)}, u32[]{:S(2)}) %collective-permute-start.17) | collective-permute-done | bytes 317472 | tf_op jit(solution)/shard_map/ppermute | solution.py:42
  89.8 3.5 %collective-permute-start.18 = (f32[79360]{0:T(1024)S(1)}, f32[79360]{0:T(1024)S(1)}, u32[]{:S(2)}, u32[]{:S(2)}) collective-permute-start(f32[79360]{0:T(1024)S(1)} %add.106), channel_id=1, source_target_pairs={{0,4},{1,5},{2,6},{3,7},{4,0},{5,1},{6,2},{7,3},{8,12},{9,13},{10,... | collective-permute-start | bytes 952328 | tf_op jit(solution)/shard_map/ppermute | solution.py:42
  93.5 1.3 collective-permute-start.14
  96.1 5.2 %collective-permute-done.18 = f32[79360]{0:T(1024)S(1)} collective-permute-done((f32[79360]{0:T(1024)S(1)}, f32[79360]{0:T(1024)S(1)}, u32[]{:S(2)}, u32[]{:S(2)}) %collective-permute-start.18) | collective-permute-done | bytes 317472 | tf_op jit(solution)/shard_map/ppermute | solution.py:42
  101.3 5.4 %collective-permute-start.19 = (f32[79360]{0:T(1024)S(1)}, f32[79360]{0:T(1024)S(1)}, u32[]{:S(2)}, u32[]{:S(2)}) collective-permute-start(f32[79360]{0:T(1024)S(1)} %add.107), channel_id=1, source_target_pairs={{0,8},{8,0},{16,24},{24,16},{32,40},{40,32},{48,56},{56,48},{64,72... | collective-permute-start | bytes 952328 | tf_op jit(solution)/shard_map/ppermute | solution.py:42
  108.2 3.8 %collective-permute-done.19 = f32[79360]{0:T(1024)S(1)} collective-permute-done((f32[79360]{0:T(1024)S(1)}, f32[79360]{0:T(1024)S(1)}, u32[]{:S(2)}, u32[]{:S(2)}) %collective-permute-start.19) | collective-permute-done | bytes 317472 | tf_op jit(solution)/shard_map/ppermute | solution.py:42
  112.0 9.6 %collective-permute-start.20 = (f32[79360]{0:T(1024)S(1)}, f32[79360]{0:T(1024)S(1)}, u32[]{:S(2)}, u32[]{:S(2)}) collective-permute-start(f32[79360]{0:T(1024)S(1)} %add.108), channel_id=1, source_target_pairs={{0,16},{8,24},{16,0},{24,8},{32,48},{40,56},{48,32},{56,40},{64,80... | collective-permute-start | bytes 952328 | tf_op jit(solution)/shard_map/ppermute | solution.py:42
  121.6 2.8 %fusion.81 = (bf16[16,16,12,128]{3,2,1,0:T(8,128)(2,1)S(1)}, bf16[16,16,12,128]{3,2,1,0:T(8,128)(2,1)S(1)}, bf16[16,16,12,128]{3,2,1,0:T(8,128)(2,1)S(1)}, bf16[...) fusion(bf16[18,18,12,128]{3,2,1,0:T(8,128)(2,1)S(1)} %reshape.119), kind=kLoop, calls=%fused_computation.149 | loop fusion | bytes 14155776 | tf_op jit(solution)/shard_map/slice | solution.py:76
  127.1 3.6 %collective-permute-start.21 = (f32[79360]{0:T(1024)S(1)}, f32[79360]{0:T(1024)S(1)}, u32[]{:S(2)}, u32[]{:S(2)}) collective-permute-start(f32[79360]{0:T(1024)S(1)} %add.109), channel_id=1, source_target_pairs={{0,32},{8,40},{16,48},{24,56},{32,0},{40,8},{48,16},{56,24},{64,96... | collective-permute-start | bytes 952328 | tf_op jit(solution)/shard_map/ppermute | solution.py:42
  132.3 4.7 %collective-permute-done.21 = f32[79360]{0:T(1024)S(1)} collective-permute-done((f32[79360]{0:T(1024)S(1)}, f32[79360]{0:T(1024)S(1)}, u32[]{:S(2)}, u32[]{:S(2)}) %collective-permute-start.21) | collective-permute-done | bytes 317472 | tf_op jit(solution)/shard_map/ppermute | solution.py:42
  137.0 6.1 %collective-permute-start.22 = (f32[79360]{0:T(1024)S(1)}, f32[79360]{0:T(1024)S(1)}, u32[]{:S(2)}, u32[]{:S(2)}) collective-permute-start(f32[79360]{0:T(1024)S(1)} %add.110), channel_id=1, source_target_pairs={{0,64},{8,72},{16,80},{24,88},{32,96},{40,104},{48,112},{56,120},{... | collective-permute-start | bytes 952328 | tf_op jit(solution)/shard_map/ppermute | solution.py:42
  144.3 1.4 reshape.120
  145.6 2.5 %collective-permute-done.22 = f32[79360]{0:T(1024)S(1)} collective-permute-done((f32[79360]{0:T(1024)S(1)}, f32[79360]{0:T(1024)S(1)}, u32[]{:S(2)}, u32[]{:S(2)}) %collective-permute-start.22) | collective-permute-done | bytes 317472 | tf_op jit(solution)/shard_map/ppermute | solution.py:42
  (182 shorter events, 43.9 us)
Async XLA Ops:
  0.6 43.6 %copy-start = (bf16[128,20]{0,1:T(8,128)(2,1)S(1)}, bf16[128,20]{0,1:T(8,128)(2,1)}, u32[]{:S(2)}) copy-start(bf16[128,20]{0,1:T(8,128)(2,1)} %param.11) | copy-start | bytes 15364
  1.4 8.9 %collective-permute-start.1 = (bf16[1,16,768]{2,1,0:T(8,128)(2,1)S(1)}, bf16[1,16,768]{2,1,0:T(8,128)(2,1)S(1)}, u32[]{:S(2)}, u32[]{:S(2)}) collective-permute-start(bf16[1,16,768]{2,1,0:T(8,128)(2,1)S(1)} %get-tuple-element.39), channel_id=1, source_target_pairs={{8,0},{16,8},{24,16},{32,24},{40,32},{48,40},{56,48},{64,56},{72,6... | collective-permute-start | bytes 73736 | tf_op jit(solution)/shard_map/ppermute | solution.py:30
  2.7 7.3 %collective-permute-start = (bf16[1,16,768]{2,1,0:T(8,128)(2,1)S(1)}, bf16[1,16,768]{2,1,0:T(8,128)(2,1)S(1)}, u32[]{:S(2)}, u32[]{:S(2)}) collective-permute-start(bf16[1,16,768]{2,1,0:T(8,128)(2,1)S(1)} %get-tuple-element.40), channel_id=1, source_target_pairs={{0,8},{8,16},{16,24},{24,32},{32,40},{40,48},{48,56},{56,64},{64,7... | collective-permute-start | bytes 73736 | tf_op jit(solution)/shard_map/ppermute | solution.py:28
  9.3 3.8 %copy-start.22 = (s32[16,16]{1,0:T(8,128)S(1)}, s32[16,16]{1,0:T(8,128)}, u32[]{:S(2)}) copy-start(s32[16,16]{1,0:T(8,128)} %param.12) | copy-start | bytes 3076
  10.5 4.2 %collective-permute-start.2 = (bf16[18,1,768]{2,1,0:T(2,128)(2,1)S(1)}, bf16[18,1,768]{2,1,0:T(2,128)(2,1)S(1)}, u32[]{:S(2)}, u32[]{:S(2)}) collective-permute-start(bf16[18,1,768]{2,1,0:T(2,128)(2,1)S(1)} %get-tuple-element.37), channel_id=1, source_target_pairs={{0,1},{1,2},{2,3},{3,4},{4,5},{5,6},{6,7},{8,9},{9,10},{10,11},{11... | collective-permute-start | bytes 82952 | tf_op jit(solution)/shard_map/ppermute | solution.py:28
  11.8 5.1 %collective-permute-start.3 = (bf16[18,1,768]{2,1,0:T(2,128)(2,1)S(1)}, bf16[18,1,768]{2,1,0:T(2,128)(2,1)S(1)}, u32[]{:S(2)}, u32[]{:S(2)}) collective-permute-start(bf16[18,1,768]{2,1,0:T(2,128)(2,1)S(1)} %get-tuple-element.38), channel_id=1, source_target_pairs={{1,0},{2,1},{3,2},{4,3},{5,4},{6,5},{7,6},{9,8},{10,9},{11,10},{12... | collective-permute-start | bytes 82952 | tf_op jit(solution)/shard_map/ppermute | solution.py:30
  20.8 4.1 %copy-start.2 = (bf16[16,16,12,64]{3,1,2,0:T(8,128)(2,1)}, bf16[16,16,12,64]{3,1,2,0:T(8,128)(2,1)S(1)}, u32[]{:S(2)}) copy-start(bf16[16,16,12,64]{3,1,2,0:T(8,128)(2,1)S(1)} %copy.65) | copy-start | bytes 1179652
  21.0 3.9 %copy-start.4 = (bf16[16,16,12,64]{3,1,2,0:T(8,128)(2,1)}, bf16[16,16,12,64]{3,1,2,0:T(8,128)(2,1)S(1)}, u32[]{:S(2)}) copy-start(bf16[16,16,12,64]{3,1,2,0:T(8,128)(2,1)S(1)} %copy.66) | copy-start | bytes 1179652
  21.2 2.8 %copy-start.6 = (bf16[16,16,12,64]{3,1,2,0:T(8,128)(2,1)}, bf16[16,16,12,64]{3,1,2,0:T(8,128)(2,1)S(1)}, u32[]{:S(2)}) copy-start(bf16[16,16,12,64]{3,1,2,0:T(8,128)(2,1)S(1)} %copy.64) | copy-start | bytes 1179652
  21.5 2.6 %copy-start.8 = (bf16[16,16,12,64]{3,1,2,0:T(8,128)(2,1)}, bf16[16,16,12,64]{3,1,2,0:T(8,128)(2,1)S(1)}, u32[]{:S(2)}) copy-start(bf16[16,16,12,64]{3,1,2,0:T(8,128)(2,1)S(1)} %copy.63) | copy-start | bytes 1179652
  28.0 16.4 %copy-start.25 = (s32[1,1,32]{2,1,0:T(1,128)S(1)}, s32[1,1,32]{2,1,0:T(1,128)}, u32[]{:S(2)}) copy-start(s32[1,1,32]{2,1,0:T(1,128)} %param.15) | copy-start | bytes 388
  29.1 5.9 %collective-permute-start.5 = (bf16[1,3,32,128]{3,2,1,0:T(8,128)(2,1)S(1)}, bf16[1,3,32,128]{3,2,1,0:T(8,128)(2,1)S(1)}, u32[]{:S(2)}, u32[]{:S(2)}) collective-permute-start(bf16[1,3,32,128]{3,2,1,0:T(8,128)(2,1)S(1)} %bitcast.207), channel_id=1, source_target_pairs={{8,0},{16,8},{24,16},{32,24},{40,32},{48,40},{56,48},{64,56},{72,6... | collective-permute-start | bytes 73736 | tf_op jit(solution)/shard_map/ppermute | solution.py:30
  30.4 6.1 %collective-permute-start.4 = (bf16[1,3,32,128]{3,2,1,0:T(8,128)(2,1)S(1)}, bf16[1,3,32,128]{3,2,1,0:T(8,128)(2,1)S(1)}, u32[]{:S(2)}, u32[]{:S(2)}) collective-permute-start(bf16[1,3,32,128]{3,2,1,0:T(8,128)(2,1)S(1)} %bitcast.206), channel_id=1, source_target_pairs={{0,8},{8,16},{16,24},{24,32},{32,40},{40,48},{48,56},{56,64},{64,7... | collective-permute-start | bytes 73736 | tf_op jit(solution)/shard_map/ppermute | solution.py:28
  36.5 4.9 %collective-permute-start.6 = (bf16[5,1,32,128]{3,2,1,0:T(8,128)(2,1)S(1)}, bf16[5,1,32,128]{3,2,1,0:T(8,128)(2,1)S(1)}, u32[]{:S(2)}, u32[]{:S(2)}) collective-permute-start(bf16[5,1,32,128]{3,2,1,0:T(8,128)(2,1)S(1)} %get-tuple-element.53), channel_id=1, source_target_pairs={{0,1},{1,2},{2,3},{3,4},{4,5},{5,6},{6,7},{8,9},{9,10},{10,11},{11... | collective-permute-start | bytes 122888 | tf_op jit(solution)/shard_map/ppermute | solution.py:28
  40.1 3.7 %collective-permute-start.7 = (bf16[5,1,32,128]{3,2,1,0:T(8,128)(2,1)S(1)}, bf16[5,1,32,128]{3,2,1,0:T(8,128)(2,1)S(1)}, u32[]{:S(2)}, u32[]{:S(2)}) collective-permute-start(bf16[5,1,32,128]{3,2,1,0:T(8,128)(2,1)S(1)} %get-tuple-element.54), channel_id=1, source_target_pairs={{1,0},{2,1},{3,2},{4,3},{5,4},{6,5},{7,6},{9,8},{10,9},{11,10},{12... | collective-permute-start | bytes 122888 | tf_op jit(solution)/shard_map/ppermute | solution.py:30
  44.9 6.2 %collective-permute-start.9 = (bf16[1,1,32,128]{3,2,1,0:T(8,128)(2,1)S(1)}, bf16[1,1,32,128]{3,2,1,0:T(8,128)(2,1)S(1)}, u32[]{:S(2)}, u32[]{:S(2)}) collective-permute-start(bf16[1,1,32,128]{3,2,1,0:T(8,128)(2,1)S(1)} %fusion.60), channel_id=1, source_target_pairs={{8,0},{16,8},{24,16},{32,24},{40,32},{48,40},{56,48},{64,56},{72,6... | collective-permute-start | bytes 24584 | tf_op jit(solution)/shard_map/ppermute | solution.py:30
  46.2 6.2 %collective-permute-start.8 = (bf16[1,1,32,128]{3,2,1,0:T(8,128)(2,1)S(1)}, bf16[1,1,32,128]{3,2,1,0:T(8,128)(2,1)S(1)}, u32[]{:S(2)}, u32[]{:S(2)}) collective-permute-start(bf16[1,1,32,128]{3,2,1,0:T(8,128)(2,1)S(1)} %fusion.60), channel_id=1, source_target_pairs={{0,8},{8,16},{16,24},{24,32},{32,40},{40,48},{48,56},{56,64},{64,7... | collective-permute-start | bytes 24584 | tf_op jit(solution)/shard_map/ppermute | solution.py:28
  52.4 6.3 %collective-permute-start.11 = (bf16[3,1,32,128]{3,2,1,0:T(8,128)(2,1)S(1)}, bf16[3,1,32,128]{3,2,1,0:T(8,128)(2,1)S(1)}, u32[]{:S(2)}, u32[]{:S(2)}) collective-permute-start(bf16[3,1,32,128]{3,2,1,0:T(8,128)(2,1)S(1)} %pad_maximum_fusion.19), channel_id=1, source_target_pairs={{1,0},{2,1},{3,2},{4,3},{5,4},{6,5},{7,6},{9,8},{10,9},{11,10},{12... | collective-permute-start | bytes 73736 | tf_op jit(solution)/shard_map/ppermute | solution.py:30
  53.6 5.2 %collective-permute-start.10 = (bf16[3,1,32,128]{3,2,1,0:T(8,128)(2,1)S(1)}, bf16[3,1,32,128]{3,2,1,0:T(8,128)(2,1)S(1)}, u32[]{:S(2)}, u32[]{:S(2)}) collective-permute-start(bf16[3,1,32,128]{3,2,1,0:T(8,128)(2,1)S(1)} %pad_maximum_fusion.19), channel_id=1, source_target_pairs={{0,1},{1,2},{2,3},{3,4},{4,5},{5,6},{6,7},{8,9},{9,10},{10,11},{11... | collective-permute-start | bytes 73736 | tf_op jit(solution)/shard_map/ppermute | solution.py:28
  72.3 7.6 %collective-permute-start.16 = (f32[79360]{0:T(1024)S(1)}, f32[79360]{0:T(1024)S(1)}, u32[]{:S(2)}, u32[]{:S(2)}) collective-permute-start(f32[79360]{0:T(1024)S(1)} %pad_maximum_fusion.5), channel_id=1, source_target_pairs={{0,1},{1,0},{2,3},{3,2},{4,5},{5,4},{6,7},{7,6},{8,9},{9,8},{10,11... | collective-permute-start | bytes 952328 | tf_op jit(solution)/shard_map/ppermute | solution.py:42
  74.2 5.6 %collective-permute-start.12 = (bf16[1,16,1536]{2,1,0:T(8,128)(2,1)S(1)}, bf16[1,16,1536]{2,1,0:T(8,128)(2,1)S(1)}, u32[]{:S(2)}, u32[]{:S(2)}) collective-permute-start(bf16[1,16,1536]{2,1,0:T(8,128)(2,1)S(1)} %bitcast.204), channel_id=1, source_target_pairs={{0,8},{8,16},{16,24},{24,32},{32,40},{40,48},{48,56},{56,64},{64,7... | collective-permute-start | bytes 147464 | tf_op jit(solution)/shard_map/ppermute | solution.py:28
  78.1 8.1 %collective-permute-start.13 = (bf16[1,16,1536]{2,1,0:T(8,128)(2,1)S(1)}, bf16[1,16,1536]{2,1,0:T(8,128)(2,1)S(1)}, u32[]{:S(2)}, u32[]{:S(2)}) collective-permute-start(bf16[1,16,1536]{2,1,0:T(8,128)(2,1)S(1)} %bitcast.203), channel_id=1, source_target_pairs={{8,0},{16,8},{24,16},{32,24},{40,32},{48,40},{56,48},{64,56},{72,6... | collective-permute-start | bytes 147464 | tf_op jit(solution)/shard_map/ppermute | solution.py:30
  79.9 9.8 %collective-permute-start.17 = (f32[79360]{0:T(1024)S(1)}, f32[79360]{0:T(1024)S(1)}, u32[]{:S(2)}, u32[]{:S(2)}) collective-permute-start(f32[79360]{0:T(1024)S(1)} %fusion.78), channel_id=1, source_target_pairs={{0,2},{1,3},{2,0},{3,1},{4,6},{5,7},{6,4},{7,5},{8,10},{9,11},{10,... | collective-permute-start | bytes 952328 | tf_op jit(solution)/shard_map/ppermute | solution.py:42
  82.3 24.4 %copy-start.20 = (bf16[3,3,64,128]{3,2,1,0:T(8,128)(2,1)S(1)}, bf16[3,3,64,128]{3,2,1,0:T(8,128)(2,1)}, u32[]{:S(2)}) copy-start(bf16[3,3,64,128]{3,2,1,0:T(8,128)(2,1)} %param.9) | copy-start | bytes 442372
  89.8 11.4 %collective-permute-start.18 = (f32[79360]{0:T(1024)S(1)}, f32[79360]{0:T(1024)S(1)}, u32[]{:S(2)}, u32[]{:S(2)}) collective-permute-start(f32[79360]{0:T(1024)S(1)} %add.106), channel_id=1, source_target_pairs={{0,4},{1,5},{2,6},{3,7},{4,0},{5,1},{6,2},{7,3},{8,12},{9,13},{10,... | collective-permute-start | bytes 952328 | tf_op jit(solution)/shard_map/ppermute | solution.py:42
  93.5 13.2 %collective-permute-start.14 = (bf16[18,1,1536]{2,1,0:T(2,128)(2,1)S(1)}, bf16[18,1,1536]{2,1,0:T(2,128)(2,1)S(1)}, u32[]{:S(2)}, u32[]{:S(2)}) collective-permute-start(bf16[18,1,1536]{2,1,0:T(2,128)(2,1)S(1)} %get-tuple-element.33), channel_id=1, source_target_pairs={{0,1},{1,2},{2,3},{3,4},{4,5},{5,6},{6,7},{8,9},{9,10},{10,11},{11... | collective-permute-start | bytes 165896 | tf_op jit(solution)/shard_map/ppermute | solution.py:28
  94.8 11.9 %collective-permute-start.15 = (bf16[18,1,1536]{2,1,0:T(2,128)(2,1)S(1)}, bf16[18,1,1536]{2,1,0:T(2,128)(2,1)S(1)}, u32[]{:S(2)}, u32[]{:S(2)}) collective-permute-start(bf16[18,1,1536]{2,1,0:T(2,128)(2,1)S(1)} %get-tuple-element.34), channel_id=1, source_target_pairs={{1,0},{2,1},{3,2},{4,3},{5,4},{6,5},{7,6},{9,8},{10,9},{11,10},{12... | collective-permute-start | bytes 165896 | tf_op jit(solution)/shard_map/ppermute | solution.py:30
  101.3 10.7 %collective-permute-start.19 = (f32[79360]{0:T(1024)S(1)}, f32[79360]{0:T(1024)S(1)}, u32[]{:S(2)}, u32[]{:S(2)}) collective-permute-start(f32[79360]{0:T(1024)S(1)} %add.107), channel_id=1, source_target_pairs={{0,8},{8,0},{16,24},{24,16},{32,40},{40,32},{48,56},{56,48},{64,72... | collective-permute-start | bytes 952328 | tf_op jit(solution)/shard_map/ppermute | solution.py:42
  112.0 15.1 %collective-permute-start.20 = (f32[79360]{0:T(1024)S(1)}, f32[79360]{0:T(1024)S(1)}, u32[]{:S(2)}, u32[]{:S(2)}) collective-permute-start(f32[79360]{0:T(1024)S(1)} %add.108), channel_id=1, source_target_pairs={{0,16},{8,24},{16,0},{24,8},{32,48},{40,56},{48,32},{56,40},{64,80... | collective-permute-start | bytes 952328 | tf_op jit(solution)/shard_map/ppermute | solution.py:42
  127.1 9.9 %collective-permute-start.21 = (f32[79360]{0:T(1024)S(1)}, f32[79360]{0:T(1024)S(1)}, u32[]{:S(2)}, u32[]{:S(2)}) collective-permute-start(f32[79360]{0:T(1024)S(1)} %add.109), channel_id=1, source_target_pairs={{0,32},{8,40},{16,48},{24,56},{32,0},{40,8},{48,16},{56,24},{64,96... | collective-permute-start | bytes 952328 | tf_op jit(solution)/shard_map/ppermute | solution.py:42
  137.0 11.1 %collective-permute-start.22 = (f32[79360]{0:T(1024)S(1)}, f32[79360]{0:T(1024)S(1)}, u32[]{:S(2)}, u32[]{:S(2)}) collective-permute-start(f32[79360]{0:T(1024)S(1)} %add.110), channel_id=1, source_target_pairs={{0,64},{8,72},{16,80},{24,88},{32,96},{40,104},{48,112},{56,120},{... | collective-permute-start | bytes 952328 | tf_op jit(solution)/shard_map/ppermute | solution.py:42
  144.0 6.6 %copy-start.1 = (bf16[128,20]{0,1:T(8,128)(2,1)S(1)}, bf16[128,20]{0,1:T(8,128)(2,1)}, u32[]{:S(2)}) copy-start(bf16[128,20]{0,1:T(8,128)(2,1)} %param.11) | copy-start | bytes 15364
  (18 other events, 24.7 us)

commit v2 on v1

--- a/solution.py
+++ b/solution.py
@@ -34,13 +34,30 @@
     return cells
 
 
-def butterfly_sum(flat):
+def exchange(value, axis, bit):
+    size = lax.axis_size(axis)
+    return lax.ppermute(value, axis, [(i, i ^ bit) for i in range(size)])
+
+
+def butterfly_sum(flat, halvings=2):
+    steps = []
     for axis in ("col", "row"):
-        size = lax.axis_size(axis)
         bit = 1
-        while bit < size:
-            flat = flat + lax.ppermute(flat, axis, [(i, i ^ bit) for i in range(size)])
+        while bit < lax.axis_size(axis):
+            steps.append((axis, bit))
             bit *= 2
+    for axis, bit in steps[:halvings]:
+        upper = (lax.axis_index(axis) // bit) % 2 == 1
+        half = flat.shape[0] // 2
+        low, high = flat[:half], flat[half:]
+        keep = jnp.where(upper, high, low)
+        flat = keep + exchange(jnp.where(upper, low, high), axis, bit)
+    for axis, bit in steps[halvings:]:
+        flat = flat + exchange(flat, axis, bit)
+    for axis, bit in reversed(steps[:halvings]):
+        upper = (lax.axis_index(axis) // bit) % 2 == 1
+        other = exchange(flat, axis, bit)
+        flat = jnp.where(upper, jnp.concatenate([other, flat]), jnp.concatenate([flat, other]))
     return flat
 
 

time: 151 us -> 141 us (0.934)
  the two profiles are of different devices: /device:TPU:0 before, /device:TPU:1 now
where the time goes in v2:
time: 141 us; the launch traced here: 140 us
  starting transfers between devices  67.5 us (48%)
  local copies, waits for them, and re-layouts  27.2 us (19%)
  waiting for transfers between devices  23.4 us (17%)
  matrix products  17.1 us (12%)
  other arithmetic  3.39 us (2%)
  between operations  1.77 us (1%)
    ppermute x8, starting transfers between devices, with_halo(): lax.ppermute(tail, axis, [(i, (i + 1) % count) for i in range(ends)])  31.9 us
    ppermute x9, starting transfers between devices, exchange(): return lax.ppermute(value, axis, [(i, i ^ bit) for i in range(size)])  22.6 us
    ppermute x8, waiting for transfers between devices, with_halo(): lax.ppermute(head, axis, [((i + 1) % count, i) for i in range(ends)])  18.4 us
    ppermute x8, starting transfers between devices, with_halo(): lax.ppermute(head, axis, [((i + 1) % count, i) for i in range(ends)])  13 us
    unnamed x78, local copies, waits for them, and re-layouts  7.97 us
    ppermute x9, waiting for transfers between devices, exchange(): return lax.ppermute(value, axis, [(i, i ^ bit) for i in range(size)])  5.02 us
    dot_general x3, matrix products, spatial_forward(): jnp.dot(tap_patch, conv_weight[row_tap].reshape(3 * C_IN, C_OUT), preferr...  4.08 us
    dot_general x3, matrix products, per_device(): jnp.einsum('ijtc,ijtd->cd', tap_patch, grad_pre, preferred_element_type=j...  3.58 us
  transfers between devices with their start and end apart: 25, of which 12 were waited for; matrix products, arithmetic and copies ran while one was open for 11% of the time, Pallas kernels for 0%

profile of v2, /device:TPU:1, one launch (start us, length us, event | category | flops | bytes accessed | tf_op | source)
XLA Modules:
  0.0 140.4 jit_solution(16947159737780800418)
XLA Ops:
  1.4 3.9 %collective-permute-start = (bf16[1,16,768]{2,1,0:T(8,128)(2,1)S(1)}, bf16[1,16,768]{2,1,0:T(8,128)(2,1)S(1)}, u32[]{:S(2)}, u32[]{:S(2)}) collective-permute-start(bf16[1,16,768]{2,1,0:T(8,128)(2,1)S(1)} %get-tuple-element.44), channel_id=1, source_target_pairs={{0,8},{8,16},{16,24},{24,32},{32,40},{40,48},{48,56},{56,64},{64,7... | collective-permute-start | bytes 73736 | tf_op jit(solution)/shard_map/ppermute | solution.py:28
  5.3 1.3 collective-permute-start.1
  10.0 5.2 %collective-permute-start.2 = (bf16[18,1,768]{2,1,0:T(2,128)(2,1)S(1)}, bf16[18,1,768]{2,1,0:T(2,128)(2,1)S(1)}, u32[]{:S(2)}, u32[]{:S(2)}) collective-permute-start(bf16[18,1,768]{2,1,0:T(2,128)(2,1)S(1)} %get-tuple-element.41), channel_id=1, source_target_pairs={{0,1},{1,2},{2,3},{3,4},{4,5},{5,6},{6,7},{8,9},{9,10},{10,11},{11... | collective-permute-start | bytes 82952 | tf_op jit(solution)/shard_map/ppermute | solution.py:28
  15.2 1.9 %collective-permute-start.3 = (bf16[18,1,768]{2,1,0:T(2,128)(2,1)S(1)}, bf16[18,1,768]{2,1,0:T(2,128)(2,1)S(1)}, u32[]{:S(2)}, u32[]{:S(2)}) collective-permute-start(bf16[18,1,768]{2,1,0:T(2,128)(2,1)S(1)} %get-tuple-element.42), channel_id=1, source_target_pairs={{1,0},{2,1},{3,2},{4,3},{5,4},{6,5},{7,6},{9,8},{10,9},{11,10},{12... | collective-permute-start | bytes 82952 | tf_op jit(solution)/shard_map/ppermute | solution.py:30
  18.8 1.9 %collective-permute-done.3 = bf16[18,1,768]{2,1,0:T(2,128)(2,1)S(1)} collective-permute-done((bf16[18,1,768]{2,1,0:T(2,128)(2,1)S(1)}, bf16[18,1,768]{2,1,0:T(2,128)(2,1)S(1)}, u32[]{:S(2)}, u32[]{:S(2)}) %collective-permute-start.3) | collective-permute-done | bytes 27680 | tf_op jit(solution)/shard_map/ppermute | solution.py:30
  21.8 2.6 %fusion.82 = (bf16[16,16,12,64]{3,2,1,0:T(8,128)(2,1)S(1)}, bf16[16,16,12,64]{3,2,1,0:T(8,128)(2,1)S(1)}, bf16[16,16,12,64]{3,2,1,0:T(8,128)(2,1)S(1)}, bf16[16,...) fusion(bf16[18,18,12,64]{3,2,1,0:T(8,128)(2,1)S(1)} %reshape.116), kind=kLoop, calls=%fused_computation.160 | loop fusion | bytes 7077888 | tf_op jit(solution)/shard_map/slice | solution.py:74
  28.3 2.4 %multiply_convert_fusion.2 = (bf16[16,16,12,128]{3,1,2,0:T(8,128)(2,1)S(1)}, f32[16,16,12,128]{3,1,2,0:T(8,128)}) fusion(bf16[192,128,1,1]{1,0,3,2:T(8,128)(2,1)S(1)} %bitcast.200, bf16[16,16,12,64]{3,1,2,0:T(8,128)(2,1)S(1)} %copy.98, bf16[16,16,12,64]{3,1,2,0:T(8,128)(2,1)S(1)} %copy.97, bf16[16,16,12,64]{3,1,2,0:T(8,128)(2,1)S(1)} %copy.96, ...), kind=kOutput, calls=%fused_computation.28 | convolution fusion | flops 157286400 | bytes 6733824 | tf_op jit(solution)/shard_map/dot_general | solution.py:79
  32.4 3.1 %collective-permute-start.4 = (bf16[1,3,32,128]{3,2,1,0:T(8,128)(2,1)S(1)}, bf16[1,3,32,128]{3,2,1,0:T(8,128)(2,1)S(1)}, u32[]{:S(2)}, u32[]{:S(2)}) collective-permute-start(bf16[1,3,32,128]{3,2,1,0:T(8,128)(2,1)S(1)} %bitcast.207), channel_id=1, source_target_pairs={{0,8},{8,16},{16,24},{24,32},{32,40},{40,48},{48,56},{56,64},{64,7... | collective-permute-start | bytes 73736 | tf_op jit(solution)/shard_map/ppermute | solution.py:28
  35.5 1.3 collective-permute-start.5
  36.8 3.3 %collective-permute-done.5 = bf16[1,3,32,128]{3,2,1,0:T(8,128)(2,1)S(1)} collective-permute-done((bf16[1,3,32,128]{3,2,1,0:T(8,128)(2,1)S(1)}, bf16[1,3,32,128]{3,2,1,0:T(8,128)(2,1)S(1)}, u32[]{:S(2)}, u32[]{:S(2)}) %collective-permute-start.5) | collective-permute-done | bytes 24608 | tf_op jit(solution)/shard_map/ppermute | solution.py:30
  40.1 3.3 %collective-permute-start.6 = (bf16[5,1,32,128]{3,2,1,0:T(8,128)(2,1)S(1)}, bf16[5,1,32,128]{3,2,1,0:T(8,128)(2,1)S(1)}, u32[]{:S(2)}, u32[]{:S(2)}) collective-permute-start(bf16[5,1,32,128]{3,2,1,0:T(8,128)(2,1)S(1)} %get-tuple-element.57), channel_id=1, source_target_pairs={{0,1},{1,2},{2,3},{3,4},{4,5},{5,6},{6,7},{8,9},{9,10},{10,11},{11... | collective-permute-start | bytes 122888 | tf_op jit(solution)/shard_map/ppermute | solution.py:28
  43.5 1.9 %collective-permute-start.7 = (bf16[5,1,32,128]{3,2,1,0:T(8,128)(2,1)S(1)}, bf16[5,1,32,128]{3,2,1,0:T(8,128)(2,1)S(1)}, u32[]{:S(2)}, u32[]{:S(2)}) collective-permute-start(bf16[5,1,32,128]{3,2,1,0:T(8,128)(2,1)S(1)} %get-tuple-element.58), channel_id=1, source_target_pairs={{1,0},{2,1},{3,2},{4,3},{5,4},{6,5},{7,6},{9,8},{10,9},{11,10},{12... | collective-permute-start | bytes 122888 | tf_op jit(solution)/shard_map/ppermute | solution.py:30
  45.4 3.4 %collective-permute-done.7 = bf16[5,1,32,128]{3,2,1,0:T(8,128)(2,1)S(1)} collective-permute-done((bf16[5,1,32,128]{3,2,1,0:T(8,128)(2,1)S(1)}, bf16[5,1,32,128]{3,2,1,0:T(8,128)(2,1)S(1)}, u32[]{:S(2)}, u32[]{:S(2)}) %collective-permute-start.7) | collective-permute-done | bytes 40992 | tf_op jit(solution)/shard_map/ppermute | solution.py:30
  49.8 4.7 %collective-permute-start.8 = (bf16[1,1,32,128]{3,2,1,0:T(8,128)(2,1)S(1)}, bf16[1,1,32,128]{3,2,1,0:T(8,128)(2,1)S(1)}, u32[]{:S(2)}, u32[]{:S(2)}) collective-permute-start(bf16[1,1,32,128]{3,2,1,0:T(8,128)(2,1)S(1)} %fusion.61), channel_id=1, source_target_pairs={{0,8},{8,16},{16,24},{24,32},{32,40},{40,48},{48,56},{56,64},{64,7... | collective-permute-start | bytes 24584 | tf_op jit(solution)/shard_map/ppermute | solution.py:28
  55.9 3.3 %collective-permute-done.9 = bf16[1,1,32,128]{3,2,1,0:T(8,128)(2,1)S(1)} collective-permute-done((bf16[1,1,32,128]{3,2,1,0:T(8,128)(2,1)S(1)}, bf16[1,1,32,128]{3,2,1,0:T(8,128)(2,1)S(1)}, u32[]{:S(2)}, u32[]{:S(2)}) %collective-permute-start.9) | collective-permute-done | bytes 8224 | tf_op jit(solution)/shard_map/ppermute | solution.py:30
  59.2 3.0 %collective-permute-start.10 = (bf16[3,1,32,128]{3,2,1,0:T(8,128)(2,1)S(1)}, bf16[3,1,32,128]{3,2,1,0:T(8,128)(2,1)S(1)}, u32[]{:S(2)}, u32[]{:S(2)}) collective-permute-start(bf16[3,1,32,128]{3,2,1,0:T(8,128)(2,1)S(1)} %pad_maximum_fusion.20), channel_id=1, source_target_pairs={{0,1},{1,2},{2,3},{3,4},{4,5},{5,6},{6,7},{8,9},{9,10},{10,11},{11... | collective-permute-start | bytes 73736 | tf_op jit(solution)/shard_map/ppermute | solution.py:28
  62.3 2.1 %collective-permute-start.11 = (bf16[3,1,32,128]{3,2,1,0:T(8,128)(2,1)S(1)}, bf16[3,1,32,128]{3,2,1,0:T(8,128)(2,1)S(1)}, u32[]{:S(2)}, u32[]{:S(2)}) collective-permute-start(bf16[3,1,32,128]{3,2,1,0:T(8,128)(2,1)S(1)} %pad_maximum_fusion.20), channel_id=1, source_target_pairs={{1,0},{2,1},{3,2},{4,3},{5,4},{6,5},{7,6},{9,8},{10,9},{11,10},{12... | collective-permute-start | bytes 73736 | tf_op jit(solution)/shard_map/ppermute | solution.py:30
  64.8 2.6 %collective-permute-done.11 = bf16[3,1,32,128]{3,2,1,0:T(8,128)(2,1)S(1)} collective-permute-done((bf16[3,1,32,128]{3,2,1,0:T(8,128)(2,1)S(1)}, bf16[3,1,32,128]{3,2,1,0:T(8,128)(2,1)S(1)}, u32[]{:S(2)}, u32[]{:S(2)}) %collective-permute-start.11) | collective-permute-done | bytes 24608 | tf_op jit(solution)/shard_map/ppermute | solution.py:30
  80.8 5.1 %collective-permute-start.12 = (bf16[1,16,1536]{2,1,0:T(8,128)(2,1)S(1)}, bf16[1,16,1536]{2,1,0:T(8,128)(2,1)S(1)}, u32[]{:S(2)}, u32[]{:S(2)}) collective-permute-start(bf16[1,16,1536]{2,1,0:T(8,128)(2,1)S(1)} %bitcast.203), channel_id=1, source_target_pairs={{0,8},{8,16},{16,24},{24,32},{32,40},{40,48},{48,56},{56,64},{64,7... | collective-permute-start | bytes 147464 | tf_op jit(solution)/shard_map/ppermute | solution.py:28
  87.5 3.7 %collective-permute-done.13 = bf16[1,16,1536]{2,1,0:T(8,128)(2,1)S(1)} collective-permute-done((bf16[1,16,1536]{2,1,0:T(8,128)(2,1)S(1)}, bf16[1,16,1536]{2,1,0:T(8,128)(2,1)S(1)}, u32[]{:S(2)}, u32[]{:S(2)}) %collective-permute-start.13) | collective-permute-done | bytes 49184 | tf_op jit(solution)/shard_map/ppermute | solution.py:30
  91.3 1.5 %collective-permute-start.17 = (f32[19840]{0:T(1024)S(1)}, f32[19840]{0:T(1024)S(1)}, u32[]{:S(2)}, u32[]{:S(2)}) collective-permute-start(f32[19840]{0:T(1024)S(1)} %slice_select_fusion.1), channel_id=1, source_target_pairs={{0,2},{1,3},{2,0},{3,1},{4,6},{5,7},{6,4},{7,5},{8,10},{9,11},{10,... | collective-permute-start | bytes 238088 | tf_op jit(solution)/shard_map/ppermute | solution.py:39
  92.9 3.5 %collective-permute-start.14 = (bf16[18,1,1536]{2,1,0:T(2,128)(2,1)S(1)}, bf16[18,1,1536]{2,1,0:T(2,128)(2,1)S(1)}, u32[]{:S(2)}, u32[]{:S(2)}) collective-permute-start(bf16[18,1,1536]{2,1,0:T(2,128)(2,1)S(1)} %get-tuple-element.37), channel_id=1, source_target_pairs={{0,1},{1,2},{2,3},{3,4},{4,5},{5,6},{6,7},{8,9},{9,10},{10,11},{11... | collective-permute-start | bytes 165896 | tf_op jit(solution)/shard_map/ppermute | solution.py:28
  96.4 1.9 %collective-permute-start.15 = (bf16[18,1,1536]{2,1,0:T(2,128)(2,1)S(1)}, bf16[18,1,1536]{2,1,0:T(2,128)(2,1)S(1)}, u32[]{:S(2)}, u32[]{:S(2)}) collective-permute-start(bf16[18,1,1536]{2,1,0:T(2,128)(2,1)S(1)} %get-tuple-element.38), channel_id=1, source_target_pairs={{1,0},{2,1},{3,2},{4,3},{5,4},{6,5},{7,6},{9,8},{10,9},{11,10},{12... | collective-permute-start | bytes 165896 | tf_op jit(solution)/shard_map/ppermute | solution.py:30
  98.4 2.7 %collective-permute-start.18 = (f32[19840]{0:T(1024)S(1)}, f32[19840]{0:T(1024)S(1)}, u32[]{:S(2)}, u32[]{:S(2)}) collective-permute-start(f32[19840]{0:T(1024)S(1)} %select_add_fusion.1), channel_id=1, source_target_pairs={{0,4},{1,5},{2,6},{3,7},{4,0},{5,1},{6,2},{7,3},{8,12},{9,13},{10,... | collective-permute-start | bytes 238088 | tf_op jit(solution)/shard_map/ppermute | solution.py:39
  101.1 2.9 %collective-permute-done.18 = f32[19840]{0:T(1024)S(1)} collective-permute-done((f32[19840]{0:T(1024)S(1)}, f32[19840]{0:T(1024)S(1)}, u32[]{:S(2)}, u32[]{:S(2)}) %collective-permute-start.18) | collective-permute-done | bytes 79392 | tf_op jit(solution)/shard_map/ppermute | solution.py:39
  104.0 2.2 %collective-permute-start.19 = (f32[19840]{0:T(1024)S(1)}, f32[19840]{0:T(1024)S(1)}, u32[]{:S(2)}, u32[]{:S(2)}) collective-permute-start(f32[19840]{0:T(1024)S(1)} %add.120), channel_id=1, source_target_pairs={{0,8},{8,0},{16,24},{24,16},{32,40},{40,32},{48,56},{56,48},{64,72... | collective-permute-start | bytes 238088 | tf_op jit(solution)/shard_map/ppermute | solution.py:39
  108.0 5.2 %collective-permute-start.20 = (f32[19840]{0:T(1024)S(1)}, f32[19840]{0:T(1024)S(1)}, u32[]{:S(2)}, u32[]{:S(2)}) collective-permute-start(f32[19840]{0:T(1024)S(1)} %add.121), channel_id=1, source_target_pairs={{0,16},{8,24},{16,0},{24,8},{32,48},{40,56},{48,32},{56,40},{64,80... | collective-permute-start | bytes 238088 | tf_op jit(solution)/shard_map/ppermute | solution.py:39
  113.2 2.8 %fusion.81 = (bf16[16,16,12,128]{3,2,1,0:T(8,128)(2,1)S(1)}, bf16[16,16,12,128]{3,2,1,0:T(8,128)(2,1)S(1)}, bf16[16,16,12,128]{3,2,1,0:T(8,128)(2,1)S(1)}, bf16[...) fusion(bf16[18,18,12,128]{3,2,1,0:T(8,128)(2,1)S(1)} %reshape.120), kind=kLoop, calls=%fused_computation.159 | loop fusion | bytes 14155776 | tf_op jit(solution)/shard_map/slice | solution.py:93
  116.6 1.8 %collective-permute-start.21 = (f32[19840]{0:T(1024)S(1)}, f32[19840]{0:T(1024)S(1)}, u32[]{:S(2)}, u32[]{:S(2)}) collective-permute-start(f32[19840]{0:T(1024)S(1)} %add.122), channel_id=1, source_target_pairs={{0,32},{8,40},{16,48},{24,56},{32,0},{40,8},{48,16},{56,24},{64,96... | collective-permute-start | bytes 238088 | tf_op jit(solution)/shard_map/ppermute | solution.py:39
  120.2 3.2 %collective-permute-start.22 = (f32[19840]{0:T(1024)S(1)}, f32[19840]{0:T(1024)S(1)}, u32[]{:S(2)}, u32[]{:S(2)}) collective-permute-start(f32[19840]{0:T(1024)S(1)} %add.123), channel_id=1, source_target_pairs={{0,64},{8,72},{16,80},{24,88},{32,96},{40,104},{48,112},{56,120},{... | collective-permute-start | bytes 238088 | tf_op jit(solution)/shard_map/ppermute | solution.py:39
  126.5 1.4 reshape.121
  129.4 6.0 %collective-permute-start.24 = (f32[39680]{0:T(1024)S(1)}, f32[39680]{0:T(1024)S(1)}, u32[]{:S(2)}, u32[]{:S(2)}) collective-permute-start(f32[39680]{0:T(1024)S(1)} %maximum_select_fusion.2), channel_id=1, source_target_pairs={{0,1},{1,0},{2,3},{3,2},{4,5},{5,4},{6,7},{7,6},{8,9},{9,8},{10,11... | collective-permute-start | bytes 476168 | tf_op jit(solution)/shard_map/ppermute | solution.py:39
  (194 shorter events, 43.6 us)
Async XLA Ops:
  0.6 48.5 %copy-start = (bf16[128,20]{0,1:T(8,128)(2,1)S(1)}, bf16[128,20]{0,1:T(8,128)(2,1)}, u32[]{:S(2)}) copy-start(bf16[128,20]{0,1:T(8,128)(2,1)} %param.11) | copy-start | bytes 15364
  1.4 7.9 %collective-permute-start = (bf16[1,16,768]{2,1,0:T(8,128)(2,1)S(1)}, bf16[1,16,768]{2,1,0:T(8,128)(2,1)S(1)}, u32[]{:S(2)}, u32[]{:S(2)}) collective-permute-start(bf16[1,16,768]{2,1,0:T(8,128)(2,1)S(1)} %get-tuple-element.44), channel_id=1, source_target_pairs={{0,8},{8,16},{16,24},{24,32},{32,40},{40,48},{48,56},{56,64},{64,7... | collective-permute-start | bytes 73736 | tf_op jit(solution)/shard_map/ppermute | solution.py:28
  5.3 4.6 %collective-permute-start.1 = (bf16[1,16,768]{2,1,0:T(8,128)(2,1)S(1)}, bf16[1,16,768]{2,1,0:T(8,128)(2,1)S(1)}, u32[]{:S(2)}, u32[]{:S(2)}) collective-permute-start(bf16[1,16,768]{2,1,0:T(8,128)(2,1)S(1)} %get-tuple-element.43), channel_id=1, source_target_pairs={{8,0},{16,8},{24,16},{32,24},{40,32},{48,40},{56,48},{64,56},{72,6... | collective-permute-start | bytes 73736 | tf_op jit(solution)/shard_map/ppermute | solution.py:30
  9.3 9.4 %copy-start.22 = (s32[16,16]{1,0:T(8,128)S(1)}, s32[16,16]{1,0:T(8,128)}, u32[]{:S(2)}) copy-start(s32[16,16]{1,0:T(8,128)} %param.12) | copy-start | bytes 3076
  10.0 8.8 %collective-permute-start.2 = (bf16[18,1,768]{2,1,0:T(2,128)(2,1)S(1)}, bf16[18,1,768]{2,1,0:T(2,128)(2,1)S(1)}, u32[]{:S(2)}, u32[]{:S(2)}) collective-permute-start(bf16[18,1,768]{2,1,0:T(2,128)(2,1)S(1)} %get-tuple-element.41), channel_id=1, source_target_pairs={{0,1},{1,2},{2,3},{3,4},{4,5},{5,6},{6,7},{8,9},{9,10},{10,11},{11... | collective-permute-start | bytes 82952 | tf_op jit(solution)/shard_map/ppermute | solution.py:28
  15.2 5.5 %collective-permute-start.3 = (bf16[18,1,768]{2,1,0:T(2,128)(2,1)S(1)}, bf16[18,1,768]{2,1,0:T(2,128)(2,1)S(1)}, u32[]{:S(2)}, u32[]{:S(2)}) collective-permute-start(bf16[18,1,768]{2,1,0:T(2,128)(2,1)S(1)} %get-tuple-element.42), channel_id=1, source_target_pairs={{1,0},{2,1},{3,2},{4,3},{5,4},{6,5},{7,6},{9,8},{10,9},{11,10},{12... | collective-permute-start | bytes 82952 | tf_op jit(solution)/shard_map/ppermute | solution.py:30
  26.0 2.2 %copy-start.8 = (bf16[16,16,12,64]{3,1,2,0:T(8,128)(2,1)}, bf16[16,16,12,64]{3,1,2,0:T(8,128)(2,1)S(1)}, u32[]{:S(2)}) copy-start(bf16[16,16,12,64]{3,1,2,0:T(8,128)(2,1)S(1)} %copy.96) | copy-start | bytes 1179652
  26.2 2.0 %copy-start.10 = (bf16[16,16,12,64]{3,1,2,0:T(8,128)(2,1)}, bf16[16,16,12,64]{3,1,2,0:T(8,128)(2,1)S(1)}, u32[]{:S(2)}) copy-start(bf16[16,16,12,64]{3,1,2,0:T(8,128)(2,1)S(1)} %copy.97) | copy-start | bytes 1179652
  31.4 18.0 %copy-start.25 = (s32[1,1,32]{2,1,0:T(1,128)S(1)}, s32[1,1,32]{2,1,0:T(1,128)}, u32[]{:S(2)}) copy-start(s32[1,1,32]{2,1,0:T(1,128)} %param.15) | copy-start | bytes 388
  32.4 4.4 %collective-permute-start.4 = (bf16[1,3,32,128]{3,2,1,0:T(8,128)(2,1)S(1)}, bf16[1,3,32,128]{3,2,1,0:T(8,128)(2,1)S(1)}, u32[]{:S(2)}, u32[]{:S(2)}) collective-permute-start(bf16[1,3,32,128]{3,2,1,0:T(8,128)(2,1)S(1)} %bitcast.207), channel_id=1, source_target_pairs={{0,8},{8,16},{16,24},{24,32},{32,40},{40,48},{48,56},{56,64},{64,7... | collective-permute-start | bytes 73736 | tf_op jit(solution)/shard_map/ppermute | solution.py:28
  35.5 4.6 %collective-permute-start.5 = (bf16[1,3,32,128]{3,2,1,0:T(8,128)(2,1)S(1)}, bf16[1,3,32,128]{3,2,1,0:T(8,128)(2,1)S(1)}, u32[]{:S(2)}, u32[]{:S(2)}) collective-permute-start(bf16[1,3,32,128]{3,2,1,0:T(8,128)(2,1)S(1)} %bitcast.206), channel_id=1, source_target_pairs={{8,0},{16,8},{24,16},{32,24},{40,32},{48,40},{56,48},{64,56},{72,6... | collective-permute-start | bytes 73736 | tf_op jit(solution)/shard_map/ppermute | solution.py:30
  40.1 5.3 %collective-permute-start.6 = (bf16[5,1,32,128]{3,2,1,0:T(8,128)(2,1)S(1)}, bf16[5,1,32,128]{3,2,1,0:T(8,128)(2,1)S(1)}, u32[]{:S(2)}, u32[]{:S(2)}) collective-permute-start(bf16[5,1,32,128]{3,2,1,0:T(8,128)(2,1)S(1)} %get-tuple-element.57), channel_id=1, source_target_pairs={{0,1},{1,2},{2,3},{3,4},{4,5},{5,6},{6,7},{8,9},{9,10},{10,11},{11... | collective-permute-start | bytes 122888 | tf_op jit(solution)/shard_map/ppermute | solution.py:28
  43.5 5.3 %collective-permute-start.7 = (bf16[5,1,32,128]{3,2,1,0:T(8,128)(2,1)S(1)}, bf16[5,1,32,128]{3,2,1,0:T(8,128)(2,1)S(1)}, u32[]{:S(2)}, u32[]{:S(2)}) collective-permute-start(bf16[5,1,32,128]{3,2,1,0:T(8,128)(2,1)S(1)} %get-tuple-element.58), channel_id=1, source_target_pairs={{1,0},{2,1},{3,2},{4,3},{5,4},{6,5},{7,6},{9,8},{10,9},{11,10},{12... | collective-permute-start | bytes 122888 | tf_op jit(solution)/shard_map/ppermute | solution.py:30
  49.8 6.1 %collective-permute-start.8 = (bf16[1,1,32,128]{3,2,1,0:T(8,128)(2,1)S(1)}, bf16[1,1,32,128]{3,2,1,0:T(8,128)(2,1)S(1)}, u32[]{:S(2)}, u32[]{:S(2)}) collective-permute-start(bf16[1,1,32,128]{3,2,1,0:T(8,128)(2,1)S(1)} %fusion.61), channel_id=1, source_target_pairs={{0,8},{8,16},{16,24},{24,32},{32,40},{40,48},{48,56},{56,64},{64,7... | collective-permute-start | bytes 24584 | tf_op jit(solution)/shard_map/ppermute | solution.py:28
  54.6 4.7 %collective-permute-start.9 = (bf16[1,1,32,128]{3,2,1,0:T(8,128)(2,1)S(1)}, bf16[1,1,32,128]{3,2,1,0:T(8,128)(2,1)S(1)}, u32[]{:S(2)}, u32[]{:S(2)}) collective-permute-start(bf16[1,1,32,128]{3,2,1,0:T(8,128)(2,1)S(1)} %fusion.61), channel_id=1, source_target_pairs={{8,0},{16,8},{24,16},{32,24},{40,32},{48,40},{56,48},{64,56},{72,6... | collective-permute-start | bytes 24584 | tf_op jit(solution)/shard_map/ppermute | solution.py:30
  59.2 5.6 %collective-permute-start.10 = (bf16[3,1,32,128]{3,2,1,0:T(8,128)(2,1)S(1)}, bf16[3,1,32,128]{3,2,1,0:T(8,128)(2,1)S(1)}, u32[]{:S(2)}, u32[]{:S(2)}) collective-permute-start(bf16[3,1,32,128]{3,2,1,0:T(8,128)(2,1)S(1)} %pad_maximum_fusion.20), channel_id=1, source_target_pairs={{0,1},{1,2},{2,3},{3,4},{4,5},{5,6},{6,7},{8,9},{9,10},{10,11},{11... | collective-permute-start | bytes 73736 | tf_op jit(solution)/shard_map/ppermute | solution.py:28
  62.3 5.1 %collective-permute-start.11 = (bf16[3,1,32,128]{3,2,1,0:T(8,128)(2,1)S(1)}, bf16[3,1,32,128]{3,2,1,0:T(8,128)(2,1)S(1)}, u32[]{:S(2)}, u32[]{:S(2)}) collective-permute-start(bf16[3,1,32,128]{3,2,1,0:T(8,128)(2,1)S(1)} %pad_maximum_fusion.20), channel_id=1, source_target_pairs={{1,0},{2,1},{3,2},{4,3},{5,4},{6,5},{7,6},{9,8},{10,9},{11,10},{12... | collective-permute-start | bytes 73736 | tf_op jit(solution)/shard_map/ppermute | solution.py:30
  80.8 6.5 %collective-permute-start.12 = (bf16[1,16,1536]{2,1,0:T(8,128)(2,1)S(1)}, bf16[1,16,1536]{2,1,0:T(8,128)(2,1)S(1)}, u32[]{:S(2)}, u32[]{:S(2)}) collective-permute-start(bf16[1,16,1536]{2,1,0:T(8,128)(2,1)S(1)} %bitcast.203), channel_id=1, source_target_pairs={{0,8},{8,16},{16,24},{24,32},{32,40},{40,48},{48,56},{56,64},{64,7... | collective-permute-start | bytes 147464 | tf_op jit(solution)/shard_map/ppermute | solution.py:28
  86.0 5.2 %collective-permute-start.16 = (f32[39680]{0:T(1024)S(1)}, f32[39680]{0:T(1024)S(1)}, u32[]{:S(2)}, u32[]{:S(2)}) collective-permute-start(f32[39680]{0:T(1024)S(1)} %slice_select_fusion), channel_id=1, source_target_pairs={{0,1},{1,0},{2,3},{3,2},{4,5},{5,4},{6,7},{7,6},{8,9},{9,8},{10,11... | collective-permute-start | bytes 476168 | tf_op jit(solution)/shard_map/ppermute | solution.py:39
  86.1 5.1 %collective-permute-start.13 = (bf16[1,16,1536]{2,1,0:T(8,128)(2,1)S(1)}, bf16[1,16,1536]{2,1,0:T(8,128)(2,1)S(1)}, u32[]{:S(2)}, u32[]{:S(2)}) collective-permute-start(bf16[1,16,1536]{2,1,0:T(8,128)(2,1)S(1)} %bitcast.204), channel_id=1, source_target_pairs={{8,0},{16,8},{24,16},{32,24},{40,32},{48,40},{56,48},{64,56},{72,6... | collective-permute-start | bytes 147464 | tf_op jit(solution)/shard_map/ppermute | solution.py:30
  87.4 13.7 %copy-start.20 = (bf16[3,3,64,128]{3,2,1,0:T(8,128)(2,1)S(1)}, bf16[3,3,64,128]{3,2,1,0:T(8,128)(2,1)}, u32[]{:S(2)}) copy-start(bf16[3,3,64,128]{3,2,1,0:T(8,128)(2,1)} %param.9) | copy-start | bytes 442372
  91.3 7.1 %collective-permute-start.17 = (f32[19840]{0:T(1024)S(1)}, f32[19840]{0:T(1024)S(1)}, u32[]{:S(2)}, u32[]{:S(2)}) collective-permute-start(f32[19840]{0:T(1024)S(1)} %slice_select_fusion.1), channel_id=1, source_target_pairs={{0,2},{1,3},{2,0},{3,1},{4,6},{5,7},{6,4},{7,5},{8,10},{9,11},{10,... | collective-permute-start | bytes 238088 | tf_op jit(solution)/shard_map/ppermute | solution.py:39
  92.9 13.3 %collective-permute-start.14 = (bf16[18,1,1536]{2,1,0:T(2,128)(2,1)S(1)}, bf16[18,1,1536]{2,1,0:T(2,128)(2,1)S(1)}, u32[]{:S(2)}, u32[]{:S(2)}) collective-permute-start(bf16[18,1,1536]{2,1,0:T(2,128)(2,1)S(1)} %get-tuple-element.37), channel_id=1, source_target_pairs={{0,1},{1,2},{2,3},{3,4},{4,5},{5,6},{6,7},{8,9},{9,10},{10,11},{11... | collective-permute-start | bytes 165896 | tf_op jit(solution)/shard_map/ppermute | solution.py:28
  96.4 9.7 %collective-permute-start.15 = (bf16[18,1,1536]{2,1,0:T(2,128)(2,1)S(1)}, bf16[18,1,1536]{2,1,0:T(2,128)(2,1)S(1)}, u32[]{:S(2)}, u32[]{:S(2)}) collective-permute-start(bf16[18,1,1536]{2,1,0:T(2,128)(2,1)S(1)} %get-tuple-element.38), channel_id=1, source_target_pairs={{1,0},{2,1},{3,2},{4,3},{5,4},{6,5},{7,6},{9,8},{10,9},{11,10},{12... | collective-permute-start | bytes 165896 | tf_op jit(solution)/shard_map/ppermute | solution.py:30
  98.4 5.6 %collective-permute-start.18 = (f32[19840]{0:T(1024)S(1)}, f32[19840]{0:T(1024)S(1)}, u32[]{:S(2)}, u32[]{:S(2)}) collective-permute-start(f32[19840]{0:T(1024)S(1)} %select_add_fusion.1), channel_id=1, source_target_pairs={{0,4},{1,5},{2,6},{3,7},{4,0},{5,1},{6,2},{7,3},{8,12},{9,13},{10,... | collective-permute-start | bytes 238088 | tf_op jit(solution)/shard_map/ppermute | solution.py:39
  104.0 4.0 %collective-permute-start.19 = (f32[19840]{0:T(1024)S(1)}, f32[19840]{0:T(1024)S(1)}, u32[]{:S(2)}, u32[]{:S(2)}) collective-permute-start(f32[19840]{0:T(1024)S(1)} %add.120), channel_id=1, source_target_pairs={{0,8},{8,0},{16,24},{24,16},{32,40},{40,32},{48,56},{56,48},{64,72... | collective-permute-start | bytes 238088 | tf_op jit(solution)/shard_map/ppermute | solution.py:39
  108.0 8.6 %collective-permute-start.20 = (f32[19840]{0:T(1024)S(1)}, f32[19840]{0:T(1024)S(1)}, u32[]{:S(2)}, u32[]{:S(2)}) collective-permute-start(f32[19840]{0:T(1024)S(1)} %add.121), channel_id=1, source_target_pairs={{0,16},{8,24},{16,0},{24,8},{32,48},{40,56},{48,32},{56,40},{64,80... | collective-permute-start | bytes 238088 | tf_op jit(solution)/shard_map/ppermute | solution.py:39
  116.6 3.6 %collective-permute-start.21 = (f32[19840]{0:T(1024)S(1)}, f32[19840]{0:T(1024)S(1)}, u32[]{:S(2)}, u32[]{:S(2)}) collective-permute-start(f32[19840]{0:T(1024)S(1)} %add.122), channel_id=1, source_target_pairs={{0,32},{8,40},{16,48},{24,56},{32,0},{40,8},{48,16},{56,24},{64,96... | collective-permute-start | bytes 238088 | tf_op jit(solution)/shard_map/ppermute | solution.py:39
  120.2 5.0 %collective-permute-start.22 = (f32[19840]{0:T(1024)S(1)}, f32[19840]{0:T(1024)S(1)}, u32[]{:S(2)}, u32[]{:S(2)}) collective-permute-start(f32[19840]{0:T(1024)S(1)} %add.123), channel_id=1, source_target_pairs={{0,64},{8,72},{16,80},{24,88},{32,96},{40,104},{48,112},{56,120},{... | collective-permute-start | bytes 238088 | tf_op jit(solution)/shard_map/ppermute | solution.py:39
  125.3 3.4 %collective-permute-start.23 = (f32[19840]{0:T(1024)S(1)}, f32[19840]{0:T(1024)S(1)}, u32[]{:S(2)}, u32[]{:S(2)}) collective-permute-start(f32[19840]{0:T(1024)S(1)} %add.124), channel_id=1, source_target_pairs={{0,2},{1,3},{2,0},{3,1},{4,6},{5,7},{6,4},{7,5},{8,10},{9,11},{10,... | collective-permute-start | bytes 238088 | tf_op jit(solution)/shard_map/ppermute | solution.py:39
  129.4 7.0 %collective-permute-start.24 = (f32[39680]{0:T(1024)S(1)}, f32[39680]{0:T(1024)S(1)}, u32[]{:S(2)}, u32[]{:S(2)}) collective-permute-start(f32[39680]{0:T(1024)S(1)} %maximum_select_fusion.2), channel_id=1, source_target_pairs={{0,1},{1,0},{2,3},{3,2},{4,5},{5,4},{6,7},{7,6},{8,9},{9,8},{10,11... | collective-permute-start | bytes 476168 | tf_op jit(solution)/shard_map/ppermute | solution.py:39
  136.5 3.8 %copy-start.1 = (bf16[128,20]{0,1:T(8,128)(2,1)S(1)}, bf16[128,20]{0,1:T(8,128)(2,1)}, u32[]{:S(2)}) copy-start(bf16[128,20]{0,1:T(8,128)(2,1)} %param.11) | copy-start | bytes 15364
  (20 other events, 28.2 us)

commit v3 on v2

--- a/solution.py
+++ b/solution.py
@@ -20,16 +20,17 @@
 def with_halo(cells, sides, width):
     for axis, dim in sides:
         count = lax.axis_size(axis)
-        ends = count - 1
+        odd = lax.axis_index(axis) % 2 == 1
         head = lax.slice_in_dim(cells, 0, width, axis=dim)
         tail = lax.slice_in_dim(cells, cells.shape[dim] - width, cells.shape[dim], axis=dim)
+        inner = lax.ppermute(jnp.where(odd, head, tail), axis, [(i, i ^ 1) for i in range(count)])
+        outer = lax.ppermute(
+            jnp.where(odd, tail, head),
+            axis,
+            [pair for k in range(1, count - 1, 2) for pair in ((k, k + 1), (k + 1, k))],
+        )
         cells = jnp.concatenate(
-            [
-                lax.ppermute(tail, axis, [(i, (i + 1) % count) for i in range(ends)]),
-                cells,
-                lax.ppermute(head, axis, [((i + 1) % count, i) for i in range(ends)]),
-            ],
-            axis=dim,
+            [jnp.where(odd, inner, outer), cells, jnp.where(odd, outer, inner)], axis=dim
         )
     return cells
 

time: 141 us -> 124 us (0.88)
  waiting for transfers between devices: 23.4 us -> 11.4 us
  starting transfers between devices: 67.5 us -> 61.2 us
  other arithmetic: 3.39 us -> 5.25 us
    ppermute x16, waiting for transfers between devices: 18.4 us -> 4.18 us  [the longest x8 2.67 us: with_halo(): lax.ppermute(jnp.where(odd, tail, head), axis, [pair for k in range(1, co...]
    ppermute x16, starting transfers between devices: 44.9 us -> 35.2 us  [the longest x8 18.8 us: with_halo(): lax.ppermute(jnp.where(odd, head, tail), axis, [(i, i ^ 1) for i in range...]
    ppermute x9, starting transfers between devices: 22.6 us -> 26 us  [exchange(): return lax.ppermute(value, axis, [(i, i ^ bit) for i in range(size)])]
    ppermute x9, waiting for transfers between devices: 5.02 us -> 7.22 us  [exchange(): return lax.ppermute(value, axis, [(i, i ^ bit) for i in range(size)])]
    select_n x0 -> x15, other arithmetic: none -> 1.82 us  [the longest x5 1.14 us: with_halo(): jnp.where(odd, head, tail)]
    unnamed x78 -> x83, local copies, waits for them, and re-layouts: 7.97 us -> 7.86 us
  transfers between devices with their start and end apart: 25 -> 25, of which waited for: 12 -> 13; matrix products, arithmetic and copies ran while one was open for 11% -> 14% of each run, Pallas kernels for 0% -> 0%
where the time goes in v3:
time: 124 us; the launch traced here: 123 us
  starting transfers between devices  61.2 us (49%)
  local copies, waits for them, and re-layouts  26.7 us (22%)
  matrix products  17.1 us (14%)
  waiting for transfers between devices  11.4 us (9%)
  other arithmetic  5.25 us (4%)
  between operations  1.81 us (1%)
    ppermute x9, starting transfers between devices, exchange(): return lax.ppermute(value, axis, [(i, i ^ bit) for i in range(size)])  26 us
    ppermute x8, starting transfers between devices, with_halo(): lax.ppermute(jnp.where(odd, head, tail), axis, [(i, i ^ 1) for i in range...  18.8 us
    ppermute x8, starting transfers between devices, with_halo(): lax.ppermute(jnp.where(odd, tail, head), axis, [pair for k in range(1, co...  16.4 us
    unnamed x83, local copies, waits for them, and re-layouts  7.86 us
    ppermute x9, waiting for transfers between devices, exchange(): return lax.ppermute(value, axis, [(i, i ^ bit) for i in range(size)])  7.22 us
    dot_general x3, matrix products, spatial_forward(): jnp.dot(tap_patch, conv_weight[row_tap].reshape(3 * C_IN, C_OUT), preferr...  4.09 us
    dot_general x3, matrix products, per_device(): jnp.einsum('ijtc,ijtd->cd', tap_patch, grad_pre, preferred_element_type=j...  3.58 us
    concatenate x6, local copies, waits for them, and re-layouts, butterfly_sum(): jnp.concatenate([other, flat])  3.02 us
  transfers between devices with their start and end apart: 25, of which 13 were waited for; matrix products, arithmetic and copies ran while one was open for 14% of the time, Pallas kernels for 0%

profile of v3, /device:TPU:1, one launch (start us, length us, event | category | flops | bytes accessed | tf_op | source)
XLA Modules:
  0.0 123.4 jit_solution(10889765449909324493)
XLA Ops:
  1.4 2.0 %collective-permute-start = (bf16[1,16,768]{2,1,0:T(8,128)(2,1)S(1)}, bf16[1,16,768]{2,1,0:T(8,128)(2,1)S(1)}, u32[]{:S(2)}, u32[]{:S(2)}) collective-permute-start(bf16[1,16,768]{2,1,0:T(8,128)(2,1)S(1)} %get-tuple-element.45), channel_id=1, source_target_pairs={{0,8},{8,0},{16,24},{24,16},{32,40},{40,32},{48,56},{56,48},{64,72... | collective-permute-start | bytes 73736 | tf_op jit(solution)/shard_map/ppermute | solution.py:26
  5.0 0.9 copy.48
  7.4 4.0 %collective-permute-start.3 = (bf16[18,1,768]{2,1,0:T(2,128)(2,1)S(1)}, bf16[18,1,768]{2,1,0:T(2,128)(2,1)S(1)}, u32[]{:S(2)}, u32[]{:S(2)}) collective-permute-start(bf16[18,1,768]{2,1,0:T(2,128)(2,1)S(1)} %broadcast_select_fusion.6), channel_id=1, source_target_pairs={{1,2},{2,1},{3,4},{4,3},{5,6},{6,5},{9,10},{10,9},{11,12},{12,11},... | collective-permute-start | bytes 82952 | tf_op jit(solution)/shard_map/ppermute | solution.py:27
  14.5 2.6 %fusion.82 = (bf16[16,16,12,64]{3,2,1,0:T(8,128)(2,1)S(1)}, bf16[16,16,12,64]{3,2,1,0:T(8,128)(2,1)S(1)}, bf16[16,16,12,64]{3,2,1,0:T(8,128)(2,1)S(1)}, bf16[16,...) fusion(bf16[18,18,12,64]{3,2,1,0:T(8,128)(2,1)S(1)} %reshape.164), kind=kLoop, calls=%fused_computation.187 | loop fusion | bytes 7077888 | tf_op jit(solution)/shard_map/slice | solution.py:75
  21.0 2.4 %multiply_convert_fusion.2 = (bf16[16,16,12,128]{3,1,2,0:T(8,128)(2,1)S(1)}, f32[16,16,12,128]{3,1,2,0:T(8,128)}) fusion(bf16[192,128,1,1]{1,0,3,2:T(8,128)(2,1)S(1)} %bitcast.200, bf16[16,16,12,64]{3,1,2,0:T(8,128)(2,1)S(1)} %copy.98, bf16[16,16,12,64]{3,1,2,0:T(8,128)(2,1)S(1)} %copy.97, bf16[16,16,12,64]{3,1,2,0:T(8,128)(2,1)S(1)} %copy.96, ...), kind=kOutput, calls=%fused_computation.28 | convolution fusion | flops 157286400 | bytes 6733824 | tf_op jit(solution)/shard_map/dot_general | solution.py:80
  25.2 3.7 %collective-permute-start.4 = (bf16[1,3,32,128]{3,2,1,0:T(8,128)(2,1)S(1)}, bf16[1,3,32,128]{3,2,1,0:T(8,128)(2,1)S(1)}, u32[]{:S(2)}, u32[]{:S(2)}) collective-permute-start(bf16[1,3,32,128]{3,2,1,0:T(8,128)(2,1)S(1)} %bitcast.207), channel_id=1, source_target_pairs={{0,8},{8,0},{16,24},{24,16},{32,40},{40,32},{48,56},{56,48},{64,72... | collective-permute-start | bytes 73736 | tf_op jit(solution)/shard_map/ppermute | solution.py:26
  30.1 1.6 %collective-permute-start.6 = (bf16[5,1,32,128]{3,2,1,0:T(8,128)(2,1)S(1)}, bf16[5,1,32,128]{3,2,1,0:T(8,128)(2,1)S(1)}, u32[]{:S(2)}, u32[]{:S(2)}) collective-permute-start(bf16[5,1,32,128]{3,2,1,0:T(8,128)(2,1)S(1)} %get-tuple-element.61), channel_id=1, source_target_pairs={{0,1},{1,0},{2,3},{3,2},{4,5},{5,4},{6,7},{7,6},{8,9},{9,8},{10,11... | collective-permute-start | bytes 122888 | tf_op jit(solution)/shard_map/ppermute | solution.py:26
  31.7 3.2 %collective-permute-start.7 = (bf16[5,1,32,128]{3,2,1,0:T(8,128)(2,1)S(1)}, bf16[5,1,32,128]{3,2,1,0:T(8,128)(2,1)S(1)}, u32[]{:S(2)}, u32[]{:S(2)}) collective-permute-start(bf16[5,1,32,128]{3,2,1,0:T(8,128)(2,1)S(1)} %get-tuple-element.62), channel_id=1, source_target_pairs={{1,2},{2,1},{3,4},{4,3},{5,6},{6,5},{9,10},{10,9},{11,12},{12,11},... | collective-permute-start | bytes 122888 | tf_op jit(solution)/shard_map/ppermute | solution.py:27
  35.6 1.4 %collective-permute-done.7 = bf16[5,1,32,128]{3,2,1,0:T(8,128)(2,1)S(1)} collective-permute-done((bf16[5,1,32,128]{3,2,1,0:T(8,128)(2,1)S(1)}, bf16[5,1,32,128]{3,2,1,0:T(8,128)(2,1)S(1)}, u32[]{:S(2)}, u32[]{:S(2)}) %collective-permute-start.7) | collective-permute-done | bytes 40992 | tf_op jit(solution)/shard_map/ppermute | solution.py:27
  38.1 5.4 %collective-permute-start.8 = (bf16[1,1,32,128]{3,2,1,0:T(8,128)(2,1)S(1)}, bf16[1,1,32,128]{3,2,1,0:T(8,128)(2,1)S(1)}, u32[]{:S(2)}, u32[]{:S(2)}) collective-permute-start(bf16[1,1,32,128]{3,2,1,0:T(8,128)(2,1)S(1)} %fusion.61), channel_id=1, source_target_pairs={{0,8},{8,0},{16,24},{24,16},{32,40},{40,32},{48,56},{56,48},{64,72... | collective-permute-start | bytes 24584 | tf_op jit(solution)/shard_map/ppermute | solution.py:26
  44.6 4.1 %collective-permute-start.11 = (bf16[3,1,32,128]{3,2,1,0:T(8,128)(2,1)S(1)}, bf16[3,1,32,128]{3,2,1,0:T(8,128)(2,1)S(1)}, u32[]{:S(2)}, u32[]{:S(2)}) collective-permute-start(bf16[3,1,32,128]{3,2,1,0:T(8,128)(2,1)S(1)} %pad_maximum_fusion.26), channel_id=1, source_target_pairs={{1,2},{2,1},{3,4},{4,3},{5,6},{6,5},{9,10},{10,9},{11,12},{12,11},... | collective-permute-start | bytes 73736 | tf_op jit(solution)/shard_map/ppermute | solution.py:27
  49.2 1.1 collective-permute-done.11
  53.2 1.0 copy-done.31
  55.9 1.2 fusion.23
  57.5 1.2 fusion.21
  59.1 1.2 fusion.20
  63.6 5.8 %collective-permute-start.12 = (bf16[1,16,1536]{2,1,0:T(8,128)(2,1)S(1)}, bf16[1,16,1536]{2,1,0:T(8,128)(2,1)S(1)}, u32[]{:S(2)}, u32[]{:S(2)}) collective-permute-start(bf16[1,16,1536]{2,1,0:T(8,128)(2,1)S(1)} %bitcast.203), channel_id=1, source_target_pairs={{0,8},{8,0},{16,24},{24,16},{32,40},{40,32},{48,56},{56,48},{64,72... | collective-permute-start | bytes 147464 | tf_op jit(solution)/shard_map/ppermute | solution.py:26
  71.8 2.2 %collective-permute-start.17 = (f32[19840]{0:T(1024)S(1)}, f32[19840]{0:T(1024)S(1)}, u32[]{:S(2)}, u32[]{:S(2)}) collective-permute-start(f32[19840]{0:T(1024)S(1)} %slice_select_fusion.1), channel_id=1, source_target_pairs={{0,2},{1,3},{2,0},{3,1},{4,6},{5,7},{6,4},{7,5},{8,10},{9,11},{10,... | collective-permute-start | bytes 238088 | tf_op jit(solution)/shard_map/ppermute | solution.py:40
  74.2 2.4 %collective-permute-start.15 = (bf16[18,1,1536]{2,1,0:T(2,128)(2,1)S(1)}, bf16[18,1,1536]{2,1,0:T(2,128)(2,1)S(1)}, u32[]{:S(2)}, u32[]{:S(2)}) collective-permute-start(bf16[18,1,1536]{2,1,0:T(2,128)(2,1)S(1)} %broadcast_select_fusion.2), channel_id=1, source_target_pairs={{1,2},{2,1},{3,4},{4,3},{5,6},{6,5},{9,10},{10,9},{11,12},{12,11},... | collective-permute-start | bytes 165896 | tf_op jit(solution)/shard_map/ppermute | solution.py:27
  76.7 3.4 %collective-permute-start.18 = (f32[19840]{0:T(1024)S(1)}, f32[19840]{0:T(1024)S(1)}, u32[]{:S(2)}, u32[]{:S(2)}) collective-permute-start(f32[19840]{0:T(1024)S(1)} %select_add_fusion.1), channel_id=1, source_target_pairs={{0,4},{1,5},{2,6},{3,7},{4,0},{5,1},{6,2},{7,3},{8,12},{9,13},{10,... | collective-permute-start | bytes 238088 | tf_op jit(solution)/shard_map/ppermute | solution.py:40
  80.5 3.5 %collective-permute-done.18 = f32[19840]{0:T(1024)S(1)} collective-permute-done((f32[19840]{0:T(1024)S(1)}, f32[19840]{0:T(1024)S(1)}, u32[]{:S(2)}, u32[]{:S(2)}) %collective-permute-start.18) | collective-permute-done | bytes 79392 | tf_op jit(solution)/shard_map/ppermute | solution.py:40
  84.0 5.6 %collective-permute-start.19 = (f32[19840]{0:T(1024)S(1)}, f32[19840]{0:T(1024)S(1)}, u32[]{:S(2)}, u32[]{:S(2)}) collective-permute-start(f32[19840]{0:T(1024)S(1)} %add.131), channel_id=1, source_target_pairs={{0,8},{8,0},{16,24},{24,16},{32,40},{40,32},{48,56},{56,48},{64,72... | collective-permute-start | bytes 238088 | tf_op jit(solution)/shard_map/ppermute | solution.py:40
  91.0 0.9 collective-permute-done.19
  92.0 4.0 %collective-permute-start.20 = (f32[19840]{0:T(1024)S(1)}, f32[19840]{0:T(1024)S(1)}, u32[]{:S(2)}, u32[]{:S(2)}) collective-permute-start(f32[19840]{0:T(1024)S(1)} %add.132), channel_id=1, source_target_pairs={{0,16},{8,24},{16,0},{24,8},{32,48},{40,56},{48,32},{56,40},{64,80... | collective-permute-start | bytes 238088 | tf_op jit(solution)/shard_map/ppermute | solution.py:40
  96.0 2.8 %fusion.81 = (bf16[16,16,12,128]{3,2,1,0:T(8,128)(2,1)S(1)}, bf16[16,16,12,128]{3,2,1,0:T(8,128)(2,1)S(1)}, bf16[16,16,12,128]{3,2,1,0:T(8,128)(2,1)S(1)}, bf16[...) fusion(bf16[18,18,12,128]{3,2,1,0:T(8,128)(2,1)S(1)} %reshape.168), kind=kLoop, calls=%fused_computation.186 | loop fusion | bytes 14155776 | tf_op jit(solution)/shard_map/slice | solution.py:94
  99.5 1.7 %collective-permute-start.21 = (f32[19840]{0:T(1024)S(1)}, f32[19840]{0:T(1024)S(1)}, u32[]{:S(2)}, u32[]{:S(2)}) collective-permute-start(f32[19840]{0:T(1024)S(1)} %add.133), channel_id=1, source_target_pairs={{0,32},{8,40},{16,48},{24,56},{32,0},{40,8},{48,16},{56,24},{64,96... | collective-permute-start | bytes 238088 | tf_op jit(solution)/shard_map/ppermute | solution.py:40
  103.0 3.5 %collective-permute-start.22 = (f32[19840]{0:T(1024)S(1)}, f32[19840]{0:T(1024)S(1)}, u32[]{:S(2)}, u32[]{:S(2)}) collective-permute-start(f32[19840]{0:T(1024)S(1)} %add.134), channel_id=1, source_target_pairs={{0,64},{8,72},{16,80},{24,88},{32,96},{40,104},{48,112},{56,120},{... | collective-permute-start | bytes 238088 | tf_op jit(solution)/shard_map/ppermute | solution.py:40
  107.9 1.0 collective-permute-done.22
  110.1 1.4 %reshape.169 = bf16[16,16,768]{2,1,0:T(8,128)(2,1)} reshape(bf16[16,16,12,64]{3,2,1,0:T(8,128)(2,1)S(1)} %copy.61) | data formatting | bytes 786432 | tf_op jit(solution)/shard_map/reshape | solution.py:229
  113.1 5.4 %collective-permute-start.24 = (f32[39680]{0:T(1024)S(1)}, f32[39680]{0:T(1024)S(1)}, u32[]{:S(2)}, u32[]{:S(2)}) collective-permute-start(f32[39680]{0:T(1024)S(1)} %maximum_select_fusion.2), channel_id=1, source_target_pairs={{0,1},{1,0},{2,3},{3,2},{4,5},{5,4},{6,7},{7,6},{8,9},{9,8},{10,11... | collective-permute-start | bytes 476168 | tf_op jit(solution)/shard_map/ppermute | solution.py:40
  118.6 0.9 collective-permute-done.24
  120.3 1.2 concatenate.113
  (209 shorter events, 38.8 us)
Async XLA Ops:
  0.6 36.8 %copy-start = (bf16[128,20]{0,1:T(8,128)(2,1)S(1)}, bf16[128,20]{0,1:T(8,128)(2,1)}, u32[]{:S(2)}) copy-start(bf16[128,20]{0,1:T(8,128)(2,1)} %param.11) | copy-start | bytes 15364
  1.4 5.4 %collective-permute-start = (bf16[1,16,768]{2,1,0:T(8,128)(2,1)S(1)}, bf16[1,16,768]{2,1,0:T(8,128)(2,1)S(1)}, u32[]{:S(2)}, u32[]{:S(2)}) collective-permute-start(bf16[1,16,768]{2,1,0:T(8,128)(2,1)S(1)} %get-tuple-element.45), channel_id=1, source_target_pairs={{0,8},{8,0},{16,24},{24,16},{32,40},{40,32},{48,56},{56,48},{64,72... | collective-permute-start | bytes 73736 | tf_op jit(solution)/shard_map/ppermute | solution.py:26
  3.5 3.4 %collective-permute-start.1 = (bf16[1,16,768]{2,1,0:T(8,128)(2,1)S(1)}, bf16[1,16,768]{2,1,0:T(8,128)(2,1)S(1)}, u32[]{:S(2)}, u32[]{:S(2)}) collective-permute-start(bf16[1,16,768]{2,1,0:T(8,128)(2,1)S(1)} %get-tuple-element.46), channel_id=1, source_target_pairs={{8,16},{16,8},{24,32},{32,24},{40,48},{48,40},{56,64},{64,56},{72,... | collective-permute-start | bytes 73736 | tf_op jit(solution)/shard_map/ppermute | solution.py:27
  6.8 6.3 %copy-start.27 = (s32[16,16]{1,0:T(8,128)S(1)}, s32[16,16]{1,0:T(8,128)}, u32[]{:S(2)}) copy-start(s32[16,16]{1,0:T(8,128)} %param.12) | copy-start | bytes 3076
  7.4 5.9 %collective-permute-start.3 = (bf16[18,1,768]{2,1,0:T(2,128)(2,1)S(1)}, bf16[18,1,768]{2,1,0:T(2,128)(2,1)S(1)}, u32[]{:S(2)}, u32[]{:S(2)}) collective-permute-start(bf16[18,1,768]{2,1,0:T(2,128)(2,1)S(1)} %broadcast_select_fusion.6), channel_id=1, source_target_pairs={{1,2},{2,1},{3,4},{4,3},{5,6},{6,5},{9,10},{10,9},{11,12},{12,11},... | collective-permute-start | bytes 82952 | tf_op jit(solution)/shard_map/ppermute | solution.py:27
  11.4 1.8 %collective-permute-start.2 = (bf16[18,1,768]{2,1,0:T(2,128)(2,1)S(1)}, bf16[18,1,768]{2,1,0:T(2,128)(2,1)S(1)}, u32[]{:S(2)}, u32[]{:S(2)}) collective-permute-start(bf16[18,1,768]{2,1,0:T(2,128)(2,1)S(1)} %get-tuple-element.19), channel_id=1, source_target_pairs={{0,1},{1,0},{2,3},{3,2},{4,5},{5,4},{6,7},{7,6},{8,9},{9,8},{10,11... | collective-permute-start | bytes 82952 | tf_op jit(solution)/shard_map/ppermute | solution.py:26
  24.1 10.9 %copy-start.21 = (bf16[3,3,64,128]{3,2,1,0:T(8,128)(2,1)S(1)}, bf16[3,3,64,128]{3,2,1,0:T(8,128)(2,1)}, u32[]{:S(2)}) copy-start(bf16[3,3,64,128]{3,2,1,0:T(8,128)(2,1)} %param.9) | copy-start | bytes 442372
  24.7 12.9 %copy-start.30 = (s32[1,1,32]{2,1,0:T(1,128)S(1)}, s32[1,1,32]{2,1,0:T(1,128)}, u32[]{:S(2)}) copy-start(s32[1,1,32]{2,1,0:T(1,128)} %param.15) | copy-start | bytes 388
  25.2 5.0 %collective-permute-start.4 = (bf16[1,3,32,128]{3,2,1,0:T(8,128)(2,1)S(1)}, bf16[1,3,32,128]{3,2,1,0:T(8,128)(2,1)S(1)}, u32[]{:S(2)}, u32[]{:S(2)}) collective-permute-start(bf16[1,3,32,128]{3,2,1,0:T(8,128)(2,1)S(1)} %bitcast.207), channel_id=1, source_target_pairs={{0,8},{8,0},{16,24},{24,16},{32,40},{40,32},{48,56},{56,48},{64,72... | collective-permute-start | bytes 73736 | tf_op jit(solution)/shard_map/ppermute | solution.py:26
  28.9 1.2 collective-permute-start.5
  30.1 5.4 %collective-permute-start.6 = (bf16[5,1,32,128]{3,2,1,0:T(8,128)(2,1)S(1)}, bf16[5,1,32,128]{3,2,1,0:T(8,128)(2,1)S(1)}, u32[]{:S(2)}, u32[]{:S(2)}) collective-permute-start(bf16[5,1,32,128]{3,2,1,0:T(8,128)(2,1)S(1)} %get-tuple-element.61), channel_id=1, source_target_pairs={{0,1},{1,0},{2,3},{3,2},{4,5},{5,4},{6,7},{7,6},{8,9},{9,8},{10,11... | collective-permute-start | bytes 122888 | tf_op jit(solution)/shard_map/ppermute | solution.py:26
  31.7 5.3 %collective-permute-start.7 = (bf16[5,1,32,128]{3,2,1,0:T(8,128)(2,1)S(1)}, bf16[5,1,32,128]{3,2,1,0:T(8,128)(2,1)S(1)}, u32[]{:S(2)}, u32[]{:S(2)}) collective-permute-start(bf16[5,1,32,128]{3,2,1,0:T(8,128)(2,1)S(1)} %get-tuple-element.62), channel_id=1, source_target_pairs={{1,2},{2,1},{3,4},{4,3},{5,6},{6,5},{9,10},{10,9},{11,12},{12,11},... | collective-permute-start | bytes 122888 | tf_op jit(solution)/shard_map/ppermute | solution.py:27
  38.1 6.4 %collective-permute-start.8 = (bf16[1,1,32,128]{3,2,1,0:T(8,128)(2,1)S(1)}, bf16[1,1,32,128]{3,2,1,0:T(8,128)(2,1)S(1)}, u32[]{:S(2)}, u32[]{:S(2)}) collective-permute-start(bf16[1,1,32,128]{3,2,1,0:T(8,128)(2,1)S(1)} %fusion.61), channel_id=1, source_target_pairs={{0,8},{8,0},{16,24},{24,16},{32,40},{40,32},{48,56},{56,48},{64,72... | collective-permute-start | bytes 24584 | tf_op jit(solution)/shard_map/ppermute | solution.py:26
  43.5 1.0 collective-permute-start.9
  44.5 4.6 %collective-permute-start.10 = (bf16[3,1,32,128]{3,2,1,0:T(8,128)(2,1)S(1)}, bf16[3,1,32,128]{3,2,1,0:T(8,128)(2,1)S(1)}, u32[]{:S(2)}, u32[]{:S(2)}) collective-permute-start(bf16[3,1,32,128]{3,2,1,0:T(8,128)(2,1)S(1)} %pad_maximum_fusion.26), channel_id=1, source_target_pairs={{0,1},{1,0},{2,3},{3,2},{4,5},{5,4},{6,7},{7,6},{8,9},{9,8},{10,11... | collective-permute-start | bytes 73736 | tf_op jit(solution)/shard_map/ppermute | solution.py:26
  44.6 5.6 %collective-permute-start.11 = (bf16[3,1,32,128]{3,2,1,0:T(8,128)(2,1)S(1)}, bf16[3,1,32,128]{3,2,1,0:T(8,128)(2,1)S(1)}, u32[]{:S(2)}, u32[]{:S(2)}) collective-permute-start(bf16[3,1,32,128]{3,2,1,0:T(8,128)(2,1)S(1)} %pad_maximum_fusion.26), channel_id=1, source_target_pairs={{1,2},{2,1},{3,4},{4,3},{5,6},{6,5},{9,10},{10,9},{11,12},{12,11},... | collective-permute-start | bytes 73736 | tf_op jit(solution)/shard_map/ppermute | solution.py:27
  63.6 7.3 %collective-permute-start.12 = (bf16[1,16,1536]{2,1,0:T(8,128)(2,1)S(1)}, bf16[1,16,1536]{2,1,0:T(8,128)(2,1)S(1)}, u32[]{:S(2)}, u32[]{:S(2)}) collective-permute-start(bf16[1,16,1536]{2,1,0:T(8,128)(2,1)S(1)} %bitcast.203), channel_id=1, source_target_pairs={{0,8},{8,0},{16,24},{24,16},{32,40},{40,32},{48,56},{56,48},{64,72... | collective-permute-start | bytes 147464 | tf_op jit(solution)/shard_map/ppermute | solution.py:26
  69.5 1.5 %collective-permute-start.13 = (bf16[1,16,1536]{2,1,0:T(8,128)(2,1)S(1)}, bf16[1,16,1536]{2,1,0:T(8,128)(2,1)S(1)}, u32[]{:S(2)}, u32[]{:S(2)}) collective-permute-start(bf16[1,16,1536]{2,1,0:T(8,128)(2,1)S(1)} %bitcast.204), channel_id=1, source_target_pairs={{8,16},{16,8},{24,32},{32,24},{40,48},{48,40},{56,64},{64,56},{72,... | collective-permute-start | bytes 147464 | tf_op jit(solution)/shard_map/ppermute | solution.py:27
  70.2 1.5 %collective-permute-start.16 = (f32[39680]{0:T(1024)S(1)}, f32[39680]{0:T(1024)S(1)}, u32[]{:S(2)}, u32[]{:S(2)}) collective-permute-start(f32[39680]{0:T(1024)S(1)} %slice_select_fusion), channel_id=1, source_target_pairs={{0,1},{1,0},{2,3},{3,2},{4,5},{5,4},{6,7},{7,6},{8,9},{9,8},{10,11... | collective-permute-start | bytes 476168 | tf_op jit(solution)/shard_map/ppermute | solution.py:40
  71.8 4.9 %collective-permute-start.17 = (f32[19840]{0:T(1024)S(1)}, f32[19840]{0:T(1024)S(1)}, u32[]{:S(2)}, u32[]{:S(2)}) collective-permute-start(f32[19840]{0:T(1024)S(1)} %slice_select_fusion.1), channel_id=1, source_target_pairs={{0,2},{1,3},{2,0},{3,1},{4,6},{5,7},{6,4},{7,5},{8,10},{9,11},{10,... | collective-permute-start | bytes 238088 | tf_op jit(solution)/shard_map/ppermute | solution.py:40
  74.2 6.1 %collective-permute-start.15 = (bf16[18,1,1536]{2,1,0:T(2,128)(2,1)S(1)}, bf16[18,1,1536]{2,1,0:T(2,128)(2,1)S(1)}, u32[]{:S(2)}, u32[]{:S(2)}) collective-permute-start(bf16[18,1,1536]{2,1,0:T(2,128)(2,1)S(1)} %broadcast_select_fusion.2), channel_id=1, source_target_pairs={{1,2},{2,1},{3,4},{4,3},{5,6},{6,5},{9,10},{10,9},{11,12},{12,11},... | collective-permute-start | bytes 165896 | tf_op jit(solution)/shard_map/ppermute | solution.py:27
  76.6 3.6 %collective-permute-start.14 = (bf16[18,1,1536]{2,1,0:T(2,128)(2,1)S(1)}, bf16[18,1,1536]{2,1,0:T(2,128)(2,1)S(1)}, u32[]{:S(2)}, u32[]{:S(2)}) collective-permute-start(bf16[18,1,1536]{2,1,0:T(2,128)(2,1)S(1)} %get-tuple-element.16), channel_id=1, source_target_pairs={{0,1},{1,0},{2,3},{3,2},{4,5},{5,4},{6,7},{7,6},{8,9},{9,8},{10,11... | collective-permute-start | bytes 165896 | tf_op jit(solution)/shard_map/ppermute | solution.py:26
  76.7 7.2 %collective-permute-start.18 = (f32[19840]{0:T(1024)S(1)}, f32[19840]{0:T(1024)S(1)}, u32[]{:S(2)}, u32[]{:S(2)}) collective-permute-start(f32[19840]{0:T(1024)S(1)} %select_add_fusion.1), channel_id=1, source_target_pairs={{0,4},{1,5},{2,6},{3,7},{4,0},{5,1},{6,2},{7,3},{8,12},{9,13},{10,... | collective-permute-start | bytes 238088 | tf_op jit(solution)/shard_map/ppermute | solution.py:40
  84.0 8.0 %collective-permute-start.19 = (f32[19840]{0:T(1024)S(1)}, f32[19840]{0:T(1024)S(1)}, u32[]{:S(2)}, u32[]{:S(2)}) collective-permute-start(f32[19840]{0:T(1024)S(1)} %add.131), channel_id=1, source_target_pairs={{0,8},{8,0},{16,24},{24,16},{32,40},{40,32},{48,56},{56,48},{64,72... | collective-permute-start | bytes 238088 | tf_op jit(solution)/shard_map/ppermute | solution.py:40
  92.0 7.5 %collective-permute-start.20 = (f32[19840]{0:T(1024)S(1)}, f32[19840]{0:T(1024)S(1)}, u32[]{:S(2)}, u32[]{:S(2)}) collective-permute-start(f32[19840]{0:T(1024)S(1)} %add.132), channel_id=1, source_target_pairs={{0,16},{8,24},{16,0},{24,8},{32,48},{40,56},{48,32},{56,40},{64,80... | collective-permute-start | bytes 238088 | tf_op jit(solution)/shard_map/ppermute | solution.py:40
  99.5 3.6 %collective-permute-start.21 = (f32[19840]{0:T(1024)S(1)}, f32[19840]{0:T(1024)S(1)}, u32[]{:S(2)}, u32[]{:S(2)}) collective-permute-start(f32[19840]{0:T(1024)S(1)} %add.133), channel_id=1, source_target_pairs={{0,32},{8,40},{16,48},{24,56},{32,0},{40,8},{48,16},{56,24},{64,96... | collective-permute-start | bytes 238088 | tf_op jit(solution)/shard_map/ppermute | solution.py:40
  102.2 4.4 %copy-start.22 = (bf16[128,64]{0,1:T(8,128)(2,1)S(1)}, bf16[128,64]{0,1:T(8,128)(2,1)}, u32[]{:S(2)}) copy-start(bf16[128,64]{0,1:T(8,128)(2,1)} %get-tuple-element.54) | copy-start | bytes 49156
  102.2 4.3 %copy-start.23 = (bf16[128,64]{0,1:T(8,128)(2,1)S(1)}, bf16[128,64]{0,1:T(8,128)(2,1)}, u32[]{:S(2)}) copy-start(bf16[128,64]{0,1:T(8,128)(2,1)} %get-tuple-element.55) | copy-start | bytes 49156
  103.0 5.9 %collective-permute-start.22 = (f32[19840]{0:T(1024)S(1)}, f32[19840]{0:T(1024)S(1)}, u32[]{:S(2)}, u32[]{:S(2)}) collective-permute-start(f32[19840]{0:T(1024)S(1)} %add.134), channel_id=1, source_target_pairs={{0,64},{8,72},{16,80},{24,88},{32,96},{40,104},{48,112},{56,120},{... | collective-permute-start | bytes 238088 | tf_op jit(solution)/shard_map/ppermute | solution.py:40
  108.9 3.4 %collective-permute-start.23 = (f32[19840]{0:T(1024)S(1)}, f32[19840]{0:T(1024)S(1)}, u32[]{:S(2)}, u32[]{:S(2)}) collective-permute-start(f32[19840]{0:T(1024)S(1)} %add.135), channel_id=1, source_target_pairs={{0,2},{1,3},{2,0},{3,1},{4,6},{5,7},{6,4},{7,5},{8,10},{9,11},{10,... | collective-permute-start | bytes 238088 | tf_op jit(solution)/shard_map/ppermute | solution.py:40
  113.1 6.4 %collective-permute-start.24 = (f32[39680]{0:T(1024)S(1)}, f32[39680]{0:T(1024)S(1)}, u32[]{:S(2)}, u32[]{:S(2)}) collective-permute-start(f32[39680]{0:T(1024)S(1)} %maximum_select_fusion.2), channel_id=1, source_target_pairs={{0,1},{1,0},{2,3},{3,2},{4,5},{5,4},{6,7},{7,6},{8,9},{9,8},{10,11... | collective-permute-start | bytes 476168 | tf_op jit(solution)/shard_map/ppermute | solution.py:40
  119.6 3.8 %copy-start.1 = (bf16[128,20]{0,1:T(8,128)(2,1)S(1)}, bf16[128,20]{0,1:T(8,128)(2,1)}, u32[]{:S(2)}) copy-start(bf16[128,20]{0,1:T(8,128)(2,1)} %param.11) | copy-start | bytes 15364
  (25 other events, 39.1 us)

commit v4 on v3

--- a/solution.py
+++ b/solution.py
@@ -40,7 +40,33 @@
     return lax.ppermute(value, axis, [(i, i ^ bit) for i in range(size)])
 
 
-def butterfly_sum(flat, halvings=2):
+def swap_with(value, axis, bit, extra):
+    size = value.shape[0]
+    both = exchange(jnp.concatenate([value, extra.astype(value.dtype).reshape(-1)]), axis, bit)
+    return both[:size], both[size:].reshape(extra.shape).astype(extra.dtype)
+
+
+def halo_ends(cells, axis, dim):
+    odd = lax.axis_index(axis) % 2 == 1
+    head = lax.slice_in_dim(cells, 0, 1, axis=dim)
+    tail = lax.slice_in_dim(cells, cells.shape[dim] - 1, cells.shape[dim], axis=dim)
+    return odd, jnp.where(odd, head, tail), jnp.where(odd, tail, head)
+
+
+def outer_swap(piece, axis):
+    count = lax.axis_size(axis)
+    return lax.ppermute(
+        piece, axis, [pair for k in range(1, count - 1, 2) for pair in ((k, k + 1), (k + 1, k))]
+    )
+
+
+def halo_join(cells, odd, inner, outer, dim):
+    return jnp.concatenate(
+        [jnp.where(odd, inner, outer), cells, jnp.where(odd, outer, inner)], axis=dim
+    )
+
+
+def butterfly_sum(flat, cells, halvings=2):
     steps = []
     for axis in ("col", "row"):
         bit = 1
@@ -52,14 +78,29 @@
         half = flat.shape[0] // 2
         low, high = flat[:half], flat[half:]
         keep = jnp.where(upper, high, low)
-        flat = keep + exchange(jnp.where(upper, low, high), axis, bit)
+        give = jnp.where(upper, low, high)
+        if (axis, bit) == ("col", 1):
+            odd, inner_piece, outer_piece = halo_ends(cells, "col", 1)
+            outer = outer_swap(outer_piece, "col")
+            got, inner = swap_with(give, axis, bit, inner_piece)
+            cells = halo_join(cells, odd, inner, outer, 1)
+        else:
+            got = exchange(give, axis, bit)
+        flat = keep + got
     for axis, bit in steps[halvings:]:
-        flat = flat + exchange(flat, axis, bit)
+        if (axis, bit) == ("row", 1):
+            odd, inner_piece, outer_piece = halo_ends(cells, "row", 0)
+            outer = outer_swap(outer_piece, "row")
+            got, inner = swap_with(flat, axis, bit, inner_piece)
+            cells = halo_join(cells, odd, inner, outer, 0)
+        else:
+            got = exchange(flat, axis, bit)
+        flat = flat + got
     for axis, bit in reversed(steps[:halvings]):
         upper = (lax.axis_index(axis) // bit) % 2 == 1
         other = exchange(flat, axis, bit)
         flat = jnp.where(upper, jnp.concatenate([other, flat]), jnp.concatenate([flat, other]))
-    return flat
+    return flat, cells
 
 
 def silu_slope(value):
@@ -222,14 +263,13 @@
             ).reshape(3, C_IN, C_OUT)
         )
     conv_term = jnp.stack(conv_rows)
-    padded_grad = with_halo(
-        grad_pre.reshape(tile_rows, tile_cols, DATES * C_OUT), (("row", 0), ("col", 1)), 1
-    ).reshape(tile_rows + 2, tile_cols + 2, DATES, C_OUT)
+    flat, padded_grad = butterfly_sum(
+        jnp.concatenate([conv_term.reshape(-1), time_term.reshape(-1), class_term.reshape(-1)]),
+        grad_pre.reshape(tile_rows, tile_cols, DATES * C_OUT),
+    )
+    padded_grad = padded_grad.reshape(tile_rows + 2, tile_cols + 2, DATES, C_OUT)
     input_sum = transposed_conv(padded_grad, conv_weight, tile_rows, tile_cols)
     input_grad = input_sum.astype(jnp.bfloat16).reshape(tile_rows, tile_cols, DATES * C_IN)
-    flat = butterfly_sum(
-        jnp.concatenate([conv_term.reshape(-1), time_term.reshape(-1), class_term.reshape(-1)])
-    )
     conv_size, time_size = (conv_term.size, time_term.size)
     conv_grad = flat[:conv_size].reshape(conv_term.shape)
     time_grad = flat[conv_size : conv_size + time_size].reshape(time_term.shape)

time: 124 us -> 123 us (level)
  starting transfers between devices: 61.2 us -> 58.3 us
  waiting for transfers between devices: 11.4 us -> 12.7 us
  matrix products: 17.1 us -> 18.4 us
    ppermute x8 -> x6, starting transfers between devices: 18.8 us -> 13.2 us  [with_halo(): lax.ppermute(jnp.where(odd, head, tail), axis, [(i, i ^ 1) for i in range...]
    ppermute x0 -> x2, starting transfers between devices: none -> 4.42 us  [outer_swap(): lax.ppermute(piece, axis, [pair for k in range(1, count - 1, 2) for pair...]
    ppermute x8 -> x6, starting transfers between devices: 16.4 us -> 13 us  [with_halo(): lax.ppermute(jnp.where(odd, tail, head), axis, [pair for k in range(1, co...]
    ppermute x9, starting transfers between devices: 26 us -> 27.6 us  [exchange(): return lax.ppermute(value, axis, [(i, i ^ bit) for i in range(size)])]
    dot_general x3, matrix products: 1.25 us -> 2.52 us  [per_device(): jnp.einsum('ijtc,ijtd->cd', padded_hidden[:, :, time_tap:time_tap + DATES...]
    ppermute x8 -> x6, waiting for transfers between devices: 2.67 us -> 3.23 us  [with_halo(): lax.ppermute(jnp.where(odd, tail, head), axis, [pair for k in range(1, co...]
    unnamed x83 -> x73, local copies, waits for them, and re-layouts: 7.86 us -> 8.09 us
  transfers between devices with their start and end apart: 25 -> 23, of which waited for: 13 -> 12; matrix products, arithmetic and copies ran while one was open for 14% -> 13% of each run, Pallas kernels for 0% -> 0%
where the time goes in v4:
time: 123 us
  starting transfers between devices  58.3 us (47%)
  local copies, waits for them, and re-layouts  26.5 us (22%)
  matrix products  18.4 us (15%)
  waiting for transfers between devices  12.7 us (10%)
  other arithmetic  5.01 us (4%)
  between operations  1.77 us (1%)
    ppermute x9, starting transfers between devices, exchange(): return lax.ppermute(value, axis, [(i, i ^ bit) for i in range(size)])  27.6 us
    ppermute x6, starting transfers between devices, with_halo(): lax.ppermute(jnp.where(odd, head, tail), axis, [(i, i ^ 1) for i in range...  13.2 us
    ppermute x6, starting transfers between devices, with_halo(): lax.ppermute(jnp.where(odd, tail, head), axis, [pair for k in range(1, co...  13 us
    unnamed x73, local copies, waits for them, and re-layouts  8.09 us
    ppermute x9, waiting for transfers between devices, exchange(): return lax.ppermute(value, axis, [(i, i ^ bit) for i in range(size)])  7.75 us
    ppermute x2, starting transfers between devices, outer_swap(): lax.ppermute(piece, axis, [pair for k in range(1, count - 1, 2) for pair...  4.42 us
    dot_general x3, matrix products, spatial_forward(): jnp.dot(tap_patch, conv_weight[row_tap].reshape(3 * C_IN, C_OUT), preferr...  4.06 us
    dot_general x3, matrix products, per_device(): jnp.einsum('ijtc,ijtd->cd', tap_patch, grad_pre, preferred_element_type=j...  3.62 us
  transfers between devices with their start and end apart: 23, of which 12 were waited for; matrix products, arithmetic and copies ran while one was open for 13% of the time, Pallas kernels for 0%

profile of v4, /device:TPU:1, one launch (start us, length us, event | category | flops | bytes accessed | tf_op | source)
XLA Modules:
  0.0 122.6 jit_solution(3433020371564878574)
XLA Ops:
  1.4 2.0 %collective-permute-start = (bf16[1,16,768]{2,1,0:T(8,128)(2,1)S(1)}, bf16[1,16,768]{2,1,0:T(8,128)(2,1)S(1)}, u32[]{:S(2)}, u32[]{:S(2)}) collective-permute-start(bf16[1,16,768]{2,1,0:T(8,128)(2,1)S(1)} %get-tuple-element.45), channel_id=1, source_target_pairs={{0,8},{8,0},{16,24},{24,16},{32,40},{40,32},{48,56},{56,48},{64,72... | collective-permute-start | bytes 73736 | tf_op jit(solution)/shard_map/ppermute | solution.py:26
  7.4 4.0 %collective-permute-start.3 = (bf16[18,1,768]{2,1,0:T(2,128)(2,1)S(1)}, bf16[18,1,768]{2,1,0:T(2,128)(2,1)S(1)}, u32[]{:S(2)}, u32[]{:S(2)}) collective-permute-start(bf16[18,1,768]{2,1,0:T(2,128)(2,1)S(1)} %broadcast_select_fusion.6), channel_id=1, source_target_pairs={{1,2},{2,1},{3,4},{4,3},{5,6},{6,5},{9,10},{10,9},{11,12},{12,11},... | collective-permute-start | bytes 82952 | tf_op jit(solution)/shard_map/ppermute | solution.py:27
  14.5 2.6 %fusion.83 = (bf16[16,16,12,64]{3,2,1,0:T(8,128)(2,1)S(1)}, bf16[16,16,12,64]{3,2,1,0:T(8,128)(2,1)S(1)}, bf16[16,16,12,64]{3,2,1,0:T(8,128)(2,1)S(1)}, bf16[16,...) fusion(bf16[18,18,12,64]{3,2,1,0:T(8,128)(2,1)S(1)} %reshape.158), kind=kLoop, calls=%fused_computation.191 | loop fusion | bytes 7077888 | tf_op jit(solution)/shard_map/slice | solution.py:116
  21.0 2.3 %multiply_convert_fusion.2 = (bf16[16,16,12,128]{3,1,2,0:T(8,128)(2,1)S(1)}, f32[16,16,12,128]{3,1,2,0:T(8,128)}) fusion(bf16[192,128,1,1]{1,0,3,2:T(8,128)(2,1)S(1)} %bitcast.192, bf16[16,16,12,64]{3,1,2,0:T(8,128)(2,1)S(1)} %copy.98, bf16[16,16,12,64]{3,1,2,0:T(8,128)(2,1)S(1)} %copy.97, bf16[16,16,12,64]{3,1,2,0:T(8,128)(2,1)S(1)} %copy.96, ...), kind=kOutput, calls=%fused_computation.28 | convolution fusion | flops 157286400 | bytes 6733824 | tf_op jit(solution)/shard_map/dot_general | solution.py:121
  25.1 3.7 %collective-permute-start.4 = (bf16[1,3,32,128]{3,2,1,0:T(8,128)(2,1)S(1)}, bf16[1,3,32,128]{3,2,1,0:T(8,128)(2,1)S(1)}, u32[]{:S(2)}, u32[]{:S(2)}) collective-permute-start(bf16[1,3,32,128]{3,2,1,0:T(8,128)(2,1)S(1)} %bitcast.197), channel_id=1, source_target_pairs={{0,8},{8,0},{16,24},{24,16},{32,40},{40,32},{48,56},{56,48},{64,72... | collective-permute-start | bytes 73736 | tf_op jit(solution)/shard_map/ppermute | solution.py:26
  30.1 1.6 %collective-permute-start.6 = (bf16[5,1,32,128]{3,2,1,0:T(8,128)(2,1)S(1)}, bf16[5,1,32,128]{3,2,1,0:T(8,128)(2,1)S(1)}, u32[]{:S(2)}, u32[]{:S(2)}) collective-permute-start(bf16[5,1,32,128]{3,2,1,0:T(8,128)(2,1)S(1)} %get-tuple-element.63), channel_id=1, source_target_pairs={{0,1},{1,0},{2,3},{3,2},{4,5},{5,4},{6,7},{7,6},{8,9},{9,8},{10,11... | collective-permute-start | bytes 122888 | tf_op jit(solution)/shard_map/ppermute | solution.py:26
  31.6 3.2 %collective-permute-start.7 = (bf16[5,1,32,128]{3,2,1,0:T(8,128)(2,1)S(1)}, bf16[5,1,32,128]{3,2,1,0:T(8,128)(2,1)S(1)}, u32[]{:S(2)}, u32[]{:S(2)}) collective-permute-start(bf16[5,1,32,128]{3,2,1,0:T(8,128)(2,1)S(1)} %get-tuple-element.64), channel_id=1, source_target_pairs={{1,2},{2,1},{3,4},{4,3},{5,6},{6,5},{9,10},{10,9},{11,12},{12,11},... | collective-permute-start | bytes 122888 | tf_op jit(solution)/shard_map/ppermute | solution.py:27
  34.9 2.1 %collective-permute-done.7 = bf16[5,1,32,128]{3,2,1,0:T(8,128)(2,1)S(1)} collective-permute-done((bf16[5,1,32,128]{3,2,1,0:T(8,128)(2,1)S(1)}, bf16[5,1,32,128]{3,2,1,0:T(8,128)(2,1)S(1)}, u32[]{:S(2)}, u32[]{:S(2)}) %collective-permute-start.7) | collective-permute-done | bytes 40992 | tf_op jit(solution)/shard_map/ppermute | solution.py:27
  38.0 5.7 %collective-permute-start.8 = (bf16[1,1,32,128]{3,2,1,0:T(8,128)(2,1)S(1)}, bf16[1,1,32,128]{3,2,1,0:T(8,128)(2,1)S(1)}, u32[]{:S(2)}, u32[]{:S(2)}) collective-permute-start(bf16[1,1,32,128]{3,2,1,0:T(8,128)(2,1)S(1)} %fusion.62), channel_id=1, source_target_pairs={{0,8},{8,0},{16,24},{24,16},{32,40},{40,32},{48,56},{56,48},{64,72... | collective-permute-start | bytes 24584 | tf_op jit(solution)/shard_map/ppermute | solution.py:26
  44.9 3.8 %collective-permute-start.11 = (bf16[3,1,32,128]{3,2,1,0:T(8,128)(2,1)S(1)}, bf16[3,1,32,128]{3,2,1,0:T(8,128)(2,1)S(1)}, u32[]{:S(2)}, u32[]{:S(2)}) collective-permute-start(bf16[3,1,32,128]{3,2,1,0:T(8,128)(2,1)S(1)} %pad_maximum_fusion.28), channel_id=1, source_target_pairs={{1,2},{2,1},{3,4},{4,3},{5,6},{6,5},{9,10},{10,9},{11,12},{12,11},... | collective-permute-start | bytes 73736 | tf_op jit(solution)/shard_map/ppermute | solution.py:27
  49.1 1.1 collective-permute-done.11
  51.6 1.1 convolution_bitcast_fusion.2
  52.6 1.1 convolution_bitcast_fusion
  54.4 1.0 copy-done.26
  57.1 1.2 %fusion.23 = f32[192,128,1,1]{1,0,3,2:T(8,128)S(1)} fusion(bf16[16,16,12,128]{3,1,2,0:T(8,128)(2,1)S(1)} %multiply_convert_fusion, bf16[16,16,12,64]{3,1,2,0:T(8,128)(2,1)S(1)} %copy-done.18, bf16[16,16,12,64]{3,1,2,0:T(8,128)(2,1)S(1)} %copy-done.14, bf16[16,16,12,64]{3,1,2,0:T(8,128)(2,1)S(1)} %copy-done.12), kind=kOutput, calls=%fused_computation.47 | convolution fusion | flops 154533888 | bytes 2064384 | tf_op jit(solution)/shard_map/ijtc,ijtd->cd/dot_general | solution.py:261
  58.4 1.2 fusion.21
  60.0 1.2 fusion.20
  65.6 3.8 %collective-permute-start.15 = (bf16[16,1,1536]{2,1,0:T(2,128)(2,1)S(1)}, bf16[16,1,1536]{2,1,0:T(2,128)(2,1)S(1)}, u32[]{:S(2)}, u32[]{:S(2)}) collective-permute-start(bf16[16,1,1536]{2,1,0:T(2,128)(2,1)S(1)} %get-tuple-element.44), channel_id=1, source_target_pairs={{1,2},{2,1},{3,4},{4,3},{5,6},{6,5},{9,10},{10,9},{11,12},{12,11},... | collective-permute-start | bytes 147464 | tf_op jit(solution)/shard_map/ppermute | solution.py:58
  69.4 1.4 %collective-permute-start.13 = (f32[19840]{0:T(1024)S(1)}, f32[19840]{0:T(1024)S(1)}, u32[]{:S(2)}, u32[]{:S(2)}) collective-permute-start(f32[19840]{0:T(1024)S(1)} %slice_select_fusion.1), channel_id=1, source_target_pairs={{0,2},{1,3},{2,0},{3,1},{4,6},{5,7},{6,4},{7,5},{8,10},{9,11},{10,... | collective-permute-start | bytes 238088 | tf_op jit(solution)/shard_map/ppermute | solution.py:40
  71.9 1.6 %collective-permute-done.13 = f32[19840]{0:T(1024)S(1)} collective-permute-done((f32[19840]{0:T(1024)S(1)}, f32[19840]{0:T(1024)S(1)}, u32[]{:S(2)}, u32[]{:S(2)}) %collective-permute-start.13) | collective-permute-done | bytes 79392 | tf_op jit(solution)/shard_map/ppermute | solution.py:40
  73.5 3.3 %collective-permute-start.14 = (f32[19840]{0:T(1024)S(1)}, f32[19840]{0:T(1024)S(1)}, u32[]{:S(2)}, u32[]{:S(2)}) collective-permute-start(f32[19840]{0:T(1024)S(1)} %select_add_fusion), channel_id=1, source_target_pairs={{0,4},{1,5},{2,6},{3,7},{4,0},{5,1},{6,2},{7,3},{8,12},{9,13},{10,... | collective-permute-start | bytes 238088 | tf_op jit(solution)/shard_map/ppermute | solution.py:40
  76.9 1.7 %collective-permute-done.14 = f32[19840]{0:T(1024)S(1)} collective-permute-done((f32[19840]{0:T(1024)S(1)}, f32[19840]{0:T(1024)S(1)}, u32[]{:S(2)}, u32[]{:S(2)}) %collective-permute-start.14) | collective-permute-done | bytes 79392 | tf_op jit(solution)/shard_map/ppermute | solution.py:40
  78.7 5.8 %collective-permute-start.16 = (f32[47488]{0:T(1024)S(1)}, f32[47488]{0:T(1024)S(1)}, u32[]{:S(2)}, u32[]{:S(2)}) collective-permute-start(f32[47488]{0:T(1024)S(1)} %pad_maximum_fusion.15), channel_id=1, source_target_pairs={{0,8},{8,0},{16,24},{24,16},{32,40},{40,32},{48,56},{56,48},{64,72... | collective-permute-start | bytes 569864 | tf_op jit(solution)/shard_map/ppermute | solution.py:40
  85.2 2.7 %collective-permute-done.16 = f32[47488]{0:T(1024)S(1)} collective-permute-done((f32[47488]{0:T(1024)S(1)}, f32[47488]{0:T(1024)S(1)}, u32[]{:S(2)}, u32[]{:S(2)}) %collective-permute-start.16) | collective-permute-done | bytes 189984 | tf_op jit(solution)/shard_map/ppermute | solution.py:40
  87.9 4.0 %collective-permute-start.18 = (f32[19840]{0:T(1024)S(1)}, f32[19840]{0:T(1024)S(1)}, u32[]{:S(2)}, u32[]{:S(2)}) collective-permute-start(f32[19840]{0:T(1024)S(1)} %slice_add_fusion.1), channel_id=1, source_target_pairs={{0,16},{8,24},{16,0},{24,8},{32,48},{40,56},{48,32},{56,40},{64,80... | collective-permute-start | bytes 238088 | tf_op jit(solution)/shard_map/ppermute | solution.py:40
  93.4 2.8 %fusion.82 = (bf16[16,16,12,128]{3,2,1,0:T(8,128)(2,1)S(1)}, bf16[16,16,12,128]{3,2,1,0:T(8,128)(2,1)S(1)}, bf16[16,16,12,128]{3,2,1,0:T(8,128)(2,1)S(1)}, bf16[...) fusion(bf16[18,18,12,128]{3,2,1,0:T(8,128)(2,1)S(1)} %reshape.172), kind=kLoop, calls=%fused_computation.190 | loop fusion | bytes 14155776 | tf_op jit(solution)/shard_map/slice | solution.py:135
  96.9 2.6 %collective-permute-start.19 = (f32[19840]{0:T(1024)S(1)}, f32[19840]{0:T(1024)S(1)}, u32[]{:S(2)}, u32[]{:S(2)}) collective-permute-start(f32[19840]{0:T(1024)S(1)} %add.133), channel_id=1, source_target_pairs={{0,32},{8,40},{16,48},{24,56},{32,0},{40,8},{48,16},{56,24},{64,96... | collective-permute-start | bytes 238088 | tf_op jit(solution)/shard_map/ppermute | solution.py:40
  101.4 3.2 %collective-permute-start.20 = (f32[19840]{0:T(1024)S(1)}, f32[19840]{0:T(1024)S(1)}, u32[]{:S(2)}, u32[]{:S(2)}) collective-permute-start(f32[19840]{0:T(1024)S(1)} %add.134), channel_id=1, source_target_pairs={{0,64},{8,72},{16,80},{24,88},{32,96},{40,104},{48,112},{56,120},{... | collective-permute-start | bytes 238088 | tf_op jit(solution)/shard_map/ppermute | solution.py:40
  106.5 1.8 %collective-permute-start.21 = (f32[19840]{0:T(1024)S(1)}, f32[19840]{0:T(1024)S(1)}, u32[]{:S(2)}, u32[]{:S(2)}) collective-permute-start(f32[19840]{0:T(1024)S(1)} %add.135), channel_id=1, source_target_pairs={{0,2},{1,3},{2,0},{3,1},{4,6},{5,7},{6,4},{7,5},{8,10},{9,11},{10,... | collective-permute-start | bytes 238088 | tf_op jit(solution)/shard_map/ppermute | solution.py:40
  109.4 1.4 %reshape.173 = bf16[16,16,768]{2,1,0:T(8,128)(2,1)} reshape(bf16[16,16,12,64]{3,2,1,0:T(8,128)(2,1)S(1)} %copy.62) | data formatting | bytes 786432 | tf_op jit(solution)/shard_map/reshape | solution.py:272
  112.4 5.3 %collective-permute-start.22 = (f32[39680]{0:T(1024)S(1)}, f32[39680]{0:T(1024)S(1)}, u32[]{:S(2)}, u32[]{:S(2)}) collective-permute-start(f32[39680]{0:T(1024)S(1)} %maximum_select_fusion.2), channel_id=1, source_target_pairs={{0,1},{1,0},{2,3},{3,2},{4,5},{5,4},{6,7},{7,6},{8,9},{9,8},{10,11... | collective-permute-start | bytes 476168 | tf_op jit(solution)/shard_map/ppermute | solution.py:40
  119.5 1.2 concatenate.121
  (200 shorter events, 39.3 us)
Async XLA Ops:
  0.6 36.7 %copy-start = (bf16[128,20]{0,1:T(8,128)(2,1)S(1)}, bf16[128,20]{0,1:T(8,128)(2,1)}, u32[]{:S(2)}) copy-start(bf16[128,20]{0,1:T(8,128)(2,1)} %param.11) | copy-start | bytes 15364
  1.4 5.4 %collective-permute-start = (bf16[1,16,768]{2,1,0:T(8,128)(2,1)S(1)}, bf16[1,16,768]{2,1,0:T(8,128)(2,1)S(1)}, u32[]{:S(2)}, u32[]{:S(2)}) collective-permute-start(bf16[1,16,768]{2,1,0:T(8,128)(2,1)S(1)} %get-tuple-element.45), channel_id=1, source_target_pairs={{0,8},{8,0},{16,24},{24,16},{32,40},{40,32},{48,56},{56,48},{64,72... | collective-permute-start | bytes 73736 | tf_op jit(solution)/shard_map/ppermute | solution.py:26
  3.5 3.4 %collective-permute-start.1 = (bf16[1,16,768]{2,1,0:T(8,128)(2,1)S(1)}, bf16[1,16,768]{2,1,0:T(8,128)(2,1)S(1)}, u32[]{:S(2)}, u32[]{:S(2)}) collective-permute-start(bf16[1,16,768]{2,1,0:T(8,128)(2,1)S(1)} %get-tuple-element.46), channel_id=1, source_target_pairs={{8,16},{16,8},{24,32},{32,24},{40,48},{48,40},{56,64},{64,56},{72,... | collective-permute-start | bytes 73736 | tf_op jit(solution)/shard_map/ppermute | solution.py:27
  6.8 6.3 %copy-start.22 = (s32[16,16]{1,0:T(8,128)S(1)}, s32[16,16]{1,0:T(8,128)}, u32[]{:S(2)}) copy-start(s32[16,16]{1,0:T(8,128)} %param.12) | copy-start | bytes 3076
  7.4 5.9 %collective-permute-start.3 = (bf16[18,1,768]{2,1,0:T(2,128)(2,1)S(1)}, bf16[18,1,768]{2,1,0:T(2,128)(2,1)S(1)}, u32[]{:S(2)}, u32[]{:S(2)}) collective-permute-start(bf16[18,1,768]{2,1,0:T(2,128)(2,1)S(1)} %broadcast_select_fusion.6), channel_id=1, source_target_pairs={{1,2},{2,1},{3,4},{4,3},{5,6},{6,5},{9,10},{10,9},{11,12},{12,11},... | collective-permute-start | bytes 82952 | tf_op jit(solution)/shard_map/ppermute | solution.py:27
  11.4 1.8 %collective-permute-start.2 = (bf16[18,1,768]{2,1,0:T(2,128)(2,1)S(1)}, bf16[18,1,768]{2,1,0:T(2,128)(2,1)S(1)}, u32[]{:S(2)}, u32[]{:S(2)}) collective-permute-start(bf16[18,1,768]{2,1,0:T(2,128)(2,1)S(1)} %get-tuple-element.19), channel_id=1, source_target_pairs={{0,1},{1,0},{2,3},{3,2},{4,5},{5,4},{6,7},{7,6},{8,9},{9,8},{10,11... | collective-permute-start | bytes 82952 | tf_op jit(solution)/shard_map/ppermute | solution.py:26
  18.0 2.0 %copy-start.11 = (bf16[16,16,12,64]{3,1,2,0:T(8,128)(2,1)}, bf16[16,16,12,64]{3,1,2,0:T(8,128)(2,1)S(1)}, u32[]{:S(2)}) copy-start(bf16[16,16,12,64]{3,1,2,0:T(8,128)(2,1)S(1)} %copy.90) | copy-start | bytes 1179652
  18.3 1.8 %copy-start.13 = (bf16[16,16,12,64]{3,1,2,0:T(8,128)(2,1)}, bf16[16,16,12,64]{3,1,2,0:T(8,128)(2,1)S(1)}, u32[]{:S(2)}) copy-start(bf16[16,16,12,64]{3,1,2,0:T(8,128)(2,1)S(1)} %copy.91) | copy-start | bytes 1179652
  18.7 2.2 %copy-start.7 = (bf16[16,16,12,64]{3,1,2,0:T(8,128)(2,1)}, bf16[16,16,12,64]{3,1,2,0:T(8,128)(2,1)S(1)}, u32[]{:S(2)}) copy-start(bf16[16,16,12,64]{3,1,2,0:T(8,128)(2,1)S(1)} %copy.96) | copy-start | bytes 1179652
  18.9 2.0 %copy-start.9 = (bf16[16,16,12,64]{3,1,2,0:T(8,128)(2,1)}, bf16[16,16,12,64]{3,1,2,0:T(8,128)(2,1)S(1)}, u32[]{:S(2)}) copy-start(bf16[16,16,12,64]{3,1,2,0:T(8,128)(2,1)S(1)} %copy.97) | copy-start | bytes 1179652
  19.2 1.8 %copy-start.15 = (bf16[16,16,12,64]{3,1,2,0:T(8,128)(2,1)}, bf16[16,16,12,64]{3,1,2,0:T(8,128)(2,1)S(1)}, u32[]{:S(2)}) copy-start(bf16[16,16,12,64]{3,1,2,0:T(8,128)(2,1)S(1)} %copy.98) | copy-start | bytes 1179652
  24.7 12.9 %copy-start.25 = (s32[1,1,32]{2,1,0:T(1,128)S(1)}, s32[1,1,32]{2,1,0:T(1,128)}, u32[]{:S(2)}) copy-start(s32[1,1,32]{2,1,0:T(1,128)} %param.15) | copy-start | bytes 388
  25.1 5.0 %collective-permute-start.4 = (bf16[1,3,32,128]{3,2,1,0:T(8,128)(2,1)S(1)}, bf16[1,3,32,128]{3,2,1,0:T(8,128)(2,1)S(1)}, u32[]{:S(2)}, u32[]{:S(2)}) collective-permute-start(bf16[1,3,32,128]{3,2,1,0:T(8,128)(2,1)S(1)} %bitcast.197), channel_id=1, source_target_pairs={{0,8},{8,0},{16,24},{24,16},{32,40},{40,32},{48,56},{56,48},{64,72... | collective-permute-start | bytes 73736 | tf_op jit(solution)/shard_map/ppermute | solution.py:26
  28.8 1.2 collective-permute-start.5
  30.1 4.8 %collective-permute-start.6 = (bf16[5,1,32,128]{3,2,1,0:T(8,128)(2,1)S(1)}, bf16[5,1,32,128]{3,2,1,0:T(8,128)(2,1)S(1)}, u32[]{:S(2)}, u32[]{:S(2)}) collective-permute-start(bf16[5,1,32,128]{3,2,1,0:T(8,128)(2,1)S(1)} %get-tuple-element.63), channel_id=1, source_target_pairs={{0,1},{1,0},{2,3},{3,2},{4,5},{5,4},{6,7},{7,6},{8,9},{9,8},{10,11... | collective-permute-start | bytes 122888 | tf_op jit(solution)/shard_map/ppermute | solution.py:26
  31.6 5.3 %collective-permute-start.7 = (bf16[5,1,32,128]{3,2,1,0:T(8,128)(2,1)S(1)}, bf16[5,1,32,128]{3,2,1,0:T(8,128)(2,1)S(1)}, u32[]{:S(2)}, u32[]{:S(2)}) collective-permute-start(bf16[5,1,32,128]{3,2,1,0:T(8,128)(2,1)S(1)} %get-tuple-element.64), channel_id=1, source_target_pairs={{1,2},{2,1},{3,4},{4,3},{5,6},{6,5},{9,10},{10,9},{11,12},{12,11},... | collective-permute-start | bytes 122888 | tf_op jit(solution)/shard_map/ppermute | solution.py:27
  38.0 6.7 %collective-permute-start.8 = (bf16[1,1,32,128]{3,2,1,0:T(8,128)(2,1)S(1)}, bf16[1,1,32,128]{3,2,1,0:T(8,128)(2,1)S(1)}, u32[]{:S(2)}, u32[]{:S(2)}) collective-permute-start(bf16[1,1,32,128]{3,2,1,0:T(8,128)(2,1)S(1)} %fusion.62), channel_id=1, source_target_pairs={{0,8},{8,0},{16,24},{24,16},{32,40},{40,32},{48,56},{56,48},{64,72... | collective-permute-start | bytes 24584 | tf_op jit(solution)/shard_map/ppermute | solution.py:26
  43.7 1.0 collective-permute-start.9
  44.8 4.3 %collective-permute-start.10 = (bf16[3,1,32,128]{3,2,1,0:T(8,128)(2,1)S(1)}, bf16[3,1,32,128]{3,2,1,0:T(8,128)(2,1)S(1)}, u32[]{:S(2)}, u32[]{:S(2)}) collective-permute-start(bf16[3,1,32,128]{3,2,1,0:T(8,128)(2,1)S(1)} %pad_maximum_fusion.28), channel_id=1, source_target_pairs={{0,1},{1,0},{2,3},{3,2},{4,5},{5,4},{6,7},{7,6},{8,9},{9,8},{10,11... | collective-permute-start | bytes 73736 | tf_op jit(solution)/shard_map/ppermute | solution.py:26
  44.9 5.3 %collective-permute-start.11 = (bf16[3,1,32,128]{3,2,1,0:T(8,128)(2,1)S(1)}, bf16[3,1,32,128]{3,2,1,0:T(8,128)(2,1)S(1)}, u32[]{:S(2)}, u32[]{:S(2)}) collective-permute-start(bf16[3,1,32,128]{3,2,1,0:T(8,128)(2,1)S(1)} %pad_maximum_fusion.28), channel_id=1, source_target_pairs={{1,2},{2,1},{3,4},{4,3},{5,6},{6,5},{9,10},{10,9},{11,12},{12,11},... | collective-permute-start | bytes 73736 | tf_op jit(solution)/shard_map/ppermute | solution.py:27
  65.1 4.2 %collective-permute-start.12 = (f32[64256]{0:T(1024)S(1)}, f32[64256]{0:T(1024)S(1)}, u32[]{:S(2)}, u32[]{:S(2)}) collective-permute-start(f32[64256]{0:T(1024)S(1)} %pad_maximum_fusion.6), channel_id=1, source_target_pairs={{0,1},{1,0},{2,3},{3,2},{4,5},{5,4},{6,7},{7,6},{8,9},{9,8},{10,11... | collective-permute-start | bytes 771080 | tf_op jit(solution)/shard_map/ppermute | solution.py:40
  65.6 6.1 %collective-permute-start.15 = (bf16[16,1,1536]{2,1,0:T(2,128)(2,1)S(1)}, bf16[16,1,1536]{2,1,0:T(2,128)(2,1)S(1)}, u32[]{:S(2)}, u32[]{:S(2)}) collective-permute-start(bf16[16,1,1536]{2,1,0:T(2,128)(2,1)S(1)} %get-tuple-element.44), channel_id=1, source_target_pairs={{1,2},{2,1},{3,4},{4,3},{5,6},{6,5},{9,10},{10,9},{11,12},{12,11},... | collective-permute-start | bytes 147464 | tf_op jit(solution)/shard_map/ppermute | solution.py:58
  69.4 4.0 %collective-permute-start.13 = (f32[19840]{0:T(1024)S(1)}, f32[19840]{0:T(1024)S(1)}, u32[]{:S(2)}, u32[]{:S(2)}) collective-permute-start(f32[19840]{0:T(1024)S(1)} %slice_select_fusion.1), channel_id=1, source_target_pairs={{0,2},{1,3},{2,0},{3,1},{4,6},{5,7},{6,4},{7,5},{8,10},{9,11},{10,... | collective-permute-start | bytes 238088 | tf_op jit(solution)/shard_map/ppermute | solution.py:40
  73.5 5.2 %collective-permute-start.14 = (f32[19840]{0:T(1024)S(1)}, f32[19840]{0:T(1024)S(1)}, u32[]{:S(2)}, u32[]{:S(2)}) collective-permute-start(f32[19840]{0:T(1024)S(1)} %select_add_fusion), channel_id=1, source_target_pairs={{0,4},{1,5},{2,6},{3,7},{4,0},{5,1},{6,2},{7,3},{8,12},{9,13},{10,... | collective-permute-start | bytes 238088 | tf_op jit(solution)/shard_map/ppermute | solution.py:40
  78.7 9.2 %collective-permute-start.16 = (f32[47488]{0:T(1024)S(1)}, f32[47488]{0:T(1024)S(1)}, u32[]{:S(2)}, u32[]{:S(2)}) collective-permute-start(f32[47488]{0:T(1024)S(1)} %pad_maximum_fusion.15), channel_id=1, source_target_pairs={{0,8},{8,0},{16,24},{24,16},{32,40},{40,32},{48,56},{56,48},{64,72... | collective-permute-start | bytes 569864 | tf_op jit(solution)/shard_map/ppermute | solution.py:40
  84.5 7.5 %collective-permute-start.17 = (bf16[1,18,1536]{2,1,0:T(8,128)(2,1)S(1)}, bf16[1,18,1536]{2,1,0:T(8,128)(2,1)S(1)}, u32[]{:S(2)}, u32[]{:S(2)}) collective-permute-start(bf16[1,18,1536]{2,1,0:T(8,128)(2,1)S(1)} %broadcast_select_fusion.10), channel_id=1, source_target_pairs={{8,16},{16,8},{24,32},{32,24},{40,48},{48,40},{56,64},{64,56},{72,... | collective-permute-start | bytes 165896 | tf_op jit(solution)/shard_map/ppermute | solution.py:58
  87.9 9.0 %collective-permute-start.18 = (f32[19840]{0:T(1024)S(1)}, f32[19840]{0:T(1024)S(1)}, u32[]{:S(2)}, u32[]{:S(2)}) collective-permute-start(f32[19840]{0:T(1024)S(1)} %slice_add_fusion.1), channel_id=1, source_target_pairs={{0,16},{8,24},{16,0},{24,8},{32,48},{40,56},{48,32},{56,40},{64,80... | collective-permute-start | bytes 238088 | tf_op jit(solution)/shard_map/ppermute | solution.py:40
  96.9 4.5 %collective-permute-start.19 = (f32[19840]{0:T(1024)S(1)}, f32[19840]{0:T(1024)S(1)}, u32[]{:S(2)}, u32[]{:S(2)}) collective-permute-start(f32[19840]{0:T(1024)S(1)} %add.133), channel_id=1, source_target_pairs={{0,32},{8,40},{16,48},{24,56},{32,0},{40,8},{48,16},{56,24},{64,96... | collective-permute-start | bytes 238088 | tf_op jit(solution)/shard_map/ppermute | solution.py:40
  101.4 5.1 %collective-permute-start.20 = (f32[19840]{0:T(1024)S(1)}, f32[19840]{0:T(1024)S(1)}, u32[]{:S(2)}, u32[]{:S(2)}) collective-permute-start(f32[19840]{0:T(1024)S(1)} %add.134), channel_id=1, source_target_pairs={{0,64},{8,72},{16,80},{24,88},{32,96},{40,104},{48,112},{56,120},{... | collective-permute-start | bytes 238088 | tf_op jit(solution)/shard_map/ppermute | solution.py:40
  106.5 5.1 %collective-permute-start.21 = (f32[19840]{0:T(1024)S(1)}, f32[19840]{0:T(1024)S(1)}, u32[]{:S(2)}, u32[]{:S(2)}) collective-permute-start(f32[19840]{0:T(1024)S(1)} %add.135), channel_id=1, source_target_pairs={{0,2},{1,3},{2,0},{3,1},{4,6},{5,7},{6,4},{7,5},{8,10},{9,11},{10,... | collective-permute-start | bytes 238088 | tf_op jit(solution)/shard_map/ppermute | solution.py:40
  112.4 6.4 %collective-permute-start.22 = (f32[39680]{0:T(1024)S(1)}, f32[39680]{0:T(1024)S(1)}, u32[]{:S(2)}, u32[]{:S(2)}) collective-permute-start(f32[39680]{0:T(1024)S(1)} %maximum_select_fusion.2), channel_id=1, source_target_pairs={{0,1},{1,0},{2,3},{3,2},{4,5},{5,4},{6,7},{7,6},{8,9},{9,8},{10,11... | collective-permute-start | bytes 476168 | tf_op jit(solution)/shard_map/ppermute | solution.py:40
  118.8 3.8 %copy-start.1 = (bf16[128,20]{0,1:T(8,128)(2,1)S(1)}, bf16[128,20]{0,1:T(8,128)(2,1)}, u32[]{:S(2)}) copy-start(bf16[128,20]{0,1:T(8,128)(2,1)} %param.11) | copy-start | bytes 15364
  (18 other events, 22.5 us)

commit v5 on v4

--- a/solution.py
+++ b/solution.py
@@ -145,9 +145,24 @@
     return input_sum
 
 
+def same_group():
+    rows = lax.broadcasted_iota(jnp.int32, (C_OUT, C_OUT), 0) // CPG
+    cols = lax.broadcasted_iota(jnp.int32, (C_OUT, C_OUT), 1) // CPG
+    return rows == cols
+
+
 def block_weights(time_weight):
-    group_eye = jnp.eye(GROUPS, dtype=jnp.bfloat16)
-    return jnp.einsum("kgco,gh->kgcho", time_weight, group_eye).reshape(3, C_OUT, C_OUT)
+    tiled = jnp.tile(time_weight.reshape(3, C_OUT, CPG), (1, 1, GROUPS))
+    return jnp.where(same_group()[None], tiled, jnp.zeros_like(tiled))
+
+
+def group_blocks(dense):
+    masked = jnp.where(same_group()[None], dense, jnp.zeros_like(dense))
+    pick = (
+        lax.broadcasted_iota(jnp.int32, (C_OUT, CPG), 0) % CPG
+        == lax.broadcasted_iota(jnp.int32, (C_OUT, CPG), 1)
+    ).astype(jnp.float32)
+    return jnp.dot(masked, pick, precision=PRECISE).reshape(3, GROUPS, CPG, CPG)
 
 
 def per_device(
@@ -226,18 +241,19 @@
         tile_rows, tile_cols, C_OUT
     )
     grad_mixed = ((pixel_grad / DATES)[:, :, None, :] * silu_slope(mixed_time)).astype(jnp.bfloat16)
-    group_eye = jnp.eye(GROUPS, dtype=jnp.float32)
-    time_taps = []
-    for time_tap in range(3):
-        dense_grad = jnp.einsum(
-            "ijtc,ijtd->cd",
-            padded_hidden[:, :, time_tap : time_tap + DATES],
-            grad_mixed,
-            preferred_element_type=jnp.float32,
-        )
-        reshaped = dense_grad.reshape(GROUPS, CPG, GROUPS, CPG)
-        time_taps.append(jnp.einsum("gchd,gh->gcd", reshaped, group_eye, precision=PRECISE))
-    time_term = jnp.stack(time_taps)
+    time_term = group_blocks(
+        jnp.stack(
+            [
+                jnp.einsum(
+                    "ijtc,ijtd->cd",
+                    padded_hidden[:, :, time_tap : time_tap + DATES],
+                    grad_mixed,
+                    preferred_element_type=jnp.float32,
+                )
+                for time_tap in range(3)
+            ]
+        )
+    )
     padded_mixed = jnp.pad(grad_mixed, ((0, 0), (0, 0), (1, 1), (0, 0)))
     grad_hidden = None
     for time_tap in range(3):

time: 123 us -> 119 us (0.967)
  local copies, waits for them, and re-layouts: 26.5 us -> 23.2 us
  matrix products: 18.4 us -> 15.9 us
  waiting for transfers between devices: 12.7 us -> 14 us
    reshape x4 -> x0, local copies, waits for them, and re-layouts: 1.83 us -> none  [the longest x3 1.7 us: per_device(): reshaped = dense_grad.reshape(GROUPS, CPG, GROUPS, CPG)]
    ppermute x6, starting transfers between devices: 13.2 us -> 11.5 us  [with_halo(): lax.ppermute(jnp.where(odd, head, tail), axis, [(i, i ^ 1) for i in range...]
    ppermute x6, starting transfers between devices: 13 us -> 14.6 us  [with_halo(): lax.ppermute(jnp.where(odd, tail, head), axis, [pair for k in range(1, co...]
    squeeze x3 -> x0, local copies, waits for them, and re-layouts: 1.49 us -> none  [per_device(): dense_time[time_tap]]
    dot_general x3, matrix products: 2.52 us -> 1.25 us  [per_device(): jnp.einsum('ijtc,ijtd->cd', padded_hidden[:, :, time_tap:time_tap + DATES...]
    unnamed x73 -> x70, local copies, waits for them, and re-layouts: 8.09 us -> 8.33 us
where the time goes in v5:
time: 119 us
  starting transfers between devices  58.2 us (49%)
  local copies, waits for them, and re-layouts  23.2 us (19%)
  matrix products  15.9 us (13%)
  waiting for transfers between devices  14 us (12%)
  other arithmetic  5.63 us (5%)
  between operations  1.75 us (1%)
    ppermute x9, starting transfers between devices, exchange(): return lax.ppermute(value, axis, [(i, i ^ bit) for i in range(size)])  27.5 us
    ppermute x6, starting transfers between devices, with_halo(): lax.ppermute(jnp.where(odd, tail, head), axis, [pair for k in range(1, co...  14.6 us
    ppermute x6, starting transfers between devices, with_halo(): lax.ppermute(jnp.where(odd, head, tail), axis, [(i, i ^ 1) for i in range...  11.5 us
    unnamed x70, local copies, waits for them, and re-layouts  8.33 us
    ppermute x9, waiting for transfers between devices, exchange(): return lax.ppermute(value, axis, [(i, i ^ bit) for i in range(size)])  7.98 us
    ppermute x2, starting transfers between devices, outer_swap(): lax.ppermute(piece, axis, [pair for k in range(1, count - 1, 2) for pair...  4.62 us
    ppermute x6, waiting for transfers between devices, with_halo(): lax.ppermute(jnp.where(odd, tail, head), axis, [pair for k in range(1, co...  4.12 us
    dot_general x3, matrix products, spatial_forward(): jnp.dot(tap_patch, conv_weight[row_tap].reshape(3 * C_IN, C_OUT), preferr...  4.06 us
  transfers between devices with their start and end apart: 23, of which 12 were waited for; matrix products, arithmetic and copies ran while one was open for 13% of the time, Pallas kernels for 0%

profile of v5, /device:TPU:1, one launch (start us, length us, event | category | flops | bytes accessed | tf_op | source)
XLA Modules:
  0.0 118.7 jit_solution(10255575857269974559)
XLA Ops:
  1.5 2.0 %collective-permute-start = (bf16[1,16,768]{2,1,0:T(8,128)(2,1)S(1)}, bf16[1,16,768]{2,1,0:T(8,128)(2,1)S(1)}, u32[]{:S(2)}, u32[]{:S(2)}) collective-permute-start(bf16[1,16,768]{2,1,0:T(8,128)(2,1)S(1)} %get-tuple-element.42), channel_id=1, source_target_pairs={{0,8},{8,0},{16,24},{24,16},{32,40},{40,32},{48,56},{56,48},{64,72... | collective-permute-start | bytes 73736 | tf_op jit(solution)/shard_map/ppermute | solution.py:26
  4.2 1.5 %fusion.83 = (bf16[1,3,64,128]{3,2,1,0:T(8,128)(2,1)S(1)}, bf16[1,3,64,128]{3,2,1,0:T(8,128)(2,1)}, bf16[1,3,64,128]{3,2,1,0:T(8,128)(2,1)}) fusion(bf16[3,3,64,128]{3,2,1,0:T(8,128)(2,1)} %param.9), kind=kLoop, calls=%fused_computation.202 | loop fusion | bytes 294912 | tf_op jit(solution)/shard_map/slice | solution.py:123
  5.7 0.9 copy.49
  8.0 4.0 %collective-permute-start.3 = (bf16[18,1,768]{2,1,0:T(2,128)(2,1)S(1)}, bf16[18,1,768]{2,1,0:T(2,128)(2,1)S(1)}, u32[]{:S(2)}, u32[]{:S(2)}) collective-permute-start(bf16[18,1,768]{2,1,0:T(2,128)(2,1)S(1)} %broadcast_select_fusion.6), channel_id=1, source_target_pairs={{1,2},{2,1},{3,4},{4,3},{5,6},{6,5},{9,10},{10,9},{11,12},{12,11},... | collective-permute-start | bytes 82952 | tf_op jit(solution)/shard_map/ppermute | solution.py:27
  12.3 1.6 %collective-permute-done.3 = bf16[18,1,768]{2,1,0:T(2,128)(2,1)S(1)} collective-permute-done((bf16[18,1,768]{2,1,0:T(2,128)(2,1)S(1)}, bf16[18,1,768]{2,1,0:T(2,128)(2,1)S(1)}, u32[]{:S(2)}, u32[]{:S(2)}) %collective-permute-start.3) | collective-permute-done | bytes 27680 | tf_op jit(solution)/shard_map/ppermute | solution.py:27
  15.1 2.6 %fusion.82 = (bf16[16,16,12,64]{3,2,1,0:T(8,128)(2,1)S(1)}, bf16[16,16,12,64]{3,2,1,0:T(8,128)(2,1)S(1)}, bf16[16,16,12,64]{3,2,1,0:T(8,128)(2,1)S(1)}, bf16[16,...) fusion(bf16[18,18,12,64]{3,2,1,0:T(8,128)(2,1)S(1)} %reshape.221), kind=kLoop, calls=%fused_computation.201 | loop fusion | bytes 7077888 | tf_op jit(solution)/shard_map/slice | solution.py:116
  22.0 2.3 %multiply_convert_fusion.2 = (bf16[16,16,12,128]{3,1,2,0:T(8,128)(2,1)S(1)}, f32[16,16,12,128]{3,1,2,0:T(8,128)}) fusion(bf16[192,128,1,1]{1,0,3,2:T(8,128)(2,1)S(1)} %bitcast.188, bf16[16,16,12,64]{3,1,2,0:T(8,128)(2,1)S(1)} %copy.98, bf16[16,16,12,64]{3,1,2,0:T(8,128)(2,1)S(1)} %copy.97, bf16[16,16,12,64]{3,1,2,0:T(8,128)(2,1)S(1)} %copy.96, ...), kind=kOutput, calls=%fused_computation.27 | convolution fusion | flops 157286400 | bytes 6733824 | tf_op jit(solution)/shard_map/dot_general | solution.py:121
  26.1 3.8 %collective-permute-start.4 = (bf16[1,3,32,128]{3,2,1,0:T(8,128)(2,1)S(1)}, bf16[1,3,32,128]{3,2,1,0:T(8,128)(2,1)S(1)}, u32[]{:S(2)}, u32[]{:S(2)}) collective-permute-start(bf16[1,3,32,128]{3,2,1,0:T(8,128)(2,1)S(1)} %bitcast.192), channel_id=1, source_target_pairs={{0,8},{8,0},{16,24},{24,16},{32,40},{40,32},{48,56},{56,48},{64,72... | collective-permute-start | bytes 73736 | tf_op jit(solution)/shard_map/ppermute | solution.py:26
  31.8 3.9 %collective-permute-start.7 = (bf16[5,1,32,128]{3,2,1,0:T(8,128)(2,1)S(1)}, bf16[5,1,32,128]{3,2,1,0:T(8,128)(2,1)S(1)}, u32[]{:S(2)}, u32[]{:S(2)}) collective-permute-start(bf16[5,1,32,128]{3,2,1,0:T(8,128)(2,1)S(1)} %get-tuple-element.61), channel_id=1, source_target_pairs={{1,2},{2,1},{3,4},{4,3},{5,6},{6,5},{9,10},{10,9},{11,12},{12,11},... | collective-permute-start | bytes 122888 | tf_op jit(solution)/shard_map/ppermute | solution.py:27
  35.7 1.6 %collective-permute-done.7 = bf16[5,1,32,128]{3,2,1,0:T(8,128)(2,1)S(1)} collective-permute-done((bf16[5,1,32,128]{3,2,1,0:T(8,128)(2,1)S(1)}, bf16[5,1,32,128]{3,2,1,0:T(8,128)(2,1)S(1)}, u32[]{:S(2)}, u32[]{:S(2)}) %collective-permute-start.7) | collective-permute-done | bytes 40992 | tf_op jit(solution)/shard_map/ppermute | solution.py:27
  38.4 5.1 %collective-permute-start.8 = (bf16[1,1,32,128]{3,2,1,0:T(8,128)(2,1)S(1)}, bf16[1,1,32,128]{3,2,1,0:T(8,128)(2,1)S(1)}, u32[]{:S(2)}, u32[]{:S(2)}) collective-permute-start(bf16[1,1,32,128]{3,2,1,0:T(8,128)(2,1)S(1)} %fusion.57), channel_id=1, source_target_pairs={{0,8},{8,0},{16,24},{24,16},{32,40},{40,32},{48,56},{56,48},{64,72... | collective-permute-start | bytes 24584 | tf_op jit(solution)/shard_map/ppermute | solution.py:26
  44.7 4.6 %collective-permute-start.11 = (bf16[3,1,32,128]{3,2,1,0:T(8,128)(2,1)S(1)}, bf16[3,1,32,128]{3,2,1,0:T(8,128)(2,1)S(1)}, u32[]{:S(2)}, u32[]{:S(2)}) collective-permute-start(bf16[3,1,32,128]{3,2,1,0:T(8,128)(2,1)S(1)} %pad_maximum_fusion.27), channel_id=1, source_target_pairs={{1,2},{2,1},{3,4},{4,3},{5,6},{6,5},{9,10},{10,9},{11,12},{12,11},... | collective-permute-start | bytes 73736 | tf_op jit(solution)/shard_map/ppermute | solution.py:27
  53.6 1.0 copy-done.24
  56.3 1.2 %fusion.23 = f32[192,128,1,1]{1,0,3,2:T(8,128)S(1)} fusion(bf16[16,16,12,128]{3,1,2,0:T(8,128)(2,1)S(1)} %multiply_convert_fusion, bf16[16,16,12,64]{3,1,2,0:T(8,128)(2,1)S(1)} %copy-done.18, bf16[16,16,12,64]{3,1,2,0:T(8,128)(2,1)S(1)} %copy-done.14, bf16[16,16,12,64]{3,1,2,0:T(8,128)(2,1)S(1)} %copy-done.12), kind=kOutput, calls=%fused_computation.46 | convolution fusion | flops 154533888 | bytes 2064384 | tf_op jit(solution)/shard_map/ijtc,ijtd->cd/dot_general | solution.py:277
  57.6 1.2 %fusion.21 = f32[192,128,1,1]{1,0,3,2:T(8,128)S(1)} fusion(bf16[16,16,12,128]{3,1,2,0:T(8,128)(2,1)S(1)} %multiply_convert_fusion, bf16[16,16,12,64]{3,1,2,0:T(8,128)(2,1)S(1)} %copy-done.6, bf16[16,16,12,64]{3,1,2,0:T(8,128)(2,1)S(1)} %copy-done.4, bf16[16,16,12,64]{3,1,2,0:T(8,128)(2,1)S(1)} %copy.93), kind=kOutput, calls=%fused_computation.44 | convolution fusion | flops 154533888 | bytes 2064384 | tf_op jit(solution)/shard_map/ijtc,ijtd->cd/dot_general | solution.py:277
  59.2 1.2 fusion.20
  61.4 4.0 %collective-permute-start.15 = (bf16[16,1,1536]{2,1,0:T(2,128)(2,1)S(1)}, bf16[16,1,1536]{2,1,0:T(2,128)(2,1)S(1)}, u32[]{:S(2)}, u32[]{:S(2)}) collective-permute-start(bf16[16,1,1536]{2,1,0:T(2,128)(2,1)S(1)} %get-tuple-element.41), channel_id=1, source_target_pairs={{1,2},{2,1},{3,4},{4,3},{5,6},{6,5},{9,10},{10,9},{11,12},{12,11},... | collective-permute-start | bytes 147464 | tf_op jit(solution)/shard_map/ppermute | solution.py:58
  65.4 1.4 %collective-permute-start.13 = (f32[19840]{0:T(1024)S(1)}, f32[19840]{0:T(1024)S(1)}, u32[]{:S(2)}, u32[]{:S(2)}) collective-permute-start(f32[19840]{0:T(1024)S(1)} %slice_select_fusion.1), channel_id=1, source_target_pairs={{0,2},{1,3},{2,0},{3,1},{4,6},{5,7},{6,4},{7,5},{8,10},{9,11},{10,... | collective-permute-start | bytes 238088 | tf_op jit(solution)/shard_map/ppermute | solution.py:40
  67.9 1.6 %collective-permute-done.13 = f32[19840]{0:T(1024)S(1)} collective-permute-done((f32[19840]{0:T(1024)S(1)}, f32[19840]{0:T(1024)S(1)}, u32[]{:S(2)}, u32[]{:S(2)}) %collective-permute-start.13) | collective-permute-done | bytes 79392 | tf_op jit(solution)/shard_map/ppermute | solution.py:40
  69.5 2.9 %collective-permute-start.14 = (f32[19840]{0:T(1024)S(1)}, f32[19840]{0:T(1024)S(1)}, u32[]{:S(2)}, u32[]{:S(2)}) collective-permute-start(f32[19840]{0:T(1024)S(1)} %select_add_fusion), channel_id=1, source_target_pairs={{0,4},{1,5},{2,6},{3,7},{4,0},{5,1},{6,2},{7,3},{8,12},{9,13},{10,... | collective-permute-start | bytes 238088 | tf_op jit(solution)/shard_map/ppermute | solution.py:40
  72.5 1.9 %collective-permute-done.14 = f32[19840]{0:T(1024)S(1)} collective-permute-done((f32[19840]{0:T(1024)S(1)}, f32[19840]{0:T(1024)S(1)}, u32[]{:S(2)}, u32[]{:S(2)}) %collective-permute-start.14) | collective-permute-done | bytes 79392 | tf_op jit(solution)/shard_map/ppermute | solution.py:40
  74.4 5.8 %collective-permute-start.16 = (f32[47488]{0:T(1024)S(1)}, f32[47488]{0:T(1024)S(1)}, u32[]{:S(2)}, u32[]{:S(2)}) collective-permute-start(f32[47488]{0:T(1024)S(1)} %pad_maximum_fusion.14), channel_id=1, source_target_pairs={{0,8},{8,0},{16,24},{24,16},{32,40},{40,32},{48,56},{56,48},{64,72... | collective-permute-start | bytes 569864 | tf_op jit(solution)/shard_map/ppermute | solution.py:40
  80.9 2.8 %collective-permute-done.16 = f32[47488]{0:T(1024)S(1)} collective-permute-done((f32[47488]{0:T(1024)S(1)}, f32[47488]{0:T(1024)S(1)}, u32[]{:S(2)}, u32[]{:S(2)}) %collective-permute-start.16) | collective-permute-done | bytes 189984 | tf_op jit(solution)/shard_map/ppermute | solution.py:40
  83.7 4.2 %collective-permute-start.18 = (f32[19840]{0:T(1024)S(1)}, f32[19840]{0:T(1024)S(1)}, u32[]{:S(2)}, u32[]{:S(2)}) collective-permute-start(f32[19840]{0:T(1024)S(1)} %slice_add_fusion.1), channel_id=1, source_target_pairs={{0,16},{8,24},{16,0},{24,8},{32,48},{40,56},{48,32},{56,40},{64,80... | collective-permute-start | bytes 238088 | tf_op jit(solution)/shard_map/ppermute | solution.py:40
  89.5 2.8 %fusion.81 = (bf16[16,16,12,128]{3,2,1,0:T(8,128)(2,1)S(1)}, bf16[16,16,12,128]{3,2,1,0:T(8,128)(2,1)S(1)}, bf16[16,16,12,128]{3,2,1,0:T(8,128)(2,1)S(1)}, bf16[...) fusion(bf16[18,18,12,128]{3,2,1,0:T(8,128)(2,1)S(1)} %reshape.231), kind=kLoop, calls=%fused_computation.200 | loop fusion | bytes 14155776 | tf_op jit(solution)/shard_map/slice | solution.py:135
  92.9 2.2 %collective-permute-start.19 = (f32[19840]{0:T(1024)S(1)}, f32[19840]{0:T(1024)S(1)}, u32[]{:S(2)}, u32[]{:S(2)}) collective-permute-start(f32[19840]{0:T(1024)S(1)} %add.145), channel_id=1, source_target_pairs={{0,32},{8,40},{16,48},{24,56},{32,0},{40,8},{48,16},{56,24},{64,96... | collective-permute-start | bytes 238088 | tf_op jit(solution)/shard_map/ppermute | solution.py:40
  97.0 3.4 %collective-permute-start.20 = (f32[19840]{0:T(1024)S(1)}, f32[19840]{0:T(1024)S(1)}, u32[]{:S(2)}, u32[]{:S(2)}) collective-permute-start(f32[19840]{0:T(1024)S(1)} %add.146), channel_id=1, source_target_pairs={{0,64},{8,72},{16,80},{24,88},{32,96},{40,104},{48,112},{56,120},{... | collective-permute-start | bytes 238088 | tf_op jit(solution)/shard_map/ppermute | solution.py:40
  102.3 1.8 %collective-permute-start.21 = (f32[19840]{0:T(1024)S(1)}, f32[19840]{0:T(1024)S(1)}, u32[]{:S(2)}, u32[]{:S(2)}) collective-permute-start(f32[19840]{0:T(1024)S(1)} %add.147), channel_id=1, source_target_pairs={{0,2},{1,3},{2,0},{3,1},{4,6},{5,7},{6,4},{7,5},{8,10},{9,11},{10,... | collective-permute-start | bytes 238088 | tf_op jit(solution)/shard_map/ppermute | solution.py:40
  105.3 1.4 %reshape.232 = bf16[16,16,768]{2,1,0:T(8,128)(2,1)} reshape(bf16[16,16,12,64]{3,2,1,0:T(8,128)(2,1)S(1)} %copy.65) | data formatting | bytes 786432 | tf_op jit(solution)/shard_map/reshape | solution.py:288
  108.2 5.5 %collective-permute-start.22 = (f32[39680]{0:T(1024)S(1)}, f32[39680]{0:T(1024)S(1)}, u32[]{:S(2)}, u32[]{:S(2)}) collective-permute-start(f32[39680]{0:T(1024)S(1)} %maximum_select_fusion.4), channel_id=1, source_target_pairs={{0,1},{1,0},{2,3},{3,2},{4,5},{5,4},{6,7},{7,6},{8,9},{9,8},{10,11... | collective-permute-start | bytes 476168 | tf_op jit(solution)/shard_map/ppermute | solution.py:40
  113.9 0.9 collective-permute-done.22
  115.6 1.2 concatenate.121
  (193 shorter events, 34.4 us)
Async XLA Ops:
  0.6 37.1 %copy-start = (bf16[128,20]{0,1:T(8,128)(2,1)S(1)}, bf16[128,20]{0,1:T(8,128)(2,1)}, u32[]{:S(2)}) copy-start(bf16[128,20]{0,1:T(8,128)(2,1)} %param.11) | copy-start | bytes 15364
  0.6 7.1 %copy-start.2 = (bf16[16,16,768]{2,1,0:T(8,128)(2,1)S(1)}, bf16[16,16,768]{2,1,0:T(8,128)(2,1)}, u32[]{:S(2)}) copy-start(bf16[16,16,768]{2,1,0:T(8,128)(2,1)} %param.8) | copy-start | bytes 1179652
  0.7 11.6 %copy-start.22 = (s32[16,16]{1,0:T(8,128)S(1)}, s32[16,16]{1,0:T(8,128)}, u32[]{:S(2)}) copy-start(s32[16,16]{1,0:T(8,128)} %param.12) | copy-start | bytes 3076
  1.5 6.2 %collective-permute-start = (bf16[1,16,768]{2,1,0:T(8,128)(2,1)S(1)}, bf16[1,16,768]{2,1,0:T(8,128)(2,1)S(1)}, u32[]{:S(2)}, u32[]{:S(2)}) collective-permute-start(bf16[1,16,768]{2,1,0:T(8,128)(2,1)S(1)} %get-tuple-element.42), channel_id=1, source_target_pairs={{0,8},{8,0},{16,24},{24,16},{32,40},{40,32},{48,56},{56,48},{64,72... | collective-permute-start | bytes 73736 | tf_op jit(solution)/shard_map/ppermute | solution.py:26
  3.5 4.2 %collective-permute-start.1 = (bf16[1,16,768]{2,1,0:T(8,128)(2,1)S(1)}, bf16[1,16,768]{2,1,0:T(8,128)(2,1)S(1)}, u32[]{:S(2)}, u32[]{:S(2)}) collective-permute-start(bf16[1,16,768]{2,1,0:T(8,128)(2,1)S(1)} %get-tuple-element.43), channel_id=1, source_target_pairs={{8,16},{16,8},{24,32},{32,24},{40,48},{48,40},{56,64},{64,56},{72,... | collective-permute-start | bytes 73736 | tf_op jit(solution)/shard_map/ppermute | solution.py:27
  8.0 5.9 %collective-permute-start.3 = (bf16[18,1,768]{2,1,0:T(2,128)(2,1)S(1)}, bf16[18,1,768]{2,1,0:T(2,128)(2,1)S(1)}, u32[]{:S(2)}, u32[]{:S(2)}) collective-permute-start(bf16[18,1,768]{2,1,0:T(2,128)(2,1)S(1)} %broadcast_select_fusion.6), channel_id=1, source_target_pairs={{1,2},{2,1},{3,4},{4,3},{5,6},{6,5},{9,10},{10,9},{11,12},{12,11},... | collective-permute-start | bytes 82952 | tf_op jit(solution)/shard_map/ppermute | solution.py:27
  12.1 1.8 %collective-permute-start.2 = (bf16[18,1,768]{2,1,0:T(2,128)(2,1)S(1)}, bf16[18,1,768]{2,1,0:T(2,128)(2,1)S(1)}, u32[]{:S(2)}, u32[]{:S(2)}) collective-permute-start(bf16[18,1,768]{2,1,0:T(2,128)(2,1)S(1)} %get-tuple-element.19), channel_id=1, source_target_pairs={{0,1},{1,0},{2,3},{3,2},{4,5},{5,4},{6,7},{7,6},{8,9},{9,8},{10,11... | collective-permute-start | bytes 82952 | tf_op jit(solution)/shard_map/ppermute | solution.py:26
  18.6 2.4 %copy-start.11 = (bf16[16,16,12,64]{3,1,2,0:T(8,128)(2,1)}, bf16[16,16,12,64]{3,1,2,0:T(8,128)(2,1)S(1)}, u32[]{:S(2)}) copy-start(bf16[16,16,12,64]{3,1,2,0:T(8,128)(2,1)S(1)} %copy.90) | copy-start | bytes 1179652
  19.3 2.6 %copy-start.7 = (bf16[16,16,12,64]{3,1,2,0:T(8,128)(2,1)}, bf16[16,16,12,64]{3,1,2,0:T(8,128)(2,1)S(1)}, u32[]{:S(2)}) copy-start(bf16[16,16,12,64]{3,1,2,0:T(8,128)(2,1)S(1)} %copy.96) | copy-start | bytes 1179652
  19.6 2.4 %copy-start.9 = (bf16[16,16,12,64]{3,1,2,0:T(8,128)(2,1)}, bf16[16,16,12,64]{3,1,2,0:T(8,128)(2,1)S(1)}, u32[]{:S(2)}) copy-start(bf16[16,16,12,64]{3,1,2,0:T(8,128)(2,1)S(1)} %copy.97) | copy-start | bytes 1179652
  19.8 2.2 %copy-start.15 = (bf16[16,16,12,64]{3,1,2,0:T(8,128)(2,1)}, bf16[16,16,12,64]{3,1,2,0:T(8,128)(2,1)S(1)}, u32[]{:S(2)}) copy-start(bf16[16,16,12,64]{3,1,2,0:T(8,128)(2,1)S(1)} %copy.98) | copy-start | bytes 1179652
  25.7 12.3 %copy-start.23 = (s32[1,1,32]{2,1,0:T(1,128)S(1)}, s32[1,1,32]{2,1,0:T(1,128)}, u32[]{:S(2)}) copy-start(s32[1,1,32]{2,1,0:T(1,128)} %param.15) | copy-start | bytes 388
  26.1 5.2 %collective-permute-start.4 = (bf16[1,3,32,128]{3,2,1,0:T(8,128)(2,1)S(1)}, bf16[1,3,32,128]{3,2,1,0:T(8,128)(2,1)S(1)}, u32[]{:S(2)}, u32[]{:S(2)}) collective-permute-start(bf16[1,3,32,128]{3,2,1,0:T(8,128)(2,1)S(1)} %bitcast.192), channel_id=1, source_target_pairs={{0,8},{8,0},{16,24},{24,16},{32,40},{40,32},{48,56},{56,48},{64,72... | collective-permute-start | bytes 73736 | tf_op jit(solution)/shard_map/ppermute | solution.py:26
  29.9 1.4 %collective-permute-start.5 = (bf16[1,3,32,128]{3,2,1,0:T(8,128)(2,1)S(1)}, bf16[1,3,32,128]{3,2,1,0:T(8,128)(2,1)S(1)}, u32[]{:S(2)}, u32[]{:S(2)}) collective-permute-start(bf16[1,3,32,128]{3,2,1,0:T(8,128)(2,1)S(1)} %bitcast.191), channel_id=1, source_target_pairs={{8,16},{16,8},{24,32},{32,24},{40,48},{48,40},{56,64},{64,56},{72,... | collective-permute-start | bytes 73736 | tf_op jit(solution)/shard_map/ppermute | solution.py:27
  31.3 4.4 %collective-permute-start.6 = (bf16[5,1,32,128]{3,2,1,0:T(8,128)(2,1)S(1)}, bf16[5,1,32,128]{3,2,1,0:T(8,128)(2,1)S(1)}, u32[]{:S(2)}, u32[]{:S(2)}) collective-permute-start(bf16[5,1,32,128]{3,2,1,0:T(8,128)(2,1)S(1)} %get-tuple-element.60), channel_id=1, source_target_pairs={{0,1},{1,0},{2,3},{3,2},{4,5},{5,4},{6,7},{7,6},{8,9},{9,8},{10,11... | collective-permute-start | bytes 122888 | tf_op jit(solution)/shard_map/ppermute | solution.py:26
  31.8 5.6 %collective-permute-start.7 = (bf16[5,1,32,128]{3,2,1,0:T(8,128)(2,1)S(1)}, bf16[5,1,32,128]{3,2,1,0:T(8,128)(2,1)S(1)}, u32[]{:S(2)}, u32[]{:S(2)}) collective-permute-start(bf16[5,1,32,128]{3,2,1,0:T(8,128)(2,1)S(1)} %get-tuple-element.61), channel_id=1, source_target_pairs={{1,2},{2,1},{3,4},{4,3},{5,6},{6,5},{9,10},{10,9},{11,12},{12,11},... | collective-permute-start | bytes 122888 | tf_op jit(solution)/shard_map/ppermute | solution.py:27
  38.4 6.1 %collective-permute-start.8 = (bf16[1,1,32,128]{3,2,1,0:T(8,128)(2,1)S(1)}, bf16[1,1,32,128]{3,2,1,0:T(8,128)(2,1)S(1)}, u32[]{:S(2)}, u32[]{:S(2)}) collective-permute-start(bf16[1,1,32,128]{3,2,1,0:T(8,128)(2,1)S(1)} %fusion.57), channel_id=1, source_target_pairs={{0,8},{8,0},{16,24},{24,16},{32,40},{40,32},{48,56},{56,48},{64,72... | collective-permute-start | bytes 24584 | tf_op jit(solution)/shard_map/ppermute | solution.py:26
  43.5 1.0 collective-permute-start.9
  44.6 5.1 %collective-permute-start.10 = (bf16[3,1,32,128]{3,2,1,0:T(8,128)(2,1)S(1)}, bf16[3,1,32,128]{3,2,1,0:T(8,128)(2,1)S(1)}, u32[]{:S(2)}, u32[]{:S(2)}) collective-permute-start(bf16[3,1,32,128]{3,2,1,0:T(8,128)(2,1)S(1)} %pad_maximum_fusion.27), channel_id=1, source_target_pairs={{0,1},{1,0},{2,3},{3,2},{4,5},{5,4},{6,7},{7,6},{8,9},{9,8},{10,11... | collective-permute-start | bytes 73736 | tf_op jit(solution)/shard_map/ppermute | solution.py:26
  44.7 5.9 %collective-permute-start.11 = (bf16[3,1,32,128]{3,2,1,0:T(8,128)(2,1)S(1)}, bf16[3,1,32,128]{3,2,1,0:T(8,128)(2,1)S(1)}, u32[]{:S(2)}, u32[]{:S(2)}) collective-permute-start(bf16[3,1,32,128]{3,2,1,0:T(8,128)(2,1)S(1)} %pad_maximum_fusion.27), channel_id=1, source_target_pairs={{1,2},{2,1},{3,4},{4,3},{5,6},{6,5},{9,10},{10,9},{11,12},{12,11},... | collective-permute-start | bytes 73736 | tf_op jit(solution)/shard_map/ppermute | solution.py:27
  61.1 4.2 %collective-permute-start.12 = (f32[64256]{0:T(1024)S(1)}, f32[64256]{0:T(1024)S(1)}, u32[]{:S(2)}, u32[]{:S(2)}) collective-permute-start(f32[64256]{0:T(1024)S(1)} %pad_maximum_fusion.6), channel_id=1, source_target_pairs={{0,1},{1,0},{2,3},{3,2},{4,5},{5,4},{6,7},{7,6},{8,9},{9,8},{10,11... | collective-permute-start | bytes 771080 | tf_op jit(solution)/shard_map/ppermute | solution.py:40
  61.4 6.3 %collective-permute-start.15 = (bf16[16,1,1536]{2,1,0:T(2,128)(2,1)S(1)}, bf16[16,1,1536]{2,1,0:T(2,128)(2,1)S(1)}, u32[]{:S(2)}, u32[]{:S(2)}) collective-permute-start(bf16[16,1,1536]{2,1,0:T(2,128)(2,1)S(1)} %get-tuple-element.41), channel_id=1, source_target_pairs={{1,2},{2,1},{3,4},{4,3},{5,6},{6,5},{9,10},{10,9},{11,12},{12,11},... | collective-permute-start | bytes 147464 | tf_op jit(solution)/shard_map/ppermute | solution.py:58
  65.4 4.0 %collective-permute-start.13 = (f32[19840]{0:T(1024)S(1)}, f32[19840]{0:T(1024)S(1)}, u32[]{:S(2)}, u32[]{:S(2)}) collective-permute-start(f32[19840]{0:T(1024)S(1)} %slice_select_fusion.1), channel_id=1, source_target_pairs={{0,2},{1,3},{2,0},{3,1},{4,6},{5,7},{6,4},{7,5},{8,10},{9,11},{10,... | collective-permute-start | bytes 238088 | tf_op jit(solution)/shard_map/ppermute | solution.py:40
  69.5 4.9 %collective-permute-start.14 = (f32[19840]{0:T(1024)S(1)}, f32[19840]{0:T(1024)S(1)}, u32[]{:S(2)}, u32[]{:S(2)}) collective-permute-start(f32[19840]{0:T(1024)S(1)} %select_add_fusion), channel_id=1, source_target_pairs={{0,4},{1,5},{2,6},{3,7},{4,0},{5,1},{6,2},{7,3},{8,12},{9,13},{10,... | collective-permute-start | bytes 238088 | tf_op jit(solution)/shard_map/ppermute | solution.py:40
  74.4 9.3 %collective-permute-start.16 = (f32[47488]{0:T(1024)S(1)}, f32[47488]{0:T(1024)S(1)}, u32[]{:S(2)}, u32[]{:S(2)}) collective-permute-start(f32[47488]{0:T(1024)S(1)} %pad_maximum_fusion.14), channel_id=1, source_target_pairs={{0,8},{8,0},{16,24},{24,16},{32,40},{40,32},{48,56},{56,48},{64,72... | collective-permute-start | bytes 569864 | tf_op jit(solution)/shard_map/ppermute | solution.py:40
  80.2 7.8 %collective-permute-start.17 = (bf16[1,18,1536]{2,1,0:T(8,128)(2,1)S(1)}, bf16[1,18,1536]{2,1,0:T(8,128)(2,1)S(1)}, u32[]{:S(2)}, u32[]{:S(2)}) collective-permute-start(bf16[1,18,1536]{2,1,0:T(8,128)(2,1)S(1)} %broadcast_select_fusion.11), channel_id=1, source_target_pairs={{8,16},{16,8},{24,32},{32,24},{40,48},{48,40},{56,64},{64,56},{72,... | collective-permute-start | bytes 165896 | tf_op jit(solution)/shard_map/ppermute | solution.py:58
  83.7 9.2 %collective-permute-start.18 = (f32[19840]{0:T(1024)S(1)}, f32[19840]{0:T(1024)S(1)}, u32[]{:S(2)}, u32[]{:S(2)}) collective-permute-start(f32[19840]{0:T(1024)S(1)} %slice_add_fusion.1), channel_id=1, source_target_pairs={{0,16},{8,24},{16,0},{24,8},{32,48},{40,56},{48,32},{56,40},{64,80... | collective-permute-start | bytes 238088 | tf_op jit(solution)/shard_map/ppermute | solution.py:40
  92.9 4.1 %collective-permute-start.19 = (f32[19840]{0:T(1024)S(1)}, f32[19840]{0:T(1024)S(1)}, u32[]{:S(2)}, u32[]{:S(2)}) collective-permute-start(f32[19840]{0:T(1024)S(1)} %add.145), channel_id=1, source_target_pairs={{0,32},{8,40},{16,48},{24,56},{32,0},{40,8},{48,16},{56,24},{64,96... | collective-permute-start | bytes 238088 | tf_op jit(solution)/shard_map/ppermute | solution.py:40
  97.0 5.3 %collective-permute-start.20 = (f32[19840]{0:T(1024)S(1)}, f32[19840]{0:T(1024)S(1)}, u32[]{:S(2)}, u32[]{:S(2)}) collective-permute-start(f32[19840]{0:T(1024)S(1)} %add.146), channel_id=1, source_target_pairs={{0,64},{8,72},{16,80},{24,88},{32,96},{40,104},{48,112},{56,120},{... | collective-permute-start | bytes 238088 | tf_op jit(solution)/shard_map/ppermute | solution.py:40
  102.3 5.1 %collective-permute-start.21 = (f32[19840]{0:T(1024)S(1)}, f32[19840]{0:T(1024)S(1)}, u32[]{:S(2)}, u32[]{:S(2)}) collective-permute-start(f32[19840]{0:T(1024)S(1)} %add.147), channel_id=1, source_target_pairs={{0,2},{1,3},{2,0},{3,1},{4,6},{5,7},{6,4},{7,5},{8,10},{9,11},{10,... | collective-permute-start | bytes 238088 | tf_op jit(solution)/shard_map/ppermute | solution.py:40
  108.2 6.5 %collective-permute-start.22 = (f32[39680]{0:T(1024)S(1)}, f32[39680]{0:T(1024)S(1)}, u32[]{:S(2)}, u32[]{:S(2)}) collective-permute-start(f32[39680]{0:T(1024)S(1)} %maximum_select_fusion.4), channel_id=1, source_target_pairs={{0,1},{1,0},{2,3},{3,2},{4,5},{5,4},{6,7},{7,6},{8,9},{9,8},{10,11... | collective-permute-start | bytes 476168 | tf_op jit(solution)/shard_map/ppermute | solution.py:40
  114.8 3.8 %copy-start.1 = (bf16[128,20]{0,1:T(8,128)(2,1)S(1)}, bf16[128,20]{0,1:T(8,128)(2,1)}, u32[]{:S(2)}) copy-start(bf16[128,20]{0,1:T(8,128)(2,1)} %param.11) | copy-start | bytes 15364
  (16 other events, 22.2 us)

commit v6 on v5

--- a/solution.py
+++ b/solution.py
@@ -42,7 +42,10 @@
 
 def swap_with(value, axis, bit, extra):
     size = value.shape[0]
-    both = exchange(jnp.concatenate([value, extra.astype(value.dtype).reshape(-1)]), axis, bit)
+    lanes = value.shape[1]
+    both = exchange(
+        jnp.concatenate([value, extra.astype(value.dtype).reshape(-1, lanes)]), axis, bit
+    )
     return both[:size], both[size:].reshape(extra.shape).astype(extra.dtype)
 
 
@@ -279,17 +282,31 @@
             ).reshape(3, C_IN, C_OUT)
         )
     conv_term = jnp.stack(conv_rows)
+    lanes = C_OUT
+    conv_rows, time_rows, class_rows = (
+        conv_term.size // lanes,
+        time_term.size // lanes,
+        class_term.size // lanes,
+    )
+    used = conv_rows + time_rows + class_rows
+    total = -(-used // 32) * 32
     flat, padded_grad = butterfly_sum(
-        jnp.concatenate([conv_term.reshape(-1), time_term.reshape(-1), class_term.reshape(-1)]),
+        jnp.concatenate(
+            [
+                conv_term.reshape(conv_rows, lanes),
+                time_term.reshape(time_rows, lanes),
+                class_term.reshape(class_rows, lanes),
+                jnp.zeros((total - used, lanes), jnp.float32),
+            ]
+        ),
         grad_pre.reshape(tile_rows, tile_cols, DATES * C_OUT),
     )
     padded_grad = padded_grad.reshape(tile_rows + 2, tile_cols + 2, DATES, C_OUT)
     input_sum = transposed_conv(padded_grad, conv_weight, tile_rows, tile_cols)
     input_grad = input_sum.astype(jnp.bfloat16).reshape(tile_rows, tile_cols, DATES * C_IN)
-    conv_size, time_size = (conv_term.size, time_term.size)
-    conv_grad = flat[:conv_size].reshape(conv_term.shape)
-    time_grad = flat[conv_size : conv_size + time_size].reshape(time_term.shape)
-    class_grad = flat[conv_size + time_size :].reshape(class_term.shape)
+    conv_grad = flat[:conv_rows].reshape(conv_term.shape)
+    time_grad = flat[conv_rows : conv_rows + time_rows].reshape(time_term.shape)
+    class_grad = flat[conv_rows + time_rows : used].reshape(class_term.shape)
     return (input_grad, conv_grad, time_grad, class_grad)
 
 

time: 119 us -> 117 us (0.983)
  local copies, waits for them, and re-layouts: 23.2 us -> 20.9 us
    concatenate x6 -> x0, local copies, waits for them, and re-layouts: 3.03 us -> none  [butterfly_sum(): jnp.concatenate([other, flat])]
    unnamed x70 -> x71, local copies, waits for them, and re-layouts: 8.33 us -> 8.91 us
where the time goes in v6:
time: 117 us; the launch traced here: 116 us
  starting transfers between devices  59.2 us (51%)
  local copies, waits for them, and re-layouts  20.9 us (18%)
  matrix products  15.9 us (14%)
  waiting for transfers between devices  13.8 us (12%)
  other arithmetic  4.94 us (4%)
  between operations  1.73 us (1%)
    ppermute x9, starting transfers between devices, exchange(): return lax.ppermute(value, axis, [(i, i ^ bit) for i in range(size)])  28.4 us
    ppermute x6, starting transfers between devices, with_halo(): lax.ppermute(jnp.where(odd, tail, head), axis, [pair for k in range(1, co...  14.6 us
    ppermute x6, starting transfers between devices, with_halo(): lax.ppermute(jnp.where(odd, head, tail), axis, [(i, i ^ 1) for i in range...  11.5 us
    unnamed x71, local copies, waits for them, and re-layouts  8.91 us
    ppermute x9, waiting for transfers between devices, exchange(): return lax.ppermute(value, axis, [(i, i ^ bit) for i in range(size)])  7.93 us
    ppermute x2, starting transfers between devices, outer_swap(): lax.ppermute(piece, axis, [pair for k in range(1, count - 1, 2) for pair...  4.7 us
    ppermute x6, waiting for transfers between devices, with_halo(): lax.ppermute(jnp.where(odd, tail, head), axis, [pair for k in range(1, co...  4.12 us
    dot_general x3, matrix products, spatial_forward(): jnp.dot(tap_patch, conv_weight[row_tap].reshape(3 * C_IN, C_OUT), preferr...  4.06 us
  transfers between devices with their start and end apart: 23, of which 12 were waited for; matrix products, arithmetic and copies ran while one was open for 13% of the time, Pallas kernels for 0%

profile of v6, /device:TPU:1, one launch (start us, length us, event | category | flops | bytes accessed | tf_op | source)
XLA Modules:
  0.0 116.5 jit_solution(16032628104205397744)
XLA Ops:
  1.5 2.0 %collective-permute-start = (bf16[1,16,768]{2,1,0:T(8,128)(2,1)S(1)}, bf16[1,16,768]{2,1,0:T(8,128)(2,1)S(1)}, u32[]{:S(2)}, u32[]{:S(2)}) collective-permute-start(bf16[1,16,768]{2,1,0:T(8,128)(2,1)S(1)} %get-tuple-element.42), channel_id=1, source_target_pairs={{0,8},{8,0},{16,24},{24,16},{32,40},{40,32},{48,56},{56,48},{64,72... | collective-permute-start | bytes 73736 | tf_op jit(solution)/shard_map/ppermute | solution.py:26
  4.2 1.5 %fusion.83 = (bf16[1,3,64,128]{3,2,1,0:T(8,128)(2,1)S(1)}, bf16[1,3,64,128]{3,2,1,0:T(8,128)(2,1)}, bf16[1,3,64,128]{3,2,1,0:T(8,128)(2,1)}) fusion(bf16[3,3,64,128]{3,2,1,0:T(8,128)(2,1)} %param.9), kind=kLoop, calls=%fused_computation.200 | loop fusion | bytes 294912 | tf_op jit(solution)/shard_map/slice | solution.py:126
  5.7 0.9 copy.49
  8.0 4.0 %collective-permute-start.3 = (bf16[18,1,768]{2,1,0:T(2,128)(2,1)S(1)}, bf16[18,1,768]{2,1,0:T(2,128)(2,1)S(1)}, u32[]{:S(2)}, u32[]{:S(2)}) collective-permute-start(bf16[18,1,768]{2,1,0:T(2,128)(2,1)S(1)} %broadcast_select_fusion.6), channel_id=1, source_target_pairs={{1,2},{2,1},{3,4},{4,3},{5,6},{6,5},{9,10},{10,9},{11,12},{12,11},... | collective-permute-start | bytes 82952 | tf_op jit(solution)/shard_map/ppermute | solution.py:27
  12.3 1.6 %collective-permute-done.3 = bf16[18,1,768]{2,1,0:T(2,128)(2,1)S(1)} collective-permute-done((bf16[18,1,768]{2,1,0:T(2,128)(2,1)S(1)}, bf16[18,1,768]{2,1,0:T(2,128)(2,1)S(1)}, u32[]{:S(2)}, u32[]{:S(2)}) %collective-permute-start.3) | collective-permute-done | bytes 27680 | tf_op jit(solution)/shard_map/ppermute | solution.py:27
  15.1 2.6 %fusion.82 = (bf16[16,16,12,64]{3,2,1,0:T(8,128)(2,1)S(1)}, bf16[16,16,12,64]{3,2,1,0:T(8,128)(2,1)S(1)}, bf16[16,16,12,64]{3,2,1,0:T(8,128)(2,1)S(1)}, bf16[16,...) fusion(bf16[18,18,12,64]{3,2,1,0:T(8,128)(2,1)S(1)} %reshape.214), kind=kLoop, calls=%fused_computation.199 | loop fusion | bytes 7077888 | tf_op jit(solution)/shard_map/slice | solution.py:119
  20.2 0.9 fusion.22
  22.0 2.3 %multiply_convert_fusion.2 = (bf16[16,16,12,128]{3,1,2,0:T(8,128)(2,1)S(1)}, f32[16,16,12,128]{3,1,2,0:T(8,128)}) fusion(bf16[192,128,1,1]{1,0,3,2:T(8,128)(2,1)S(1)} %bitcast.188, bf16[16,16,12,64]{3,1,2,0:T(8,128)(2,1)S(1)} %copy.93, bf16[16,16,12,64]{3,1,2,0:T(8,128)(2,1)S(1)} %copy.92, bf16[16,16,12,64]{3,1,2,0:T(8,128)(2,1)S(1)} %copy.91, ...), kind=kOutput, calls=%fused_computation.27 | convolution fusion | flops 157286400 | bytes 6733824 | tf_op jit(solution)/shard_map/dot_general | solution.py:124
  26.1 3.8 %collective-permute-start.4 = (bf16[1,3,32,128]{3,2,1,0:T(8,128)(2,1)S(1)}, bf16[1,3,32,128]{3,2,1,0:T(8,128)(2,1)S(1)}, u32[]{:S(2)}, u32[]{:S(2)}) collective-permute-start(bf16[1,3,32,128]{3,2,1,0:T(8,128)(2,1)S(1)} %bitcast.192), channel_id=1, source_target_pairs={{0,8},{8,0},{16,24},{24,16},{32,40},{40,32},{48,56},{56,48},{64,72... | collective-permute-start | bytes 73736 | tf_op jit(solution)/shard_map/ppermute | solution.py:26
  31.8 3.9 %collective-permute-start.7 = (bf16[5,1,32,128]{3,2,1,0:T(8,128)(2,1)S(1)}, bf16[5,1,32,128]{3,2,1,0:T(8,128)(2,1)S(1)}, u32[]{:S(2)}, u32[]{:S(2)}) collective-permute-start(bf16[5,1,32,128]{3,2,1,0:T(8,128)(2,1)S(1)} %get-tuple-element.61), channel_id=1, source_target_pairs={{1,2},{2,1},{3,4},{4,3},{5,6},{6,5},{9,10},{10,9},{11,12},{12,11},... | collective-permute-start | bytes 122888 | tf_op jit(solution)/shard_map/ppermute | solution.py:27
  35.7 1.6 %collective-permute-done.7 = bf16[5,1,32,128]{3,2,1,0:T(8,128)(2,1)S(1)} collective-permute-done((bf16[5,1,32,128]{3,2,1,0:T(8,128)(2,1)S(1)}, bf16[5,1,32,128]{3,2,1,0:T(8,128)(2,1)S(1)}, u32[]{:S(2)}, u32[]{:S(2)}) %collective-permute-start.7) | collective-permute-done | bytes 40992 | tf_op jit(solution)/shard_map/ppermute | solution.py:27
  38.4 5.1 %collective-permute-start.8 = (bf16[1,1,32,128]{3,2,1,0:T(8,128)(2,1)S(1)}, bf16[1,1,32,128]{3,2,1,0:T(8,128)(2,1)S(1)}, u32[]{:S(2)}, u32[]{:S(2)}) collective-permute-start(bf16[1,1,32,128]{3,2,1,0:T(8,128)(2,1)S(1)} %fusion.57), channel_id=1, source_target_pairs={{0,8},{8,0},{16,24},{24,16},{32,40},{40,32},{48,56},{56,48},{64,72... | collective-permute-start | bytes 24584 | tf_op jit(solution)/shard_map/ppermute | solution.py:26
  44.7 4.6 %collective-permute-start.11 = (bf16[3,1,32,128]{3,2,1,0:T(8,128)(2,1)S(1)}, bf16[3,1,32,128]{3,2,1,0:T(8,128)(2,1)S(1)}, u32[]{:S(2)}, u32[]{:S(2)}) collective-permute-start(bf16[3,1,32,128]{3,2,1,0:T(8,128)(2,1)S(1)} %pad_maximum_fusion.27), channel_id=1, source_target_pairs={{1,2},{2,1},{3,4},{4,3},{5,6},{6,5},{9,10},{10,9},{11,12},{12,11},... | collective-permute-start | bytes 73736 | tf_op jit(solution)/shard_map/ppermute | solution.py:27
  49.7 0.9 collective-permute-done.11
  53.6 1.0 copy-done.24
  56.3 1.2 %fusion.23 = f32[192,128,1,1]{1,0,3,2:T(8,128)S(1)} fusion(bf16[16,16,12,128]{3,1,2,0:T(8,128)(2,1)S(1)} %multiply_convert_fusion, bf16[16,16,12,64]{3,1,2,0:T(8,128)(2,1)S(1)} %copy-done.18, bf16[16,16,12,64]{3,1,2,0:T(8,128)(2,1)S(1)} %copy-done.14, bf16[16,16,12,64]{3,1,2,0:T(8,128)(2,1)S(1)} %copy-done.12), kind=kOutput, calls=%fused_computation.46 | convolution fusion | flops 154533888 | bytes 2064384 | tf_op jit(solution)/shard_map/ijtc,ijtd->cd/dot_general | solution.py:280
  57.6 1.2 %fusion.21 = f32[192,128,1,1]{1,0,3,2:T(8,128)S(1)} fusion(bf16[16,16,12,128]{3,1,2,0:T(8,128)(2,1)S(1)} %multiply_convert_fusion, bf16[16,16,12,64]{3,1,2,0:T(8,128)(2,1)S(1)} %copy-done.6, bf16[16,16,12,64]{3,1,2,0:T(8,128)(2,1)S(1)} %copy-done.4, bf16[16,16,12,64]{3,1,2,0:T(8,128)(2,1)S(1)} %copy.88), kind=kOutput, calls=%fused_computation.44 | convolution fusion | flops 154533888 | bytes 2064384 | tf_op jit(solution)/shard_map/ijtc,ijtd->cd/dot_general | solution.py:280
  59.2 1.2 %fusion.20 = f32[192,128,1,1]{1,0,3,2:T(8,128)S(1)} fusion(bf16[16,16,12,128]{3,1,2,0:T(8,128)(2,1)S(1)} %multiply_convert_fusion, bf16[16,16,12,64]{3,1,2,0:T(8,128)(2,1)S(1)} %copy-done.16, bf16[16,16,12,64]{3,1,2,0:T(8,128)(2,1)S(1)} %copy-done.10, bf16[16,16,12,64]{3,1,2,0:T(8,128)(2,1)S(1)} %copy-done.8), kind=kOutput, calls=%fused_computation.43 | convolution fusion | flops 154533888 | bytes 2064384 | tf_op jit(solution)/shard_map/ijtc,ijtd->cd/dot_general | solution.py:280
  61.4 4.0 %collective-permute-start.15 = (bf16[16,1,1536]{2,1,0:T(2,128)(2,1)S(1)}, bf16[16,1,1536]{2,1,0:T(2,128)(2,1)S(1)}, u32[]{:S(2)}, u32[]{:S(2)}) collective-permute-start(bf16[16,1,1536]{2,1,0:T(2,128)(2,1)S(1)} %get-tuple-element.41), channel_id=1, source_target_pairs={{1,2},{2,1},{3,4},{4,3},{5,6},{6,5},{9,10},{10,9},{11,12},{12,11},... | collective-permute-start | bytes 147464 | tf_op jit(solution)/shard_map/ppermute | solution.py:61
  65.6 1.4 %collective-permute-start.13 = (f32[160,128]{1,0:T(8,128)S(1)}, f32[160,128]{1,0:T(8,128)S(1)}, u32[]{:S(2)}, u32[]{:S(2)}) collective-permute-start(f32[160,128]{1,0:T(8,128)S(1)} %slice_select_fusion.1), channel_id=1, source_target_pairs={{0,2},{1,3},{2,0},{3,1},{4,6},{5,7},{6,4},{7,5},{8,10},{9,11},{10,... | collective-permute-start | bytes 245768 | tf_op jit(solution)/shard_map/ppermute | solution.py:40
  68.0 1.5 %collective-permute-done.13 = f32[160,128]{1,0:T(8,128)S(1)} collective-permute-done((f32[160,128]{1,0:T(8,128)S(1)}, f32[160,128]{1,0:T(8,128)S(1)}, u32[]{:S(2)}, u32[]{:S(2)}) %collective-permute-start.13) | collective-permute-done | bytes 81952 | tf_op jit(solution)/shard_map/ppermute | solution.py:40
  69.5 2.9 %collective-permute-start.14 = (f32[160,128]{1,0:T(8,128)S(1)}, f32[160,128]{1,0:T(8,128)S(1)}, u32[]{:S(2)}, u32[]{:S(2)}) collective-permute-start(f32[160,128]{1,0:T(8,128)S(1)} %select_add_fusion), channel_id=1, source_target_pairs={{0,4},{1,5},{2,6},{3,7},{4,0},{5,1},{6,2},{7,3},{8,12},{9,13},{10,... | collective-permute-start | bytes 245768 | tf_op jit(solution)/shard_map/ppermute | solution.py:40
  72.5 1.9 %collective-permute-done.14 = f32[160,128]{1,0:T(8,128)S(1)} collective-permute-done((f32[160,128]{1,0:T(8,128)S(1)}, f32[160,128]{1,0:T(8,128)S(1)}, u32[]{:S(2)}, u32[]{:S(2)}) %collective-permute-start.14) | collective-permute-done | bytes 81952 | tf_op jit(solution)/shard_map/ppermute | solution.py:40
  74.4 5.8 %collective-permute-start.16 = (f32[376,128]{1,0:T(8,128)S(1)}, f32[376,128]{1,0:T(8,128)S(1)}, u32[]{:S(2)}, u32[]{:S(2)}) collective-permute-start(f32[376,128]{1,0:T(8,128)S(1)} %pad_maximum_fusion.14), channel_id=1, source_target_pairs={{0,8},{8,0},{16,24},{24,16},{32,40},{40,32},{48,56},{56,48},{64,72... | collective-permute-start | bytes 577544 | tf_op jit(solution)/shard_map/ppermute | solution.py:40
  80.9 2.9 %collective-permute-done.16 = f32[376,128]{1,0:T(8,128)S(1)} collective-permute-done((f32[376,128]{1,0:T(8,128)S(1)}, f32[376,128]{1,0:T(8,128)S(1)}, u32[]{:S(2)}, u32[]{:S(2)}) %collective-permute-start.16) | collective-permute-done | bytes 192544 | tf_op jit(solution)/shard_map/ppermute | solution.py:40
  83.8 4.0 %collective-permute-start.18 = (f32[160,128]{1,0:T(8,128)S(1)}, f32[160,128]{1,0:T(8,128)S(1)}, u32[]{:S(2)}, u32[]{:S(2)}) collective-permute-start(f32[160,128]{1,0:T(8,128)S(1)} %slice_add_fusion.1), channel_id=1, source_target_pairs={{0,16},{8,24},{16,0},{24,8},{32,48},{40,56},{48,32},{56,40},{64,80... | collective-permute-start | bytes 245768 | tf_op jit(solution)/shard_map/ppermute | solution.py:40
  90.2 2.7 %collective-permute-start.19 = (f32[160,128]{1,0:T(8,128)S(1)}, f32[160,128]{1,0:T(8,128)S(1)}, u32[]{:S(2)}, u32[]{:S(2)}) collective-permute-start(f32[160,128]{1,0:T(8,128)S(1)} %add.145), channel_id=1, source_target_pairs={{0,32},{8,40},{16,48},{24,56},{32,0},{40,8},{48,16},{56,24},{64,96... | collective-permute-start | bytes 245768 | tf_op jit(solution)/shard_map/ppermute | solution.py:40
  92.9 2.8 %fusion.81 = (bf16[16,16,12,128]{3,2,1,0:T(8,128)(2,1)S(1)}, bf16[16,16,12,128]{3,2,1,0:T(8,128)(2,1)S(1)}, bf16[16,16,12,128]{3,2,1,0:T(8,128)(2,1)S(1)}, bf16[...) fusion(bf16[18,18,12,128]{3,2,1,0:T(8,128)(2,1)S(1)} %reshape.224), kind=kLoop, calls=%fused_computation.198 | loop fusion | bytes 14155776 | tf_op jit(solution)/shard_map/slice | solution.py:138
  96.4 3.4 %collective-permute-start.20 = (f32[160,128]{1,0:T(8,128)S(1)}, f32[160,128]{1,0:T(8,128)S(1)}, u32[]{:S(2)}, u32[]{:S(2)}) collective-permute-start(f32[160,128]{1,0:T(8,128)S(1)} %add.146), channel_id=1, source_target_pairs={{0,64},{8,72},{16,80},{24,88},{32,96},{40,104},{48,112},{56,120},{... | collective-permute-start | bytes 245768 | tf_op jit(solution)/shard_map/ppermute | solution.py:40
  101.6 3.2 %collective-permute-start.21 = (f32[160,128]{1,0:T(8,128)S(1)}, f32[160,128]{1,0:T(8,128)S(1)}, u32[]{:S(2)}, u32[]{:S(2)}) collective-permute-start(f32[160,128]{1,0:T(8,128)S(1)} %add.147), channel_id=1, source_target_pairs={{0,2},{1,3},{2,0},{3,1},{4,6},{5,7},{6,4},{7,5},{8,10},{9,11},{10,... | collective-permute-start | bytes 245768 | tf_op jit(solution)/shard_map/ppermute | solution.py:40
  106.6 4.9 %collective-permute-start.22 = (f32[320,128]{1,0:T(8,128)S(1)}, f32[320,128]{1,0:T(8,128)S(1)}, u32[]{:S(2)}, u32[]{:S(2)}) collective-permute-start(f32[320,128]{1,0:T(8,128)S(1)} %maximum_select_fusion.3), channel_id=1, source_target_pairs={{0,1},{1,0},{2,3},{3,2},{4,5},{5,4},{6,7},{7,6},{8,9},{9,8},{10,11... | collective-permute-start | bytes 491528 | tf_op jit(solution)/shard_map/ppermute | solution.py:40
  112.6 1.4 %reshape.225 = bf16[16,16,768]{2,1,0:T(8,128)(2,1)} reshape(bf16[16,16,12,64]{3,2,1,0:T(8,128)(2,1)S(1)} %copy.65) | data formatting | bytes 786432 | tf_op jit(solution)/shard_map/reshape | solution.py:306
  (190 shorter events, 31.4 us)
Async XLA Ops:
  0.6 37.1 %copy-start = (bf16[128,20]{0,1:T(8,128)(2,1)S(1)}, bf16[128,20]{0,1:T(8,128)(2,1)}, u32[]{:S(2)}) copy-start(bf16[128,20]{0,1:T(8,128)(2,1)} %param.11) | copy-start | bytes 15364
  0.6 7.1 %copy-start.2 = (bf16[16,16,768]{2,1,0:T(8,128)(2,1)S(1)}, bf16[16,16,768]{2,1,0:T(8,128)(2,1)}, u32[]{:S(2)}) copy-start(bf16[16,16,768]{2,1,0:T(8,128)(2,1)} %param.8) | copy-start | bytes 1179652
  0.7 11.6 %copy-start.22 = (s32[16,16]{1,0:T(8,128)S(1)}, s32[16,16]{1,0:T(8,128)}, u32[]{:S(2)}) copy-start(s32[16,16]{1,0:T(8,128)} %param.12) | copy-start | bytes 3076
  1.5 6.2 %collective-permute-start = (bf16[1,16,768]{2,1,0:T(8,128)(2,1)S(1)}, bf16[1,16,768]{2,1,0:T(8,128)(2,1)S(1)}, u32[]{:S(2)}, u32[]{:S(2)}) collective-permute-start(bf16[1,16,768]{2,1,0:T(8,128)(2,1)S(1)} %get-tuple-element.42), channel_id=1, source_target_pairs={{0,8},{8,0},{16,24},{24,16},{32,40},{40,32},{48,56},{56,48},{64,72... | collective-permute-start | bytes 73736 | tf_op jit(solution)/shard_map/ppermute | solution.py:26
  3.5 4.2 %collective-permute-start.1 = (bf16[1,16,768]{2,1,0:T(8,128)(2,1)S(1)}, bf16[1,16,768]{2,1,0:T(8,128)(2,1)S(1)}, u32[]{:S(2)}, u32[]{:S(2)}) collective-permute-start(bf16[1,16,768]{2,1,0:T(8,128)(2,1)S(1)} %get-tuple-element.43), channel_id=1, source_target_pairs={{8,16},{16,8},{24,32},{32,24},{40,48},{48,40},{56,64},{64,56},{72,... | collective-permute-start | bytes 73736 | tf_op jit(solution)/shard_map/ppermute | solution.py:27
  8.0 5.9 %collective-permute-start.3 = (bf16[18,1,768]{2,1,0:T(2,128)(2,1)S(1)}, bf16[18,1,768]{2,1,0:T(2,128)(2,1)S(1)}, u32[]{:S(2)}, u32[]{:S(2)}) collective-permute-start(bf16[18,1,768]{2,1,0:T(2,128)(2,1)S(1)} %broadcast_select_fusion.6), channel_id=1, source_target_pairs={{1,2},{2,1},{3,4},{4,3},{5,6},{6,5},{9,10},{10,9},{11,12},{12,11},... | collective-permute-start | bytes 82952 | tf_op jit(solution)/shard_map/ppermute | solution.py:27
  12.1 1.8 %collective-permute-start.2 = (bf16[18,1,768]{2,1,0:T(2,128)(2,1)S(1)}, bf16[18,1,768]{2,1,0:T(2,128)(2,1)S(1)}, u32[]{:S(2)}, u32[]{:S(2)}) collective-permute-start(bf16[18,1,768]{2,1,0:T(2,128)(2,1)S(1)} %get-tuple-element.19), channel_id=1, source_target_pairs={{0,1},{1,0},{2,3},{3,2},{4,5},{5,4},{6,7},{7,6},{8,9},{9,8},{10,11... | collective-permute-start | bytes 82952 | tf_op jit(solution)/shard_map/ppermute | solution.py:26
  18.6 2.4 %copy-start.11 = (bf16[16,16,12,64]{3,1,2,0:T(8,128)(2,1)}, bf16[16,16,12,64]{3,1,2,0:T(8,128)(2,1)S(1)}, u32[]{:S(2)}) copy-start(bf16[16,16,12,64]{3,1,2,0:T(8,128)(2,1)S(1)} %copy.85) | copy-start | bytes 1179652
  19.3 2.6 %copy-start.7 = (bf16[16,16,12,64]{3,1,2,0:T(8,128)(2,1)}, bf16[16,16,12,64]{3,1,2,0:T(8,128)(2,1)S(1)}, u32[]{:S(2)}) copy-start(bf16[16,16,12,64]{3,1,2,0:T(8,128)(2,1)S(1)} %copy.91) | copy-start | bytes 1179652
  19.6 2.4 %copy-start.9 = (bf16[16,16,12,64]{3,1,2,0:T(8,128)(2,1)}, bf16[16,16,12,64]{3,1,2,0:T(8,128)(2,1)S(1)}, u32[]{:S(2)}) copy-start(bf16[16,16,12,64]{3,1,2,0:T(8,128)(2,1)S(1)} %copy.92) | copy-start | bytes 1179652
  19.8 2.2 %copy-start.15 = (bf16[16,16,12,64]{3,1,2,0:T(8,128)(2,1)}, bf16[16,16,12,64]{3,1,2,0:T(8,128)(2,1)S(1)}, u32[]{:S(2)}) copy-start(bf16[16,16,12,64]{3,1,2,0:T(8,128)(2,1)S(1)} %copy.93) | copy-start | bytes 1179652
  25.7 12.3 %copy-start.23 = (s32[1,1,32]{2,1,0:T(1,128)S(1)}, s32[1,1,32]{2,1,0:T(1,128)}, u32[]{:S(2)}) copy-start(s32[1,1,32]{2,1,0:T(1,128)} %param.15) | copy-start | bytes 388
  26.1 5.2 %collective-permute-start.4 = (bf16[1,3,32,128]{3,2,1,0:T(8,128)(2,1)S(1)}, bf16[1,3,32,128]{3,2,1,0:T(8,128)(2,1)S(1)}, u32[]{:S(2)}, u32[]{:S(2)}) collective-permute-start(bf16[1,3,32,128]{3,2,1,0:T(8,128)(2,1)S(1)} %bitcast.192), channel_id=1, source_target_pairs={{0,8},{8,0},{16,24},{24,16},{32,40},{40,32},{48,56},{56,48},{64,72... | collective-permute-start | bytes 73736 | tf_op jit(solution)/shard_map/ppermute | solution.py:26
  29.9 1.4 %collective-permute-start.5 = (bf16[1,3,32,128]{3,2,1,0:T(8,128)(2,1)S(1)}, bf16[1,3,32,128]{3,2,1,0:T(8,128)(2,1)S(1)}, u32[]{:S(2)}, u32[]{:S(2)}) collective-permute-start(bf16[1,3,32,128]{3,2,1,0:T(8,128)(2,1)S(1)} %bitcast.191), channel_id=1, source_target_pairs={{8,16},{16,8},{24,32},{32,24},{40,48},{48,40},{56,64},{64,56},{72,... | collective-permute-start | bytes 73736 | tf_op jit(solution)/shard_map/ppermute | solution.py:27
  31.3 4.4 %collective-permute-start.6 = (bf16[5,1,32,128]{3,2,1,0:T(8,128)(2,1)S(1)}, bf16[5,1,32,128]{3,2,1,0:T(8,128)(2,1)S(1)}, u32[]{:S(2)}, u32[]{:S(2)}) collective-permute-start(bf16[5,1,32,128]{3,2,1,0:T(8,128)(2,1)S(1)} %get-tuple-element.60), channel_id=1, source_target_pairs={{0,1},{1,0},{2,3},{3,2},{4,5},{5,4},{6,7},{7,6},{8,9},{9,8},{10,11... | collective-permute-start | bytes 122888 | tf_op jit(solution)/shard_map/ppermute | solution.py:26
  31.8 5.6 %collective-permute-start.7 = (bf16[5,1,32,128]{3,2,1,0:T(8,128)(2,1)S(1)}, bf16[5,1,32,128]{3,2,1,0:T(8,128)(2,1)S(1)}, u32[]{:S(2)}, u32[]{:S(2)}) collective-permute-start(bf16[5,1,32,128]{3,2,1,0:T(8,128)(2,1)S(1)} %get-tuple-element.61), channel_id=1, source_target_pairs={{1,2},{2,1},{3,4},{4,3},{5,6},{6,5},{9,10},{10,9},{11,12},{12,11},... | collective-permute-start | bytes 122888 | tf_op jit(solution)/shard_map/ppermute | solution.py:27
  38.4 6.1 %collective-permute-start.8 = (bf16[1,1,32,128]{3,2,1,0:T(8,128)(2,1)S(1)}, bf16[1,1,32,128]{3,2,1,0:T(8,128)(2,1)S(1)}, u32[]{:S(2)}, u32[]{:S(2)}) collective-permute-start(bf16[1,1,32,128]{3,2,1,0:T(8,128)(2,1)S(1)} %fusion.57), channel_id=1, source_target_pairs={{0,8},{8,0},{16,24},{24,16},{32,40},{40,32},{48,56},{56,48},{64,72... | collective-permute-start | bytes 24584 | tf_op jit(solution)/shard_map/ppermute | solution.py:26
  43.5 1.0 collective-permute-start.9
  44.6 5.1 %collective-permute-start.10 = (bf16[3,1,32,128]{3,2,1,0:T(8,128)(2,1)S(1)}, bf16[3,1,32,128]{3,2,1,0:T(8,128)(2,1)S(1)}, u32[]{:S(2)}, u32[]{:S(2)}) collective-permute-start(bf16[3,1,32,128]{3,2,1,0:T(8,128)(2,1)S(1)} %pad_maximum_fusion.27), channel_id=1, source_target_pairs={{0,1},{1,0},{2,3},{3,2},{4,5},{5,4},{6,7},{7,6},{8,9},{9,8},{10,11... | collective-permute-start | bytes 73736 | tf_op jit(solution)/shard_map/ppermute | solution.py:26
  44.7 5.9 %collective-permute-start.11 = (bf16[3,1,32,128]{3,2,1,0:T(8,128)(2,1)S(1)}, bf16[3,1,32,128]{3,2,1,0:T(8,128)(2,1)S(1)}, u32[]{:S(2)}, u32[]{:S(2)}) collective-permute-start(bf16[3,1,32,128]{3,2,1,0:T(8,128)(2,1)S(1)} %pad_maximum_fusion.27), channel_id=1, source_target_pairs={{1,2},{2,1},{3,4},{4,3},{5,6},{6,5},{9,10},{10,9},{11,12},{12,11},... | collective-permute-start | bytes 73736 | tf_op jit(solution)/shard_map/ppermute | solution.py:27
  61.2 4.2 %collective-permute-start.12 = (f32[512,128]{1,0:T(8,128)S(1)}, f32[512,128]{1,0:T(8,128)S(1)}, u32[]{:S(2)}, u32[]{:S(2)}) collective-permute-start(f32[512,128]{1,0:T(8,128)S(1)} %pad_maximum_fusion.6), channel_id=1, source_target_pairs={{0,1},{1,0},{2,3},{3,2},{4,5},{5,4},{6,7},{7,6},{8,9},{9,8},{10,11... | collective-permute-start | bytes 786440 | tf_op jit(solution)/shard_map/ppermute | solution.py:40
  61.4 6.3 %collective-permute-start.15 = (bf16[16,1,1536]{2,1,0:T(2,128)(2,1)S(1)}, bf16[16,1,1536]{2,1,0:T(2,128)(2,1)S(1)}, u32[]{:S(2)}, u32[]{:S(2)}) collective-permute-start(bf16[16,1,1536]{2,1,0:T(2,128)(2,1)S(1)} %get-tuple-element.41), channel_id=1, source_target_pairs={{1,2},{2,1},{3,4},{4,3},{5,6},{6,5},{9,10},{10,9},{11,12},{12,11},... | collective-permute-start | bytes 147464 | tf_op jit(solution)/shard_map/ppermute | solution.py:61
  65.6 3.9 %collective-permute-start.13 = (f32[160,128]{1,0:T(8,128)S(1)}, f32[160,128]{1,0:T(8,128)S(1)}, u32[]{:S(2)}, u32[]{:S(2)}) collective-permute-start(f32[160,128]{1,0:T(8,128)S(1)} %slice_select_fusion.1), channel_id=1, source_target_pairs={{0,2},{1,3},{2,0},{3,1},{4,6},{5,7},{6,4},{7,5},{8,10},{9,11},{10,... | collective-permute-start | bytes 245768 | tf_op jit(solution)/shard_map/ppermute | solution.py:40
  69.5 4.9 %collective-permute-start.14 = (f32[160,128]{1,0:T(8,128)S(1)}, f32[160,128]{1,0:T(8,128)S(1)}, u32[]{:S(2)}, u32[]{:S(2)}) collective-permute-start(f32[160,128]{1,0:T(8,128)S(1)} %select_add_fusion), channel_id=1, source_target_pairs={{0,4},{1,5},{2,6},{3,7},{4,0},{5,1},{6,2},{7,3},{8,12},{9,13},{10,... | collective-permute-start | bytes 245768 | tf_op jit(solution)/shard_map/ppermute | solution.py:40
  74.4 9.4 %collective-permute-start.16 = (f32[376,128]{1,0:T(8,128)S(1)}, f32[376,128]{1,0:T(8,128)S(1)}, u32[]{:S(2)}, u32[]{:S(2)}) collective-permute-start(f32[376,128]{1,0:T(8,128)S(1)} %pad_maximum_fusion.14), channel_id=1, source_target_pairs={{0,8},{8,0},{16,24},{24,16},{32,40},{40,32},{48,56},{56,48},{64,72... | collective-permute-start | bytes 577544 | tf_op jit(solution)/shard_map/ppermute | solution.py:40
  80.3 7.7 %collective-permute-start.17 = (bf16[1,18,1536]{2,1,0:T(8,128)(2,1)S(1)}, bf16[1,18,1536]{2,1,0:T(8,128)(2,1)S(1)}, u32[]{:S(2)}, u32[]{:S(2)}) collective-permute-start(bf16[1,18,1536]{2,1,0:T(8,128)(2,1)S(1)} %broadcast_select_fusion.11), channel_id=1, source_target_pairs={{8,16},{16,8},{24,32},{32,24},{40,48},{48,40},{56,64},{64,56},{72,... | collective-permute-start | bytes 165896 | tf_op jit(solution)/shard_map/ppermute | solution.py:61
  83.8 6.3 %collective-permute-start.18 = (f32[160,128]{1,0:T(8,128)S(1)}, f32[160,128]{1,0:T(8,128)S(1)}, u32[]{:S(2)}, u32[]{:S(2)}) collective-permute-start(f32[160,128]{1,0:T(8,128)S(1)} %slice_add_fusion.1), channel_id=1, source_target_pairs={{0,16},{8,24},{16,0},{24,8},{32,48},{40,56},{48,32},{56,40},{64,80... | collective-permute-start | bytes 245768 | tf_op jit(solution)/shard_map/ppermute | solution.py:40
  90.2 6.2 %collective-permute-start.19 = (f32[160,128]{1,0:T(8,128)S(1)}, f32[160,128]{1,0:T(8,128)S(1)}, u32[]{:S(2)}, u32[]{:S(2)}) collective-permute-start(f32[160,128]{1,0:T(8,128)S(1)} %add.145), channel_id=1, source_target_pairs={{0,32},{8,40},{16,48},{24,56},{32,0},{40,8},{48,16},{56,24},{64,96... | collective-permute-start | bytes 245768 | tf_op jit(solution)/shard_map/ppermute | solution.py:40
  96.4 5.2 %collective-permute-start.20 = (f32[160,128]{1,0:T(8,128)S(1)}, f32[160,128]{1,0:T(8,128)S(1)}, u32[]{:S(2)}, u32[]{:S(2)}) collective-permute-start(f32[160,128]{1,0:T(8,128)S(1)} %add.146), channel_id=1, source_target_pairs={{0,64},{8,72},{16,80},{24,88},{32,96},{40,104},{48,112},{56,120},{... | collective-permute-start | bytes 245768 | tf_op jit(solution)/shard_map/ppermute | solution.py:40
  101.6 5.0 %collective-permute-start.21 = (f32[160,128]{1,0:T(8,128)S(1)}, f32[160,128]{1,0:T(8,128)S(1)}, u32[]{:S(2)}, u32[]{:S(2)}) collective-permute-start(f32[160,128]{1,0:T(8,128)S(1)} %add.147), channel_id=1, source_target_pairs={{0,2},{1,3},{2,0},{3,1},{4,6},{5,7},{6,4},{7,5},{8,10},{9,11},{10,... | collective-permute-start | bytes 245768 | tf_op jit(solution)/shard_map/ppermute | solution.py:40
  106.6 7.4 %collective-permute-start.22 = (f32[320,128]{1,0:T(8,128)S(1)}, f32[320,128]{1,0:T(8,128)S(1)}, u32[]{:S(2)}, u32[]{:S(2)}) collective-permute-start(f32[320,128]{1,0:T(8,128)S(1)} %maximum_select_fusion.3), channel_id=1, source_target_pairs={{0,1},{1,0},{2,3},{3,2},{4,5},{5,4},{6,7},{7,6},{8,9},{9,8},{10,11... | collective-permute-start | bytes 491528 | tf_op jit(solution)/shard_map/ppermute | solution.py:40
  112.3 4.1 %copy-start.1 = (bf16[128,20]{0,1:T(8,128)(2,1)S(1)}, bf16[128,20]{0,1:T(8,128)(2,1)}, u32[]{:S(2)}) copy-start(bf16[128,20]{0,1:T(8,128)(2,1)} %param.11) | copy-start | bytes 15364
  (16 other events, 22.2 us)

commit v7 on v6

--- a/solution.py
+++ b/solution.py
@@ -130,6 +130,17 @@
     return running_sum
 
 
+def window_conv(padded, kernel):
+    return lax.conv_general_dilated(
+        padded,
+        kernel,
+        window_strides=(1, 1),
+        padding="VALID",
+        dimension_numbers=("HWNC", "HWIO", "HWNC"),
+        preferred_element_type=jnp.float32,
+    )
+
+
 def transposed_conv(padded_grad, conv_weight, out_rows, out_cols):
     input_sum = None
     for row_tap in range(3):
@@ -176,7 +187,7 @@
     padded_pixels = with_halo(pixels, (("row", 0), ("col", 1)), 1).reshape(
         tile_rows + 2, tile_cols + 2, DATES, C_IN
     )
-    pre_act = spatial_forward(padded_pixels, conv_weight, tile_rows, tile_cols)
+    pre_act = window_conv(padded_pixels, conv_weight)
     hidden = jax.nn.silu(pre_act).astype(jnp.bfloat16)
     dense_time = block_weights(time_weight)
     padded_hidden = jnp.pad(hidden, ((0, 0), (0, 0), (1, 1), (0, 0)))
@@ -302,7 +313,7 @@
         grad_pre.reshape(tile_rows, tile_cols, DATES * C_OUT),
     )
     padded_grad = padded_grad.reshape(tile_rows + 2, tile_cols + 2, DATES, C_OUT)
-    input_sum = transposed_conv(padded_grad, conv_weight, tile_rows, tile_cols)
+    input_sum = window_conv(padded_grad, jnp.swapaxes(conv_weight[::-1, ::-1], 2, 3))
     input_grad = input_sum.astype(jnp.bfloat16).reshape(tile_rows, tile_cols, DATES * C_IN)
     conv_grad = flat[:conv_rows].reshape(conv_term.shape)
     time_grad = flat[conv_rows : conv_rows + time_rows].reshape(time_term.shape)

time: 117 us -> 122 us (1.043)
  local copies, waits for them, and re-layouts: 20.9 us -> 13.7 us
  matrix products: 15.9 us -> 22 us
  waiting for transfers between devices: 13.8 us -> 18.1 us
  other arithmetic: 4.94 us -> 8.1 us
  starting transfers between devices: 59.2 us -> 56.9 us
    dot_general x6 -> x0, matrix products: 6.36 us -> none  [the longest x3 4.06 us: spatial_forward(): jnp.dot(tap_patch, conv_weight[row_tap].reshape(3 * C_IN, C_OUT), preferr...]
    conv_general_dilated x0 -> x2, matrix products: none -> 5.51 us  [window_conv(): lax.conv_general_dilated(padded, kernel, window_strides=(1, 1), padding='...]
    unnamed x71 -> x35, local copies, waits for them, and re-layouts: 8.91 us -> 4.22 us
    ppermute x9, waiting for transfers between devices: 7.93 us -> 12.5 us  [exchange(): return lax.ppermute(value, axis, [(i, i ^ bit) for i in range(size)])]
    dot_general x3, matrix products: 1.52 us -> 6.04 us  [per_device(): jnp.dot(padded_mixed[:, :, 2 - time_tap:2 - time_tap + DATES], dense_time...]
    slice x3 -> x1, local copies, waits for them, and re-layouts: 6.91 us -> 3.85 us  [per_device(): padded_pixels[row_tap:row_tap + tile_rows, col_tap:col_tap + tile_cols]]
    ppermute x9, starting transfers between devices: 28.4 us -> 25.5 us  [exchange(): return lax.ppermute(value, axis, [(i, i ^ bit) for i in range(size)])]
    convert_element_type x1, other arithmetic: 0.59 us -> 2 us  [per_device(): ((pixel_grad / DATES)[:, :, None, :] * silu_slope(mixed_time)).astype(jnp...]
  transfers between devices with their start and end apart: 23 -> 23, of which waited for: 12 -> 11; matrix products, arithmetic and copies ran while one was open for 13% -> 12% of each run, Pallas kernels for 0% -> 0%
where the time goes in v7:
time: 122 us; the launch traced here: 120 us
  starting transfers between devices  56.9 us (47%)
  matrix products  22 us (18%)
  waiting for transfers between devices  18.1 us (15%)
  local copies, waits for them, and re-layouts  13.7 us (11%)
  other arithmetic  8.1 us (7%)
  between operations  1.39 us (1%)
    ppermute x9, starting transfers between devices, exchange(): return lax.ppermute(value, axis, [(i, i ^ bit) for i in range(size)])  25.5 us
    ppermute x6, starting transfers between devices, with_halo(): lax.ppermute(jnp.where(odd, tail, head), axis, [pair for k in range(1, co...  14.1 us
    ppermute x6, starting transfers between devices, with_halo(): lax.ppermute(jnp.where(odd, head, tail), axis, [(i, i ^ 1) for i in range...  12.7 us
    ppermute x9, waiting for transfers between devices, exchange(): return lax.ppermute(value, axis, [(i, i ^ bit) for i in range(size)])  12.5 us
    dot_general x3, matrix products, per_device(): jnp.dot(padded_mixed[:, :, 2 - time_tap:2 - time_tap + DATES], dense_time...  6.04 us
    conv_general_dilated x2, matrix products, window_conv(): lax.conv_general_dilated(padded, kernel, window_strides=(1, 1), padding='...  5.51 us
    dot_general x3, matrix products, per_device(): jnp.einsum('ijtc,ijtd->cd', tap_patch, grad_pre, preferred_element_type=j...  5.03 us
    ppermute x2, starting transfers between devices, outer_swap(): lax.ppermute(piece, axis, [pair for k in range(1, count - 1, 2) for pair...  4.55 us
  transfers between devices with their start and end apart: 23, of which 11 were waited for; matrix products, arithmetic and copies ran while one was open for 12% of the time, Pallas kernels for 0%

profile of v7, /device:TPU:1, one launch (start us, length us, event | category | flops | bytes accessed | tf_op | source)
XLA Modules:
  0.0 120.3 jit_solution(1405278809153131084)
XLA Ops:
  1.5 2.0 %collective-permute-start = (bf16[1,16,768]{2,1,0:T(8,128)(2,1)S(1)}, bf16[1,16,768]{2,1,0:T(8,128)(2,1)S(1)}, u32[]{:S(2)}, u32[]{:S(2)}) collective-permute-start(bf16[1,16,768]{2,1,0:T(8,128)(2,1)S(1)} %get-tuple-element.33), channel_id=1, source_target_pairs={{0,8},{8,0},{16,24},{24,16},{32,40},{40,32},{48,56},{56,48},{64,72... | collective-permute-start | bytes 73736 | tf_op jit(solution)/shard_map/ppermute | solution.py:26
  7.6 4.0 %collective-permute-start.3 = (bf16[18,1,768]{2,1,0:T(2,128)(2,1)S(1)}, bf16[18,1,768]{2,1,0:T(2,128)(2,1)S(1)}, u32[]{:S(2)}, u32[]{:S(2)}) collective-permute-start(bf16[18,1,768]{2,1,0:T(2,128)(2,1)S(1)} %broadcast_select_fusion.6), channel_id=1, source_target_pairs={{1,2},{2,1},{3,4},{4,3},{5,6},{6,5},{9,10},{10,9},{11,12},{12,11},... | collective-permute-start | bytes 82952 | tf_op jit(solution)/shard_map/ppermute | solution.py:27
  11.9 1.6 %collective-permute-done.3 = bf16[18,1,768]{2,1,0:T(2,128)(2,1)S(1)} collective-permute-done((bf16[18,1,768]{2,1,0:T(2,128)(2,1)S(1)}, bf16[18,1,768]{2,1,0:T(2,128)(2,1)S(1)}, u32[]{:S(2)}, u32[]{:S(2)}) %collective-permute-start.3) | collective-permute-done | bytes 27680 | tf_op jit(solution)/shard_map/ppermute | solution.py:27
  14.8 1.6 %fusion.61 = f32[16,16,12,128]{3,2,1,0:T(8,128)S(1)} fusion(bf16[18,18,12,64]{3,2,1,0:T(8,128)(2,1)S(1)} %reshape.214, bf16[3,3,64,128]{3,2,1,0:T(8,128)(2,1)S(1)} %copy-done), kind=kOutput, calls=%fused_computation.164 | convolution fusion | flops 452984832 | bytes 2217984 | tf_op jit(solution)/shard_map/conv_general_dilated | solution.py:134
  18.1 1.8 %multiply_reduce_fusion = (f32[16,16,128]{2,1,0:T(8,128)S(1)}, f32[16,16,12,128]{3,1,2,0:T(8,128)}) fusion(bf16[16,16,12,128]{3,1,2,0:T(8,128)(2,1)S(1)} %multiply_convert_fusion.2, bf16[3,128,128]{2,1,0:T(8,128)(2,1)S(1)} %broadcast_select_fusion.8, f32[16,16,12,128]{3,1,2,0:T(8,128)S(1)} %fusion.37, f32[16,16,12,128]{3,1,2,0:T(8,128)S(1)} %fusion.39), kind=kOutput, calls=%fused_computation.20 | convolution fusion | flops 94994432 | bytes 5668864 | tf_op jit(solution)/shard_map/dot_general | solution.py:196
  20.2 3.7 %collective-permute-start.4 = (bf16[1,3,32,128]{3,2,1,0:T(8,128)(2,1)S(1)}, bf16[1,3,32,128]{3,2,1,0:T(8,128)(2,1)S(1)}, u32[]{:S(2)}, u32[]{:S(2)}) collective-permute-start(bf16[1,3,32,128]{3,2,1,0:T(8,128)(2,1)S(1)} %bitcast.121), channel_id=1, source_target_pairs={{0,8},{8,0},{16,24},{24,16},{32,40},{40,32},{48,56},{56,48},{64,72... | collective-permute-start | bytes 73736 | tf_op jit(solution)/shard_map/ppermute | solution.py:26
  25.9 3.9 %collective-permute-start.7 = (bf16[5,1,32,128]{3,2,1,0:T(8,128)(2,1)S(1)}, bf16[5,1,32,128]{3,2,1,0:T(8,128)(2,1)S(1)}, u32[]{:S(2)}, u32[]{:S(2)}) collective-permute-start(bf16[5,1,32,128]{3,2,1,0:T(8,128)(2,1)S(1)} %get-tuple-element.40), channel_id=1, source_target_pairs={{1,2},{2,1},{3,4},{4,3},{5,6},{6,5},{9,10},{10,9},{11,12},{12,11},... | collective-permute-start | bytes 122888 | tf_op jit(solution)/shard_map/ppermute | solution.py:27
  29.9 1.6 %collective-permute-done.7 = bf16[5,1,32,128]{3,2,1,0:T(8,128)(2,1)S(1)} collective-permute-done((bf16[5,1,32,128]{3,2,1,0:T(8,128)(2,1)S(1)}, bf16[5,1,32,128]{3,2,1,0:T(8,128)(2,1)S(1)}, u32[]{:S(2)}, u32[]{:S(2)}) %collective-permute-start.7) | collective-permute-done | bytes 40992 | tf_op jit(solution)/shard_map/ppermute | solution.py:27
  32.6 6.3 %collective-permute-start.8 = (bf16[1,1,32,128]{3,2,1,0:T(8,128)(2,1)S(1)}, bf16[1,1,32,128]{3,2,1,0:T(8,128)(2,1)S(1)}, u32[]{:S(2)}, u32[]{:S(2)}) collective-permute-start(bf16[1,1,32,128]{3,2,1,0:T(8,128)(2,1)S(1)} %fusion.41), channel_id=1, source_target_pairs={{0,8},{8,0},{16,24},{24,16},{32,40},{40,32},{48,56},{56,48},{64,72... | collective-permute-start | bytes 24584 | tf_op jit(solution)/shard_map/ppermute | solution.py:26
  39.6 3.8 %fusion.59 = (bf16[16,16,12,64]{3,2,1,0:T(8,128)(2,1)}, bf16[16,16,12,64]{3,2,1,0:T(8,128)(2,1)}, bf16[16,16,12,64]{3,2,1,0:T(8,128)(2,1)}, bf16[16,16,12,64]{3,...) fusion(bf16[18,18,12,64]{3,2,1,0:T(8,128)(2,1)S(1)} %reshape.214), kind=kLoop, calls=%fused_computation.162 | loop fusion | bytes 7077888 | tf_op jit(solution)/shard_map/slice | solution.py:285
  43.5 4.2 %collective-permute-start.11 = (bf16[3,1,32,128]{3,2,1,0:T(8,128)(2,1)S(1)}, bf16[3,1,32,128]{3,2,1,0:T(8,128)(2,1)S(1)}, u32[]{:S(2)}, u32[]{:S(2)}) collective-permute-start(bf16[3,1,32,128]{3,2,1,0:T(8,128)(2,1)S(1)} %pad_maximum_fusion.18), channel_id=1, source_target_pairs={{1,2},{2,1},{3,4},{4,3},{5,6},{6,5},{9,10},{10,9},{11,12},{12,11},... | collective-permute-start | bytes 73736 | tf_op jit(solution)/shard_map/ppermute | solution.py:27
  49.5 2.0 %multiply_convert_fusion.1 = bf16[16,16,12,128]{3,1,2,0:T(8,128)(2,1)S(1)} fusion(f32[16,16,12,128]{3,1,2,0:T(8,128)} %get-tuple-element.56, f32[16,16,128]{2,1,0:T(8,128)S(1)} %bitcast.112), kind=kLoop, calls=%fused_computation.19 | loop fusion | flops 3538944 | bytes 2490368 | tf_op jit(solution)/shard_map/convert_element_type | solution.py:257
  52.7 1.5 %fusion.38 = f32[16,16,12,128]{3,1,2,0:T(8,128)} fusion(bf16[16,16,12,128]{3,1,2,0:T(8,128)(2,1)S(1)} %multiply_convert_fusion.1, bf16[3,128,128]{2,1,0:T(8,128)(2,1)S(1)} %broadcast_select_fusion.8), kind=kOutput, calls=%fused_computation.109 | convolution fusion | flops 100663296 | bytes 2392064 | tf_op jit(solution)/shard_map/dot_general | solution.py:274
  56.4 3.0 %multiply_convert_fusion = bf16[16,16,12,128]{3,1,2,0:T(8,128)(2,1)S(1)} fusion(f32[16,16,12,128]{3,1,2,0:T(8,128)} %fusion.36, f32[16,16,12,128]{3,1,2,0:T(8,128)} %fusion.38, bf16[16,16,12,128]{3,1,2,0:T(8,128)(2,1)S(1)} %multiply_convert_fusion.1, f32[16,16,12,128]{3,2,1,0:T(8,128)S(1)} %copy-done.2, bf16[3,128,128]{2,1,0:T(8,128)(2,1)S(1)} %broadcast_select_fusion.8), kind=kOutput, calls=%fused_computation.18 | convolution fusion | flops 96600064 | bytes 6848512 | tf_op jit(solution)/shard_map/dot_general | solution.py:274
  60.6 1.7 %fusion = f32[192,128,1,1]{1,0,3,2:T(8,128)S(1)} fusion(bf16[16,16,12,64]{3,2,1,0:T(8,128)(2,1)S(1)} %copy-done.11, bf16[16,16,12,64]{3,2,1,0:T(8,128)(2,1)S(1)} %copy-done.12, bf16[16,16,12,64]{3,2,1,0:T(8,128)(2,1)S(1)} %copy-done.10, bf16[16,16,12,128]{3,1,2,0:T(8,128)(2,1)S(1)} %multiply_convert_fusion), kind=kOutput, calls=%fused_computation | convolution fusion | flops 154533888 | bytes 2064384 | tf_op jit(solution)/shard_map/ijtc,ijtd->cd/dot_general | solution.py:291
  62.5 1.7 %fusion.6 = f32[192,128,1,1]{1,0,3,2:T(8,128)S(1)} fusion(bf16[16,16,12,64]{3,2,1,0:T(8,128)(2,1)S(1)} %copy-done.7, bf16[16,16,12,64]{3,2,1,0:T(8,128)(2,1)S(1)} %copy-done.8, bf16[16,16,12,64]{3,2,1,0:T(8,128)(2,1)S(1)} %copy-done.9, bf16[16,16,12,128]{3,1,2,0:T(8,128)(2,1)S(1)} %multiply_convert_fusion), kind=kOutput, calls=%fused_computation.6 | convolution fusion | flops 154533888 | bytes 2064384 | tf_op jit(solution)/shard_map/ijtc,ijtd->cd/dot_general | solution.py:291
  64.4 1.7 %fusion.12 = f32[192,128,1,1]{1,0,3,2:T(8,128)S(1)} fusion(bf16[16,16,12,64]{3,2,1,0:T(8,128)(2,1)S(1)} %copy-done.4, bf16[16,16,12,64]{3,2,1,0:T(8,128)(2,1)S(1)} %copy-done.5, bf16[16,16,12,64]{3,2,1,0:T(8,128)(2,1)S(1)} %copy-done.6, bf16[16,16,12,128]{3,1,2,0:T(8,128)(2,1)S(1)} %multiply_convert_fusion), kind=kOutput, calls=%fused_computation.12 | convolution fusion | flops 154533888 | bytes 2064384 | tf_op jit(solution)/shard_map/ijtc,ijtd->cd/dot_general | solution.py:291
  66.3 3.9 %collective-permute-start.15 = (bf16[16,1,1536]{2,1,0:T(2,128)(2,1)S(1)}, bf16[16,1,1536]{2,1,0:T(2,128)(2,1)S(1)}, u32[]{:S(2)}, u32[]{:S(2)}) collective-permute-start(bf16[16,1,1536]{2,1,0:T(2,128)(2,1)S(1)} %get-tuple-element.32), channel_id=1, source_target_pairs={{1,2},{2,1},{3,4},{4,3},{5,6},{6,5},{9,10},{10,9},{11,12},{12,11},... | collective-permute-start | bytes 147464 | tf_op jit(solution)/shard_map/ppermute | solution.py:61
  72.7 1.5 %collective-permute-done.13 = f32[160,128]{1,0:T(8,128)S(1)} collective-permute-done((f32[160,128]{1,0:T(8,128)S(1)}, f32[160,128]{1,0:T(8,128)S(1)}, u32[]{:S(2)}, u32[]{:S(2)}) %collective-permute-start.13) | collective-permute-done | bytes 81952 | tf_op jit(solution)/shard_map/ppermute | solution.py:40
  74.3 2.9 %collective-permute-start.14 = (f32[160,128]{1,0:T(8,128)S(1)}, f32[160,128]{1,0:T(8,128)S(1)}, u32[]{:S(2)}, u32[]{:S(2)}) collective-permute-start(f32[160,128]{1,0:T(8,128)S(1)} %select_add_fusion), channel_id=1, source_target_pairs={{0,4},{1,5},{2,6},{3,7},{4,0},{5,1},{6,2},{7,3},{8,12},{9,13},{10,... | collective-permute-start | bytes 245768 | tf_op jit(solution)/shard_map/ppermute | solution.py:40
  77.3 1.9 %collective-permute-done.14 = f32[160,128]{1,0:T(8,128)S(1)} collective-permute-done((f32[160,128]{1,0:T(8,128)S(1)}, f32[160,128]{1,0:T(8,128)S(1)}, u32[]{:S(2)}, u32[]{:S(2)}) %collective-permute-start.14) | collective-permute-done | bytes 81952 | tf_op jit(solution)/shard_map/ppermute | solution.py:40
  79.2 5.2 %collective-permute-start.16 = (f32[376,128]{1,0:T(8,128)S(1)}, f32[376,128]{1,0:T(8,128)S(1)}, u32[]{:S(2)}, u32[]{:S(2)}) collective-permute-start(f32[376,128]{1,0:T(8,128)S(1)} %pad_maximum_fusion.5), channel_id=1, source_target_pairs={{0,8},{8,0},{16,24},{24,16},{32,40},{40,32},{48,56},{56,48},{64,72... | collective-permute-start | bytes 577544 | tf_op jit(solution)/shard_map/ppermute | solution.py:40
  84.4 3.6 %collective-permute-done.16 = f32[376,128]{1,0:T(8,128)S(1)} collective-permute-done((f32[376,128]{1,0:T(8,128)S(1)}, f32[376,128]{1,0:T(8,128)S(1)}, u32[]{:S(2)}, u32[]{:S(2)}) %collective-permute-start.16) | collective-permute-done | bytes 192544 | tf_op jit(solution)/shard_map/ppermute | solution.py:40
  88.0 2.2 %collective-permute-start.18 = (f32[160,128]{1,0:T(8,128)S(1)}, f32[160,128]{1,0:T(8,128)S(1)}, u32[]{:S(2)}, u32[]{:S(2)}) collective-permute-start(f32[160,128]{1,0:T(8,128)S(1)} %slice_add_fusion.1), channel_id=1, source_target_pairs={{0,16},{8,24},{16,0},{24,8},{32,48},{40,56},{48,32},{56,40},{64,80... | collective-permute-start | bytes 245768 | tf_op jit(solution)/shard_map/ppermute | solution.py:40
  90.2 2.7 %collective-permute-done.18 = f32[160,128]{1,0:T(8,128)S(1)} collective-permute-done((f32[160,128]{1,0:T(8,128)S(1)}, f32[160,128]{1,0:T(8,128)S(1)}, u32[]{:S(2)}, u32[]{:S(2)}) %collective-permute-start.18) | collective-permute-done | bytes 81952 | tf_op jit(solution)/shard_map/ppermute | solution.py:40
  92.9 1.6 %collective-permute-start.19 = (f32[160,128]{1,0:T(8,128)S(1)}, f32[160,128]{1,0:T(8,128)S(1)}, u32[]{:S(2)}, u32[]{:S(2)}) collective-permute-start(f32[160,128]{1,0:T(8,128)S(1)} %add.129), channel_id=1, source_target_pairs={{0,32},{8,40},{16,48},{24,56},{32,0},{40,8},{48,16},{56,24},{64,96... | collective-permute-start | bytes 245768 | tf_op jit(solution)/shard_map/ppermute | solution.py:40
  96.4 3.9 %collective-permute-start.20 = (f32[160,128]{1,0:T(8,128)S(1)}, f32[160,128]{1,0:T(8,128)S(1)}, u32[]{:S(2)}, u32[]{:S(2)}) collective-permute-start(f32[160,128]{1,0:T(8,128)S(1)} %add.130), channel_id=1, source_target_pairs={{0,64},{8,72},{16,80},{24,88},{32,96},{40,104},{48,112},{56,120},{... | collective-permute-start | bytes 245768 | tf_op jit(solution)/shard_map/ppermute | solution.py:40
  100.3 1.8 %collective-permute-done.20 = f32[160,128]{1,0:T(8,128)S(1)} collective-permute-done((f32[160,128]{1,0:T(8,128)S(1)}, f32[160,128]{1,0:T(8,128)S(1)}, u32[]{:S(2)}, u32[]{:S(2)}) %collective-permute-start.20) | collective-permute-done | bytes 81952 | tf_op jit(solution)/shard_map/ppermute | solution.py:40
  102.1 3.0 %collective-permute-start.21 = (f32[160,128]{1,0:T(8,128)S(1)}, f32[160,128]{1,0:T(8,128)S(1)}, u32[]{:S(2)}, u32[]{:S(2)}) collective-permute-start(f32[160,128]{1,0:T(8,128)S(1)} %add.131), channel_id=1, source_target_pairs={{0,2},{1,3},{2,0},{3,1},{4,6},{5,7},{6,4},{7,5},{8,10},{9,11},{10,... | collective-permute-start | bytes 245768 | tf_op jit(solution)/shard_map/ppermute | solution.py:40
  105.6 1.7 %reshape.224 = bf16[18,18,12,128]{3,2,1,0:T(8,128)(2,1)} reshape(bf16[18,18,1536]{2,1,0:T(8,128)(2,1)S(1)} %pad_maximum_fusion) | data formatting | bytes 1990656 | tf_op jit(solution)/shard_map/reshape | solution.py:315
  107.3 5.2 %collective-permute-start.22 = (f32[320,128]{1,0:T(8,128)S(1)}, f32[320,128]{1,0:T(8,128)S(1)}, u32[]{:S(2)}, u32[]{:S(2)}) collective-permute-start(f32[320,128]{1,0:T(8,128)S(1)} %maximum_select_fusion.3), channel_id=1, source_target_pairs={{0,1},{1,0},{2,3},{3,2},{4,5},{5,4},{6,7},{7,6},{8,9},{9,8},{10,11... | collective-permute-start | bytes 491528 | tf_op jit(solution)/shard_map/ppermute | solution.py:40
  112.5 3.9 %convolution_convert_fusion = bf16[16,16,12,64]{3,2,1,0:T(8,128)(2,1)S(1)} fusion(bf16[18,18,12,128]{3,2,1,0:T(8,128)(2,1)} %reshape.224, bf16[3,3,64,128]{3,2,1,0:T(8,128)(2,1)S(1)} %copy-done), kind=kOutput, calls=%fused_computation.25 | convolution fusion | flops 453181440 | bytes 1536000 | tf_op jit(solution)/shard_map/conv_general_dilated | solution.py:134
  (147 shorter events, 27.7 us)
Async XLA Ops:
  0.6 14.1 %copy-start = (bf16[3,3,64,128]{3,2,1,0:T(8,128)(2,1)S(1)}, bf16[3,3,64,128]{3,2,1,0:T(8,128)(2,1)}, u32[]{:S(2)}) copy-start(bf16[3,3,64,128]{3,2,1,0:T(8,128)(2,1)} %param.9) | copy-start | bytes 442372
  0.6 13.0 %copy-start.3 = (bf16[16,16,768]{2,1,0:T(8,128)(2,1)S(1)}, bf16[16,16,768]{2,1,0:T(8,128)(2,1)}, u32[]{:S(2)}) copy-start(bf16[16,16,768]{2,1,0:T(8,128)(2,1)} %param.8) | copy-start | bytes 1179652
  0.7 11.2 %copy-start.13 = (s32[16,16]{1,0:T(8,128)S(1)}, s32[16,16]{1,0:T(8,128)}, u32[]{:S(2)}) copy-start(s32[16,16]{1,0:T(8,128)} %param.12) | copy-start | bytes 3076
  1.5 4.8 %collective-permute-start = (bf16[1,16,768]{2,1,0:T(8,128)(2,1)S(1)}, bf16[1,16,768]{2,1,0:T(8,128)(2,1)S(1)}, u32[]{:S(2)}, u32[]{:S(2)}) collective-permute-start(bf16[1,16,768]{2,1,0:T(8,128)(2,1)S(1)} %get-tuple-element.33), channel_id=1, source_target_pairs={{0,8},{8,0},{16,24},{24,16},{32,40},{40,32},{48,56},{56,48},{64,72... | collective-permute-start | bytes 73736 | tf_op jit(solution)/shard_map/ppermute | solution.py:26
  3.5 2.8 %collective-permute-start.1 = (bf16[1,16,768]{2,1,0:T(8,128)(2,1)S(1)}, bf16[1,16,768]{2,1,0:T(8,128)(2,1)S(1)}, u32[]{:S(2)}, u32[]{:S(2)}) collective-permute-start(bf16[1,16,768]{2,1,0:T(8,128)(2,1)S(1)} %get-tuple-element.34), channel_id=1, source_target_pairs={{8,16},{16,8},{24,32},{32,24},{40,48},{48,40},{56,64},{64,56},{72,... | collective-permute-start | bytes 73736 | tf_op jit(solution)/shard_map/ppermute | solution.py:27
  7.6 5.9 %collective-permute-start.3 = (bf16[18,1,768]{2,1,0:T(2,128)(2,1)S(1)}, bf16[18,1,768]{2,1,0:T(2,128)(2,1)S(1)}, u32[]{:S(2)}, u32[]{:S(2)}) collective-permute-start(bf16[18,1,768]{2,1,0:T(2,128)(2,1)S(1)} %broadcast_select_fusion.6), channel_id=1, source_target_pairs={{1,2},{2,1},{3,4},{4,3},{5,6},{6,5},{9,10},{10,9},{11,12},{12,11},... | collective-permute-start | bytes 82952 | tf_op jit(solution)/shard_map/ppermute | solution.py:27
  11.7 1.8 %collective-permute-start.2 = (bf16[18,1,768]{2,1,0:T(2,128)(2,1)S(1)}, bf16[18,1,768]{2,1,0:T(2,128)(2,1)S(1)}, u32[]{:S(2)}, u32[]{:S(2)}) collective-permute-start(bf16[18,1,768]{2,1,0:T(2,128)(2,1)S(1)} %get-tuple-element.19), channel_id=1, source_target_pairs={{0,1},{1,0},{2,3},{3,2},{4,5},{5,4},{6,7},{7,6},{8,9},{9,8},{10,11... | collective-permute-start | bytes 82952 | tf_op jit(solution)/shard_map/ppermute | solution.py:26
  18.1 13.8 %copy-start.14 = (bf16[128,20]{0,1:T(8,128)(2,1)S(1)}, bf16[128,20]{0,1:T(8,128)(2,1)}, u32[]{:S(2)}) copy-start(bf16[128,20]{0,1:T(8,128)(2,1)} %param.11) | copy-start | bytes 15364
  19.9 12.3 %copy-start.15 = (s32[1,1,32]{2,1,0:T(1,128)S(1)}, s32[1,1,32]{2,1,0:T(1,128)}, u32[]{:S(2)}) copy-start(s32[1,1,32]{2,1,0:T(1,128)} %param.15) | copy-start | bytes 388
  20.2 5.2 %collective-permute-start.4 = (bf16[1,3,32,128]{3,2,1,0:T(8,128)(2,1)S(1)}, bf16[1,3,32,128]{3,2,1,0:T(8,128)(2,1)S(1)}, u32[]{:S(2)}, u32[]{:S(2)}) collective-permute-start(bf16[1,3,32,128]{3,2,1,0:T(8,128)(2,1)S(1)} %bitcast.121), channel_id=1, source_target_pairs={{0,8},{8,0},{16,24},{24,16},{32,40},{40,32},{48,56},{56,48},{64,72... | collective-permute-start | bytes 73736 | tf_op jit(solution)/shard_map/ppermute | solution.py:26
  24.0 1.4 %collective-permute-start.5 = (bf16[1,3,32,128]{3,2,1,0:T(8,128)(2,1)S(1)}, bf16[1,3,32,128]{3,2,1,0:T(8,128)(2,1)S(1)}, u32[]{:S(2)}, u32[]{:S(2)}) collective-permute-start(bf16[1,3,32,128]{3,2,1,0:T(8,128)(2,1)S(1)} %bitcast.120), channel_id=1, source_target_pairs={{8,16},{16,8},{24,32},{32,24},{40,48},{48,40},{56,64},{64,56},{72,... | collective-permute-start | bytes 73736 | tf_op jit(solution)/shard_map/ppermute | solution.py:27
  25.5 4.4 %collective-permute-start.6 = (bf16[5,1,32,128]{3,2,1,0:T(8,128)(2,1)S(1)}, bf16[5,1,32,128]{3,2,1,0:T(8,128)(2,1)S(1)}, u32[]{:S(2)}, u32[]{:S(2)}) collective-permute-start(bf16[5,1,32,128]{3,2,1,0:T(8,128)(2,1)S(1)} %get-tuple-element.39), channel_id=1, source_target_pairs={{0,1},{1,0},{2,3},{3,2},{4,5},{5,4},{6,7},{7,6},{8,9},{9,8},{10,11... | collective-permute-start | bytes 122888 | tf_op jit(solution)/shard_map/ppermute | solution.py:26
  25.9 5.6 %collective-permute-start.7 = (bf16[5,1,32,128]{3,2,1,0:T(8,128)(2,1)S(1)}, bf16[5,1,32,128]{3,2,1,0:T(8,128)(2,1)S(1)}, u32[]{:S(2)}, u32[]{:S(2)}) collective-permute-start(bf16[5,1,32,128]{3,2,1,0:T(8,128)(2,1)S(1)} %get-tuple-element.40), channel_id=1, source_target_pairs={{1,2},{2,1},{3,4},{4,3},{5,6},{6,5},{9,10},{10,9},{11,12},{12,11},... | collective-permute-start | bytes 122888 | tf_op jit(solution)/shard_map/ppermute | solution.py:27
  32.6 10.8 %collective-permute-start.8 = (bf16[1,1,32,128]{3,2,1,0:T(8,128)(2,1)S(1)}, bf16[1,1,32,128]{3,2,1,0:T(8,128)(2,1)S(1)}, u32[]{:S(2)}, u32[]{:S(2)}) collective-permute-start(bf16[1,1,32,128]{3,2,1,0:T(8,128)(2,1)S(1)} %fusion.41), channel_id=1, source_target_pairs={{0,8},{8,0},{16,24},{24,16},{32,40},{40,32},{48,56},{56,48},{64,72... | collective-permute-start | bytes 24584 | tf_op jit(solution)/shard_map/ppermute | solution.py:26
  38.9 4.5 %collective-permute-start.9 = (bf16[1,1,32,128]{3,2,1,0:T(8,128)(2,1)S(1)}, bf16[1,1,32,128]{3,2,1,0:T(8,128)(2,1)S(1)}, u32[]{:S(2)}, u32[]{:S(2)}) collective-permute-start(bf16[1,1,32,128]{3,2,1,0:T(8,128)(2,1)S(1)} %fusion.41), channel_id=1, source_target_pairs={{8,16},{16,8},{24,32},{32,24},{40,48},{48,40},{56,64},{64,56},{72,... | collective-permute-start | bytes 24584 | tf_op jit(solution)/shard_map/ppermute | solution.py:27
  43.5 4.7 %collective-permute-start.10 = (bf16[3,1,32,128]{3,2,1,0:T(8,128)(2,1)S(1)}, bf16[3,1,32,128]{3,2,1,0:T(8,128)(2,1)S(1)}, u32[]{:S(2)}, u32[]{:S(2)}) collective-permute-start(bf16[3,1,32,128]{3,2,1,0:T(8,128)(2,1)S(1)} %pad_maximum_fusion.18), channel_id=1, source_target_pairs={{0,1},{1,0},{2,3},{3,2},{4,5},{5,4},{6,7},{7,6},{8,9},{9,8},{10,11... | collective-permute-start | bytes 73736 | tf_op jit(solution)/shard_map/ppermute | solution.py:26
  43.5 5.5 %collective-permute-start.11 = (bf16[3,1,32,128]{3,2,1,0:T(8,128)(2,1)S(1)}, bf16[3,1,32,128]{3,2,1,0:T(8,128)(2,1)S(1)}, u32[]{:S(2)}, u32[]{:S(2)}) collective-permute-start(bf16[3,1,32,128]{3,2,1,0:T(8,128)(2,1)S(1)} %pad_maximum_fusion.18), channel_id=1, source_target_pairs={{1,2},{2,1},{3,4},{4,3},{5,6},{6,5},{9,10},{10,9},{11,12},{12,11},... | collective-permute-start | bytes 73736 | tf_op jit(solution)/shard_map/ppermute | solution.py:27
  54.3 2.2 %copy-start.2 = (f32[16,16,12,128]{3,2,1,0:T(8,128)S(1)}, f32[16,16,12,128]{3,2,1,0:T(8,128)}, u32[]{:S(2)}) copy-start(f32[16,16,12,128]{3,2,1,0:T(8,128)} %copy-done.1) | copy-start | bytes 4718596
  56.4 3.3 %copy-start.11 = (bf16[16,16,12,64]{3,2,1,0:T(8,128)(2,1)S(1)}, bf16[16,16,12,64]{3,2,1,0:T(8,128)(2,1)}, u32[]{:S(2)}) copy-start(bf16[16,16,12,64]{3,2,1,0:T(8,128)(2,1)} %get-tuple-element.29) | copy-start | bytes 1179652
  56.4 3.3 %copy-start.12 = (bf16[16,16,12,64]{3,2,1,0:T(8,128)(2,1)S(1)}, bf16[16,16,12,64]{3,2,1,0:T(8,128)(2,1)}, u32[]{:S(2)}) copy-start(bf16[16,16,12,64]{3,2,1,0:T(8,128)(2,1)} %get-tuple-element.30) | copy-start | bytes 1179652
  60.6 1.9 %copy-start.9 = (bf16[16,16,12,64]{3,2,1,0:T(8,128)(2,1)S(1)}, bf16[16,16,12,64]{3,2,1,0:T(8,128)(2,1)}, u32[]{:S(2)}) copy-start(bf16[16,16,12,64]{3,2,1,0:T(8,128)(2,1)} %get-tuple-element.28) | copy-start | bytes 1179652
  66.2 4.0 %collective-permute-start.12 = (f32[512,128]{1,0:T(8,128)S(1)}, f32[512,128]{1,0:T(8,128)S(1)}, u32[]{:S(2)}, u32[]{:S(2)}) collective-permute-start(f32[512,128]{1,0:T(8,128)S(1)} %pad_maximum_fusion.3), channel_id=1, source_target_pairs={{0,1},{1,0},{2,3},{3,2},{4,5},{5,4},{6,7},{7,6},{8,9},{9,8},{10,11... | collective-permute-start | bytes 786440 | tf_op jit(solution)/shard_map/ppermute | solution.py:40
  66.3 6.2 %collective-permute-start.15 = (bf16[16,1,1536]{2,1,0:T(2,128)(2,1)S(1)}, bf16[16,1,1536]{2,1,0:T(2,128)(2,1)S(1)}, u32[]{:S(2)}, u32[]{:S(2)}) collective-permute-start(bf16[16,1,1536]{2,1,0:T(2,128)(2,1)S(1)} %get-tuple-element.32), channel_id=1, source_target_pairs={{1,2},{2,1},{3,4},{4,3},{5,6},{6,5},{9,10},{10,9},{11,12},{12,11},... | collective-permute-start | bytes 147464 | tf_op jit(solution)/shard_map/ppermute | solution.py:61
  70.4 3.9 %collective-permute-start.13 = (f32[160,128]{1,0:T(8,128)S(1)}, f32[160,128]{1,0:T(8,128)S(1)}, u32[]{:S(2)}, u32[]{:S(2)}) collective-permute-start(f32[160,128]{1,0:T(8,128)S(1)} %slice_select_fusion.1), channel_id=1, source_target_pairs={{0,2},{1,3},{2,0},{3,1},{4,6},{5,7},{6,4},{7,5},{8,10},{9,11},{10,... | collective-permute-start | bytes 245768 | tf_op jit(solution)/shard_map/ppermute | solution.py:40
  74.3 4.9 %collective-permute-start.14 = (f32[160,128]{1,0:T(8,128)S(1)}, f32[160,128]{1,0:T(8,128)S(1)}, u32[]{:S(2)}, u32[]{:S(2)}) collective-permute-start(f32[160,128]{1,0:T(8,128)S(1)} %select_add_fusion), channel_id=1, source_target_pairs={{0,4},{1,5},{2,6},{3,7},{4,0},{5,1},{6,2},{7,3},{8,12},{9,13},{10,... | collective-permute-start | bytes 245768 | tf_op jit(solution)/shard_map/ppermute | solution.py:40
  79.2 8.8 %collective-permute-start.16 = (f32[376,128]{1,0:T(8,128)S(1)}, f32[376,128]{1,0:T(8,128)S(1)}, u32[]{:S(2)}, u32[]{:S(2)}) collective-permute-start(f32[376,128]{1,0:T(8,128)S(1)} %pad_maximum_fusion.5), channel_id=1, source_target_pairs={{0,8},{8,0},{16,24},{24,16},{32,40},{40,32},{48,56},{56,48},{64,72... | collective-permute-start | bytes 577544 | tf_op jit(solution)/shard_map/ppermute | solution.py:40
  88.0 4.9 %collective-permute-start.18 = (f32[160,128]{1,0:T(8,128)S(1)}, f32[160,128]{1,0:T(8,128)S(1)}, u32[]{:S(2)}, u32[]{:S(2)}) collective-permute-start(f32[160,128]{1,0:T(8,128)S(1)} %slice_add_fusion.1), channel_id=1, source_target_pairs={{0,16},{8,24},{16,0},{24,8},{32,48},{40,56},{48,32},{56,40},{64,80... | collective-permute-start | bytes 245768 | tf_op jit(solution)/shard_map/ppermute | solution.py:40
  92.9 3.4 %collective-permute-start.19 = (f32[160,128]{1,0:T(8,128)S(1)}, f32[160,128]{1,0:T(8,128)S(1)}, u32[]{:S(2)}, u32[]{:S(2)}) collective-permute-start(f32[160,128]{1,0:T(8,128)S(1)} %add.129), channel_id=1, source_target_pairs={{0,32},{8,40},{16,48},{24,56},{32,0},{40,8},{48,16},{56,24},{64,96... | collective-permute-start | bytes 245768 | tf_op jit(solution)/shard_map/ppermute | solution.py:40
  94.5 5.7 %collective-permute-start.17 = (bf16[1,18,1536]{2,1,0:T(8,128)(2,1)S(1)}, bf16[1,18,1536]{2,1,0:T(8,128)(2,1)S(1)}, u32[]{:S(2)}, u32[]{:S(2)}) collective-permute-start(bf16[1,18,1536]{2,1,0:T(8,128)(2,1)S(1)} %broadcast_select_fusion.11), channel_id=1, source_target_pairs={{8,16},{16,8},{24,32},{32,24},{40,48},{48,40},{56,64},{64,56},{72,... | collective-permute-start | bytes 165896 | tf_op jit(solution)/shard_map/ppermute | solution.py:61
  96.4 5.7 %collective-permute-start.20 = (f32[160,128]{1,0:T(8,128)S(1)}, f32[160,128]{1,0:T(8,128)S(1)}, u32[]{:S(2)}, u32[]{:S(2)}) collective-permute-start(f32[160,128]{1,0:T(8,128)S(1)} %add.130), channel_id=1, source_target_pairs={{0,64},{8,72},{16,80},{24,88},{32,96},{40,104},{48,112},{56,120},{... | collective-permute-start | bytes 245768 | tf_op jit(solution)/shard_map/ppermute | solution.py:40
  102.1 5.2 %collective-permute-start.21 = (f32[160,128]{1,0:T(8,128)S(1)}, f32[160,128]{1,0:T(8,128)S(1)}, u32[]{:S(2)}, u32[]{:S(2)}) collective-permute-start(f32[160,128]{1,0:T(8,128)S(1)} %add.131), channel_id=1, source_target_pairs={{0,2},{1,3},{2,0},{3,1},{4,6},{5,7},{6,4},{7,5},{8,10},{9,11},{10,... | collective-permute-start | bytes 245768 | tf_op jit(solution)/shard_map/ppermute | solution.py:40
  107.3 10.5 %collective-permute-start.22 = (f32[320,128]{1,0:T(8,128)S(1)}, f32[320,128]{1,0:T(8,128)S(1)}, u32[]{:S(2)}, u32[]{:S(2)}) collective-permute-start(f32[320,128]{1,0:T(8,128)S(1)} %maximum_select_fusion.3), channel_id=1, source_target_pairs={{0,1},{1,0},{2,3},{3,2},{4,5},{5,4},{6,7},{7,6},{8,9},{9,8},{10,11... | collective-permute-start | bytes 491528 | tf_op jit(solution)/shard_map/ppermute | solution.py:40
  (7 other events, 11.2 us)

commit v8 on v7

--- a/solution.py
+++ b/solution.py
@@ -313,7 +313,7 @@
         grad_pre.reshape(tile_rows, tile_cols, DATES * C_OUT),
     )
     padded_grad = padded_grad.reshape(tile_rows + 2, tile_cols + 2, DATES, C_OUT)
-    input_sum = window_conv(padded_grad, jnp.swapaxes(conv_weight[::-1, ::-1], 2, 3))
+    input_sum = transposed_conv(padded_grad, conv_weight, tile_rows, tile_cols)
     input_grad = input_sum.astype(jnp.bfloat16).reshape(tile_rows, tile_cols, DATES * C_IN)
     conv_grad = flat[:conv_rows].reshape(conv_term.shape)
     time_grad = flat[conv_rows : conv_rows + time_rows].reshape(time_term.shape)

time: 122 us -> 118 us (0.967); the launches traced: 120 us -> 118 us
  local copies, waits for them, and re-layouts: 13.7 us -> 17.8 us
  waiting for transfers between devices: 18.1 us -> 14.1 us
  matrix products: 22 us -> 20.5 us
    ppermute x9, waiting for transfers between devices: 12.5 us -> 8.5 us  [exchange(): return lax.ppermute(value, axis, [(i, i ^ bit) for i in range(size)])]
    conv_general_dilated x2 -> x1, matrix products: 5.51 us -> 1.59 us  [window_conv(): lax.conv_general_dilated(padded, kernel, window_strides=(1, 1), padding='...]
    slice x0 -> x1, local copies, waits for them, and re-layouts: none -> 2.81 us  [transposed_conv(): padded_grad[2 - row_tap:2 - row_tap + out_rows, 2 - col_tap:2 - col_tap +...]
    dot_general x0 -> x3, matrix products: none -> 2.29 us  [transposed_conv(): tap_term = jnp.dot(grad_patch, flipped, preferred_element_type=jnp.float32)]
    unnamed x35 -> x44, local copies, waits for them, and re-layouts: 4.22 us -> 6.04 us
  transfers between devices with their start and end apart: 23 -> 23, of which waited for: 11 -> 11; matrix products, arithmetic and copies ran while one was open for 12% -> 14% of each run, Pallas kernels for 0% -> 0%
where the time goes in v8:
time: 118 us
  starting transfers between devices  56 us (47%)
  matrix products  20.5 us (17%)
  local copies, waits for them, and re-layouts  17.8 us (15%)
  waiting for transfers between devices  14.1 us (12%)
  other arithmetic  8.11 us (7%)
  between operations  1.51 us (1%)
    ppermute x9, starting transfers between devices, exchange(): return lax.ppermute(value, axis, [(i, i ^ bit) for i in range(size)])  24.5 us
    ppermute x6, starting transfers between devices, with_halo(): lax.ppermute(jnp.where(odd, tail, head), axis, [pair for k in range(1, co...  14.1 us
    ppermute x6, starting transfers between devices, with_halo(): lax.ppermute(jnp.where(odd, head, tail), axis, [(i, i ^ 1) for i in range...  12.8 us
    ppermute x9, waiting for transfers between devices, exchange(): return lax.ppermute(value, axis, [(i, i ^ bit) for i in range(size)])  8.5 us
    dot_general x3, matrix products, per_device(): jnp.dot(padded_mixed[:, :, 2 - time_tap:2 - time_tap + DATES], dense_time...  6.06 us
    unnamed x44, local copies, waits for them, and re-layouts  6.04 us
    dot_general x3, matrix products, per_device(): jnp.einsum('ijtc,ijtd->cd', tap_patch, grad_pre, preferred_element_type=j...  5.04 us
    ppermute x2, starting transfers between devices, outer_swap(): lax.ppermute(piece, axis, [pair for k in range(1, count - 1, 2) for pair...  4.56 us
  transfers between devices with their start and end apart: 23, of which 11 were waited for; matrix products, arithmetic and copies ran while one was open for 14% of the time, Pallas kernels for 0%

profile of v8, /device:TPU:1, one launch (start us, length us, event | category | flops | bytes accessed | tf_op | source)
XLA Modules:
  0.0 117.9 jit_solution(1735437198827506434)
XLA Ops:
  1.5 2.0 %collective-permute-start = (bf16[1,16,768]{2,1,0:T(8,128)(2,1)S(1)}, bf16[1,16,768]{2,1,0:T(8,128)(2,1)S(1)}, u32[]{:S(2)}, u32[]{:S(2)}) collective-permute-start(bf16[1,16,768]{2,1,0:T(8,128)(2,1)S(1)} %get-tuple-element.42), channel_id=1, source_target_pairs={{0,8},{8,0},{16,24},{24,16},{32,40},{40,32},{48,56},{56,48},{64,72... | collective-permute-start | bytes 73736 | tf_op jit(solution)/shard_map/ppermute | solution.py:26
  7.6 4.0 %collective-permute-start.3 = (bf16[18,1,768]{2,1,0:T(2,128)(2,1)S(1)}, bf16[18,1,768]{2,1,0:T(2,128)(2,1)S(1)}, u32[]{:S(2)}, u32[]{:S(2)}) collective-permute-start(bf16[18,1,768]{2,1,0:T(2,128)(2,1)S(1)} %broadcast_select_fusion.6), channel_id=1, source_target_pairs={{1,2},{2,1},{3,4},{4,3},{5,6},{6,5},{9,10},{10,9},{11,12},{12,11},... | collective-permute-start | bytes 82952 | tf_op jit(solution)/shard_map/ppermute | solution.py:27
  11.9 1.6 %collective-permute-done.3 = bf16[18,1,768]{2,1,0:T(2,128)(2,1)S(1)} collective-permute-done((bf16[18,1,768]{2,1,0:T(2,128)(2,1)S(1)}, bf16[18,1,768]{2,1,0:T(2,128)(2,1)S(1)}, u32[]{:S(2)}, u32[]{:S(2)}) %collective-permute-start.3) | collective-permute-done | bytes 27680 | tf_op jit(solution)/shard_map/ppermute | solution.py:27
  14.8 1.6 %fusion.97 = f32[16,16,12,128]{3,2,1,0:T(8,128)S(1)} fusion(bf16[18,18,12,64]{3,2,1,0:T(8,128)(2,1)S(1)} %reshape.214, bf16[3,3,64,128]{3,2,1,0:T(8,128)(2,1)S(1)} %copy-done.13), kind=kOutput, calls=%fused_computation.210 | convolution fusion | flops 452984832 | bytes 2217984 | tf_op jit(solution)/shard_map/conv_general_dilated | solution.py:134
  18.1 1.8 %multiply_reduce_fusion = (f32[16,16,128]{2,1,0:T(8,128)S(1)}, f32[16,16,12,128]{3,1,2,0:T(8,128)}) fusion(bf16[16,16,12,128]{3,1,2,0:T(8,128)(2,1)S(1)} %multiply_convert_fusion.2, bf16[3,128,128]{2,1,0:T(8,128)(2,1)S(1)} %broadcast_select_fusion.8, f32[16,16,12,128]{3,1,2,0:T(8,128)S(1)} %fusion.69, f32[16,16,12,128]{3,1,2,0:T(8,128)S(1)} %fusion.71), kind=kOutput, calls=%fused_computation.39 | convolution fusion | flops 94994432 | bytes 5668864 | tf_op jit(solution)/shard_map/dot_general | solution.py:196
  20.2 3.7 %collective-permute-start.4 = (bf16[1,3,32,128]{3,2,1,0:T(8,128)(2,1)S(1)}, bf16[1,3,32,128]{3,2,1,0:T(8,128)(2,1)S(1)}, u32[]{:S(2)}, u32[]{:S(2)}) collective-permute-start(bf16[1,3,32,128]{3,2,1,0:T(8,128)(2,1)S(1)} %bitcast.170), channel_id=1, source_target_pairs={{0,8},{8,0},{16,24},{24,16},{32,40},{40,32},{48,56},{56,48},{64,72... | collective-permute-start | bytes 73736 | tf_op jit(solution)/shard_map/ppermute | solution.py:26
  25.9 3.9 %collective-permute-start.7 = (bf16[5,1,32,128]{3,2,1,0:T(8,128)(2,1)S(1)}, bf16[5,1,32,128]{3,2,1,0:T(8,128)(2,1)S(1)}, u32[]{:S(2)}, u32[]{:S(2)}) collective-permute-start(bf16[5,1,32,128]{3,2,1,0:T(8,128)(2,1)S(1)} %get-tuple-element.58), channel_id=1, source_target_pairs={{1,2},{2,1},{3,4},{4,3},{5,6},{6,5},{9,10},{10,9},{11,12},{12,11},... | collective-permute-start | bytes 122888 | tf_op jit(solution)/shard_map/ppermute | solution.py:27
  29.9 1.6 %collective-permute-done.7 = bf16[5,1,32,128]{3,2,1,0:T(8,128)(2,1)S(1)} collective-permute-done((bf16[5,1,32,128]{3,2,1,0:T(8,128)(2,1)S(1)}, bf16[5,1,32,128]{3,2,1,0:T(8,128)(2,1)S(1)}, u32[]{:S(2)}, u32[]{:S(2)}) %collective-permute-start.7) | collective-permute-done | bytes 40992 | tf_op jit(solution)/shard_map/ppermute | solution.py:27
  32.6 6.4 %collective-permute-start.8 = (bf16[1,1,32,128]{3,2,1,0:T(8,128)(2,1)S(1)}, bf16[1,1,32,128]{3,2,1,0:T(8,128)(2,1)S(1)}, u32[]{:S(2)}, u32[]{:S(2)}) collective-permute-start(bf16[1,1,32,128]{3,2,1,0:T(8,128)(2,1)S(1)} %fusion.73), channel_id=1, source_target_pairs={{0,8},{8,0},{16,24},{24,16},{32,40},{40,32},{48,56},{56,48},{64,72... | collective-permute-start | bytes 24584 | tf_op jit(solution)/shard_map/ppermute | solution.py:26
  39.6 3.8 %fusion.95 = (bf16[16,16,12,64]{3,2,1,0:T(8,128)(2,1)}, bf16[16,16,12,64]{3,2,1,0:T(8,128)(2,1)}, bf16[16,16,12,64]{3,2,1,0:T(8,128)(2,1)}, bf16[16,16,12,64]{3,...) fusion(bf16[18,18,12,64]{3,2,1,0:T(8,128)(2,1)S(1)} %reshape.214), kind=kLoop, calls=%fused_computation.208 | loop fusion | bytes 7077888 | tf_op jit(solution)/shard_map/slice | solution.py:285
  43.5 4.2 %collective-permute-start.11 = (bf16[3,1,32,128]{3,2,1,0:T(8,128)(2,1)S(1)}, bf16[3,1,32,128]{3,2,1,0:T(8,128)(2,1)S(1)}, u32[]{:S(2)}, u32[]{:S(2)}) collective-permute-start(bf16[3,1,32,128]{3,2,1,0:T(8,128)(2,1)S(1)} %pad_maximum_fusion.18), channel_id=1, source_target_pairs={{1,2},{2,1},{3,4},{4,3},{5,6},{6,5},{9,10},{10,9},{11,12},{12,11},... | collective-permute-start | bytes 73736 | tf_op jit(solution)/shard_map/ppermute | solution.py:27
  49.4 2.0 %multiply_convert_fusion.1 = bf16[16,16,12,128]{3,1,2,0:T(8,128)(2,1)S(1)} fusion(f32[16,16,12,128]{3,1,2,0:T(8,128)} %get-tuple-element.74, f32[16,16,128]{2,1,0:T(8,128)S(1)} %bitcast.161), kind=kLoop, calls=%fused_computation.38 | loop fusion | flops 3538944 | bytes 2490368 | tf_op jit(solution)/shard_map/convert_element_type | solution.py:257
  52.7 1.5 %fusion.70 = f32[16,16,12,128]{3,1,2,0:T(8,128)} fusion(bf16[16,16,12,128]{3,1,2,0:T(8,128)(2,1)S(1)} %multiply_convert_fusion.1, bf16[3,128,128]{2,1,0:T(8,128)(2,1)S(1)} %broadcast_select_fusion.8), kind=kOutput, calls=%fused_computation.142 | convolution fusion | flops 100663296 | bytes 2392064 | tf_op jit(solution)/shard_map/dot_general | solution.py:274
  54.2 1.5 %fusion.68 = f32[16,16,12,128]{3,1,2,0:T(8,128)} fusion(bf16[16,16,12,128]{3,1,2,0:T(8,128)(2,1)S(1)} %multiply_convert_fusion.1, bf16[3,128,128]{2,1,0:T(8,128)(2,1)S(1)} %broadcast_select_fusion.8), kind=kOutput, calls=%fused_computation.140 | convolution fusion | flops 92274688 | bytes 2392064 | tf_op jit(solution)/shard_map/dot_general | solution.py:274
  56.4 3.0 %multiply_convert_fusion = bf16[16,16,12,128]{3,1,2,0:T(8,128)(2,1)S(1)} fusion(f32[16,16,12,128]{3,1,2,0:T(8,128)} %fusion.68, f32[16,16,12,128]{3,1,2,0:T(8,128)} %fusion.70, bf16[16,16,12,128]{3,1,2,0:T(8,128)(2,1)S(1)} %multiply_convert_fusion.1, f32[16,16,12,128]{3,2,1,0:T(8,128)S(1)} %copy-done.2, bf16[3,128,128]{2,1,0:T(8,128)(2,1)S(1)} %broadcast_select_fusion.8), kind=kOutput, calls=%fused_computation.37 | convolution fusion | flops 96600064 | bytes 6848512 | tf_op jit(solution)/shard_map/dot_general | solution.py:274
  60.6 1.7 %fusion.18 = f32[192,128,1,1]{1,0,3,2:T(8,128)S(1)} fusion(bf16[16,16,12,64]{3,2,1,0:T(8,128)(2,1)S(1)} %copy-done.11, bf16[16,16,12,64]{3,2,1,0:T(8,128)(2,1)S(1)} %copy-done.12, bf16[16,16,12,64]{3,2,1,0:T(8,128)(2,1)S(1)} %copy-done.10, bf16[16,16,12,128]{3,1,2,0:T(8,128)(2,1)S(1)} %multiply_convert_fusion), kind=kOutput, calls=%fused_computation.18 | convolution fusion | flops 154533888 | bytes 2064384 | tf_op jit(solution)/shard_map/ijtc,ijtd->cd/dot_general | solution.py:291
  62.5 1.7 %fusion.24 = f32[192,128,1,1]{1,0,3,2:T(8,128)S(1)} fusion(bf16[16,16,12,64]{3,2,1,0:T(8,128)(2,1)S(1)} %copy-done.7, bf16[16,16,12,64]{3,2,1,0:T(8,128)(2,1)S(1)} %copy-done.8, bf16[16,16,12,64]{3,2,1,0:T(8,128)(2,1)S(1)} %copy-done.9, bf16[16,16,12,128]{3,1,2,0:T(8,128)(2,1)S(1)} %multiply_convert_fusion), kind=kOutput, calls=%fused_computation.24 | convolution fusion | flops 154533888 | bytes 2064384 | tf_op jit(solution)/shard_map/ijtc,ijtd->cd/dot_general | solution.py:291
  64.4 1.7 %fusion.30 = f32[192,128,1,1]{1,0,3,2:T(8,128)S(1)} fusion(bf16[16,16,12,64]{3,2,1,0:T(8,128)(2,1)S(1)} %copy-done.4, bf16[16,16,12,64]{3,2,1,0:T(8,128)(2,1)S(1)} %copy-done.5, bf16[16,16,12,64]{3,2,1,0:T(8,128)(2,1)S(1)} %copy-done.6, bf16[16,16,12,128]{3,1,2,0:T(8,128)(2,1)S(1)} %multiply_convert_fusion), kind=kOutput, calls=%fused_computation.30 | convolution fusion | flops 154533888 | bytes 2064384 | tf_op jit(solution)/shard_map/ijtc,ijtd->cd/dot_general | solution.py:291
  66.4 3.9 %collective-permute-start.15 = (bf16[16,1,1536]{2,1,0:T(2,128)(2,1)S(1)}, bf16[16,1,1536]{2,1,0:T(2,128)(2,1)S(1)}, u32[]{:S(2)}, u32[]{:S(2)}) collective-permute-start(bf16[16,1,1536]{2,1,0:T(2,128)(2,1)S(1)} %get-tuple-element.41), channel_id=1, source_target_pairs={{1,2},{2,1},{3,4},{4,3},{5,6},{6,5},{9,10},{10,9},{11,12},{12,11},... | collective-permute-start | bytes 147464 | tf_op jit(solution)/shard_map/ppermute | solution.py:61
  70.4 1.4 %collective-permute-start.13 = (f32[160,128]{1,0:T(8,128)S(1)}, f32[160,128]{1,0:T(8,128)S(1)}, u32[]{:S(2)}, u32[]{:S(2)}) collective-permute-start(f32[160,128]{1,0:T(8,128)S(1)} %slice_select_fusion.1), channel_id=1, source_target_pairs={{0,2},{1,3},{2,0},{3,1},{4,6},{5,7},{6,4},{7,5},{8,10},{9,11},{10,... | collective-permute-start | bytes 245768 | tf_op jit(solution)/shard_map/ppermute | solution.py:40
  72.8 1.5 %collective-permute-done.13 = f32[160,128]{1,0:T(8,128)S(1)} collective-permute-done((f32[160,128]{1,0:T(8,128)S(1)}, f32[160,128]{1,0:T(8,128)S(1)}, u32[]{:S(2)}, u32[]{:S(2)}) %collective-permute-start.13) | collective-permute-done | bytes 81952 | tf_op jit(solution)/shard_map/ppermute | solution.py:40
  74.3 2.9 %collective-permute-start.14 = (f32[160,128]{1,0:T(8,128)S(1)}, f32[160,128]{1,0:T(8,128)S(1)}, u32[]{:S(2)}, u32[]{:S(2)}) collective-permute-start(f32[160,128]{1,0:T(8,128)S(1)} %select_add_fusion), channel_id=1, source_target_pairs={{0,4},{1,5},{2,6},{3,7},{4,0},{5,1},{6,2},{7,3},{8,12},{9,13},{10,... | collective-permute-start | bytes 245768 | tf_op jit(solution)/shard_map/ppermute | solution.py:40
  77.3 1.9 %collective-permute-done.14 = f32[160,128]{1,0:T(8,128)S(1)} collective-permute-done((f32[160,128]{1,0:T(8,128)S(1)}, f32[160,128]{1,0:T(8,128)S(1)}, u32[]{:S(2)}, u32[]{:S(2)}) %collective-permute-start.14) | collective-permute-done | bytes 81952 | tf_op jit(solution)/shard_map/ppermute | solution.py:40
  79.2 5.2 %collective-permute-start.16 = (f32[376,128]{1,0:T(8,128)S(1)}, f32[376,128]{1,0:T(8,128)S(1)}, u32[]{:S(2)}, u32[]{:S(2)}) collective-permute-start(f32[376,128]{1,0:T(8,128)S(1)} %pad_maximum_fusion.5), channel_id=1, source_target_pairs={{0,8},{8,0},{16,24},{24,16},{32,40},{40,32},{48,56},{56,48},{64,72... | collective-permute-start | bytes 577544 | tf_op jit(solution)/shard_map/ppermute | solution.py:40
  85.1 2.9 %collective-permute-done.16 = f32[376,128]{1,0:T(8,128)S(1)} collective-permute-done((f32[376,128]{1,0:T(8,128)S(1)}, f32[376,128]{1,0:T(8,128)S(1)}, u32[]{:S(2)}, u32[]{:S(2)}) %collective-permute-start.16) | collective-permute-done | bytes 192544 | tf_op jit(solution)/shard_map/ppermute | solution.py:40
  88.0 2.5 %collective-permute-start.18 = (f32[160,128]{1,0:T(8,128)S(1)}, f32[160,128]{1,0:T(8,128)S(1)}, u32[]{:S(2)}, u32[]{:S(2)}) collective-permute-start(f32[160,128]{1,0:T(8,128)S(1)} %slice_add_fusion.1), channel_id=1, source_target_pairs={{0,16},{8,24},{16,0},{24,8},{32,48},{40,56},{48,32},{56,40},{64,80... | collective-permute-start | bytes 245768 | tf_op jit(solution)/shard_map/ppermute | solution.py:40
  93.1 1.7 %collective-permute-start.19 = (f32[160,128]{1,0:T(8,128)S(1)}, f32[160,128]{1,0:T(8,128)S(1)}, u32[]{:S(2)}, u32[]{:S(2)}) collective-permute-start(f32[160,128]{1,0:T(8,128)S(1)} %add.137), channel_id=1, source_target_pairs={{0,32},{8,40},{16,48},{24,56},{32,0},{40,8},{48,16},{56,24},{64,96... | collective-permute-start | bytes 245768 | tf_op jit(solution)/shard_map/ppermute | solution.py:40
  94.8 2.8 %fusion.94 = (bf16[16,16,12,128]{3,2,1,0:T(8,128)(2,1)S(1)}, bf16[16,16,12,128]{3,2,1,0:T(8,128)(2,1)S(1)}, bf16[16,16,12,128]{3,2,1,0:T(8,128)(2,1)S(1)}, bf16[...) fusion(bf16[18,18,12,128]{3,2,1,0:T(8,128)(2,1)S(1)} %reshape.224), kind=kLoop, calls=%fused_computation.207 | loop fusion | bytes 14155776 | tf_op jit(solution)/shard_map/slice | solution.py:149
  98.3 3.4 %collective-permute-start.20 = (f32[160,128]{1,0:T(8,128)S(1)}, f32[160,128]{1,0:T(8,128)S(1)}, u32[]{:S(2)}, u32[]{:S(2)}) collective-permute-start(f32[160,128]{1,0:T(8,128)S(1)} %add.138), channel_id=1, source_target_pairs={{0,64},{8,72},{16,80},{24,88},{32,96},{40,104},{48,112},{56,120},{... | collective-permute-start | bytes 245768 | tf_op jit(solution)/shard_map/ppermute | solution.py:40
  103.7 2.9 %collective-permute-start.21 = (f32[160,128]{1,0:T(8,128)S(1)}, f32[160,128]{1,0:T(8,128)S(1)}, u32[]{:S(2)}, u32[]{:S(2)}) collective-permute-start(f32[160,128]{1,0:T(8,128)S(1)} %add.139), channel_id=1, source_target_pairs={{0,2},{1,3},{2,0},{3,1},{4,6},{5,7},{6,4},{7,5},{8,10},{9,11},{10,... | collective-permute-start | bytes 245768 | tf_op jit(solution)/shard_map/ppermute | solution.py:40
  108.5 4.5 %collective-permute-start.22 = (f32[320,128]{1,0:T(8,128)S(1)}, f32[320,128]{1,0:T(8,128)S(1)}, u32[]{:S(2)}, u32[]{:S(2)}) collective-permute-start(f32[320,128]{1,0:T(8,128)S(1)} %maximum_select_fusion.3), channel_id=1, source_target_pairs={{0,1},{1,0},{2,3},{3,2},{4,5},{5,4},{6,7},{7,6},{8,9},{9,8},{10,11... | collective-permute-start | bytes 491528 | tf_op jit(solution)/shard_map/ppermute | solution.py:40
  114.1 1.4 %reshape.225 = bf16[16,16,768]{2,1,0:T(8,128)(2,1)} reshape(bf16[16,16,12,64]{3,2,1,0:T(8,128)(2,1)S(1)} %copy.106) | data formatting | bytes 786432 | tf_op jit(solution)/shard_map/reshape | solution.py:317
  (161 shorter events, 29.8 us)
Async XLA Ops:
  0.6 31.3 %copy-start = (bf16[128,20]{0,1:T(8,128)(2,1)S(1)}, bf16[128,20]{0,1:T(8,128)(2,1)}, u32[]{:S(2)}) copy-start(bf16[128,20]{0,1:T(8,128)(2,1)} %param.11) | copy-start | bytes 15364
  0.6 13.0 %copy-start.3 = (bf16[16,16,768]{2,1,0:T(8,128)(2,1)S(1)}, bf16[16,16,768]{2,1,0:T(8,128)(2,1)}, u32[]{:S(2)}) copy-start(bf16[16,16,768]{2,1,0:T(8,128)(2,1)} %param.8) | copy-start | bytes 1179652
  0.7 11.2 %copy-start.14 = (s32[16,16]{1,0:T(8,128)S(1)}, s32[16,16]{1,0:T(8,128)}, u32[]{:S(2)}) copy-start(s32[16,16]{1,0:T(8,128)} %param.12) | copy-start | bytes 3076
  1.5 4.8 %collective-permute-start = (bf16[1,16,768]{2,1,0:T(8,128)(2,1)S(1)}, bf16[1,16,768]{2,1,0:T(8,128)(2,1)S(1)}, u32[]{:S(2)}, u32[]{:S(2)}) collective-permute-start(bf16[1,16,768]{2,1,0:T(8,128)(2,1)S(1)} %get-tuple-element.42), channel_id=1, source_target_pairs={{0,8},{8,0},{16,24},{24,16},{32,40},{40,32},{48,56},{56,48},{64,72... | collective-permute-start | bytes 73736 | tf_op jit(solution)/shard_map/ppermute | solution.py:26
  3.5 2.8 %collective-permute-start.1 = (bf16[1,16,768]{2,1,0:T(8,128)(2,1)S(1)}, bf16[1,16,768]{2,1,0:T(8,128)(2,1)S(1)}, u32[]{:S(2)}, u32[]{:S(2)}) collective-permute-start(bf16[1,16,768]{2,1,0:T(8,128)(2,1)S(1)} %get-tuple-element.43), channel_id=1, source_target_pairs={{8,16},{16,8},{24,32},{32,24},{40,48},{48,40},{56,64},{64,56},{72,... | collective-permute-start | bytes 73736 | tf_op jit(solution)/shard_map/ppermute | solution.py:27
  7.6 5.9 %collective-permute-start.3 = (bf16[18,1,768]{2,1,0:T(2,128)(2,1)S(1)}, bf16[18,1,768]{2,1,0:T(2,128)(2,1)S(1)}, u32[]{:S(2)}, u32[]{:S(2)}) collective-permute-start(bf16[18,1,768]{2,1,0:T(2,128)(2,1)S(1)} %broadcast_select_fusion.6), channel_id=1, source_target_pairs={{1,2},{2,1},{3,4},{4,3},{5,6},{6,5},{9,10},{10,9},{11,12},{12,11},... | collective-permute-start | bytes 82952 | tf_op jit(solution)/shard_map/ppermute | solution.py:27
  11.6 1.8 %collective-permute-start.2 = (bf16[18,1,768]{2,1,0:T(2,128)(2,1)S(1)}, bf16[18,1,768]{2,1,0:T(2,128)(2,1)S(1)}, u32[]{:S(2)}, u32[]{:S(2)}) collective-permute-start(bf16[18,1,768]{2,1,0:T(2,128)(2,1)S(1)} %get-tuple-element.19), channel_id=1, source_target_pairs={{0,1},{1,0},{2,3},{3,2},{4,5},{5,4},{6,7},{7,6},{8,9},{9,8},{10,11... | collective-permute-start | bytes 82952 | tf_op jit(solution)/shard_map/ppermute | solution.py:26
  19.9 12.3 %copy-start.15 = (s32[1,1,32]{2,1,0:T(1,128)S(1)}, s32[1,1,32]{2,1,0:T(1,128)}, u32[]{:S(2)}) copy-start(s32[1,1,32]{2,1,0:T(1,128)} %param.15) | copy-start | bytes 388
  20.2 5.1 %collective-permute-start.4 = (bf16[1,3,32,128]{3,2,1,0:T(8,128)(2,1)S(1)}, bf16[1,3,32,128]{3,2,1,0:T(8,128)(2,1)S(1)}, u32[]{:S(2)}, u32[]{:S(2)}) collective-permute-start(bf16[1,3,32,128]{3,2,1,0:T(8,128)(2,1)S(1)} %bitcast.170), channel_id=1, source_target_pairs={{0,8},{8,0},{16,24},{24,16},{32,40},{40,32},{48,56},{56,48},{64,72... | collective-permute-start | bytes 73736 | tf_op jit(solution)/shard_map/ppermute | solution.py:26
  24.0 1.4 %collective-permute-start.5 = (bf16[1,3,32,128]{3,2,1,0:T(8,128)(2,1)S(1)}, bf16[1,3,32,128]{3,2,1,0:T(8,128)(2,1)S(1)}, u32[]{:S(2)}, u32[]{:S(2)}) collective-permute-start(bf16[1,3,32,128]{3,2,1,0:T(8,128)(2,1)S(1)} %bitcast.169), channel_id=1, source_target_pairs={{8,16},{16,8},{24,32},{32,24},{40,48},{48,40},{56,64},{64,56},{72,... | collective-permute-start | bytes 73736 | tf_op jit(solution)/shard_map/ppermute | solution.py:27
  25.4 4.4 %collective-permute-start.6 = (bf16[5,1,32,128]{3,2,1,0:T(8,128)(2,1)S(1)}, bf16[5,1,32,128]{3,2,1,0:T(8,128)(2,1)S(1)}, u32[]{:S(2)}, u32[]{:S(2)}) collective-permute-start(bf16[5,1,32,128]{3,2,1,0:T(8,128)(2,1)S(1)} %get-tuple-element.57), channel_id=1, source_target_pairs={{0,1},{1,0},{2,3},{3,2},{4,5},{5,4},{6,7},{7,6},{8,9},{9,8},{10,11... | collective-permute-start | bytes 122888 | tf_op jit(solution)/shard_map/ppermute | solution.py:26
  25.9 5.6 %collective-permute-start.7 = (bf16[5,1,32,128]{3,2,1,0:T(8,128)(2,1)S(1)}, bf16[5,1,32,128]{3,2,1,0:T(8,128)(2,1)S(1)}, u32[]{:S(2)}, u32[]{:S(2)}) collective-permute-start(bf16[5,1,32,128]{3,2,1,0:T(8,128)(2,1)S(1)} %get-tuple-element.58), channel_id=1, source_target_pairs={{1,2},{2,1},{3,4},{4,3},{5,6},{6,5},{9,10},{10,9},{11,12},{12,11},... | collective-permute-start | bytes 122888 | tf_op jit(solution)/shard_map/ppermute | solution.py:27
  32.6 10.9 %collective-permute-start.8 = (bf16[1,1,32,128]{3,2,1,0:T(8,128)(2,1)S(1)}, bf16[1,1,32,128]{3,2,1,0:T(8,128)(2,1)S(1)}, u32[]{:S(2)}, u32[]{:S(2)}) collective-permute-start(bf16[1,1,32,128]{3,2,1,0:T(8,128)(2,1)S(1)} %fusion.73), channel_id=1, source_target_pairs={{0,8},{8,0},{16,24},{24,16},{32,40},{40,32},{48,56},{56,48},{64,72... | collective-permute-start | bytes 24584 | tf_op jit(solution)/shard_map/ppermute | solution.py:26
  38.9 4.5 %collective-permute-start.9 = (bf16[1,1,32,128]{3,2,1,0:T(8,128)(2,1)S(1)}, bf16[1,1,32,128]{3,2,1,0:T(8,128)(2,1)S(1)}, u32[]{:S(2)}, u32[]{:S(2)}) collective-permute-start(bf16[1,1,32,128]{3,2,1,0:T(8,128)(2,1)S(1)} %fusion.73), channel_id=1, source_target_pairs={{8,16},{16,8},{24,32},{32,24},{40,48},{48,40},{56,64},{64,56},{72,... | collective-permute-start | bytes 24584 | tf_op jit(solution)/shard_map/ppermute | solution.py:27
  43.4 4.7 %collective-permute-start.10 = (bf16[3,1,32,128]{3,2,1,0:T(8,128)(2,1)S(1)}, bf16[3,1,32,128]{3,2,1,0:T(8,128)(2,1)S(1)}, u32[]{:S(2)}, u32[]{:S(2)}) collective-permute-start(bf16[3,1,32,128]{3,2,1,0:T(8,128)(2,1)S(1)} %pad_maximum_fusion.18), channel_id=1, source_target_pairs={{0,1},{1,0},{2,3},{3,2},{4,5},{5,4},{6,7},{7,6},{8,9},{9,8},{10,11... | collective-permute-start | bytes 73736 | tf_op jit(solution)/shard_map/ppermute | solution.py:26
  43.5 5.5 %collective-permute-start.11 = (bf16[3,1,32,128]{3,2,1,0:T(8,128)(2,1)S(1)}, bf16[3,1,32,128]{3,2,1,0:T(8,128)(2,1)S(1)}, u32[]{:S(2)}, u32[]{:S(2)}) collective-permute-start(bf16[3,1,32,128]{3,2,1,0:T(8,128)(2,1)S(1)} %pad_maximum_fusion.18), channel_id=1, source_target_pairs={{1,2},{2,1},{3,4},{4,3},{5,6},{6,5},{9,10},{10,9},{11,12},{12,11},... | collective-permute-start | bytes 73736 | tf_op jit(solution)/shard_map/ppermute | solution.py:27
  54.2 2.2 %copy-start.2 = (f32[16,16,12,128]{3,2,1,0:T(8,128)S(1)}, f32[16,16,12,128]{3,2,1,0:T(8,128)}, u32[]{:S(2)}) copy-start(f32[16,16,12,128]{3,2,1,0:T(8,128)} %copy-done.1) | copy-start | bytes 4718596
  56.4 3.3 %copy-start.11 = (bf16[16,16,12,64]{3,2,1,0:T(8,128)(2,1)S(1)}, bf16[16,16,12,64]{3,2,1,0:T(8,128)(2,1)}, u32[]{:S(2)}) copy-start(bf16[16,16,12,64]{3,2,1,0:T(8,128)(2,1)} %get-tuple-element.38) | copy-start | bytes 1179652
  56.4 3.3 %copy-start.12 = (bf16[16,16,12,64]{3,2,1,0:T(8,128)(2,1)S(1)}, bf16[16,16,12,64]{3,2,1,0:T(8,128)(2,1)}, u32[]{:S(2)}) copy-start(bf16[16,16,12,64]{3,2,1,0:T(8,128)(2,1)} %get-tuple-element.39) | copy-start | bytes 1179652
  60.6 1.9 %copy-start.9 = (bf16[16,16,12,64]{3,2,1,0:T(8,128)(2,1)S(1)}, bf16[16,16,12,64]{3,2,1,0:T(8,128)(2,1)}, u32[]{:S(2)}) copy-start(bf16[16,16,12,64]{3,2,1,0:T(8,128)(2,1)} %get-tuple-element.37) | copy-start | bytes 1179652
  62.5 1.9 %copy-start.6 = (bf16[16,16,12,64]{3,2,1,0:T(8,128)(2,1)S(1)}, bf16[16,16,12,64]{3,2,1,0:T(8,128)(2,1)}, u32[]{:S(2)}) copy-start(bf16[16,16,12,64]{3,2,1,0:T(8,128)(2,1)} %get-tuple-element.34) | copy-start | bytes 1179652
  66.2 4.1 %collective-permute-start.12 = (f32[512,128]{1,0:T(8,128)S(1)}, f32[512,128]{1,0:T(8,128)S(1)}, u32[]{:S(2)}, u32[]{:S(2)}) collective-permute-start(f32[512,128]{1,0:T(8,128)S(1)} %pad_maximum_fusion.3), channel_id=1, source_target_pairs={{0,1},{1,0},{2,3},{3,2},{4,5},{5,4},{6,7},{7,6},{8,9},{9,8},{10,11... | collective-permute-start | bytes 786440 | tf_op jit(solution)/shard_map/ppermute | solution.py:40
  66.4 6.2 %collective-permute-start.15 = (bf16[16,1,1536]{2,1,0:T(2,128)(2,1)S(1)}, bf16[16,1,1536]{2,1,0:T(2,128)(2,1)S(1)}, u32[]{:S(2)}, u32[]{:S(2)}) collective-permute-start(bf16[16,1,1536]{2,1,0:T(2,128)(2,1)S(1)} %get-tuple-element.41), channel_id=1, source_target_pairs={{1,2},{2,1},{3,4},{4,3},{5,6},{6,5},{9,10},{10,9},{11,12},{12,11},... | collective-permute-start | bytes 147464 | tf_op jit(solution)/shard_map/ppermute | solution.py:61
  70.4 3.9 %collective-permute-start.13 = (f32[160,128]{1,0:T(8,128)S(1)}, f32[160,128]{1,0:T(8,128)S(1)}, u32[]{:S(2)}, u32[]{:S(2)}) collective-permute-start(f32[160,128]{1,0:T(8,128)S(1)} %slice_select_fusion.1), channel_id=1, source_target_pairs={{0,2},{1,3},{2,0},{3,1},{4,6},{5,7},{6,4},{7,5},{8,10},{9,11},{10,... | collective-permute-start | bytes 245768 | tf_op jit(solution)/shard_map/ppermute | solution.py:40
  74.3 4.9 %collective-permute-start.14 = (f32[160,128]{1,0:T(8,128)S(1)}, f32[160,128]{1,0:T(8,128)S(1)}, u32[]{:S(2)}, u32[]{:S(2)}) collective-permute-start(f32[160,128]{1,0:T(8,128)S(1)} %select_add_fusion), channel_id=1, source_target_pairs={{0,4},{1,5},{2,6},{3,7},{4,0},{5,1},{6,2},{7,3},{8,12},{9,13},{10,... | collective-permute-start | bytes 245768 | tf_op jit(solution)/shard_map/ppermute | solution.py:40
  79.2 8.8 %collective-permute-start.16 = (f32[376,128]{1,0:T(8,128)S(1)}, f32[376,128]{1,0:T(8,128)S(1)}, u32[]{:S(2)}, u32[]{:S(2)}) collective-permute-start(f32[376,128]{1,0:T(8,128)S(1)} %pad_maximum_fusion.5), channel_id=1, source_target_pairs={{0,8},{8,0},{16,24},{24,16},{32,40},{40,32},{48,56},{56,48},{64,72... | collective-permute-start | bytes 577544 | tf_op jit(solution)/shard_map/ppermute | solution.py:40
  84.4 6.2 %collective-permute-start.17 = (bf16[1,18,1536]{2,1,0:T(8,128)(2,1)S(1)}, bf16[1,18,1536]{2,1,0:T(8,128)(2,1)S(1)}, u32[]{:S(2)}, u32[]{:S(2)}) collective-permute-start(bf16[1,18,1536]{2,1,0:T(8,128)(2,1)S(1)} %broadcast_select_fusion.11), channel_id=1, source_target_pairs={{8,16},{16,8},{24,32},{32,24},{40,48},{48,40},{56,64},{64,56},{72,... | collective-permute-start | bytes 165896 | tf_op jit(solution)/shard_map/ppermute | solution.py:61
  88.0 5.1 %collective-permute-start.18 = (f32[160,128]{1,0:T(8,128)S(1)}, f32[160,128]{1,0:T(8,128)S(1)}, u32[]{:S(2)}, u32[]{:S(2)}) collective-permute-start(f32[160,128]{1,0:T(8,128)S(1)} %slice_add_fusion.1), channel_id=1, source_target_pairs={{0,16},{8,24},{16,0},{24,8},{32,48},{40,56},{48,32},{56,40},{64,80... | collective-permute-start | bytes 245768 | tf_op jit(solution)/shard_map/ppermute | solution.py:40
  93.1 5.1 %collective-permute-start.19 = (f32[160,128]{1,0:T(8,128)S(1)}, f32[160,128]{1,0:T(8,128)S(1)}, u32[]{:S(2)}, u32[]{:S(2)}) collective-permute-start(f32[160,128]{1,0:T(8,128)S(1)} %add.137), channel_id=1, source_target_pairs={{0,32},{8,40},{16,48},{24,56},{32,0},{40,8},{48,16},{56,24},{64,96... | collective-permute-start | bytes 245768 | tf_op jit(solution)/shard_map/ppermute | solution.py:40
  98.3 5.4 %collective-permute-start.20 = (f32[160,128]{1,0:T(8,128)S(1)}, f32[160,128]{1,0:T(8,128)S(1)}, u32[]{:S(2)}, u32[]{:S(2)}) collective-permute-start(f32[160,128]{1,0:T(8,128)S(1)} %add.138), channel_id=1, source_target_pairs={{0,64},{8,72},{16,80},{24,88},{32,96},{40,104},{48,112},{56,120},{... | collective-permute-start | bytes 245768 | tf_op jit(solution)/shard_map/ppermute | solution.py:40
  103.7 4.7 %collective-permute-start.21 = (f32[160,128]{1,0:T(8,128)S(1)}, f32[160,128]{1,0:T(8,128)S(1)}, u32[]{:S(2)}, u32[]{:S(2)}) collective-permute-start(f32[160,128]{1,0:T(8,128)S(1)} %add.139), channel_id=1, source_target_pairs={{0,2},{1,3},{2,0},{3,1},{4,6},{5,7},{6,4},{7,5},{8,10},{9,11},{10,... | collective-permute-start | bytes 245768 | tf_op jit(solution)/shard_map/ppermute | solution.py:40
  108.5 7.0 %collective-permute-start.22 = (f32[320,128]{1,0:T(8,128)S(1)}, f32[320,128]{1,0:T(8,128)S(1)}, u32[]{:S(2)}, u32[]{:S(2)}) collective-permute-start(f32[320,128]{1,0:T(8,128)S(1)} %maximum_select_fusion.3), channel_id=1, source_target_pairs={{0,1},{1,0},{2,3},{3,2},{4,5},{5,4},{6,7},{7,6},{8,9},{9,8},{10,11... | collective-permute-start | bytes 491528 | tf_op jit(solution)/shard_map/ppermute | solution.py:40
  (7 other events, 10.5 us)

commit v9 on v8

--- a/solution.py
+++ b/solution.py
@@ -278,21 +278,14 @@
         )
         grad_hidden = tap_term if grad_hidden is None else grad_hidden + tap_term
     grad_pre = (grad_hidden * silu_slope(pre_act)).astype(jnp.bfloat16)
-    conv_rows = []
-    for row_tap in range(3):
-        tap_patch = jnp.concatenate(
-            [
-                padded_pixels[row_tap : row_tap + tile_rows, col_tap : col_tap + tile_cols]
-                for col_tap in range(3)
-            ],
-            axis=-1,
-        )
-        conv_rows.append(
-            jnp.einsum(
-                "ijtc,ijtd->cd", tap_patch, grad_pre, preferred_element_type=jnp.float32
-            ).reshape(3, C_IN, C_OUT)
-        )
-    conv_term = jnp.stack(conv_rows)
+    conv_term = lax.conv_general_dilated(
+        padded_pixels,
+        grad_pre,
+        window_strides=(1, 1),
+        padding="VALID",
+        dimension_numbers=("HWCN", "HWIO", "HWNC"),
+        preferred_element_type=jnp.float32,
+    )
     lanes = C_OUT
     conv_rows, time_rows, class_rows = (
         conv_term.size // lanes,

time: 118 us -> 111 us (0.941)
  matrix products: 20.5 us -> 12.6 us
  starting transfers between devices: 56 us -> 59.8 us
  local copies, waits for them, and re-layouts: 17.8 us -> 16 us
  other arithmetic: 8.11 us -> 6.67 us
    dot_general x3 -> x0, matrix products: 5.04 us -> none  [per_device(): jnp.einsum('ijtc,ijtd->cd', tap_patch, grad_pre, preferred_element_type=j...]
    dot_general x3, matrix products: 6.06 us -> 1.73 us  [per_device(): jnp.dot(padded_mixed[:, :, 2 - time_tap:2 - time_tap + DATES], dense_time...]
    slice x1 -> x0, local copies, waits for them, and re-layouts: 3.83 us -> none  [per_device(): padded_pixels[row_tap:row_tap + tile_rows, col_tap:col_tap + tile_cols]]
    ppermute x9, starting transfers between devices: 24.5 us -> 28 us  [exchange(): return lax.ppermute(value, axis, [(i, i ^ bit) for i in range(size)])]
    conv_general_dilated x0 -> x1, matrix products: none -> 2.6 us  [per_device(): lax.conv_general_dilated(padded_pixels, grad_pre, window_strides=(1, 1),...]
    unnamed x44 -> x30, local copies, waits for them, and re-layouts: 6.04 us -> 8.06 us
    convert_element_type x1, other arithmetic: 2.01 us -> 0.59 us  [per_device(): ((pixel_grad / DATES)[:, :, None, :] * silu_slope(mixed_time)).astype(jnp...]
  transfers between devices with their start and end apart: 23 -> 23, of which waited for: 11 -> 12; matrix products, arithmetic and copies ran while one was open for 14% -> 12% of each run, Pallas kernels for 0% -> 0%
where the time goes in v9:
time: 111 us
  starting transfers between devices  59.8 us (54%)
  local copies, waits for them, and re-layouts  16 us (14%)
  waiting for transfers between devices  14.4 us (13%)
  matrix products  12.6 us (11%)
  other arithmetic  6.67 us (6%)
  between operations  1.47 us (1%)
    ppermute x9, starting transfers between devices, exchange(): return lax.ppermute(value, axis, [(i, i ^ bit) for i in range(size)])  28 us
    ppermute x6, starting transfers between devices, with_halo(): lax.ppermute(jnp.where(odd, tail, head), axis, [pair for k in range(1, co...  13.8 us
    ppermute x6, starting transfers between devices, with_halo(): lax.ppermute(jnp.where(odd, head, tail), axis, [(i, i ^ 1) for i in range...  13.2 us
    ppermute x9, waiting for transfers between devices, exchange(): return lax.ppermute(value, axis, [(i, i ^ bit) for i in range(size)])  8.14 us
    unnamed x30, local copies, waits for them, and re-layouts  8.06 us
    ppermute x6, waiting for transfers between devices, with_halo(): lax.ppermute(jnp.where(odd, tail, head), axis, [pair for k in range(1, co...  4.74 us
    ppermute x2, starting transfers between devices, outer_swap(): lax.ppermute(piece, axis, [pair for k in range(1, count - 1, 2) for pair...  4.72 us
    slice x1, local copies, waits for them, and re-layouts, transposed_conv(): padded_grad[2 - row_tap:2 - row_tap + out_rows, 2 - col_tap:2 - col_tap +...  2.81 us
  transfers between devices with their start and end apart: 23, of which 12 were waited for; matrix products, arithmetic and copies ran while one was open for 12% of the time, Pallas kernels for 0%

profile of v9, /device:TPU:1, one launch (start us, length us, event | category | flops | bytes accessed | tf_op | source)
XLA Modules:
  0.0 110.9 jit_solution(11074800374247551949)
XLA Ops:
  1.5 2.0 %collective-permute-start = (bf16[1,16,768]{2,1,0:T(8,128)(2,1)S(1)}, bf16[1,16,768]{2,1,0:T(8,128)(2,1)S(1)}, u32[]{:S(2)}, u32[]{:S(2)}) collective-permute-start(bf16[1,16,768]{2,1,0:T(8,128)(2,1)S(1)} %get-tuple-element.33), channel_id=1, source_target_pairs={{0,8},{8,0},{16,24},{24,16},{32,40},{40,32},{48,56},{56,48},{64,72... | collective-permute-start | bytes 73736 | tf_op jit(solution)/shard_map/ppermute | solution.py:26
  4.2 0.9 copy.68
  6.3 1.1 %broadcast_select_fusion.7 = (bf16[18,1,768]{2,1,0:T(2,128)(2,1)S(1)}, bf16[18,1,768]{2,1,0:T(2,128)(2,1)S(1)}, bf16[18,1,768]{2,1,0:T(2,128)(2,1)S(1)}) fusion(pred[]{:T(512)S(6)} %eq.104, bf16[1,16,768]{2,1,0:T(8,128)(2,1)S(1)} %get-tuple-element.61, bf16[16,16,768]{2,1,0:T(8,128)(2,1)} %param.8, bf16[1,16,768]{2,1,0:T(8,128)(2,1)S(1)} %get-tuple-element.60), kind=kLoop, calls=%fused_computation.66 | loop fusion | flops 179712 | bytes 525313 | tf_op jit(solution)/shard_map/jit(_where)/select_n | solution.py:26
  7.4 1.0 collective-permute-start.2
  8.5 3.1 %collective-permute-start.3 = (bf16[18,1,768]{2,1,0:T(2,128)(2,1)S(1)}, bf16[18,1,768]{2,1,0:T(2,128)(2,1)S(1)}, u32[]{:S(2)}, u32[]{:S(2)}) collective-permute-start(bf16[18,1,768]{2,1,0:T(2,128)(2,1)S(1)} %broadcast_select_fusion.6), channel_id=1, source_target_pairs={{1,2},{2,1},{3,4},{4,3},{5,6},{6,5},{9,10},{10,9},{11,12},{12,11},... | collective-permute-start | bytes 82952 | tf_op jit(solution)/shard_map/ppermute | solution.py:27
  11.8 2.2 %collective-permute-done.3 = bf16[18,1,768]{2,1,0:T(2,128)(2,1)S(1)} collective-permute-done((bf16[18,1,768]{2,1,0:T(2,128)(2,1)S(1)}, bf16[18,1,768]{2,1,0:T(2,128)(2,1)S(1)}, u32[]{:S(2)}, u32[]{:S(2)}) %collective-permute-start.3) | collective-permute-done | bytes 27680 | tf_op jit(solution)/shard_map/ppermute | solution.py:27
  15.3 1.1 copy-done.4
  16.4 1.6 %fusion.74 = f32[16,16,12,128]{3,2,1,0:T(8,128)S(1)} fusion(bf16[18,18,12,64]{3,2,1,0:T(8,128)(2,1)S(1)} %reshape.214, bf16[3,3,64,128]{3,2,1,0:T(8,128)(2,1)S(1)} %copy-done.6), kind=kOutput, calls=%fused_computation.186 | convolution fusion | flops 452984832 | bytes 2217984 | tf_op jit(solution)/shard_map/conv_general_dilated | solution.py:134
  20.8 3.7 %collective-permute-start.4 = (bf16[1,3,32,128]{3,2,1,0:T(8,128)(2,1)S(1)}, bf16[1,3,32,128]{3,2,1,0:T(8,128)(2,1)S(1)}, u32[]{:S(2)}, u32[]{:S(2)}) collective-permute-start(bf16[1,3,32,128]{3,2,1,0:T(8,128)(2,1)S(1)} %bitcast.153), channel_id=1, source_target_pairs={{0,8},{8,0},{16,24},{24,16},{32,40},{40,32},{48,56},{56,48},{64,72... | collective-permute-start | bytes 73736 | tf_op jit(solution)/shard_map/ppermute | solution.py:26
  25.9 4.0 %collective-permute-start.7 = (bf16[5,1,32,128]{3,2,1,0:T(8,128)(2,1)S(1)}, bf16[5,1,32,128]{3,2,1,0:T(8,128)(2,1)S(1)}, u32[]{:S(2)}, u32[]{:S(2)}) collective-permute-start(bf16[5,1,32,128]{3,2,1,0:T(8,128)(2,1)S(1)} %get-tuple-element.49), channel_id=1, source_target_pairs={{1,2},{2,1},{3,4},{4,3},{5,6},{6,5},{9,10},{10,9},{11,12},{12,11},... | collective-permute-start | bytes 122888 | tf_op jit(solution)/shard_map/ppermute | solution.py:27
  29.9 1.6 %collective-permute-done.7 = bf16[5,1,32,128]{3,2,1,0:T(8,128)(2,1)S(1)} collective-permute-done((bf16[5,1,32,128]{3,2,1,0:T(8,128)(2,1)S(1)}, bf16[5,1,32,128]{3,2,1,0:T(8,128)(2,1)S(1)}, u32[]{:S(2)}, u32[]{:S(2)}) %collective-permute-start.7) | collective-permute-done | bytes 40992 | tf_op jit(solution)/shard_map/ppermute | solution.py:27
  32.6 6.3 %collective-permute-start.8 = (bf16[1,1,32,128]{3,2,1,0:T(8,128)(2,1)S(1)}, bf16[1,1,32,128]{3,2,1,0:T(8,128)(2,1)S(1)}, u32[]{:S(2)}, u32[]{:S(2)}) collective-permute-start(bf16[1,1,32,128]{3,2,1,0:T(8,128)(2,1)S(1)} %fusion.54), channel_id=1, source_target_pairs={{0,8},{8,0},{16,24},{24,16},{32,40},{40,32},{48,56},{56,48},{64,72... | collective-permute-start | bytes 24584 | tf_op jit(solution)/shard_map/ppermute | solution.py:26
  40.1 4.7 %collective-permute-start.11 = (bf16[3,1,32,128]{3,2,1,0:T(8,128)(2,1)S(1)}, bf16[3,1,32,128]{3,2,1,0:T(8,128)(2,1)S(1)}, u32[]{:S(2)}, u32[]{:S(2)}) collective-permute-start(bf16[3,1,32,128]{3,2,1,0:T(8,128)(2,1)S(1)} %pad_maximum_fusion.17), channel_id=1, source_target_pairs={{1,2},{2,1},{3,4},{4,3},{5,6},{6,5},{9,10},{10,9},{11,12},{12,11},... | collective-permute-start | bytes 73736 | tf_op jit(solution)/shard_map/ppermute | solution.py:27
  45.2 0.9 collective-permute-done.11
  47.8 1.2 %copy-done.2 = f32[16,16,12,128]{3,2,1,0:T(8,128)S(1)} copy-done((f32[16,16,12,128]{3,2,1,0:T(8,128)S(1)}, f32[16,16,12,128]{3,2,1,0:T(8,128)}, u32[]{:S(2)}) %copy-start.2) | copy-done | bytes 1572888
  49.0 1.0 multiply_convert_fusion
  50.1 1.3 %copy-done.5 = bf16[18,18,12,64]{3,2,1,0:T(8,128)(2,1)S(1)} copy-done((bf16[18,18,12,64]{3,2,1,0:T(8,128)(2,1)S(1)}, bf16[18,18,12,64]{3,2,1,0:T(8,128)(2,1)}, u32[]{:S(2)}) %copy-start.5) | copy-done | bytes 497688
  51.4 2.6 %fusion.20 = f32[3,3,64,128]{3,2,1,0:T(8,128)S(1)} fusion(bf16[18,18,12,64]{3,2,1,0:T(8,128)(2,1)S(1)} %copy-done.5, bf16[16,16,12,128]{3,1,2,0:T(8,128)(2,1)S(1)} %multiply_convert_fusion), kind=kOutput, calls=%fused_computation.34 | convolution fusion | flops 452984832 | bytes 1579008 | tf_op jit(solution)/shard_map/conv_general_dilated | solution.py:281
  56.1 4.1 %collective-permute-start.15 = (bf16[16,1,1536]{2,1,0:T(2,128)(2,1)S(1)}, bf16[16,1,1536]{2,1,0:T(2,128)(2,1)S(1)}, u32[]{:S(2)}, u32[]{:S(2)}) collective-permute-start(bf16[16,1,1536]{2,1,0:T(2,128)(2,1)S(1)} %get-tuple-element.32), channel_id=1, source_target_pairs={{1,2},{2,1},{3,4},{4,3},{5,6},{6,5},{9,10},{10,9},{11,12},{12,11},... | collective-permute-start | bytes 147464 | tf_op jit(solution)/shard_map/ppermute | solution.py:61
  60.4 1.4 %collective-permute-start.13 = (f32[160,128]{1,0:T(8,128)S(1)}, f32[160,128]{1,0:T(8,128)S(1)}, u32[]{:S(2)}, u32[]{:S(2)}) collective-permute-start(f32[160,128]{1,0:T(8,128)S(1)} %slice_select_fusion.1), channel_id=1, source_target_pairs={{0,2},{1,3},{2,0},{3,1},{4,6},{5,7},{6,4},{7,5},{8,10},{9,11},{10,... | collective-permute-start | bytes 245768 | tf_op jit(solution)/shard_map/ppermute | solution.py:40
  62.7 1.5 %collective-permute-done.13 = f32[160,128]{1,0:T(8,128)S(1)} collective-permute-done((f32[160,128]{1,0:T(8,128)S(1)}, f32[160,128]{1,0:T(8,128)S(1)}, u32[]{:S(2)}, u32[]{:S(2)}) %collective-permute-start.13) | collective-permute-done | bytes 81952 | tf_op jit(solution)/shard_map/ppermute | solution.py:40
  64.2 3.0 %collective-permute-start.14 = (f32[160,128]{1,0:T(8,128)S(1)}, f32[160,128]{1,0:T(8,128)S(1)}, u32[]{:S(2)}, u32[]{:S(2)}) collective-permute-start(f32[160,128]{1,0:T(8,128)S(1)} %select_add_fusion), channel_id=1, source_target_pairs={{0,4},{1,5},{2,6},{3,7},{4,0},{5,1},{6,2},{7,3},{8,12},{9,13},{10,... | collective-permute-start | bytes 245768 | tf_op jit(solution)/shard_map/ppermute | solution.py:40
  67.3 1.8 %collective-permute-done.14 = f32[160,128]{1,0:T(8,128)S(1)} collective-permute-done((f32[160,128]{1,0:T(8,128)S(1)}, f32[160,128]{1,0:T(8,128)S(1)}, u32[]{:S(2)}, u32[]{:S(2)}) %collective-permute-start.14) | collective-permute-done | bytes 81952 | tf_op jit(solution)/shard_map/ppermute | solution.py:40
  69.1 5.8 %collective-permute-start.16 = (f32[376,128]{1,0:T(8,128)S(1)}, f32[376,128]{1,0:T(8,128)S(1)}, u32[]{:S(2)}, u32[]{:S(2)}) collective-permute-start(f32[376,128]{1,0:T(8,128)S(1)} %pad_maximum_fusion.4), channel_id=1, source_target_pairs={{0,8},{8,0},{16,24},{24,16},{32,40},{40,32},{48,56},{56,48},{64,72... | collective-permute-start | bytes 577544 | tf_op jit(solution)/shard_map/ppermute | solution.py:40
  75.7 2.9 %collective-permute-done.16 = f32[376,128]{1,0:T(8,128)S(1)} collective-permute-done((f32[376,128]{1,0:T(8,128)S(1)}, f32[376,128]{1,0:T(8,128)S(1)}, u32[]{:S(2)}, u32[]{:S(2)}) %collective-permute-start.16) | collective-permute-done | bytes 192544 | tf_op jit(solution)/shard_map/ppermute | solution.py:40
  78.7 4.0 %collective-permute-start.18 = (f32[160,128]{1,0:T(8,128)S(1)}, f32[160,128]{1,0:T(8,128)S(1)}, u32[]{:S(2)}, u32[]{:S(2)}) collective-permute-start(f32[160,128]{1,0:T(8,128)S(1)} %slice_add_fusion.1), channel_id=1, source_target_pairs={{0,16},{8,24},{16,0},{24,8},{32,48},{40,56},{48,32},{56,40},{64,80... | collective-permute-start | bytes 245768 | tf_op jit(solution)/shard_map/ppermute | solution.py:40
  84.9 2.4 %collective-permute-start.19 = (f32[160,128]{1,0:T(8,128)S(1)}, f32[160,128]{1,0:T(8,128)S(1)}, u32[]{:S(2)}, u32[]{:S(2)}) collective-permute-start(f32[160,128]{1,0:T(8,128)S(1)} %add.137), channel_id=1, source_target_pairs={{0,32},{8,40},{16,48},{24,56},{32,0},{40,8},{48,16},{56,24},{64,96... | collective-permute-start | bytes 245768 | tf_op jit(solution)/shard_map/ppermute | solution.py:40
  87.2 2.8 %fusion.72 = (bf16[16,16,12,128]{3,2,1,0:T(8,128)(2,1)S(1)}, bf16[16,16,12,128]{3,2,1,0:T(8,128)(2,1)S(1)}, bf16[16,16,12,128]{3,2,1,0:T(8,128)(2,1)S(1)}, bf16[...) fusion(bf16[18,18,12,128]{3,2,1,0:T(8,128)(2,1)S(1)} %reshape.224), kind=kLoop, calls=%fused_computation.184 | loop fusion | bytes 14155776 | tf_op jit(solution)/shard_map/slice | solution.py:149
  90.7 3.8 %collective-permute-start.20 = (f32[160,128]{1,0:T(8,128)S(1)}, f32[160,128]{1,0:T(8,128)S(1)}, u32[]{:S(2)}, u32[]{:S(2)}) collective-permute-start(f32[160,128]{1,0:T(8,128)S(1)} %add.138), channel_id=1, source_target_pairs={{0,64},{8,72},{16,80},{24,88},{32,96},{40,104},{48,112},{56,120},{... | collective-permute-start | bytes 245768 | tf_op jit(solution)/shard_map/ppermute | solution.py:40
  96.6 2.7 %collective-permute-start.21 = (f32[160,128]{1,0:T(8,128)S(1)}, f32[160,128]{1,0:T(8,128)S(1)}, u32[]{:S(2)}, u32[]{:S(2)}) collective-permute-start(f32[160,128]{1,0:T(8,128)S(1)} %add.139), channel_id=1, source_target_pairs={{0,2},{1,3},{2,0},{3,1},{4,6},{5,7},{6,4},{7,5},{8,10},{9,11},{10,... | collective-permute-start | bytes 245768 | tf_op jit(solution)/shard_map/ppermute | solution.py:40
  101.1 4.9 %collective-permute-start.22 = (f32[320,128]{1,0:T(8,128)S(1)}, f32[320,128]{1,0:T(8,128)S(1)}, u32[]{:S(2)}, u32[]{:S(2)}) collective-permute-start(f32[320,128]{1,0:T(8,128)S(1)} %maximum_select_fusion.3), channel_id=1, source_target_pairs={{0,1},{1,0},{2,3},{3,2},{4,5},{5,4},{6,7},{7,6},{8,9},{9,8},{10,11... | collective-permute-start | bytes 491528 | tf_op jit(solution)/shard_map/ppermute | solution.py:40
  107.1 1.4 %reshape.225 = bf16[16,16,768]{2,1,0:T(8,128)(2,1)} reshape(bf16[16,16,12,64]{3,2,1,0:T(8,128)(2,1)S(1)} %copy.92) | data formatting | bytes 786432 | tf_op jit(solution)/shard_map/reshape | solution.py:310
  (143 shorter events, 26.6 us)
Async XLA Ops:
  0.6 31.3 %copy-start = (bf16[128,20]{0,1:T(8,128)(2,1)S(1)}, bf16[128,20]{0,1:T(8,128)(2,1)}, u32[]{:S(2)}) copy-start(bf16[128,20]{0,1:T(8,128)(2,1)} %param.11) | copy-start | bytes 15364
  0.6 13.5 %copy-start.3 = (bf16[16,16,768]{2,1,0:T(8,128)(2,1)S(1)}, bf16[16,16,768]{2,1,0:T(8,128)(2,1)}, u32[]{:S(2)}) copy-start(bf16[16,16,768]{2,1,0:T(8,128)(2,1)} %param.8) | copy-start | bytes 1179652
  0.7 11.1 %copy-start.7 = (s32[16,16]{1,0:T(8,128)S(1)}, s32[16,16]{1,0:T(8,128)}, u32[]{:S(2)}) copy-start(s32[16,16]{1,0:T(8,128)} %param.12) | copy-start | bytes 3076
  1.5 4.8 %collective-permute-start = (bf16[1,16,768]{2,1,0:T(8,128)(2,1)S(1)}, bf16[1,16,768]{2,1,0:T(8,128)(2,1)S(1)}, u32[]{:S(2)}, u32[]{:S(2)}) collective-permute-start(bf16[1,16,768]{2,1,0:T(8,128)(2,1)S(1)} %get-tuple-element.33), channel_id=1, source_target_pairs={{0,8},{8,0},{16,24},{24,16},{32,40},{40,32},{48,56},{56,48},{64,72... | collective-permute-start | bytes 73736 | tf_op jit(solution)/shard_map/ppermute | solution.py:26
  3.5 2.7 %collective-permute-start.1 = (bf16[1,16,768]{2,1,0:T(8,128)(2,1)S(1)}, bf16[1,16,768]{2,1,0:T(8,128)(2,1)S(1)}, u32[]{:S(2)}, u32[]{:S(2)}) collective-permute-start(bf16[1,16,768]{2,1,0:T(8,128)(2,1)S(1)} %get-tuple-element.34), channel_id=1, source_target_pairs={{8,16},{16,8},{24,32},{32,24},{40,48},{48,40},{56,64},{64,56},{72,... | collective-permute-start | bytes 73736 | tf_op jit(solution)/shard_map/ppermute | solution.py:27
  7.4 4.4 %collective-permute-start.2 = (bf16[18,1,768]{2,1,0:T(2,128)(2,1)S(1)}, bf16[18,1,768]{2,1,0:T(2,128)(2,1)S(1)}, u32[]{:S(2)}, u32[]{:S(2)}) collective-permute-start(bf16[18,1,768]{2,1,0:T(2,128)(2,1)S(1)} %get-tuple-element.19), channel_id=1, source_target_pairs={{0,1},{1,0},{2,3},{3,2},{4,5},{5,4},{6,7},{7,6},{8,9},{9,8},{10,11... | collective-permute-start | bytes 82952 | tf_op jit(solution)/shard_map/ppermute | solution.py:26
  8.5 5.5 %collective-permute-start.3 = (bf16[18,1,768]{2,1,0:T(2,128)(2,1)S(1)}, bf16[18,1,768]{2,1,0:T(2,128)(2,1)S(1)}, u32[]{:S(2)}, u32[]{:S(2)}) collective-permute-start(bf16[18,1,768]{2,1,0:T(2,128)(2,1)S(1)} %broadcast_select_fusion.6), channel_id=1, source_target_pairs={{1,2},{2,1},{3,4},{4,3},{5,6},{6,5},{9,10},{10,9},{11,12},{12,11},... | collective-permute-start | bytes 82952 | tf_op jit(solution)/shard_map/ppermute | solution.py:27
  14.2 2.2 %copy-start.6 = (bf16[3,3,64,128]{3,2,1,0:T(8,128)(2,1)S(1)}, bf16[3,3,64,128]{3,2,1,0:T(8,128)(2,1)}, u32[]{:S(2)}) copy-start(bf16[3,3,64,128]{3,2,1,0:T(8,128)(2,1)} %param.9) | copy-start | bytes 442372
  15.3 1.1 copy-start.4
  18.0 1.4 %copy-start.1 = (f32[16,16,12,128]{3,2,1,0:T(8,128)}, f32[16,16,12,128]{3,2,1,0:T(8,128)S(1)}, u32[]{:S(2)}) copy-start(f32[16,16,12,128]{3,2,1,0:T(8,128)S(1)} %fusion.74) | copy-start | bytes 4718596
  20.4 11.8 %copy-start.8 = (s32[1,1,32]{2,1,0:T(1,128)S(1)}, s32[1,1,32]{2,1,0:T(1,128)}, u32[]{:S(2)}) copy-start(s32[1,1,32]{2,1,0:T(1,128)} %param.15) | copy-start | bytes 388
  20.8 5.0 %collective-permute-start.4 = (bf16[1,3,32,128]{3,2,1,0:T(8,128)(2,1)S(1)}, bf16[1,3,32,128]{3,2,1,0:T(8,128)(2,1)S(1)}, u32[]{:S(2)}, u32[]{:S(2)}) collective-permute-start(bf16[1,3,32,128]{3,2,1,0:T(8,128)(2,1)S(1)} %bitcast.153), channel_id=1, source_target_pairs={{0,8},{8,0},{16,24},{24,16},{32,40},{40,32},{48,56},{56,48},{64,72... | collective-permute-start | bytes 73736 | tf_op jit(solution)/shard_map/ppermute | solution.py:26
  24.5 1.2 %collective-permute-start.5 = (bf16[1,3,32,128]{3,2,1,0:T(8,128)(2,1)S(1)}, bf16[1,3,32,128]{3,2,1,0:T(8,128)(2,1)S(1)}, u32[]{:S(2)}, u32[]{:S(2)}) collective-permute-start(bf16[1,3,32,128]{3,2,1,0:T(8,128)(2,1)S(1)} %bitcast.152), channel_id=1, source_target_pairs={{8,16},{16,8},{24,32},{32,24},{40,48},{48,40},{56,64},{64,56},{72,... | collective-permute-start | bytes 73736 | tf_op jit(solution)/shard_map/ppermute | solution.py:27
  25.8 4.2 %collective-permute-start.6 = (bf16[5,1,32,128]{3,2,1,0:T(8,128)(2,1)S(1)}, bf16[5,1,32,128]{3,2,1,0:T(8,128)(2,1)S(1)}, u32[]{:S(2)}, u32[]{:S(2)}) collective-permute-start(bf16[5,1,32,128]{3,2,1,0:T(8,128)(2,1)S(1)} %get-tuple-element.48), channel_id=1, source_target_pairs={{0,1},{1,0},{2,3},{3,2},{4,5},{5,4},{6,7},{7,6},{8,9},{9,8},{10,11... | collective-permute-start | bytes 122888 | tf_op jit(solution)/shard_map/ppermute | solution.py:26
  25.9 5.7 %collective-permute-start.7 = (bf16[5,1,32,128]{3,2,1,0:T(8,128)(2,1)S(1)}, bf16[5,1,32,128]{3,2,1,0:T(8,128)(2,1)S(1)}, u32[]{:S(2)}, u32[]{:S(2)}) collective-permute-start(bf16[5,1,32,128]{3,2,1,0:T(8,128)(2,1)S(1)} %get-tuple-element.49), channel_id=1, source_target_pairs={{1,2},{2,1},{3,4},{4,3},{5,6},{6,5},{9,10},{10,9},{11,12},{12,11},... | collective-permute-start | bytes 122888 | tf_op jit(solution)/shard_map/ppermute | solution.py:27
  32.6 7.3 %collective-permute-start.8 = (bf16[1,1,32,128]{3,2,1,0:T(8,128)(2,1)S(1)}, bf16[1,1,32,128]{3,2,1,0:T(8,128)(2,1)S(1)}, u32[]{:S(2)}, u32[]{:S(2)}) collective-permute-start(bf16[1,1,32,128]{3,2,1,0:T(8,128)(2,1)S(1)} %fusion.54), channel_id=1, source_target_pairs={{0,8},{8,0},{16,24},{24,16},{32,40},{40,32},{48,56},{56,48},{64,72... | collective-permute-start | bytes 24584 | tf_op jit(solution)/shard_map/ppermute | solution.py:26
  38.9 1.0 collective-permute-start.9
  40.0 5.2 %collective-permute-start.10 = (bf16[3,1,32,128]{3,2,1,0:T(8,128)(2,1)S(1)}, bf16[3,1,32,128]{3,2,1,0:T(8,128)(2,1)S(1)}, u32[]{:S(2)}, u32[]{:S(2)}) collective-permute-start(bf16[3,1,32,128]{3,2,1,0:T(8,128)(2,1)S(1)} %pad_maximum_fusion.17), channel_id=1, source_target_pairs={{0,1},{1,0},{2,3},{3,2},{4,5},{5,4},{6,7},{7,6},{8,9},{9,8},{10,11... | collective-permute-start | bytes 73736 | tf_op jit(solution)/shard_map/ppermute | solution.py:26
  40.1 6.0 %collective-permute-start.11 = (bf16[3,1,32,128]{3,2,1,0:T(8,128)(2,1)S(1)}, bf16[3,1,32,128]{3,2,1,0:T(8,128)(2,1)S(1)}, u32[]{:S(2)}, u32[]{:S(2)}) collective-permute-start(bf16[3,1,32,128]{3,2,1,0:T(8,128)(2,1)S(1)} %pad_maximum_fusion.17), channel_id=1, source_target_pairs={{1,2},{2,1},{3,4},{4,3},{5,6},{6,5},{9,10},{10,9},{11,12},{12,11},... | collective-permute-start | bytes 73736 | tf_op jit(solution)/shard_map/ppermute | solution.py:27
  47.5 1.6 %copy-start.2 = (f32[16,16,12,128]{3,2,1,0:T(8,128)S(1)}, f32[16,16,12,128]{3,2,1,0:T(8,128)}, u32[]{:S(2)}) copy-start(f32[16,16,12,128]{3,2,1,0:T(8,128)} %copy-done.1) | copy-start | bytes 4718596
  50.0 1.3 %copy-start.5 = (bf16[18,18,12,64]{3,2,1,0:T(8,128)(2,1)S(1)}, bf16[18,18,12,64]{3,2,1,0:T(8,128)(2,1)}, u32[]{:S(2)}) copy-start(bf16[18,18,12,64]{3,2,1,0:T(8,128)(2,1)} %copy-done.4) | copy-start | bytes 1492996
  56.0 4.2 %collective-permute-start.12 = (f32[512,128]{1,0:T(8,128)S(1)}, f32[512,128]{1,0:T(8,128)S(1)}, u32[]{:S(2)}, u32[]{:S(2)}) collective-permute-start(f32[512,128]{1,0:T(8,128)S(1)} %pad_maximum_fusion.2), channel_id=1, source_target_pairs={{0,1},{1,0},{2,3},{3,2},{4,5},{5,4},{6,7},{7,6},{8,9},{9,8},{10,11... | collective-permute-start | bytes 786440 | tf_op jit(solution)/shard_map/ppermute | solution.py:40
  56.1 6.4 %collective-permute-start.15 = (bf16[16,1,1536]{2,1,0:T(2,128)(2,1)S(1)}, bf16[16,1,1536]{2,1,0:T(2,128)(2,1)S(1)}, u32[]{:S(2)}, u32[]{:S(2)}) collective-permute-start(bf16[16,1,1536]{2,1,0:T(2,128)(2,1)S(1)} %get-tuple-element.32), channel_id=1, source_target_pairs={{1,2},{2,1},{3,4},{4,3},{5,6},{6,5},{9,10},{10,9},{11,12},{12,11},... | collective-permute-start | bytes 147464 | tf_op jit(solution)/shard_map/ppermute | solution.py:61
  60.4 3.9 %collective-permute-start.13 = (f32[160,128]{1,0:T(8,128)S(1)}, f32[160,128]{1,0:T(8,128)S(1)}, u32[]{:S(2)}, u32[]{:S(2)}) collective-permute-start(f32[160,128]{1,0:T(8,128)S(1)} %slice_select_fusion.1), channel_id=1, source_target_pairs={{0,2},{1,3},{2,0},{3,1},{4,6},{5,7},{6,4},{7,5},{8,10},{9,11},{10,... | collective-permute-start | bytes 245768 | tf_op jit(solution)/shard_map/ppermute | solution.py:40
  64.2 4.9 %collective-permute-start.14 = (f32[160,128]{1,0:T(8,128)S(1)}, f32[160,128]{1,0:T(8,128)S(1)}, u32[]{:S(2)}, u32[]{:S(2)}) collective-permute-start(f32[160,128]{1,0:T(8,128)S(1)} %select_add_fusion), channel_id=1, source_target_pairs={{0,4},{1,5},{2,6},{3,7},{4,0},{5,1},{6,2},{7,3},{8,12},{9,13},{10,... | collective-permute-start | bytes 245768 | tf_op jit(solution)/shard_map/ppermute | solution.py:40
  69.1 9.4 %collective-permute-start.16 = (f32[376,128]{1,0:T(8,128)S(1)}, f32[376,128]{1,0:T(8,128)S(1)}, u32[]{:S(2)}, u32[]{:S(2)}) collective-permute-start(f32[376,128]{1,0:T(8,128)S(1)} %pad_maximum_fusion.4), channel_id=1, source_target_pairs={{0,8},{8,0},{16,24},{24,16},{32,40},{40,32},{48,56},{56,48},{64,72... | collective-permute-start | bytes 577544 | tf_op jit(solution)/shard_map/ppermute | solution.py:40
  75.0 7.7 %collective-permute-start.17 = (bf16[1,18,1536]{2,1,0:T(8,128)(2,1)S(1)}, bf16[1,18,1536]{2,1,0:T(8,128)(2,1)S(1)}, u32[]{:S(2)}, u32[]{:S(2)}) collective-permute-start(bf16[1,18,1536]{2,1,0:T(8,128)(2,1)S(1)} %broadcast_select_fusion.11), channel_id=1, source_target_pairs={{8,16},{16,8},{24,32},{32,24},{40,48},{48,40},{56,64},{64,56},{72,... | collective-permute-start | bytes 165896 | tf_op jit(solution)/shard_map/ppermute | solution.py:61
  78.7 6.1 %collective-permute-start.18 = (f32[160,128]{1,0:T(8,128)S(1)}, f32[160,128]{1,0:T(8,128)S(1)}, u32[]{:S(2)}, u32[]{:S(2)}) collective-permute-start(f32[160,128]{1,0:T(8,128)S(1)} %slice_add_fusion.1), channel_id=1, source_target_pairs={{0,16},{8,24},{16,0},{24,8},{32,48},{40,56},{48,32},{56,40},{64,80... | collective-permute-start | bytes 245768 | tf_op jit(solution)/shard_map/ppermute | solution.py:40
  84.9 5.8 %collective-permute-start.19 = (f32[160,128]{1,0:T(8,128)S(1)}, f32[160,128]{1,0:T(8,128)S(1)}, u32[]{:S(2)}, u32[]{:S(2)}) collective-permute-start(f32[160,128]{1,0:T(8,128)S(1)} %add.137), channel_id=1, source_target_pairs={{0,32},{8,40},{16,48},{24,56},{32,0},{40,8},{48,16},{56,24},{64,96... | collective-permute-start | bytes 245768 | tf_op jit(solution)/shard_map/ppermute | solution.py:40
  90.7 5.9 %collective-permute-start.20 = (f32[160,128]{1,0:T(8,128)S(1)}, f32[160,128]{1,0:T(8,128)S(1)}, u32[]{:S(2)}, u32[]{:S(2)}) collective-permute-start(f32[160,128]{1,0:T(8,128)S(1)} %add.138), channel_id=1, source_target_pairs={{0,64},{8,72},{16,80},{24,88},{32,96},{40,104},{48,112},{56,120},{... | collective-permute-start | bytes 245768 | tf_op jit(solution)/shard_map/ppermute | solution.py:40
  96.6 4.5 %collective-permute-start.21 = (f32[160,128]{1,0:T(8,128)S(1)}, f32[160,128]{1,0:T(8,128)S(1)}, u32[]{:S(2)}, u32[]{:S(2)}) collective-permute-start(f32[160,128]{1,0:T(8,128)S(1)} %add.139), channel_id=1, source_target_pairs={{0,2},{1,3},{2,0},{3,1},{4,6},{5,7},{6,4},{7,5},{8,10},{9,11},{10,... | collective-permute-start | bytes 245768 | tf_op jit(solution)/shard_map/ppermute | solution.py:40
  101.1 7.3 %collective-permute-start.22 = (f32[320,128]{1,0:T(8,128)S(1)}, f32[320,128]{1,0:T(8,128)S(1)}, u32[]{:S(2)}, u32[]{:S(2)}) collective-permute-start(f32[320,128]{1,0:T(8,128)S(1)} %maximum_select_fusion.3), channel_id=1, source_target_pairs={{0,1},{1,0},{2,3},{3,2},{4,5},{5,4},{6,7},{7,6},{8,9},{9,8},{10,11... | collective-permute-start | bytes 491528 | tf_op jit(solution)/shard_map/ppermute | solution.py:40

commit v10 on v9

--- a/solution.py
+++ b/solution.py
@@ -306,7 +306,7 @@
         grad_pre.reshape(tile_rows, tile_cols, DATES * C_OUT),
     )
     padded_grad = padded_grad.reshape(tile_rows + 2, tile_cols + 2, DATES, C_OUT)
-    input_sum = transposed_conv(padded_grad, conv_weight, tile_rows, tile_cols)
+    input_sum = window_conv(padded_grad, jnp.swapaxes(conv_weight[::-1, ::-1], 2, 3))
     input_grad = input_sum.astype(jnp.bfloat16).reshape(tile_rows, tile_cols, DATES * C_IN)
     conv_grad = flat[:conv_rows].reshape(conv_term.shape)
     time_grad = flat[conv_rows : conv_rows + time_rows].reshape(time_term.shape)

time: 111 us -> 116 us (1.045); the launches traced: 111 us -> 114 us
  local copies, waits for them, and re-layouts: 16 us -> 9.32 us
  matrix products: 12.6 us -> 16.7 us
  waiting for transfers between devices: 14.4 us -> 18.1 us
  other arithmetic: 6.67 us -> 8.08 us
    unnamed x30 -> x15, local copies, waits for them, and re-layouts: 8.06 us -> 2.56 us
    conv_general_dilated x1 -> x2, matrix products: 1.59 us -> 6.82 us  [window_conv(): lax.conv_general_dilated(padded, kernel, window_strides=(1, 1), padding='...]
    ppermute x9, waiting for transfers between devices: 8.14 us -> 12.2 us  [exchange(): return lax.ppermute(value, axis, [(i, i ^ bit) for i in range(size)])]
    slice x1 -> x0, local copies, waits for them, and re-layouts: 2.81 us -> none  [transposed_conv(): padded_grad[2 - row_tap:2 - row_tap + out_rows, 2 - col_tap:2 - col_tap +...]
    dot_general x3 -> x0, matrix products: 2.29 us -> none  [transposed_conv(): tap_term = jnp.dot(grad_patch, flipped, preferred_element_type=jnp.float32)]
    convert_element_type x1, other arithmetic: 0.59 us -> 2 us  [per_device(): ((pixel_grad / DATES)[:, :, None, :] * silu_slope(mixed_time)).astype(jnp...]
  transfers between devices with their start and end apart: 23 -> 23, of which waited for: 12 -> 12; matrix products, arithmetic and copies ran while one was open for 12% -> 9% of each run, Pallas kernels for 0% -> 0%
where the time goes in v10:
time: 116 us; the launch traced here: 114 us
  starting transfers between devices  60.7 us (52%)
  waiting for transfers between devices  18.1 us (16%)
  matrix products  16.7 us (14%)
  local copies, waits for them, and re-layouts  9.32 us (8%)
  other arithmetic  8.08 us (7%)
  between operations  1.29 us (1%)
    ppermute x9, starting transfers between devices, exchange(): return lax.ppermute(value, axis, [(i, i ^ bit) for i in range(size)])  28.6 us
    ppermute x6, starting transfers between devices, with_halo(): lax.ppermute(jnp.where(odd, tail, head), axis, [pair for k in range(1, co...  14.5 us
    ppermute x6, starting transfers between devices, with_halo(): lax.ppermute(jnp.where(odd, head, tail), axis, [(i, i ^ 1) for i in range...  12.9 us
    ppermute x9, waiting for transfers between devices, exchange(): return lax.ppermute(value, axis, [(i, i ^ bit) for i in range(size)])  12.2 us
    conv_general_dilated x2, matrix products, window_conv(): lax.conv_general_dilated(padded, kernel, window_strides=(1, 1), padding='...  6.82 us
    ppermute x2, starting transfers between devices, outer_swap(): lax.ppermute(piece, axis, [pair for k in range(1, count - 1, 2) for pair...  4.73 us
    ppermute x6, waiting for transfers between devices, with_halo(): lax.ppermute(jnp.where(odd, tail, head), axis, [pair for k in range(1, co...  4.12 us
    conv_general_dilated x1, matrix products, per_device(): lax.conv_general_dilated(padded_pixels, grad_pre, window_strides=(1, 1),...  2.6 us
  transfers between devices with their start and end apart: 23, of which 12 were waited for; matrix products, arithmetic and copies ran while one was open for 9% of the time, Pallas kernels for 0%

profile of v10, /device:TPU:1, one launch (start us, length us, event | category | flops | bytes accessed | tf_op | source)
XLA Modules:
  0.0 114.2 jit_solution(1332328101857714956)
XLA Ops:
  1.5 2.0 %collective-permute-start = (bf16[1,16,768]{2,1,0:T(8,128)(2,1)S(1)}, bf16[1,16,768]{2,1,0:T(8,128)(2,1)S(1)}, u32[]{:S(2)}, u32[]{:S(2)}) collective-permute-start(bf16[1,16,768]{2,1,0:T(8,128)(2,1)S(1)} %get-tuple-element.24), channel_id=1, source_target_pairs={{0,8},{8,0},{16,24},{24,16},{32,40},{40,32},{48,56},{56,48},{64,72... | collective-permute-start | bytes 73736 | tf_op jit(solution)/shard_map/ppermute | solution.py:26
  6.3 1.1 %broadcast_select_fusion.7 = (bf16[18,1,768]{2,1,0:T(2,128)(2,1)S(1)}, bf16[18,1,768]{2,1,0:T(2,128)(2,1)S(1)}, bf16[18,1,768]{2,1,0:T(2,128)(2,1)S(1)}) fusion(pred[]{:T(512)S(6)} %eq.104, bf16[1,16,768]{2,1,0:T(8,128)(2,1)S(1)} %get-tuple-element.43, bf16[16,16,768]{2,1,0:T(8,128)(2,1)} %param.8, bf16[1,16,768]{2,1,0:T(8,128)(2,1)S(1)} %get-tuple-element.42), kind=kLoop, calls=%fused_computation.48 | loop fusion | flops 179712 | bytes 525313 | tf_op jit(solution)/shard_map/jit(_where)/select_n | solution.py:26
  7.5 4.0 %collective-permute-start.3 = (bf16[18,1,768]{2,1,0:T(2,128)(2,1)S(1)}, bf16[18,1,768]{2,1,0:T(2,128)(2,1)S(1)}, u32[]{:S(2)}, u32[]{:S(2)}) collective-permute-start(bf16[18,1,768]{2,1,0:T(2,128)(2,1)S(1)} %broadcast_select_fusion.6), channel_id=1, source_target_pairs={{1,2},{2,1},{3,4},{4,3},{5,6},{6,5},{9,10},{10,9},{11,12},{12,11},... | collective-permute-start | bytes 82952 | tf_op jit(solution)/shard_map/ppermute | solution.py:27
  11.8 1.6 %collective-permute-done.3 = bf16[18,1,768]{2,1,0:T(2,128)(2,1)S(1)} collective-permute-done((bf16[18,1,768]{2,1,0:T(2,128)(2,1)S(1)}, bf16[18,1,768]{2,1,0:T(2,128)(2,1)S(1)}, u32[]{:S(2)}, u32[]{:S(2)}) %collective-permute-start.3) | collective-permute-done | bytes 27680 | tf_op jit(solution)/shard_map/ppermute | solution.py:27
  13.9 1.9 %reshape.214 = bf16[18,18,12,64]{3,2,1,0:T(8,128)(2,1)} reshape(bf16[18,18,768]{2,1,0:T(8,128)(2,1)S(1)} %pad_maximum_fusion.1) | data formatting | bytes 995328 | tf_op jit(solution)/shard_map/reshape | solution.py:187
  15.7 2.9 %fusion.38 = f32[16,16,12,128]{3,2,1,0:T(8,128)S(1)} fusion(bf16[18,18,12,64]{3,2,1,0:T(8,128)(2,1)} %reshape.214, bf16[3,3,64,128]{3,2,1,0:T(8,128)(2,1)S(1)} %copy-done), kind=kOutput, calls=%fused_computation.140 | convolution fusion | flops 452984832 | bytes 2217984 | tf_op jit(solution)/shard_map/conv_general_dilated | solution.py:134
  20.1 1.7 %multiply_reduce_fusion = (f32[16,16,128]{2,1,0:T(8,128)S(1)}, f32[16,16,12,128]{3,1,2,0:T(8,128)}) fusion(bf16[16,16,12,128]{3,1,2,0:T(8,128)(2,1)S(1)} %multiply_convert_fusion.2, bf16[3,128,128]{2,1,0:T(8,128)(2,1)S(1)} %broadcast_select_fusion.8, f32[16,16,12,128]{3,1,2,0:T(8,128)S(1)} %fusion.18, f32[16,16,12,128]{3,1,2,0:T(8,128)S(1)} %fusion.20), kind=kOutput, calls=%fused_computation.2 | convolution fusion | flops 94994432 | bytes 5668864 | tf_op jit(solution)/shard_map/dot_general | solution.py:196
  22.2 3.7 %collective-permute-start.4 = (bf16[1,3,32,128]{3,2,1,0:T(8,128)(2,1)S(1)}, bf16[1,3,32,128]{3,2,1,0:T(8,128)(2,1)S(1)}, u32[]{:S(2)}, u32[]{:S(2)}) collective-permute-start(bf16[1,3,32,128]{3,2,1,0:T(8,128)(2,1)S(1)} %bitcast.104), channel_id=1, source_target_pairs={{0,8},{8,0},{16,24},{24,16},{32,40},{40,32},{48,56},{56,48},{64,72... | collective-permute-start | bytes 73736 | tf_op jit(solution)/shard_map/ppermute | solution.py:26
  27.9 3.9 %collective-permute-start.7 = (bf16[5,1,32,128]{3,2,1,0:T(8,128)(2,1)S(1)}, bf16[5,1,32,128]{3,2,1,0:T(8,128)(2,1)S(1)}, u32[]{:S(2)}, u32[]{:S(2)}) collective-permute-start(bf16[5,1,32,128]{3,2,1,0:T(8,128)(2,1)S(1)} %get-tuple-element.31), channel_id=1, source_target_pairs={{1,2},{2,1},{3,4},{4,3},{5,6},{6,5},{9,10},{10,9},{11,12},{12,11},... | collective-permute-start | bytes 122888 | tf_op jit(solution)/shard_map/ppermute | solution.py:27
  31.8 1.6 %collective-permute-done.7 = bf16[5,1,32,128]{3,2,1,0:T(8,128)(2,1)S(1)} collective-permute-done((bf16[5,1,32,128]{3,2,1,0:T(8,128)(2,1)S(1)}, bf16[5,1,32,128]{3,2,1,0:T(8,128)(2,1)S(1)}, u32[]{:S(2)}, u32[]{:S(2)}) %collective-permute-start.7) | collective-permute-done | bytes 40992 | tf_op jit(solution)/shard_map/ppermute | solution.py:27
  34.5 6.4 %collective-permute-start.8 = (bf16[1,1,32,128]{3,2,1,0:T(8,128)(2,1)S(1)}, bf16[1,1,32,128]{3,2,1,0:T(8,128)(2,1)S(1)}, u32[]{:S(2)}, u32[]{:S(2)}) collective-permute-start(bf16[1,1,32,128]{3,2,1,0:T(8,128)(2,1)S(1)} %fusion.22), channel_id=1, source_target_pairs={{0,8},{8,0},{16,24},{24,16},{32,40},{40,32},{48,56},{56,48},{64,72... | collective-permute-start | bytes 24584 | tf_op jit(solution)/shard_map/ppermute | solution.py:26
  42.1 4.6 %collective-permute-start.11 = (bf16[3,1,32,128]{3,2,1,0:T(8,128)(2,1)S(1)}, bf16[3,1,32,128]{3,2,1,0:T(8,128)(2,1)S(1)}, u32[]{:S(2)}, u32[]{:S(2)}) collective-permute-start(bf16[3,1,32,128]{3,2,1,0:T(8,128)(2,1)S(1)} %pad_maximum_fusion.17), channel_id=1, source_target_pairs={{1,2},{2,1},{3,4},{4,3},{5,6},{6,5},{9,10},{10,9},{11,12},{12,11},... | collective-permute-start | bytes 73736 | tf_op jit(solution)/shard_map/ppermute | solution.py:27
  48.4 2.0 %multiply_convert_fusion.1 = bf16[16,16,12,128]{3,1,2,0:T(8,128)(2,1)S(1)} fusion(f32[16,16,12,128]{3,1,2,0:T(8,128)} %get-tuple-element.47, f32[16,16,128]{2,1,0:T(8,128)S(1)} %bitcast.98), kind=kLoop, calls=%fused_computation.1 | loop fusion | flops 3538944 | bytes 2490368 | tf_op jit(solution)/shard_map/convert_element_type | solution.py:257
  52.5 1.1 multiply_convert_fusion
  53.8 2.6 %fusion = f32[3,3,64,128]{3,2,1,0:T(8,128)S(1)} fusion(bf16[18,18,12,64]{3,2,1,0:T(8,128)(2,1)S(1)} %copy-done.2, bf16[16,16,12,128]{3,1,2,0:T(8,128)(2,1)S(1)} %multiply_convert_fusion), kind=kOutput, calls=%fused_computation.16 | convolution fusion | flops 452984832 | bytes 1579008 | tf_op jit(solution)/shard_map/conv_general_dilated | solution.py:281
  57.3 4.1 %collective-permute-start.15 = (bf16[16,1,1536]{2,1,0:T(2,128)(2,1)S(1)}, bf16[16,1,1536]{2,1,0:T(2,128)(2,1)S(1)}, u32[]{:S(2)}, u32[]{:S(2)}) collective-permute-start(bf16[16,1,1536]{2,1,0:T(2,128)(2,1)S(1)} %get-tuple-element.23), channel_id=1, source_target_pairs={{1,2},{2,1},{3,4},{4,3},{5,6},{6,5},{9,10},{10,9},{11,12},{12,11},... | collective-permute-start | bytes 147464 | tf_op jit(solution)/shard_map/ppermute | solution.py:61
  61.5 1.4 %collective-permute-start.13 = (f32[160,128]{1,0:T(8,128)S(1)}, f32[160,128]{1,0:T(8,128)S(1)}, u32[]{:S(2)}, u32[]{:S(2)}) collective-permute-start(f32[160,128]{1,0:T(8,128)S(1)} %slice_select_fusion.1), channel_id=1, source_target_pairs={{0,2},{1,3},{2,0},{3,1},{4,6},{5,7},{6,4},{7,5},{8,10},{9,11},{10,... | collective-permute-start | bytes 245768 | tf_op jit(solution)/shard_map/ppermute | solution.py:40
  63.8 1.5 %collective-permute-done.13 = f32[160,128]{1,0:T(8,128)S(1)} collective-permute-done((f32[160,128]{1,0:T(8,128)S(1)}, f32[160,128]{1,0:T(8,128)S(1)}, u32[]{:S(2)}, u32[]{:S(2)}) %collective-permute-start.13) | collective-permute-done | bytes 81952 | tf_op jit(solution)/shard_map/ppermute | solution.py:40
  65.4 2.9 %collective-permute-start.14 = (f32[160,128]{1,0:T(8,128)S(1)}, f32[160,128]{1,0:T(8,128)S(1)}, u32[]{:S(2)}, u32[]{:S(2)}) collective-permute-start(f32[160,128]{1,0:T(8,128)S(1)} %select_add_fusion), channel_id=1, source_target_pairs={{0,4},{1,5},{2,6},{3,7},{4,0},{5,1},{6,2},{7,3},{8,12},{9,13},{10,... | collective-permute-start | bytes 245768 | tf_op jit(solution)/shard_map/ppermute | solution.py:40
  68.4 1.9 %collective-permute-done.14 = f32[160,128]{1,0:T(8,128)S(1)} collective-permute-done((f32[160,128]{1,0:T(8,128)S(1)}, f32[160,128]{1,0:T(8,128)S(1)}, u32[]{:S(2)}, u32[]{:S(2)}) %collective-permute-start.14) | collective-permute-done | bytes 81952 | tf_op jit(solution)/shard_map/ppermute | solution.py:40
  70.3 5.8 %collective-permute-start.16 = (f32[376,128]{1,0:T(8,128)S(1)}, f32[376,128]{1,0:T(8,128)S(1)}, u32[]{:S(2)}, u32[]{:S(2)}) collective-permute-start(f32[376,128]{1,0:T(8,128)S(1)} %pad_maximum_fusion.4), channel_id=1, source_target_pairs={{0,8},{8,0},{16,24},{24,16},{32,40},{40,32},{48,56},{56,48},{64,72... | collective-permute-start | bytes 577544 | tf_op jit(solution)/shard_map/ppermute | solution.py:40
  76.1 3.6 %collective-permute-done.16 = f32[376,128]{1,0:T(8,128)S(1)} collective-permute-done((f32[376,128]{1,0:T(8,128)S(1)}, f32[376,128]{1,0:T(8,128)S(1)}, u32[]{:S(2)}, u32[]{:S(2)}) %collective-permute-start.16) | collective-permute-done | bytes 192544 | tf_op jit(solution)/shard_map/ppermute | solution.py:40
  79.7 4.0 %collective-permute-start.18 = (f32[160,128]{1,0:T(8,128)S(1)}, f32[160,128]{1,0:T(8,128)S(1)}, u32[]{:S(2)}, u32[]{:S(2)}) collective-permute-start(f32[160,128]{1,0:T(8,128)S(1)} %slice_add_fusion.1), channel_id=1, source_target_pairs={{0,16},{8,24},{16,0},{24,8},{32,48},{40,56},{48,32},{56,40},{64,80... | collective-permute-start | bytes 245768 | tf_op jit(solution)/shard_map/ppermute | solution.py:40
  83.7 2.3 %collective-permute-done.18 = f32[160,128]{1,0:T(8,128)S(1)} collective-permute-done((f32[160,128]{1,0:T(8,128)S(1)}, f32[160,128]{1,0:T(8,128)S(1)}, u32[]{:S(2)}, u32[]{:S(2)}) %collective-permute-start.18) | collective-permute-done | bytes 81952 | tf_op jit(solution)/shard_map/ppermute | solution.py:40
  86.0 2.4 %collective-permute-start.19 = (f32[160,128]{1,0:T(8,128)S(1)}, f32[160,128]{1,0:T(8,128)S(1)}, u32[]{:S(2)}, u32[]{:S(2)}) collective-permute-start(f32[160,128]{1,0:T(8,128)S(1)} %add.129), channel_id=1, source_target_pairs={{0,32},{8,40},{16,48},{24,56},{32,0},{40,8},{48,16},{56,24},{64,96... | collective-permute-start | bytes 245768 | tf_op jit(solution)/shard_map/ppermute | solution.py:40
  90.3 3.3 %collective-permute-start.20 = (f32[160,128]{1,0:T(8,128)S(1)}, f32[160,128]{1,0:T(8,128)S(1)}, u32[]{:S(2)}, u32[]{:S(2)}) collective-permute-start(f32[160,128]{1,0:T(8,128)S(1)} %add.130), channel_id=1, source_target_pairs={{0,64},{8,72},{16,80},{24,88},{32,96},{40,104},{48,112},{56,120},{... | collective-permute-start | bytes 245768 | tf_op jit(solution)/shard_map/ppermute | solution.py:40
  93.7 1.9 %collective-permute-done.20 = f32[160,128]{1,0:T(8,128)S(1)} collective-permute-done((f32[160,128]{1,0:T(8,128)S(1)}, f32[160,128]{1,0:T(8,128)S(1)}, u32[]{:S(2)}, u32[]{:S(2)}) %collective-permute-start.20) | collective-permute-done | bytes 81952 | tf_op jit(solution)/shard_map/ppermute | solution.py:40
  95.6 2.5 %collective-permute-start.21 = (f32[160,128]{1,0:T(8,128)S(1)}, f32[160,128]{1,0:T(8,128)S(1)}, u32[]{:S(2)}, u32[]{:S(2)}) collective-permute-start(f32[160,128]{1,0:T(8,128)S(1)} %add.131), channel_id=1, source_target_pairs={{0,2},{1,3},{2,0},{3,1},{4,6},{5,7},{6,4},{7,5},{8,10},{9,11},{10,... | collective-permute-start | bytes 245768 | tf_op jit(solution)/shard_map/ppermute | solution.py:40
  98.7 1.7 %reshape.224 = bf16[18,18,12,128]{3,2,1,0:T(8,128)(2,1)} reshape(bf16[18,18,1536]{2,1,0:T(8,128)(2,1)S(1)} %pad_maximum_fusion) | data formatting | bytes 1990656 | tf_op jit(solution)/shard_map/reshape | solution.py:308
  100.4 6.1 %collective-permute-start.22 = (f32[320,128]{1,0:T(8,128)S(1)}, f32[320,128]{1,0:T(8,128)S(1)}, u32[]{:S(2)}, u32[]{:S(2)}) collective-permute-start(f32[320,128]{1,0:T(8,128)S(1)} %maximum_select_fusion.3), channel_id=1, source_target_pairs={{0,1},{1,0},{2,3},{3,2},{4,5},{5,4},{6,7},{7,6},{8,9},{9,8},{10,11... | collective-permute-start | bytes 491528 | tf_op jit(solution)/shard_map/ppermute | solution.py:40
  106.5 3.9 %convolution_convert_fusion = bf16[16,16,12,64]{3,2,1,0:T(8,128)(2,1)S(1)} fusion(bf16[18,18,12,128]{3,2,1,0:T(8,128)(2,1)} %reshape.224, bf16[3,3,64,128]{3,2,1,0:T(8,128)(2,1)S(1)} %copy-done), kind=kOutput, calls=%fused_computation.7 | convolution fusion | flops 453181440 | bytes 1536000 | tf_op jit(solution)/shard_map/conv_general_dilated | solution.py:134
  110.4 1.4 %reshape.225 = bf16[16,16,768]{2,1,0:T(8,128)(2,1)} reshape(bf16[16,16,12,64]{3,2,1,0:T(8,128)(2,1)S(1)} %convolution_convert_fusion) | data formatting | bytes 786432 | tf_op jit(solution)/shard_map/reshape | solution.py:310
  (123 shorter events, 20.9 us)
Async XLA Ops:
  0.6 15.1 %copy-start = (bf16[3,3,64,128]{3,2,1,0:T(8,128)(2,1)S(1)}, bf16[3,3,64,128]{3,2,1,0:T(8,128)(2,1)}, u32[]{:S(2)}) copy-start(bf16[3,3,64,128]{3,2,1,0:T(8,128)(2,1)} %param.9) | copy-start | bytes 442372
  0.6 12.9 %copy-start.1 = (bf16[16,16,768]{2,1,0:T(8,128)(2,1)S(1)}, bf16[16,16,768]{2,1,0:T(8,128)(2,1)}, u32[]{:S(2)}) copy-start(bf16[16,16,768]{2,1,0:T(8,128)(2,1)} %param.8) | copy-start | bytes 1179652
  0.7 11.1 %copy-start.3 = (s32[16,16]{1,0:T(8,128)S(1)}, s32[16,16]{1,0:T(8,128)}, u32[]{:S(2)}) copy-start(s32[16,16]{1,0:T(8,128)} %param.12) | copy-start | bytes 3076
  1.5 4.8 %collective-permute-start = (bf16[1,16,768]{2,1,0:T(8,128)(2,1)S(1)}, bf16[1,16,768]{2,1,0:T(8,128)(2,1)S(1)}, u32[]{:S(2)}, u32[]{:S(2)}) collective-permute-start(bf16[1,16,768]{2,1,0:T(8,128)(2,1)S(1)} %get-tuple-element.24), channel_id=1, source_target_pairs={{0,8},{8,0},{16,24},{24,16},{32,40},{40,32},{48,56},{56,48},{64,72... | collective-permute-start | bytes 73736 | tf_op jit(solution)/shard_map/ppermute | solution.py:26
  3.5 2.7 %collective-permute-start.1 = (bf16[1,16,768]{2,1,0:T(8,128)(2,1)S(1)}, bf16[1,16,768]{2,1,0:T(8,128)(2,1)S(1)}, u32[]{:S(2)}, u32[]{:S(2)}) collective-permute-start(bf16[1,16,768]{2,1,0:T(8,128)(2,1)S(1)} %get-tuple-element.25), channel_id=1, source_target_pairs={{8,16},{16,8},{24,32},{32,24},{40,48},{48,40},{56,64},{64,56},{72,... | collective-permute-start | bytes 73736 | tf_op jit(solution)/shard_map/ppermute | solution.py:27
  7.5 5.9 %collective-permute-start.3 = (bf16[18,1,768]{2,1,0:T(2,128)(2,1)S(1)}, bf16[18,1,768]{2,1,0:T(2,128)(2,1)S(1)}, u32[]{:S(2)}, u32[]{:S(2)}) collective-permute-start(bf16[18,1,768]{2,1,0:T(2,128)(2,1)S(1)} %broadcast_select_fusion.6), channel_id=1, source_target_pairs={{1,2},{2,1},{3,4},{4,3},{5,6},{6,5},{9,10},{10,9},{11,12},{12,11},... | collective-permute-start | bytes 82952 | tf_op jit(solution)/shard_map/ppermute | solution.py:27
  11.6 1.8 %collective-permute-start.2 = (bf16[18,1,768]{2,1,0:T(2,128)(2,1)S(1)}, bf16[18,1,768]{2,1,0:T(2,128)(2,1)S(1)}, u32[]{:S(2)}, u32[]{:S(2)}) collective-permute-start(bf16[18,1,768]{2,1,0:T(2,128)(2,1)S(1)} %get-tuple-element.19), channel_id=1, source_target_pairs={{0,1},{1,0},{2,3},{3,2},{4,5},{5,4},{6,7},{7,6},{8,9},{9,8},{10,11... | collective-permute-start | bytes 82952 | tf_op jit(solution)/shard_map/ppermute | solution.py:26
  20.1 13.8 %copy-start.4 = (bf16[128,20]{0,1:T(8,128)(2,1)S(1)}, bf16[128,20]{0,1:T(8,128)(2,1)}, u32[]{:S(2)}) copy-start(bf16[128,20]{0,1:T(8,128)(2,1)} %param.11) | copy-start | bytes 15364
  21.8 12.3 %copy-start.5 = (s32[1,1,32]{2,1,0:T(1,128)S(1)}, s32[1,1,32]{2,1,0:T(1,128)}, u32[]{:S(2)}) copy-start(s32[1,1,32]{2,1,0:T(1,128)} %param.15) | copy-start | bytes 388
  22.2 5.1 %collective-permute-start.4 = (bf16[1,3,32,128]{3,2,1,0:T(8,128)(2,1)S(1)}, bf16[1,3,32,128]{3,2,1,0:T(8,128)(2,1)S(1)}, u32[]{:S(2)}, u32[]{:S(2)}) collective-permute-start(bf16[1,3,32,128]{3,2,1,0:T(8,128)(2,1)S(1)} %bitcast.104), channel_id=1, source_target_pairs={{0,8},{8,0},{16,24},{24,16},{32,40},{40,32},{48,56},{56,48},{64,72... | collective-permute-start | bytes 73736 | tf_op jit(solution)/shard_map/ppermute | solution.py:26
  26.0 1.4 %collective-permute-start.5 = (bf16[1,3,32,128]{3,2,1,0:T(8,128)(2,1)S(1)}, bf16[1,3,32,128]{3,2,1,0:T(8,128)(2,1)S(1)}, u32[]{:S(2)}, u32[]{:S(2)}) collective-permute-start(bf16[1,3,32,128]{3,2,1,0:T(8,128)(2,1)S(1)} %bitcast.103), channel_id=1, source_target_pairs={{8,16},{16,8},{24,32},{32,24},{40,48},{48,40},{56,64},{64,56},{72,... | collective-permute-start | bytes 73736 | tf_op jit(solution)/shard_map/ppermute | solution.py:27
  27.4 4.4 %collective-permute-start.6 = (bf16[5,1,32,128]{3,2,1,0:T(8,128)(2,1)S(1)}, bf16[5,1,32,128]{3,2,1,0:T(8,128)(2,1)S(1)}, u32[]{:S(2)}, u32[]{:S(2)}) collective-permute-start(bf16[5,1,32,128]{3,2,1,0:T(8,128)(2,1)S(1)} %get-tuple-element.30), channel_id=1, source_target_pairs={{0,1},{1,0},{2,3},{3,2},{4,5},{5,4},{6,7},{7,6},{8,9},{9,8},{10,11... | collective-permute-start | bytes 122888 | tf_op jit(solution)/shard_map/ppermute | solution.py:26
  27.9 5.6 %collective-permute-start.7 = (bf16[5,1,32,128]{3,2,1,0:T(8,128)(2,1)S(1)}, bf16[5,1,32,128]{3,2,1,0:T(8,128)(2,1)S(1)}, u32[]{:S(2)}, u32[]{:S(2)}) collective-permute-start(bf16[5,1,32,128]{3,2,1,0:T(8,128)(2,1)S(1)} %get-tuple-element.31), channel_id=1, source_target_pairs={{1,2},{2,1},{3,4},{4,3},{5,6},{6,5},{9,10},{10,9},{11,12},{12,11},... | collective-permute-start | bytes 122888 | tf_op jit(solution)/shard_map/ppermute | solution.py:27
  34.5 7.5 %collective-permute-start.8 = (bf16[1,1,32,128]{3,2,1,0:T(8,128)(2,1)S(1)}, bf16[1,1,32,128]{3,2,1,0:T(8,128)(2,1)S(1)}, u32[]{:S(2)}, u32[]{:S(2)}) collective-permute-start(bf16[1,1,32,128]{3,2,1,0:T(8,128)(2,1)S(1)} %fusion.22), channel_id=1, source_target_pairs={{0,8},{8,0},{16,24},{24,16},{32,40},{40,32},{48,56},{56,48},{64,72... | collective-permute-start | bytes 24584 | tf_op jit(solution)/shard_map/ppermute | solution.py:26
  41.0 1.0 collective-permute-start.9
  42.0 5.1 %collective-permute-start.10 = (bf16[3,1,32,128]{3,2,1,0:T(8,128)(2,1)S(1)}, bf16[3,1,32,128]{3,2,1,0:T(8,128)(2,1)S(1)}, u32[]{:S(2)}, u32[]{:S(2)}) collective-permute-start(bf16[3,1,32,128]{3,2,1,0:T(8,128)(2,1)S(1)} %pad_maximum_fusion.17), channel_id=1, source_target_pairs={{0,1},{1,0},{2,3},{3,2},{4,5},{5,4},{6,7},{7,6},{8,9},{9,8},{10,11... | collective-permute-start | bytes 73736 | tf_op jit(solution)/shard_map/ppermute | solution.py:26
  42.1 5.9 %collective-permute-start.11 = (bf16[3,1,32,128]{3,2,1,0:T(8,128)(2,1)S(1)}, bf16[3,1,32,128]{3,2,1,0:T(8,128)(2,1)S(1)}, u32[]{:S(2)}, u32[]{:S(2)}) collective-permute-start(bf16[3,1,32,128]{3,2,1,0:T(8,128)(2,1)S(1)} %pad_maximum_fusion.17), channel_id=1, source_target_pairs={{1,2},{2,1},{3,4},{4,3},{5,6},{6,5},{9,10},{10,9},{11,12},{12,11},... | collective-permute-start | bytes 73736 | tf_op jit(solution)/shard_map/ppermute | solution.py:27
  52.4 1.3 %copy-start.2 = (bf16[18,18,12,64]{3,2,1,0:T(8,128)(2,1)S(1)}, bf16[18,18,12,64]{3,2,1,0:T(8,128)(2,1)}, u32[]{:S(2)}) copy-start(bf16[18,18,12,64]{3,2,1,0:T(8,128)(2,1)} %reshape.214) | copy-start | bytes 1492996
  57.1 4.2 %collective-permute-start.12 = (f32[512,128]{1,0:T(8,128)S(1)}, f32[512,128]{1,0:T(8,128)S(1)}, u32[]{:S(2)}, u32[]{:S(2)}) collective-permute-start(f32[512,128]{1,0:T(8,128)S(1)} %pad_maximum_fusion.2), channel_id=1, source_target_pairs={{0,1},{1,0},{2,3},{3,2},{4,5},{5,4},{6,7},{7,6},{8,9},{9,8},{10,11... | collective-permute-start | bytes 786440 | tf_op jit(solution)/shard_map/ppermute | solution.py:40
  57.3 6.4 %collective-permute-start.15 = (bf16[16,1,1536]{2,1,0:T(2,128)(2,1)S(1)}, bf16[16,1,1536]{2,1,0:T(2,128)(2,1)S(1)}, u32[]{:S(2)}, u32[]{:S(2)}) collective-permute-start(bf16[16,1,1536]{2,1,0:T(2,128)(2,1)S(1)} %get-tuple-element.23), channel_id=1, source_target_pairs={{1,2},{2,1},{3,4},{4,3},{5,6},{6,5},{9,10},{10,9},{11,12},{12,11},... | collective-permute-start | bytes 147464 | tf_op jit(solution)/shard_map/ppermute | solution.py:61
  61.5 3.9 %collective-permute-start.13 = (f32[160,128]{1,0:T(8,128)S(1)}, f32[160,128]{1,0:T(8,128)S(1)}, u32[]{:S(2)}, u32[]{:S(2)}) collective-permute-start(f32[160,128]{1,0:T(8,128)S(1)} %slice_select_fusion.1), channel_id=1, source_target_pairs={{0,2},{1,3},{2,0},{3,1},{4,6},{5,7},{6,4},{7,5},{8,10},{9,11},{10,... | collective-permute-start | bytes 245768 | tf_op jit(solution)/shard_map/ppermute | solution.py:40
  65.4 4.9 %collective-permute-start.14 = (f32[160,128]{1,0:T(8,128)S(1)}, f32[160,128]{1,0:T(8,128)S(1)}, u32[]{:S(2)}, u32[]{:S(2)}) collective-permute-start(f32[160,128]{1,0:T(8,128)S(1)} %select_add_fusion), channel_id=1, source_target_pairs={{0,4},{1,5},{2,6},{3,7},{4,0},{5,1},{6,2},{7,3},{8,12},{9,13},{10,... | collective-permute-start | bytes 245768 | tf_op jit(solution)/shard_map/ppermute | solution.py:40
  70.3 9.4 %collective-permute-start.16 = (f32[376,128]{1,0:T(8,128)S(1)}, f32[376,128]{1,0:T(8,128)S(1)}, u32[]{:S(2)}, u32[]{:S(2)}) collective-permute-start(f32[376,128]{1,0:T(8,128)S(1)} %pad_maximum_fusion.4), channel_id=1, source_target_pairs={{0,8},{8,0},{16,24},{24,16},{32,40},{40,32},{48,56},{56,48},{64,72... | collective-permute-start | bytes 577544 | tf_op jit(solution)/shard_map/ppermute | solution.py:40
  79.7 6.3 %collective-permute-start.18 = (f32[160,128]{1,0:T(8,128)S(1)}, f32[160,128]{1,0:T(8,128)S(1)}, u32[]{:S(2)}, u32[]{:S(2)}) collective-permute-start(f32[160,128]{1,0:T(8,128)S(1)} %slice_add_fusion.1), channel_id=1, source_target_pairs={{0,16},{8,24},{16,0},{24,8},{32,48},{40,56},{48,32},{56,40},{64,80... | collective-permute-start | bytes 245768 | tf_op jit(solution)/shard_map/ppermute | solution.py:40
  86.0 4.3 %collective-permute-start.19 = (f32[160,128]{1,0:T(8,128)S(1)}, f32[160,128]{1,0:T(8,128)S(1)}, u32[]{:S(2)}, u32[]{:S(2)}) collective-permute-start(f32[160,128]{1,0:T(8,128)S(1)} %add.129), channel_id=1, source_target_pairs={{0,32},{8,40},{16,48},{24,56},{32,0},{40,8},{48,16},{56,24},{64,96... | collective-permute-start | bytes 245768 | tf_op jit(solution)/shard_map/ppermute | solution.py:40
  88.5 5.2 %collective-permute-start.17 = (bf16[1,18,1536]{2,1,0:T(8,128)(2,1)S(1)}, bf16[1,18,1536]{2,1,0:T(8,128)(2,1)S(1)}, u32[]{:S(2)}, u32[]{:S(2)}) collective-permute-start(bf16[1,18,1536]{2,1,0:T(8,128)(2,1)S(1)} %broadcast_select_fusion.11), channel_id=1, source_target_pairs={{8,16},{16,8},{24,32},{32,24},{40,48},{48,40},{56,64},{64,56},{72,... | collective-permute-start | bytes 165896 | tf_op jit(solution)/shard_map/ppermute | solution.py:61
  90.3 5.2 %collective-permute-start.20 = (f32[160,128]{1,0:T(8,128)S(1)}, f32[160,128]{1,0:T(8,128)S(1)}, u32[]{:S(2)}, u32[]{:S(2)}) collective-permute-start(f32[160,128]{1,0:T(8,128)S(1)} %add.130), channel_id=1, source_target_pairs={{0,64},{8,72},{16,80},{24,88},{32,96},{40,104},{48,112},{56,120},{... | collective-permute-start | bytes 245768 | tf_op jit(solution)/shard_map/ppermute | solution.py:40
  95.6 4.8 %collective-permute-start.21 = (f32[160,128]{1,0:T(8,128)S(1)}, f32[160,128]{1,0:T(8,128)S(1)}, u32[]{:S(2)}, u32[]{:S(2)}) collective-permute-start(f32[160,128]{1,0:T(8,128)S(1)} %add.131), channel_id=1, source_target_pairs={{0,2},{1,3},{2,0},{3,1},{4,6},{5,7},{6,4},{7,5},{8,10},{9,11},{10,... | collective-permute-start | bytes 245768 | tf_op jit(solution)/shard_map/ppermute | solution.py:40
  100.4 11.4 %collective-permute-start.22 = (f32[320,128]{1,0:T(8,128)S(1)}, f32[320,128]{1,0:T(8,128)S(1)}, u32[]{:S(2)}, u32[]{:S(2)}) collective-permute-start(f32[320,128]{1,0:T(8,128)S(1)} %maximum_select_fusion.3), channel_id=1, source_target_pairs={{0,1},{1,0},{2,3},{3,2},{4,5},{5,4},{6,7},{7,6},{8,9},{9,8},{10,11... | collective-permute-start | bytes 491528 | tf_op jit(solution)/shard_map/ppermute | solution.py:40

commit v11 on v9

--- a/solution.py
+++ b/solution.py
@@ -99,11 +99,14 @@
         else:
             got = exchange(flat, axis, bit)
         flat = flat + got
-    for axis, bit in reversed(steps[:halvings]):
+    for axis, bit in reversed(steps[1:halvings]):
         upper = (lax.axis_index(axis) // bit) % 2 == 1
         other = exchange(flat, axis, bit)
         flat = jnp.where(upper, jnp.concatenate([other, flat]), jnp.concatenate([flat, other]))
-    return flat, cells
+    axis, bit = steps[0]
+    upper = (lax.axis_index(axis) // bit) % 2 == 1
+    other = exchange(flat, axis, bit)
+    return (jnp.where(upper, other, flat), jnp.where(upper, flat, other)), cells
 
 
 def silu_slope(value):
@@ -308,9 +311,11 @@
     padded_grad = padded_grad.reshape(tile_rows + 2, tile_cols + 2, DATES, C_OUT)
     input_sum = transposed_conv(padded_grad, conv_weight, tile_rows, tile_cols)
     input_grad = input_sum.astype(jnp.bfloat16).reshape(tile_rows, tile_cols, DATES * C_IN)
-    conv_grad = flat[:conv_rows].reshape(conv_term.shape)
-    time_grad = flat[conv_rows : conv_rows + time_rows].reshape(time_term.shape)
-    class_grad = flat[conv_rows + time_rows : used].reshape(class_term.shape)
+    low, high = flat
+    split = low.shape[0]
+    conv_grad = jnp.concatenate([low, high[: conv_rows - split]]).reshape(conv_term.shape)
+    time_grad = high[conv_rows - split : conv_rows - split + time_rows].reshape(time_term.shape)
+    class_grad = high[conv_rows - split + time_rows : used - split].reshape(class_term.shape)
     return (input_grad, conv_grad, time_grad, class_grad)
 
 

time: 111 us -> 111 us (level)
  no operation moved by 1% of the time
where the time goes in v11:
time: 111 us
  starting transfers between devices  59.8 us (54%)
  local copies, waits for them, and re-layouts  15.2 us (14%)
  waiting for transfers between devices  14.4 us (13%)
  matrix products  12.6 us (11%)
  other arithmetic  7.4 us (7%)
  between operations  1.49 us (1%)
    ppermute x9, starting transfers between devices, exchange(): return lax.ppermute(value, axis, [(i, i ^ bit) for i in range(size)])  28 us
    ppermute x6, starting transfers between devices, with_halo(): lax.ppermute(jnp.where(odd, tail, head), axis, [pair for k in range(1, co...  13.8 us
    ppermute x6, starting transfers between devices, with_halo(): lax.ppermute(jnp.where(odd, head, tail), axis, [(i, i ^ 1) for i in range...  13.2 us
    ppermute x9, waiting for transfers between devices, exchange(): return lax.ppermute(value, axis, [(i, i ^ bit) for i in range(size)])  8.12 us
    unnamed x30, local copies, waits for them, and re-layouts  8.06 us
    ppermute x6, waiting for transfers between devices, with_halo(): lax.ppermute(jnp.where(odd, tail, head), axis, [pair for k in range(1, co...  4.74 us
    ppermute x2, starting transfers between devices, outer_swap(): lax.ppermute(piece, axis, [pair for k in range(1, count - 1, 2) for pair...  4.74 us
    slice x1, local copies, waits for them, and re-layouts, transposed_conv(): padded_grad[2 - row_tap:2 - row_tap + out_rows, 2 - col_tap:2 - col_tap +...  2.81 us
  transfers between devices with their start and end apart: 23, of which 12 were waited for; matrix products, arithmetic and copies ran while one was open for 12% of the time, Pallas kernels for 0%

profile of v11, /device:TPU:1, one launch (start us, length us, event | category | flops | bytes accessed | tf_op | source)
XLA Modules:
  0.0 111.0 jit_solution(5503931883758607793)
XLA Ops:
  1.5 2.0 %collective-permute-start = (bf16[1,16,768]{2,1,0:T(8,128)(2,1)S(1)}, bf16[1,16,768]{2,1,0:T(8,128)(2,1)S(1)}, u32[]{:S(2)}, u32[]{:S(2)}) collective-permute-start(bf16[1,16,768]{2,1,0:T(8,128)(2,1)S(1)} %get-tuple-element.33), channel_id=1, source_target_pairs={{0,8},{8,0},{16,24},{24,16},{32,40},{40,32},{48,56},{56,48},{64,72... | collective-permute-start | bytes 73736 | tf_op jit(solution)/shard_map/ppermute | solution.py:26
  4.2 0.9 copy.68
  6.3 1.1 %broadcast_select_fusion.7 = (bf16[18,1,768]{2,1,0:T(2,128)(2,1)S(1)}, bf16[18,1,768]{2,1,0:T(2,128)(2,1)S(1)}, bf16[18,1,768]{2,1,0:T(2,128)(2,1)S(1)}) fusion(pred[]{:T(512)S(6)} %eq.104, bf16[1,16,768]{2,1,0:T(8,128)(2,1)S(1)} %get-tuple-element.63, bf16[16,16,768]{2,1,0:T(8,128)(2,1)} %param.8, bf16[1,16,768]{2,1,0:T(8,128)(2,1)S(1)} %get-tuple-element.62), kind=kLoop, calls=%fused_computation.66 | loop fusion | flops 179712 | bytes 525313 | tf_op jit(solution)/shard_map/jit(_where)/select_n | solution.py:26
  7.4 1.0 collective-permute-start.2
  8.5 3.1 %collective-permute-start.3 = (bf16[18,1,768]{2,1,0:T(2,128)(2,1)S(1)}, bf16[18,1,768]{2,1,0:T(2,128)(2,1)S(1)}, u32[]{:S(2)}, u32[]{:S(2)}) collective-permute-start(bf16[18,1,768]{2,1,0:T(2,128)(2,1)S(1)} %broadcast_select_fusion.6), channel_id=1, source_target_pairs={{1,2},{2,1},{3,4},{4,3},{5,6},{6,5},{9,10},{10,9},{11,12},{12,11},... | collective-permute-start | bytes 82952 | tf_op jit(solution)/shard_map/ppermute | solution.py:27
  11.8 2.2 %collective-permute-done.3 = bf16[18,1,768]{2,1,0:T(2,128)(2,1)S(1)} collective-permute-done((bf16[18,1,768]{2,1,0:T(2,128)(2,1)S(1)}, bf16[18,1,768]{2,1,0:T(2,128)(2,1)S(1)}, u32[]{:S(2)}, u32[]{:S(2)}) %collective-permute-start.3) | collective-permute-done | bytes 27680 | tf_op jit(solution)/shard_map/ppermute | solution.py:27
  15.3 1.1 copy-done.4
  16.4 1.6 %fusion.74 = f32[16,16,12,128]{3,2,1,0:T(8,128)S(1)} fusion(bf16[18,18,12,64]{3,2,1,0:T(8,128)(2,1)S(1)} %reshape.214, bf16[3,3,64,128]{3,2,1,0:T(8,128)(2,1)S(1)} %copy-done.6), kind=kOutput, calls=%fused_computation.188 | convolution fusion | flops 452984832 | bytes 2217984 | tf_op jit(solution)/shard_map/conv_general_dilated | solution.py:137
  20.8 3.7 %collective-permute-start.4 = (bf16[1,3,32,128]{3,2,1,0:T(8,128)(2,1)S(1)}, bf16[1,3,32,128]{3,2,1,0:T(8,128)(2,1)S(1)}, u32[]{:S(2)}, u32[]{:S(2)}) collective-permute-start(bf16[1,3,32,128]{3,2,1,0:T(8,128)(2,1)S(1)} %bitcast.153), channel_id=1, source_target_pairs={{0,8},{8,0},{16,24},{24,16},{32,40},{40,32},{48,56},{56,48},{64,72... | collective-permute-start | bytes 73736 | tf_op jit(solution)/shard_map/ppermute | solution.py:26
  25.8 4.0 %collective-permute-start.7 = (bf16[5,1,32,128]{3,2,1,0:T(8,128)(2,1)S(1)}, bf16[5,1,32,128]{3,2,1,0:T(8,128)(2,1)S(1)}, u32[]{:S(2)}, u32[]{:S(2)}) collective-permute-start(bf16[5,1,32,128]{3,2,1,0:T(8,128)(2,1)S(1)} %get-tuple-element.51), channel_id=1, source_target_pairs={{1,2},{2,1},{3,4},{4,3},{5,6},{6,5},{9,10},{10,9},{11,12},{12,11},... | collective-permute-start | bytes 122888 | tf_op jit(solution)/shard_map/ppermute | solution.py:27
  29.9 1.6 %collective-permute-done.7 = bf16[5,1,32,128]{3,2,1,0:T(8,128)(2,1)S(1)} collective-permute-done((bf16[5,1,32,128]{3,2,1,0:T(8,128)(2,1)S(1)}, bf16[5,1,32,128]{3,2,1,0:T(8,128)(2,1)S(1)}, u32[]{:S(2)}, u32[]{:S(2)}) %collective-permute-start.7) | collective-permute-done | bytes 40992 | tf_op jit(solution)/shard_map/ppermute | solution.py:27
  32.6 6.3 %collective-permute-start.8 = (bf16[1,1,32,128]{3,2,1,0:T(8,128)(2,1)S(1)}, bf16[1,1,32,128]{3,2,1,0:T(8,128)(2,1)S(1)}, u32[]{:S(2)}, u32[]{:S(2)}) collective-permute-start(bf16[1,1,32,128]{3,2,1,0:T(8,128)(2,1)S(1)} %fusion.54), channel_id=1, source_target_pairs={{0,8},{8,0},{16,24},{24,16},{32,40},{40,32},{48,56},{56,48},{64,72... | collective-permute-start | bytes 24584 | tf_op jit(solution)/shard_map/ppermute | solution.py:26
  40.1 4.7 %collective-permute-start.11 = (bf16[3,1,32,128]{3,2,1,0:T(8,128)(2,1)S(1)}, bf16[3,1,32,128]{3,2,1,0:T(8,128)(2,1)S(1)}, u32[]{:S(2)}, u32[]{:S(2)}) collective-permute-start(bf16[3,1,32,128]{3,2,1,0:T(8,128)(2,1)S(1)} %pad_maximum_fusion.18), channel_id=1, source_target_pairs={{1,2},{2,1},{3,4},{4,3},{5,6},{6,5},{9,10},{10,9},{11,12},{12,11},... | collective-permute-start | bytes 73736 | tf_op jit(solution)/shard_map/ppermute | solution.py:27
  45.2 0.9 collective-permute-done.11
  47.8 1.2 %copy-done.2 = f32[16,16,12,128]{3,2,1,0:T(8,128)S(1)} copy-done((f32[16,16,12,128]{3,2,1,0:T(8,128)S(1)}, f32[16,16,12,128]{3,2,1,0:T(8,128)}, u32[]{:S(2)}) %copy-start.2) | copy-done | bytes 1572888
  49.0 1.0 multiply_convert_fusion
  50.1 1.3 %copy-done.5 = bf16[18,18,12,64]{3,2,1,0:T(8,128)(2,1)S(1)} copy-done((bf16[18,18,12,64]{3,2,1,0:T(8,128)(2,1)S(1)}, bf16[18,18,12,64]{3,2,1,0:T(8,128)(2,1)}, u32[]{:S(2)}) %copy-start.5) | copy-done | bytes 497688
  51.3 2.6 %fusion.20 = f32[3,3,64,128]{3,2,1,0:T(8,128)S(1)} fusion(bf16[18,18,12,64]{3,2,1,0:T(8,128)(2,1)S(1)} %copy-done.5, bf16[16,16,12,128]{3,1,2,0:T(8,128)(2,1)S(1)} %multiply_convert_fusion), kind=kOutput, calls=%fused_computation.34 | convolution fusion | flops 452984832 | bytes 1579008 | tf_op jit(solution)/shard_map/conv_general_dilated | solution.py:284
  56.1 4.1 %collective-permute-start.15 = (bf16[16,1,1536]{2,1,0:T(2,128)(2,1)S(1)}, bf16[16,1,1536]{2,1,0:T(2,128)(2,1)S(1)}, u32[]{:S(2)}, u32[]{:S(2)}) collective-permute-start(bf16[16,1,1536]{2,1,0:T(2,128)(2,1)S(1)} %get-tuple-element.32), channel_id=1, source_target_pairs={{1,2},{2,1},{3,4},{4,3},{5,6},{6,5},{9,10},{10,9},{11,12},{12,11},... | collective-permute-start | bytes 147464 | tf_op jit(solution)/shard_map/ppermute | solution.py:61
  60.3 1.4 %collective-permute-start.13 = (f32[160,128]{1,0:T(8,128)S(1)}, f32[160,128]{1,0:T(8,128)S(1)}, u32[]{:S(2)}, u32[]{:S(2)}) collective-permute-start(f32[160,128]{1,0:T(8,128)S(1)} %slice_select_fusion.1), channel_id=1, source_target_pairs={{0,2},{1,3},{2,0},{3,1},{4,6},{5,7},{6,4},{7,5},{8,10},{9,11},{10,... | collective-permute-start | bytes 245768 | tf_op jit(solution)/shard_map/ppermute | solution.py:40
  62.7 1.5 %collective-permute-done.13 = f32[160,128]{1,0:T(8,128)S(1)} collective-permute-done((f32[160,128]{1,0:T(8,128)S(1)}, f32[160,128]{1,0:T(8,128)S(1)}, u32[]{:S(2)}, u32[]{:S(2)}) %collective-permute-start.13) | collective-permute-done | bytes 81952 | tf_op jit(solution)/shard_map/ppermute | solution.py:40
  64.2 3.0 %collective-permute-start.14 = (f32[160,128]{1,0:T(8,128)S(1)}, f32[160,128]{1,0:T(8,128)S(1)}, u32[]{:S(2)}, u32[]{:S(2)}) collective-permute-start(f32[160,128]{1,0:T(8,128)S(1)} %select_add_fusion), channel_id=1, source_target_pairs={{0,4},{1,5},{2,6},{3,7},{4,0},{5,1},{6,2},{7,3},{8,12},{9,13},{10,... | collective-permute-start | bytes 245768 | tf_op jit(solution)/shard_map/ppermute | solution.py:40
  67.3 1.8 %collective-permute-done.14 = f32[160,128]{1,0:T(8,128)S(1)} collective-permute-done((f32[160,128]{1,0:T(8,128)S(1)}, f32[160,128]{1,0:T(8,128)S(1)}, u32[]{:S(2)}, u32[]{:S(2)}) %collective-permute-start.14) | collective-permute-done | bytes 81952 | tf_op jit(solution)/shard_map/ppermute | solution.py:40
  69.1 5.8 %collective-permute-start.16 = (f32[376,128]{1,0:T(8,128)S(1)}, f32[376,128]{1,0:T(8,128)S(1)}, u32[]{:S(2)}, u32[]{:S(2)}) collective-permute-start(f32[376,128]{1,0:T(8,128)S(1)} %pad_maximum_fusion.5), channel_id=1, source_target_pairs={{0,8},{8,0},{16,24},{24,16},{32,40},{40,32},{48,56},{56,48},{64,72... | collective-permute-start | bytes 577544 | tf_op jit(solution)/shard_map/ppermute | solution.py:40
  75.6 2.9 %collective-permute-done.16 = f32[376,128]{1,0:T(8,128)S(1)} collective-permute-done((f32[376,128]{1,0:T(8,128)S(1)}, f32[376,128]{1,0:T(8,128)S(1)}, u32[]{:S(2)}, u32[]{:S(2)}) %collective-permute-start.16) | collective-permute-done | bytes 192544 | tf_op jit(solution)/shard_map/ppermute | solution.py:40
  78.7 4.0 %collective-permute-start.18 = (f32[160,128]{1,0:T(8,128)S(1)}, f32[160,128]{1,0:T(8,128)S(1)}, u32[]{:S(2)}, u32[]{:S(2)}) collective-permute-start(f32[160,128]{1,0:T(8,128)S(1)} %slice_add_fusion.1), channel_id=1, source_target_pairs={{0,16},{8,24},{16,0},{24,8},{32,48},{40,56},{48,32},{56,40},{64,80... | collective-permute-start | bytes 245768 | tf_op jit(solution)/shard_map/ppermute | solution.py:40
  84.8 2.7 %collective-permute-start.19 = (f32[160,128]{1,0:T(8,128)S(1)}, f32[160,128]{1,0:T(8,128)S(1)}, u32[]{:S(2)}, u32[]{:S(2)}) collective-permute-start(f32[160,128]{1,0:T(8,128)S(1)} %add.137), channel_id=1, source_target_pairs={{0,32},{8,40},{16,48},{24,56},{32,0},{40,8},{48,16},{56,24},{64,96... | collective-permute-start | bytes 245768 | tf_op jit(solution)/shard_map/ppermute | solution.py:40
  87.5 2.8 %fusion.72 = (bf16[16,16,12,128]{3,2,1,0:T(8,128)(2,1)S(1)}, bf16[16,16,12,128]{3,2,1,0:T(8,128)(2,1)S(1)}, bf16[16,16,12,128]{3,2,1,0:T(8,128)(2,1)S(1)}, bf16[...) fusion(bf16[18,18,12,128]{3,2,1,0:T(8,128)(2,1)S(1)} %reshape.224), kind=kLoop, calls=%fused_computation.186 | loop fusion | bytes 14155776 | tf_op jit(solution)/shard_map/slice | solution.py:152
  91.0 3.5 %collective-permute-start.20 = (f32[160,128]{1,0:T(8,128)S(1)}, f32[160,128]{1,0:T(8,128)S(1)}, u32[]{:S(2)}, u32[]{:S(2)}) collective-permute-start(f32[160,128]{1,0:T(8,128)S(1)} %add.138), channel_id=1, source_target_pairs={{0,64},{8,72},{16,80},{24,88},{32,96},{40,104},{48,112},{56,120},{... | collective-permute-start | bytes 245768 | tf_op jit(solution)/shard_map/ppermute | solution.py:40
  96.5 2.7 %collective-permute-start.21 = (f32[160,128]{1,0:T(8,128)S(1)}, f32[160,128]{1,0:T(8,128)S(1)}, u32[]{:S(2)}, u32[]{:S(2)}) collective-permute-start(f32[160,128]{1,0:T(8,128)S(1)} %add.139), channel_id=1, source_target_pairs={{0,2},{1,3},{2,0},{3,1},{4,6},{5,7},{6,4},{7,5},{8,10},{9,11},{10,... | collective-permute-start | bytes 245768 | tf_op jit(solution)/shard_map/ppermute | solution.py:40
  101.1 4.9 %collective-permute-start.22 = (f32[320,128]{1,0:T(8,128)S(1)}, f32[320,128]{1,0:T(8,128)S(1)}, u32[]{:S(2)}, u32[]{:S(2)}) collective-permute-start(f32[320,128]{1,0:T(8,128)S(1)} %maximum_select_fusion.2), channel_id=1, source_target_pairs={{0,1},{1,0},{2,3},{3,2},{4,5},{5,4},{6,7},{7,6},{8,9},{9,8},{10,11... | collective-permute-start | bytes 491528 | tf_op jit(solution)/shard_map/ppermute | solution.py:40
  107.1 1.4 %reshape.225 = bf16[16,16,768]{2,1,0:T(8,128)(2,1)} reshape(bf16[16,16,12,64]{3,2,1,0:T(8,128)(2,1)S(1)} %copy.92) | data formatting | bytes 786432 | tf_op jit(solution)/shard_map/reshape | solution.py:313
  (144 shorter events, 26.6 us)
Async XLA Ops:
  0.6 31.3 %copy-start = (bf16[128,20]{0,1:T(8,128)(2,1)S(1)}, bf16[128,20]{0,1:T(8,128)(2,1)}, u32[]{:S(2)}) copy-start(bf16[128,20]{0,1:T(8,128)(2,1)} %param.11) | copy-start | bytes 15364
  0.6 13.5 %copy-start.3 = (bf16[16,16,768]{2,1,0:T(8,128)(2,1)S(1)}, bf16[16,16,768]{2,1,0:T(8,128)(2,1)}, u32[]{:S(2)}) copy-start(bf16[16,16,768]{2,1,0:T(8,128)(2,1)} %param.8) | copy-start | bytes 1179652
  0.7 11.1 %copy-start.7 = (s32[16,16]{1,0:T(8,128)S(1)}, s32[16,16]{1,0:T(8,128)}, u32[]{:S(2)}) copy-start(s32[16,16]{1,0:T(8,128)} %param.12) | copy-start | bytes 3076
  1.5 4.8 %collective-permute-start = (bf16[1,16,768]{2,1,0:T(8,128)(2,1)S(1)}, bf16[1,16,768]{2,1,0:T(8,128)(2,1)S(1)}, u32[]{:S(2)}, u32[]{:S(2)}) collective-permute-start(bf16[1,16,768]{2,1,0:T(8,128)(2,1)S(1)} %get-tuple-element.33), channel_id=1, source_target_pairs={{0,8},{8,0},{16,24},{24,16},{32,40},{40,32},{48,56},{56,48},{64,72... | collective-permute-start | bytes 73736 | tf_op jit(solution)/shard_map/ppermute | solution.py:26
  3.5 2.7 %collective-permute-start.1 = (bf16[1,16,768]{2,1,0:T(8,128)(2,1)S(1)}, bf16[1,16,768]{2,1,0:T(8,128)(2,1)S(1)}, u32[]{:S(2)}, u32[]{:S(2)}) collective-permute-start(bf16[1,16,768]{2,1,0:T(8,128)(2,1)S(1)} %get-tuple-element.34), channel_id=1, source_target_pairs={{8,16},{16,8},{24,32},{32,24},{40,48},{48,40},{56,64},{64,56},{72,... | collective-permute-start | bytes 73736 | tf_op jit(solution)/shard_map/ppermute | solution.py:27
  7.4 4.4 %collective-permute-start.2 = (bf16[18,1,768]{2,1,0:T(2,128)(2,1)S(1)}, bf16[18,1,768]{2,1,0:T(2,128)(2,1)S(1)}, u32[]{:S(2)}, u32[]{:S(2)}) collective-permute-start(bf16[18,1,768]{2,1,0:T(2,128)(2,1)S(1)} %get-tuple-element.19), channel_id=1, source_target_pairs={{0,1},{1,0},{2,3},{3,2},{4,5},{5,4},{6,7},{7,6},{8,9},{9,8},{10,11... | collective-permute-start | bytes 82952 | tf_op jit(solution)/shard_map/ppermute | solution.py:26
  8.5 5.5 %collective-permute-start.3 = (bf16[18,1,768]{2,1,0:T(2,128)(2,1)S(1)}, bf16[18,1,768]{2,1,0:T(2,128)(2,1)S(1)}, u32[]{:S(2)}, u32[]{:S(2)}) collective-permute-start(bf16[18,1,768]{2,1,0:T(2,128)(2,1)S(1)} %broadcast_select_fusion.6), channel_id=1, source_target_pairs={{1,2},{2,1},{3,4},{4,3},{5,6},{6,5},{9,10},{10,9},{11,12},{12,11},... | collective-permute-start | bytes 82952 | tf_op jit(solution)/shard_map/ppermute | solution.py:27
  14.2 2.2 %copy-start.6 = (bf16[3,3,64,128]{3,2,1,0:T(8,128)(2,1)S(1)}, bf16[3,3,64,128]{3,2,1,0:T(8,128)(2,1)}, u32[]{:S(2)}) copy-start(bf16[3,3,64,128]{3,2,1,0:T(8,128)(2,1)} %param.9) | copy-start | bytes 442372
  15.3 1.1 copy-start.4
  18.0 1.4 %copy-start.1 = (f32[16,16,12,128]{3,2,1,0:T(8,128)}, f32[16,16,12,128]{3,2,1,0:T(8,128)S(1)}, u32[]{:S(2)}) copy-start(f32[16,16,12,128]{3,2,1,0:T(8,128)S(1)} %fusion.74) | copy-start | bytes 4718596
  20.4 11.8 %copy-start.8 = (s32[1,1,32]{2,1,0:T(1,128)S(1)}, s32[1,1,32]{2,1,0:T(1,128)}, u32[]{:S(2)}) copy-start(s32[1,1,32]{2,1,0:T(1,128)} %param.15) | copy-start | bytes 388
  20.8 4.9 %collective-permute-start.4 = (bf16[1,3,32,128]{3,2,1,0:T(8,128)(2,1)S(1)}, bf16[1,3,32,128]{3,2,1,0:T(8,128)(2,1)S(1)}, u32[]{:S(2)}, u32[]{:S(2)}) collective-permute-start(bf16[1,3,32,128]{3,2,1,0:T(8,128)(2,1)S(1)} %bitcast.153), channel_id=1, source_target_pairs={{0,8},{8,0},{16,24},{24,16},{32,40},{40,32},{48,56},{56,48},{64,72... | collective-permute-start | bytes 73736 | tf_op jit(solution)/shard_map/ppermute | solution.py:26
  24.5 1.2 %collective-permute-start.5 = (bf16[1,3,32,128]{3,2,1,0:T(8,128)(2,1)S(1)}, bf16[1,3,32,128]{3,2,1,0:T(8,128)(2,1)S(1)}, u32[]{:S(2)}, u32[]{:S(2)}) collective-permute-start(bf16[1,3,32,128]{3,2,1,0:T(8,128)(2,1)S(1)} %bitcast.152), channel_id=1, source_target_pairs={{8,16},{16,8},{24,32},{32,24},{40,48},{48,40},{56,64},{64,56},{72,... | collective-permute-start | bytes 73736 | tf_op jit(solution)/shard_map/ppermute | solution.py:27
  25.8 4.2 %collective-permute-start.6 = (bf16[5,1,32,128]{3,2,1,0:T(8,128)(2,1)S(1)}, bf16[5,1,32,128]{3,2,1,0:T(8,128)(2,1)S(1)}, u32[]{:S(2)}, u32[]{:S(2)}) collective-permute-start(bf16[5,1,32,128]{3,2,1,0:T(8,128)(2,1)S(1)} %get-tuple-element.50), channel_id=1, source_target_pairs={{0,1},{1,0},{2,3},{3,2},{4,5},{5,4},{6,7},{7,6},{8,9},{9,8},{10,11... | collective-permute-start | bytes 122888 | tf_op jit(solution)/shard_map/ppermute | solution.py:26
  25.8 5.7 %collective-permute-start.7 = (bf16[5,1,32,128]{3,2,1,0:T(8,128)(2,1)S(1)}, bf16[5,1,32,128]{3,2,1,0:T(8,128)(2,1)S(1)}, u32[]{:S(2)}, u32[]{:S(2)}) collective-permute-start(bf16[5,1,32,128]{3,2,1,0:T(8,128)(2,1)S(1)} %get-tuple-element.51), channel_id=1, source_target_pairs={{1,2},{2,1},{3,4},{4,3},{5,6},{6,5},{9,10},{10,9},{11,12},{12,11},... | collective-permute-start | bytes 122888 | tf_op jit(solution)/shard_map/ppermute | solution.py:27
  32.6 7.3 %collective-permute-start.8 = (bf16[1,1,32,128]{3,2,1,0:T(8,128)(2,1)S(1)}, bf16[1,1,32,128]{3,2,1,0:T(8,128)(2,1)S(1)}, u32[]{:S(2)}, u32[]{:S(2)}) collective-permute-start(bf16[1,1,32,128]{3,2,1,0:T(8,128)(2,1)S(1)} %fusion.54), channel_id=1, source_target_pairs={{0,8},{8,0},{16,24},{24,16},{32,40},{40,32},{48,56},{56,48},{64,72... | collective-permute-start | bytes 24584 | tf_op jit(solution)/shard_map/ppermute | solution.py:26
  38.9 1.0 collective-permute-start.9
  40.0 5.2 %collective-permute-start.10 = (bf16[3,1,32,128]{3,2,1,0:T(8,128)(2,1)S(1)}, bf16[3,1,32,128]{3,2,1,0:T(8,128)(2,1)S(1)}, u32[]{:S(2)}, u32[]{:S(2)}) collective-permute-start(bf16[3,1,32,128]{3,2,1,0:T(8,128)(2,1)S(1)} %pad_maximum_fusion.18), channel_id=1, source_target_pairs={{0,1},{1,0},{2,3},{3,2},{4,5},{5,4},{6,7},{7,6},{8,9},{9,8},{10,11... | collective-permute-start | bytes 73736 | tf_op jit(solution)/shard_map/ppermute | solution.py:26
  40.1 6.0 %collective-permute-start.11 = (bf16[3,1,32,128]{3,2,1,0:T(8,128)(2,1)S(1)}, bf16[3,1,32,128]{3,2,1,0:T(8,128)(2,1)S(1)}, u32[]{:S(2)}, u32[]{:S(2)}) collective-permute-start(bf16[3,1,32,128]{3,2,1,0:T(8,128)(2,1)S(1)} %pad_maximum_fusion.18), channel_id=1, source_target_pairs={{1,2},{2,1},{3,4},{4,3},{5,6},{6,5},{9,10},{10,9},{11,12},{12,11},... | collective-permute-start | bytes 73736 | tf_op jit(solution)/shard_map/ppermute | solution.py:27
  47.4 1.6 %copy-start.2 = (f32[16,16,12,128]{3,2,1,0:T(8,128)S(1)}, f32[16,16,12,128]{3,2,1,0:T(8,128)}, u32[]{:S(2)}) copy-start(f32[16,16,12,128]{3,2,1,0:T(8,128)} %copy-done.1) | copy-start | bytes 4718596
  50.0 1.3 %copy-start.5 = (bf16[18,18,12,64]{3,2,1,0:T(8,128)(2,1)S(1)}, bf16[18,18,12,64]{3,2,1,0:T(8,128)(2,1)}, u32[]{:S(2)}) copy-start(bf16[18,18,12,64]{3,2,1,0:T(8,128)(2,1)} %copy-done.4) | copy-start | bytes 1492996
  55.9 4.2 %collective-permute-start.12 = (f32[512,128]{1,0:T(8,128)S(1)}, f32[512,128]{1,0:T(8,128)S(1)}, u32[]{:S(2)}, u32[]{:S(2)}) collective-permute-start(f32[512,128]{1,0:T(8,128)S(1)} %pad_maximum_fusion.3), channel_id=1, source_target_pairs={{0,1},{1,0},{2,3},{3,2},{4,5},{5,4},{6,7},{7,6},{8,9},{9,8},{10,11... | collective-permute-start | bytes 786440 | tf_op jit(solution)/shard_map/ppermute | solution.py:40
  56.1 6.4 %collective-permute-start.15 = (bf16[16,1,1536]{2,1,0:T(2,128)(2,1)S(1)}, bf16[16,1,1536]{2,1,0:T(2,128)(2,1)S(1)}, u32[]{:S(2)}, u32[]{:S(2)}) collective-permute-start(bf16[16,1,1536]{2,1,0:T(2,128)(2,1)S(1)} %get-tuple-element.32), channel_id=1, source_target_pairs={{1,2},{2,1},{3,4},{4,3},{5,6},{6,5},{9,10},{10,9},{11,12},{12,11},... | collective-permute-start | bytes 147464 | tf_op jit(solution)/shard_map/ppermute | solution.py:61
  60.3 3.9 %collective-permute-start.13 = (f32[160,128]{1,0:T(8,128)S(1)}, f32[160,128]{1,0:T(8,128)S(1)}, u32[]{:S(2)}, u32[]{:S(2)}) collective-permute-start(f32[160,128]{1,0:T(8,128)S(1)} %slice_select_fusion.1), channel_id=1, source_target_pairs={{0,2},{1,3},{2,0},{3,1},{4,6},{5,7},{6,4},{7,5},{8,10},{9,11},{10,... | collective-permute-start | bytes 245768 | tf_op jit(solution)/shard_map/ppermute | solution.py:40
  64.2 4.9 %collective-permute-start.14 = (f32[160,128]{1,0:T(8,128)S(1)}, f32[160,128]{1,0:T(8,128)S(1)}, u32[]{:S(2)}, u32[]{:S(2)}) collective-permute-start(f32[160,128]{1,0:T(8,128)S(1)} %select_add_fusion), channel_id=1, source_target_pairs={{0,4},{1,5},{2,6},{3,7},{4,0},{5,1},{6,2},{7,3},{8,12},{9,13},{10,... | collective-permute-start | bytes 245768 | tf_op jit(solution)/shard_map/ppermute | solution.py:40
  69.1 9.4 %collective-permute-start.16 = (f32[376,128]{1,0:T(8,128)S(1)}, f32[376,128]{1,0:T(8,128)S(1)}, u32[]{:S(2)}, u32[]{:S(2)}) collective-permute-start(f32[376,128]{1,0:T(8,128)S(1)} %pad_maximum_fusion.5), channel_id=1, source_target_pairs={{0,8},{8,0},{16,24},{24,16},{32,40},{40,32},{48,56},{56,48},{64,72... | collective-permute-start | bytes 577544 | tf_op jit(solution)/shard_map/ppermute | solution.py:40
  75.0 7.7 %collective-permute-start.17 = (bf16[1,18,1536]{2,1,0:T(8,128)(2,1)S(1)}, bf16[1,18,1536]{2,1,0:T(8,128)(2,1)S(1)}, u32[]{:S(2)}, u32[]{:S(2)}) collective-permute-start(bf16[1,18,1536]{2,1,0:T(8,128)(2,1)S(1)} %broadcast_select_fusion.13), channel_id=1, source_target_pairs={{8,16},{16,8},{24,32},{32,24},{40,48},{48,40},{56,64},{64,56},{72,... | collective-permute-start | bytes 165896 | tf_op jit(solution)/shard_map/ppermute | solution.py:61
  78.7 6.1 %collective-permute-start.18 = (f32[160,128]{1,0:T(8,128)S(1)}, f32[160,128]{1,0:T(8,128)S(1)}, u32[]{:S(2)}, u32[]{:S(2)}) collective-permute-start(f32[160,128]{1,0:T(8,128)S(1)} %slice_add_fusion.1), channel_id=1, source_target_pairs={{0,16},{8,24},{16,0},{24,8},{32,48},{40,56},{48,32},{56,40},{64,80... | collective-permute-start | bytes 245768 | tf_op jit(solution)/shard_map/ppermute | solution.py:40
  84.8 6.1 %collective-permute-start.19 = (f32[160,128]{1,0:T(8,128)S(1)}, f32[160,128]{1,0:T(8,128)S(1)}, u32[]{:S(2)}, u32[]{:S(2)}) collective-permute-start(f32[160,128]{1,0:T(8,128)S(1)} %add.137), channel_id=1, source_target_pairs={{0,32},{8,40},{16,48},{24,56},{32,0},{40,8},{48,16},{56,24},{64,96... | collective-permute-start | bytes 245768 | tf_op jit(solution)/shard_map/ppermute | solution.py:40
  91.0 5.5 %collective-permute-start.20 = (f32[160,128]{1,0:T(8,128)S(1)}, f32[160,128]{1,0:T(8,128)S(1)}, u32[]{:S(2)}, u32[]{:S(2)}) collective-permute-start(f32[160,128]{1,0:T(8,128)S(1)} %add.138), channel_id=1, source_target_pairs={{0,64},{8,72},{16,80},{24,88},{32,96},{40,104},{48,112},{56,120},{... | collective-permute-start | bytes 245768 | tf_op jit(solution)/shard_map/ppermute | solution.py:40
  96.5 4.6 %collective-permute-start.21 = (f32[160,128]{1,0:T(8,128)S(1)}, f32[160,128]{1,0:T(8,128)S(1)}, u32[]{:S(2)}, u32[]{:S(2)}) collective-permute-start(f32[160,128]{1,0:T(8,128)S(1)} %add.139), channel_id=1, source_target_pairs={{0,2},{1,3},{2,0},{3,1},{4,6},{5,7},{6,4},{7,5},{8,10},{9,11},{10,... | collective-permute-start | bytes 245768 | tf_op jit(solution)/shard_map/ppermute | solution.py:40
  101.1 7.4 %collective-permute-start.22 = (f32[320,128]{1,0:T(8,128)S(1)}, f32[320,128]{1,0:T(8,128)S(1)}, u32[]{:S(2)}, u32[]{:S(2)}) collective-permute-start(f32[320,128]{1,0:T(8,128)S(1)} %maximum_select_fusion.2), channel_id=1, source_target_pairs={{0,1},{1,0},{2,3},{3,2},{4,5},{5,4},{6,7},{7,6},{8,9},{9,8},{10,11... | collective-permute-start | bytes 491528 | tf_op jit(solution)/shard_map/ppermute | solution.py:40

commit v12 on v9

--- a/solution.py
+++ b/solution.py
@@ -21,11 +21,12 @@
     for axis, dim in sides:
         count = lax.axis_size(axis)
         odd = lax.axis_index(axis) % 2 == 1
-        head = lax.slice_in_dim(cells, 0, width, axis=dim)
-        tail = lax.slice_in_dim(cells, cells.shape[dim] - width, cells.shape[dim], axis=dim)
-        inner = lax.ppermute(jnp.where(odd, head, tail), axis, [(i, i ^ 1) for i in range(count)])
+        last = cells.shape[dim] - width
+        inner_piece = lax.dynamic_slice_in_dim(cells, jnp.where(odd, 0, last), width, axis=dim)
+        outer_piece = lax.dynamic_slice_in_dim(cells, jnp.where(odd, last, 0), width, axis=dim)
+        inner = lax.ppermute(inner_piece, axis, [(i, i ^ 1) for i in range(count)])
         outer = lax.ppermute(
-            jnp.where(odd, tail, head),
+            outer_piece,
             axis,
             [pair for k in range(1, count - 1, 2) for pair in ((k, k + 1), (k + 1, k))],
         )
@@ -51,9 +52,12 @@
 
 def halo_ends(cells, axis, dim):
     odd = lax.axis_index(axis) % 2 == 1
-    head = lax.slice_in_dim(cells, 0, 1, axis=dim)
-    tail = lax.slice_in_dim(cells, cells.shape[dim] - 1, cells.shape[dim], axis=dim)
-    return odd, jnp.where(odd, head, tail), jnp.where(odd, tail, head)
+    last = cells.shape[dim] - 1
+    return (
+        odd,
+        lax.dynamic_slice_in_dim(cells, jnp.where(odd, 0, last), 1, axis=dim),
+        lax.dynamic_slice_in_dim(cells, jnp.where(odd, last, 0), 1, axis=dim),
+    )
 
 
 def outer_swap(piece, axis):

time: 111 us -> 111 us (level)
    select_n x6 -> x0, other arithmetic: 2.08 us -> none  [the longest x4 1.98 us: with_halo(): jnp.where(odd, head, tail)]
where the time goes in v12:
time: 111 us
  starting transfers between devices  59.7 us (54%)
  local copies, waits for them, and re-layouts  16.9 us (15%)
  waiting for transfers between devices  14 us (13%)
  matrix products  12.6 us (11%)
  other arithmetic  6.14 us (6%)
  between operations  1.48 us (1%)
    ppermute x9, starting transfers between devices, exchange(): return lax.ppermute(value, axis, [(i, i ^ bit) for i in range(size)])  27.9 us
    ppermute x6, starting transfers between devices, with_halo(): lax.ppermute(outer_piece, axis, [pair for k in range(1, count - 1, 2) for...  13.8 us
    ppermute x6, starting transfers between devices, with_halo(): inner = lax.ppermute(inner_piece, axis, [(i, i ^ 1) for i in range(count)])  13.3 us
    unnamed x30, local copies, waits for them, and re-layouts  8.07 us
    ppermute x9, waiting for transfers between devices, exchange(): return lax.ppermute(value, axis, [(i, i ^ bit) for i in range(size)])  7.68 us
    ppermute x2, starting transfers between devices, outer_swap(): lax.ppermute(piece, axis, [pair for k in range(1, count - 1, 2) for pair...  4.73 us
    ppermute x6, waiting for transfers between devices, with_halo(): lax.ppermute(outer_piece, axis, [pair for k in range(1, count - 1, 2) for...  4.67 us
    slice x1, local copies, waits for them, and re-layouts, transposed_conv(): padded_grad[2 - row_tap:2 - row_tap + out_rows, 2 - col_tap:2 - col_tap +...  2.81 us
  transfers between devices with their start and end apart: 23, of which 12 were waited for; matrix products, arithmetic and copies ran while one was open for 12% of the time, Pallas kernels for 0%

profile of v12, /device:TPU:1, one launch (start us, length us, event | category | flops | bytes accessed | tf_op | source)
XLA Modules:
  0.0 110.9 jit_solution(11136811231646713407)
XLA Ops:
  1.5 2.0 %collective-permute-start = (bf16[1,16,768]{2,1,0:T(8,128)(2,1)S(1)}, bf16[1,16,768]{2,1,0:T(8,128)(2,1)S(1)}, u32[]{:S(2)}, u32[]{:S(2)}) collective-permute-start(bf16[1,16,768]{2,1,0:T(8,128)(2,1)S(1)} %get-tuple-element.31), channel_id=1, source_target_pairs={{0,8},{8,0},{16,24},{24,16},{32,40},{40,32},{48,56},{56,48},{64,72... | collective-permute-start | bytes 73736 | tf_op jit(solution)/shard_map/ppermute | solution.py:27
  4.2 0.9 copy.68
  6.3 1.1 pad_maximum_fusion.3
  7.5 1.0 collective-permute-start.2
  8.5 3.1 %collective-permute-start.3 = (bf16[18,1,768]{2,1,0:T(2,128)(2,1)S(1)}, bf16[18,1,768]{2,1,0:T(2,128)(2,1)S(1)}, u32[]{:S(2)}, u32[]{:S(2)}) collective-permute-start(bf16[18,1,768]{2,1,0:T(2,128)(2,1)S(1)} %get-tuple-element.30), channel_id=1, source_target_pairs={{1,2},{2,1},{3,4},{4,3},{5,6},{6,5},{9,10},{10,9},{11,12},{12,11},... | collective-permute-start | bytes 82952 | tf_op jit(solution)/shard_map/ppermute | solution.py:28
  11.8 2.2 %collective-permute-done.3 = bf16[18,1,768]{2,1,0:T(2,128)(2,1)S(1)} collective-permute-done((bf16[18,1,768]{2,1,0:T(2,128)(2,1)S(1)}, bf16[18,1,768]{2,1,0:T(2,128)(2,1)S(1)}, u32[]{:S(2)}, u32[]{:S(2)}) %collective-permute-start.3) | collective-permute-done | bytes 27680 | tf_op jit(solution)/shard_map/ppermute | solution.py:28
  15.3 1.1 copy-done.4
  16.3 1.6 %fusion.73 = f32[16,16,12,128]{3,2,1,0:T(8,128)S(1)} fusion(bf16[18,18,12,64]{3,2,1,0:T(8,128)(2,1)S(1)} %reshape.208, bf16[3,3,64,128]{3,2,1,0:T(8,128)(2,1)S(1)} %copy-done.6), kind=kOutput, calls=%fused_computation.179 | convolution fusion | flops 452984832 | bytes 2217984 | tf_op jit(solution)/shard_map/conv_general_dilated | solution.py:138
  20.7 3.7 %collective-permute-start.4 = (bf16[1,3,32,128]{3,2,1,0:T(8,128)(2,1)S(1)}, bf16[1,3,32,128]{3,2,1,0:T(8,128)(2,1)S(1)}, u32[]{:S(2)}, u32[]{:S(2)}) collective-permute-start(bf16[1,3,32,128]{3,2,1,0:T(8,128)(2,1)S(1)} %get-tuple-element.52), channel_id=1, source_target_pairs={{0,8},{8,0},{16,24},{24,16},{32,40},{40,32},{48,56},{56,48},{64,72... | collective-permute-start | bytes 73736 | tf_op jit(solution)/shard_map/ppermute | solution.py:27
  25.8 4.0 %collective-permute-start.7 = (bf16[5,1,32,128]{3,2,1,0:T(8,128)(2,1)S(1)}, bf16[5,1,32,128]{3,2,1,0:T(8,128)(2,1)S(1)}, u32[]{:S(2)}, u32[]{:S(2)}) collective-permute-start(bf16[5,1,32,128]{3,2,1,0:T(8,128)(2,1)S(1)} %get-tuple-element.47), channel_id=1, source_target_pairs={{1,2},{2,1},{3,4},{4,3},{5,6},{6,5},{9,10},{10,9},{11,12},{12,11},... | collective-permute-start | bytes 122888 | tf_op jit(solution)/shard_map/ppermute | solution.py:28
  30.0 1.6 %collective-permute-done.7 = bf16[5,1,32,128]{3,2,1,0:T(8,128)(2,1)S(1)} collective-permute-done((bf16[5,1,32,128]{3,2,1,0:T(8,128)(2,1)S(1)}, bf16[5,1,32,128]{3,2,1,0:T(8,128)(2,1)S(1)}, u32[]{:S(2)}, u32[]{:S(2)}) %collective-permute-start.7) | collective-permute-done | bytes 40992 | tf_op jit(solution)/shard_map/ppermute | solution.py:28
  32.6 6.3 %collective-permute-start.8 = (bf16[1,1,32,128]{3,2,1,0:T(8,128)(2,1)S(1)}, bf16[1,1,32,128]{3,2,1,0:T(8,128)(2,1)S(1)}, u32[]{:S(2)}, u32[]{:S(2)}) collective-permute-start(bf16[1,1,32,128]{3,2,1,0:T(8,128)(2,1)S(1)} %fusion.53), channel_id=1, source_target_pairs={{0,8},{8,0},{16,24},{24,16},{32,40},{40,32},{48,56},{56,48},{64,72... | collective-permute-start | bytes 24584 | tf_op jit(solution)/shard_map/ppermute | solution.py:27
  40.1 4.7 %collective-permute-start.11 = (bf16[3,1,32,128]{3,2,1,0:T(8,128)(2,1)S(1)}, bf16[3,1,32,128]{3,2,1,0:T(8,128)(2,1)S(1)}, u32[]{:S(2)}, u32[]{:S(2)}) collective-permute-start(bf16[3,1,32,128]{3,2,1,0:T(8,128)(2,1)S(1)} %pad_maximum_fusion.11), channel_id=1, source_target_pairs={{1,2},{2,1},{3,4},{4,3},{5,6},{6,5},{9,10},{10,9},{11,12},{12,11},... | collective-permute-start | bytes 73736 | tf_op jit(solution)/shard_map/ppermute | solution.py:28
  45.2 0.9 collective-permute-done.11
  47.8 1.2 %copy-done.2 = f32[16,16,12,128]{3,2,1,0:T(8,128)S(1)} copy-done((f32[16,16,12,128]{3,2,1,0:T(8,128)S(1)}, f32[16,16,12,128]{3,2,1,0:T(8,128)}, u32[]{:S(2)}) %copy-start.2) | copy-done | bytes 1572888
  49.0 1.0 multiply_convert_fusion
  50.1 1.3 %copy-done.5 = bf16[18,18,12,64]{3,2,1,0:T(8,128)(2,1)S(1)} copy-done((bf16[18,18,12,64]{3,2,1,0:T(8,128)(2,1)S(1)}, bf16[18,18,12,64]{3,2,1,0:T(8,128)(2,1)}, u32[]{:S(2)}) %copy-start.5) | copy-done | bytes 497688
  51.3 2.6 %fusion.20 = f32[3,3,64,128]{3,2,1,0:T(8,128)S(1)} fusion(bf16[18,18,12,64]{3,2,1,0:T(8,128)(2,1)S(1)} %copy-done.5, bf16[16,16,12,128]{3,1,2,0:T(8,128)(2,1)S(1)} %multiply_convert_fusion), kind=kOutput, calls=%fused_computation.35 | convolution fusion | flops 452984832 | bytes 1579008 | tf_op jit(solution)/shard_map/conv_general_dilated | solution.py:285
  56.0 4.1 %collective-permute-start.15 = (bf16[16,1,1536]{2,1,0:T(2,128)(2,1)S(1)}, bf16[16,1,1536]{2,1,0:T(2,128)(2,1)S(1)}, u32[]{:S(2)}, u32[]{:S(2)}) collective-permute-start(bf16[16,1,1536]{2,1,0:T(2,128)(2,1)S(1)} %get-tuple-element.28), channel_id=1, source_target_pairs={{1,2},{2,1},{3,4},{4,3},{5,6},{6,5},{9,10},{10,9},{11,12},{12,11},... | collective-permute-start | bytes 147464 | tf_op jit(solution)/shard_map/ppermute | solution.py:65
  60.3 1.4 %collective-permute-start.13 = (f32[160,128]{1,0:T(8,128)S(1)}, f32[160,128]{1,0:T(8,128)S(1)}, u32[]{:S(2)}, u32[]{:S(2)}) collective-permute-start(f32[160,128]{1,0:T(8,128)S(1)} %slice_select_fusion.1), channel_id=1, source_target_pairs={{0,2},{1,3},{2,0},{3,1},{4,6},{5,7},{6,4},{7,5},{8,10},{9,11},{10,... | collective-permute-start | bytes 245768 | tf_op jit(solution)/shard_map/ppermute | solution.py:41
  63.2 1.0 collective-permute-done.13
  64.2 3.0 %collective-permute-start.14 = (f32[160,128]{1,0:T(8,128)S(1)}, f32[160,128]{1,0:T(8,128)S(1)}, u32[]{:S(2)}, u32[]{:S(2)}) collective-permute-start(f32[160,128]{1,0:T(8,128)S(1)} %select_add_fusion), channel_id=1, source_target_pairs={{0,4},{1,5},{2,6},{3,7},{4,0},{5,1},{6,2},{7,3},{8,12},{9,13},{10,... | collective-permute-start | bytes 245768 | tf_op jit(solution)/shard_map/ppermute | solution.py:41
  67.2 1.9 %collective-permute-done.14 = f32[160,128]{1,0:T(8,128)S(1)} collective-permute-done((f32[160,128]{1,0:T(8,128)S(1)}, f32[160,128]{1,0:T(8,128)S(1)}, u32[]{:S(2)}, u32[]{:S(2)}) %collective-permute-start.14) | collective-permute-done | bytes 81952 | tf_op jit(solution)/shard_map/ppermute | solution.py:41
  69.1 5.8 %collective-permute-start.16 = (f32[376,128]{1,0:T(8,128)S(1)}, f32[376,128]{1,0:T(8,128)S(1)}, u32[]{:S(2)}, u32[]{:S(2)}) collective-permute-start(f32[376,128]{1,0:T(8,128)S(1)} %pad_maximum_fusion.6), channel_id=1, source_target_pairs={{0,8},{8,0},{16,24},{24,16},{32,40},{40,32},{48,56},{56,48},{64,72... | collective-permute-start | bytes 577544 | tf_op jit(solution)/shard_map/ppermute | solution.py:41
  75.6 2.9 %collective-permute-done.16 = f32[376,128]{1,0:T(8,128)S(1)} collective-permute-done((f32[376,128]{1,0:T(8,128)S(1)}, f32[376,128]{1,0:T(8,128)S(1)}, u32[]{:S(2)}, u32[]{:S(2)}) %collective-permute-start.16) | collective-permute-done | bytes 192544 | tf_op jit(solution)/shard_map/ppermute | solution.py:41
  78.6 4.0 %collective-permute-start.18 = (f32[160,128]{1,0:T(8,128)S(1)}, f32[160,128]{1,0:T(8,128)S(1)}, u32[]{:S(2)}, u32[]{:S(2)}) collective-permute-start(f32[160,128]{1,0:T(8,128)S(1)} %slice_add_fusion.1), channel_id=1, source_target_pairs={{0,16},{8,24},{16,0},{24,8},{32,48},{40,56},{48,32},{56,40},{64,80... | collective-permute-start | bytes 245768 | tf_op jit(solution)/shard_map/ppermute | solution.py:41
  84.8 2.7 %collective-permute-start.19 = (f32[160,128]{1,0:T(8,128)S(1)}, f32[160,128]{1,0:T(8,128)S(1)}, u32[]{:S(2)}, u32[]{:S(2)}) collective-permute-start(f32[160,128]{1,0:T(8,128)S(1)} %add.156), channel_id=1, source_target_pairs={{0,32},{8,40},{16,48},{24,56},{32,0},{40,8},{48,16},{56,24},{64,96... | collective-permute-start | bytes 245768 | tf_op jit(solution)/shard_map/ppermute | solution.py:41
  87.5 2.8 %fusion.71 = (bf16[16,16,12,128]{3,2,1,0:T(8,128)(2,1)S(1)}, bf16[16,16,12,128]{3,2,1,0:T(8,128)(2,1)S(1)}, bf16[16,16,12,128]{3,2,1,0:T(8,128)(2,1)S(1)}, bf16[...) fusion(bf16[18,18,12,128]{3,2,1,0:T(8,128)(2,1)S(1)} %reshape.218), kind=kLoop, calls=%fused_computation.177 | loop fusion | bytes 14155776 | tf_op jit(solution)/shard_map/slice | solution.py:153
  90.9 3.5 %collective-permute-start.20 = (f32[160,128]{1,0:T(8,128)S(1)}, f32[160,128]{1,0:T(8,128)S(1)}, u32[]{:S(2)}, u32[]{:S(2)}) collective-permute-start(f32[160,128]{1,0:T(8,128)S(1)} %add.157), channel_id=1, source_target_pairs={{0,64},{8,72},{16,80},{24,88},{32,96},{40,104},{48,112},{56,120},{... | collective-permute-start | bytes 245768 | tf_op jit(solution)/shard_map/ppermute | solution.py:41
  96.5 2.7 %collective-permute-start.21 = (f32[160,128]{1,0:T(8,128)S(1)}, f32[160,128]{1,0:T(8,128)S(1)}, u32[]{:S(2)}, u32[]{:S(2)}) collective-permute-start(f32[160,128]{1,0:T(8,128)S(1)} %add.158), channel_id=1, source_target_pairs={{0,2},{1,3},{2,0},{3,1},{4,6},{5,7},{6,4},{7,5},{8,10},{9,11},{10,... | collective-permute-start | bytes 245768 | tf_op jit(solution)/shard_map/ppermute | solution.py:41
  101.1 4.9 %collective-permute-start.22 = (f32[320,128]{1,0:T(8,128)S(1)}, f32[320,128]{1,0:T(8,128)S(1)}, u32[]{:S(2)}, u32[]{:S(2)}) collective-permute-start(f32[320,128]{1,0:T(8,128)S(1)} %maximum_select_fusion.3), channel_id=1, source_target_pairs={{0,1},{1,0},{2,3},{3,2},{4,5},{5,4},{6,7},{7,6},{8,9},{9,8},{10,11... | collective-permute-start | bytes 491528 | tf_op jit(solution)/shard_map/ppermute | solution.py:41
  107.0 1.4 %reshape.219 = bf16[16,16,768]{2,1,0:T(8,128)(2,1)} reshape(bf16[16,16,12,64]{3,2,1,0:T(8,128)(2,1)S(1)} %copy.92) | data formatting | bytes 786432 | tf_op jit(solution)/shard_map/reshape | solution.py:314
  (143 shorter events, 27.2 us)
Async XLA Ops:
  0.6 31.3 %copy-start = (bf16[128,20]{0,1:T(8,128)(2,1)S(1)}, bf16[128,20]{0,1:T(8,128)(2,1)}, u32[]{:S(2)}) copy-start(bf16[128,20]{0,1:T(8,128)(2,1)} %param.11) | copy-start | bytes 15364
  0.6 13.4 %copy-start.3 = (bf16[16,16,768]{2,1,0:T(8,128)(2,1)S(1)}, bf16[16,16,768]{2,1,0:T(8,128)(2,1)}, u32[]{:S(2)}) copy-start(bf16[16,16,768]{2,1,0:T(8,128)(2,1)} %param.8) | copy-start | bytes 1179652
  0.7 11.0 %copy-start.7 = (s32[16,16]{1,0:T(8,128)S(1)}, s32[16,16]{1,0:T(8,128)}, u32[]{:S(2)}) copy-start(s32[16,16]{1,0:T(8,128)} %param.12) | copy-start | bytes 3076
  1.5 4.8 %collective-permute-start = (bf16[1,16,768]{2,1,0:T(8,128)(2,1)S(1)}, bf16[1,16,768]{2,1,0:T(8,128)(2,1)S(1)}, u32[]{:S(2)}, u32[]{:S(2)}) collective-permute-start(bf16[1,16,768]{2,1,0:T(8,128)(2,1)S(1)} %get-tuple-element.31), channel_id=1, source_target_pairs={{0,8},{8,0},{16,24},{24,16},{32,40},{40,32},{48,56},{56,48},{64,72... | collective-permute-start | bytes 73736 | tf_op jit(solution)/shard_map/ppermute | solution.py:27
  3.5 2.7 %collective-permute-start.1 = (bf16[1,16,768]{2,1,0:T(8,128)(2,1)S(1)}, bf16[1,16,768]{2,1,0:T(8,128)(2,1)S(1)}, u32[]{:S(2)}, u32[]{:S(2)}) collective-permute-start(bf16[1,16,768]{2,1,0:T(8,128)(2,1)S(1)} %get-tuple-element.32), channel_id=1, source_target_pairs={{8,16},{16,8},{24,32},{32,24},{40,48},{48,40},{56,64},{64,56},{72,... | collective-permute-start | bytes 73736 | tf_op jit(solution)/shard_map/ppermute | solution.py:28
  7.5 4.3 %collective-permute-start.2 = (bf16[18,1,768]{2,1,0:T(2,128)(2,1)S(1)}, bf16[18,1,768]{2,1,0:T(2,128)(2,1)S(1)}, u32[]{:S(2)}, u32[]{:S(2)}) collective-permute-start(bf16[18,1,768]{2,1,0:T(2,128)(2,1)S(1)} %get-tuple-element.29), channel_id=1, source_target_pairs={{0,1},{1,0},{2,3},{3,2},{4,5},{5,4},{6,7},{7,6},{8,9},{9,8},{10,11... | collective-permute-start | bytes 82952 | tf_op jit(solution)/shard_map/ppermute | solution.py:27
  8.5 5.5 %collective-permute-start.3 = (bf16[18,1,768]{2,1,0:T(2,128)(2,1)S(1)}, bf16[18,1,768]{2,1,0:T(2,128)(2,1)S(1)}, u32[]{:S(2)}, u32[]{:S(2)}) collective-permute-start(bf16[18,1,768]{2,1,0:T(2,128)(2,1)S(1)} %get-tuple-element.30), channel_id=1, source_target_pairs={{1,2},{2,1},{3,4},{4,3},{5,6},{6,5},{9,10},{10,9},{11,12},{12,11},... | collective-permute-start | bytes 82952 | tf_op jit(solution)/shard_map/ppermute | solution.py:28
  14.1 2.2 %copy-start.6 = (bf16[3,3,64,128]{3,2,1,0:T(8,128)(2,1)S(1)}, bf16[3,3,64,128]{3,2,1,0:T(8,128)(2,1)}, u32[]{:S(2)}) copy-start(bf16[3,3,64,128]{3,2,1,0:T(8,128)(2,1)} %param.9) | copy-start | bytes 442372
  15.2 1.1 copy-start.4
  17.9 1.4 %copy-start.1 = (f32[16,16,12,128]{3,2,1,0:T(8,128)}, f32[16,16,12,128]{3,2,1,0:T(8,128)S(1)}, u32[]{:S(2)}) copy-start(f32[16,16,12,128]{3,2,1,0:T(8,128)S(1)} %fusion.73) | copy-start | bytes 4718596
  20.3 11.9 %copy-start.8 = (s32[1,1,32]{2,1,0:T(1,128)S(1)}, s32[1,1,32]{2,1,0:T(1,128)}, u32[]{:S(2)}) copy-start(s32[1,1,32]{2,1,0:T(1,128)} %param.15) | copy-start | bytes 388
  20.7 5.0 %collective-permute-start.4 = (bf16[1,3,32,128]{3,2,1,0:T(8,128)(2,1)S(1)}, bf16[1,3,32,128]{3,2,1,0:T(8,128)(2,1)S(1)}, u32[]{:S(2)}, u32[]{:S(2)}) collective-permute-start(bf16[1,3,32,128]{3,2,1,0:T(8,128)(2,1)S(1)} %get-tuple-element.52), channel_id=1, source_target_pairs={{0,8},{8,0},{16,24},{24,16},{32,40},{40,32},{48,56},{56,48},{64,72... | collective-permute-start | bytes 73736 | tf_op jit(solution)/shard_map/ppermute | solution.py:27
  24.4 1.2 %collective-permute-start.5 = (bf16[1,3,32,128]{3,2,1,0:T(8,128)(2,1)S(1)}, bf16[1,3,32,128]{3,2,1,0:T(8,128)(2,1)S(1)}, u32[]{:S(2)}, u32[]{:S(2)}) collective-permute-start(bf16[1,3,32,128]{3,2,1,0:T(8,128)(2,1)S(1)} %get-tuple-element.53), channel_id=1, source_target_pairs={{8,16},{16,8},{24,32},{32,24},{40,48},{48,40},{56,64},{64,56},{72,... | collective-permute-start | bytes 73736 | tf_op jit(solution)/shard_map/ppermute | solution.py:28
  25.7 4.2 %collective-permute-start.6 = (bf16[5,1,32,128]{3,2,1,0:T(8,128)(2,1)S(1)}, bf16[5,1,32,128]{3,2,1,0:T(8,128)(2,1)S(1)}, u32[]{:S(2)}, u32[]{:S(2)}) collective-permute-start(bf16[5,1,32,128]{3,2,1,0:T(8,128)(2,1)S(1)} %get-tuple-element.46), channel_id=1, source_target_pairs={{0,1},{1,0},{2,3},{3,2},{4,5},{5,4},{6,7},{7,6},{8,9},{9,8},{10,11... | collective-permute-start | bytes 122888 | tf_op jit(solution)/shard_map/ppermute | solution.py:27
  25.8 5.7 %collective-permute-start.7 = (bf16[5,1,32,128]{3,2,1,0:T(8,128)(2,1)S(1)}, bf16[5,1,32,128]{3,2,1,0:T(8,128)(2,1)S(1)}, u32[]{:S(2)}, u32[]{:S(2)}) collective-permute-start(bf16[5,1,32,128]{3,2,1,0:T(8,128)(2,1)S(1)} %get-tuple-element.47), channel_id=1, source_target_pairs={{1,2},{2,1},{3,4},{4,3},{5,6},{6,5},{9,10},{10,9},{11,12},{12,11},... | collective-permute-start | bytes 122888 | tf_op jit(solution)/shard_map/ppermute | solution.py:28
  32.6 7.3 %collective-permute-start.8 = (bf16[1,1,32,128]{3,2,1,0:T(8,128)(2,1)S(1)}, bf16[1,1,32,128]{3,2,1,0:T(8,128)(2,1)S(1)}, u32[]{:S(2)}, u32[]{:S(2)}) collective-permute-start(bf16[1,1,32,128]{3,2,1,0:T(8,128)(2,1)S(1)} %fusion.53), channel_id=1, source_target_pairs={{0,8},{8,0},{16,24},{24,16},{32,40},{40,32},{48,56},{56,48},{64,72... | collective-permute-start | bytes 24584 | tf_op jit(solution)/shard_map/ppermute | solution.py:27
  38.9 1.0 collective-permute-start.9
  40.0 5.2 %collective-permute-start.10 = (bf16[3,1,32,128]{3,2,1,0:T(8,128)(2,1)S(1)}, bf16[3,1,32,128]{3,2,1,0:T(8,128)(2,1)S(1)}, u32[]{:S(2)}, u32[]{:S(2)}) collective-permute-start(bf16[3,1,32,128]{3,2,1,0:T(8,128)(2,1)S(1)} %pad_maximum_fusion.11), channel_id=1, source_target_pairs={{0,1},{1,0},{2,3},{3,2},{4,5},{5,4},{6,7},{7,6},{8,9},{9,8},{10,11... | collective-permute-start | bytes 73736 | tf_op jit(solution)/shard_map/ppermute | solution.py:27
  40.1 6.0 %collective-permute-start.11 = (bf16[3,1,32,128]{3,2,1,0:T(8,128)(2,1)S(1)}, bf16[3,1,32,128]{3,2,1,0:T(8,128)(2,1)S(1)}, u32[]{:S(2)}, u32[]{:S(2)}) collective-permute-start(bf16[3,1,32,128]{3,2,1,0:T(8,128)(2,1)S(1)} %pad_maximum_fusion.11), channel_id=1, source_target_pairs={{1,2},{2,1},{3,4},{4,3},{5,6},{6,5},{9,10},{10,9},{11,12},{12,11},... | collective-permute-start | bytes 73736 | tf_op jit(solution)/shard_map/ppermute | solution.py:28
  47.4 1.6 %copy-start.2 = (f32[16,16,12,128]{3,2,1,0:T(8,128)S(1)}, f32[16,16,12,128]{3,2,1,0:T(8,128)}, u32[]{:S(2)}) copy-start(f32[16,16,12,128]{3,2,1,0:T(8,128)} %copy-done.1) | copy-start | bytes 4718596
  50.0 1.3 %copy-start.5 = (bf16[18,18,12,64]{3,2,1,0:T(8,128)(2,1)S(1)}, bf16[18,18,12,64]{3,2,1,0:T(8,128)(2,1)}, u32[]{:S(2)}) copy-start(bf16[18,18,12,64]{3,2,1,0:T(8,128)(2,1)} %copy-done.4) | copy-start | bytes 1492996
  55.9 4.2 %collective-permute-start.12 = (f32[512,128]{1,0:T(8,128)S(1)}, f32[512,128]{1,0:T(8,128)S(1)}, u32[]{:S(2)}, u32[]{:S(2)}) collective-permute-start(f32[512,128]{1,0:T(8,128)S(1)} %pad_maximum_fusion.4), channel_id=1, source_target_pairs={{0,1},{1,0},{2,3},{3,2},{4,5},{5,4},{6,7},{7,6},{8,9},{9,8},{10,11... | collective-permute-start | bytes 786440 | tf_op jit(solution)/shard_map/ppermute | solution.py:41
  56.0 6.4 %collective-permute-start.15 = (bf16[16,1,1536]{2,1,0:T(2,128)(2,1)S(1)}, bf16[16,1,1536]{2,1,0:T(2,128)(2,1)S(1)}, u32[]{:S(2)}, u32[]{:S(2)}) collective-permute-start(bf16[16,1,1536]{2,1,0:T(2,128)(2,1)S(1)} %get-tuple-element.28), channel_id=1, source_target_pairs={{1,2},{2,1},{3,4},{4,3},{5,6},{6,5},{9,10},{10,9},{11,12},{12,11},... | collective-permute-start | bytes 147464 | tf_op jit(solution)/shard_map/ppermute | solution.py:65
  60.3 3.9 %collective-permute-start.13 = (f32[160,128]{1,0:T(8,128)S(1)}, f32[160,128]{1,0:T(8,128)S(1)}, u32[]{:S(2)}, u32[]{:S(2)}) collective-permute-start(f32[160,128]{1,0:T(8,128)S(1)} %slice_select_fusion.1), channel_id=1, source_target_pairs={{0,2},{1,3},{2,0},{3,1},{4,6},{5,7},{6,4},{7,5},{8,10},{9,11},{10,... | collective-permute-start | bytes 245768 | tf_op jit(solution)/shard_map/ppermute | solution.py:41
  64.2 4.9 %collective-permute-start.14 = (f32[160,128]{1,0:T(8,128)S(1)}, f32[160,128]{1,0:T(8,128)S(1)}, u32[]{:S(2)}, u32[]{:S(2)}) collective-permute-start(f32[160,128]{1,0:T(8,128)S(1)} %select_add_fusion), channel_id=1, source_target_pairs={{0,4},{1,5},{2,6},{3,7},{4,0},{5,1},{6,2},{7,3},{8,12},{9,13},{10,... | collective-permute-start | bytes 245768 | tf_op jit(solution)/shard_map/ppermute | solution.py:41
  69.1 9.4 %collective-permute-start.16 = (f32[376,128]{1,0:T(8,128)S(1)}, f32[376,128]{1,0:T(8,128)S(1)}, u32[]{:S(2)}, u32[]{:S(2)}) collective-permute-start(f32[376,128]{1,0:T(8,128)S(1)} %pad_maximum_fusion.6), channel_id=1, source_target_pairs={{0,8},{8,0},{16,24},{24,16},{32,40},{40,32},{48,56},{56,48},{64,72... | collective-permute-start | bytes 577544 | tf_op jit(solution)/shard_map/ppermute | solution.py:41
  74.9 7.7 %collective-permute-start.17 = (bf16[1,18,1536]{2,1,0:T(8,128)(2,1)S(1)}, bf16[1,18,1536]{2,1,0:T(8,128)(2,1)S(1)}, u32[]{:S(2)}, u32[]{:S(2)}) collective-permute-start(bf16[1,18,1536]{2,1,0:T(8,128)(2,1)S(1)} %get-tuple-element.26), channel_id=1, source_target_pairs={{8,16},{16,8},{24,32},{32,24},{40,48},{48,40},{56,64},{64,56},{72,... | collective-permute-start | bytes 165896 | tf_op jit(solution)/shard_map/ppermute | solution.py:65
  78.6 6.1 %collective-permute-start.18 = (f32[160,128]{1,0:T(8,128)S(1)}, f32[160,128]{1,0:T(8,128)S(1)}, u32[]{:S(2)}, u32[]{:S(2)}) collective-permute-start(f32[160,128]{1,0:T(8,128)S(1)} %slice_add_fusion.1), channel_id=1, source_target_pairs={{0,16},{8,24},{16,0},{24,8},{32,48},{40,56},{48,32},{56,40},{64,80... | collective-permute-start | bytes 245768 | tf_op jit(solution)/shard_map/ppermute | solution.py:41
  84.8 6.1 %collective-permute-start.19 = (f32[160,128]{1,0:T(8,128)S(1)}, f32[160,128]{1,0:T(8,128)S(1)}, u32[]{:S(2)}, u32[]{:S(2)}) collective-permute-start(f32[160,128]{1,0:T(8,128)S(1)} %add.156), channel_id=1, source_target_pairs={{0,32},{8,40},{16,48},{24,56},{32,0},{40,8},{48,16},{56,24},{64,96... | collective-permute-start | bytes 245768 | tf_op jit(solution)/shard_map/ppermute | solution.py:41
  90.9 5.6 %collective-permute-start.20 = (f32[160,128]{1,0:T(8,128)S(1)}, f32[160,128]{1,0:T(8,128)S(1)}, u32[]{:S(2)}, u32[]{:S(2)}) collective-permute-start(f32[160,128]{1,0:T(8,128)S(1)} %add.157), channel_id=1, source_target_pairs={{0,64},{8,72},{16,80},{24,88},{32,96},{40,104},{48,112},{56,120},{... | collective-permute-start | bytes 245768 | tf_op jit(solution)/shard_map/ppermute | solution.py:41
  96.5 4.5 %collective-permute-start.21 = (f32[160,128]{1,0:T(8,128)S(1)}, f32[160,128]{1,0:T(8,128)S(1)}, u32[]{:S(2)}, u32[]{:S(2)}) collective-permute-start(f32[160,128]{1,0:T(8,128)S(1)} %add.158), channel_id=1, source_target_pairs={{0,2},{1,3},{2,0},{3,1},{4,6},{5,7},{6,4},{7,5},{8,10},{9,11},{10,... | collective-permute-start | bytes 245768 | tf_op jit(solution)/shard_map/ppermute | solution.py:41
  101.1 7.3 %collective-permute-start.22 = (f32[320,128]{1,0:T(8,128)S(1)}, f32[320,128]{1,0:T(8,128)S(1)}, u32[]{:S(2)}, u32[]{:S(2)}) collective-permute-start(f32[320,128]{1,0:T(8,128)S(1)} %maximum_select_fusion.3), channel_id=1, source_target_pairs={{0,1},{1,0},{2,3},{3,2},{4,5},{5,4},{6,7},{7,6},{8,9},{9,8},{10,11... | collective-permute-start | bytes 491528 | tf_op jit(solution)/shard_map/ppermute | solution.py:41

commit v13 on v9

--- a/solution.py
+++ b/solution.py
@@ -69,7 +69,7 @@
     )
 
 
-def butterfly_sum(flat, cells, halvings=2):
+def butterfly_sum(flat, cells, halvings=1):
     steps = []
     for axis in ("col", "row"):
         bit = 1

time: 111 us -> 116 us (1.045)
  waiting for transfers between devices: 14.4 us -> 22.1 us
  starting transfers between devices: 59.8 us -> 55.8 us
  local copies, waits for them, and re-layouts: 16 us -> 13.4 us
  matrix products: 12.6 us -> 14.9 us
  other arithmetic: 6.67 us -> 8.11 us
    ppermute x9 -> x8, waiting for transfers between devices: 8.14 us -> 16.2 us  [exchange(): return lax.ppermute(value, axis, [(i, i ^ bit) for i in range(size)])]
    ppermute x9 -> x8, starting transfers between devices: 28 us -> 23.7 us  [exchange(): return lax.ppermute(value, axis, [(i, i ^ bit) for i in range(size)])]
    unnamed x30 -> x26, local copies, waits for them, and re-layouts: 8.06 us -> 5.52 us
    convert_element_type x1, other arithmetic: 0.59 us -> 2.01 us  [per_device(): ((pixel_grad / DATES)[:, :, None, :] * silu_slope(mixed_time)).astype(jnp...]
    dot_general x3, matrix products: 1.37 us -> 2.55 us  [per_device(): jnp.dot(padded_hidden[:, :, time_tap:time_tap + DATES], dense_time[time_t...]
  transfers between devices with their start and end apart: 23 -> 22, of which waited for: 12 -> 11; matrix products, arithmetic and copies ran while one was open for 12% -> 11% of each run, Pallas kernels for 0% -> 0%
where the time goes in v13:
time: 116 us
  starting transfers between devices  55.8 us (48%)
  waiting for transfers between devices  22.1 us (19%)
  matrix products  14.9 us (13%)
  local copies, waits for them, and re-layouts  13.4 us (12%)
  other arithmetic  8.11 us (7%)
  between operations  1.38 us (1%)
    ppermute x8, starting transfers between devices, exchange(): return lax.ppermute(value, axis, [(i, i ^ bit) for i in range(size)])  23.7 us
    ppermute x8, waiting for transfers between devices, exchange(): return lax.ppermute(value, axis, [(i, i ^ bit) for i in range(size)])  16.2 us
    ppermute x6, starting transfers between devices, with_halo(): lax.ppermute(jnp.where(odd, tail, head), axis, [pair for k in range(1, co...  14.5 us
    ppermute x6, starting transfers between devices, with_halo(): lax.ppermute(jnp.where(odd, head, tail), axis, [(i, i ^ 1) for i in range...  12.8 us
    unnamed x26, local copies, waits for them, and re-layouts  5.52 us
    ppermute x2, starting transfers between devices, outer_swap(): lax.ppermute(piece, axis, [pair for k in range(1, count - 1, 2) for pair...  4.75 us
    ppermute x6, waiting for transfers between devices, with_halo(): lax.ppermute(jnp.where(odd, tail, head), axis, [pair for k in range(1, co...  4.12 us
    slice x1, local copies, waits for them, and re-layouts, transposed_conv(): padded_grad[2 - row_tap:2 - row_tap + out_rows, 2 - col_tap:2 - col_tap +...  2.8 us
  transfers between devices with their start and end apart: 22, of which 11 were waited for; matrix products, arithmetic and copies ran while one was open for 11% of the time, Pallas kernels for 0%

profile of v13, /device:TPU:1, one launch (start us, length us, event | category | flops | bytes accessed | tf_op | source)
XLA Modules:
  0.0 115.7 jit_solution(4448831968346308192)
XLA Ops:
  1.5 2.0 %collective-permute-start = (bf16[1,16,768]{2,1,0:T(8,128)(2,1)S(1)}, bf16[1,16,768]{2,1,0:T(8,128)(2,1)S(1)}, u32[]{:S(2)}, u32[]{:S(2)}) collective-permute-start(bf16[1,16,768]{2,1,0:T(8,128)(2,1)S(1)} %get-tuple-element.33), channel_id=1, source_target_pairs={{0,8},{8,0},{16,24},{24,16},{32,40},{40,32},{48,56},{56,48},{64,72... | collective-permute-start | bytes 73736 | tf_op jit(solution)/shard_map/ppermute | solution.py:26
  4.2 0.9 copy.68
  6.3 1.1 broadcast_select_fusion.7
  7.5 4.0 %collective-permute-start.3 = (bf16[18,1,768]{2,1,0:T(2,128)(2,1)S(1)}, bf16[18,1,768]{2,1,0:T(2,128)(2,1)S(1)}, u32[]{:S(2)}, u32[]{:S(2)}) collective-permute-start(bf16[18,1,768]{2,1,0:T(2,128)(2,1)S(1)} %broadcast_select_fusion.6), channel_id=1, source_target_pairs={{1,2},{2,1},{3,4},{4,3},{5,6},{6,5},{9,10},{10,9},{11,12},{12,11},... | collective-permute-start | bytes 82952 | tf_op jit(solution)/shard_map/ppermute | solution.py:27
  11.8 1.6 %collective-permute-done.3 = bf16[18,1,768]{2,1,0:T(2,128)(2,1)S(1)} collective-permute-done((bf16[18,1,768]{2,1,0:T(2,128)(2,1)S(1)}, bf16[18,1,768]{2,1,0:T(2,128)(2,1)S(1)}, u32[]{:S(2)}, u32[]{:S(2)}) %collective-permute-start.3) | collective-permute-done | bytes 27680 | tf_op jit(solution)/shard_map/ppermute | solution.py:27
  14.7 1.1 copy-done.2
  15.7 2.5 %fusion.74 = f32[16,16,12,128]{3,2,1,0:T(8,128)S(1)} fusion(bf16[18,18,12,64]{3,2,1,0:T(8,128)(2,1)S(1)} %reshape.214, bf16[3,3,64,128]{3,2,1,0:T(8,128)(2,1)} %param.9), kind=kOutput, calls=%fused_computation.183 | convolution fusion | flops 452984832 | bytes 2217984 | tf_op jit(solution)/shard_map/conv_general_dilated | solution.py:134
  19.7 1.8 %multiply_reduce_fusion = (f32[16,16,128]{2,1,0:T(8,128)S(1)}, f32[16,16,12,128]{3,1,2,0:T(8,128)}) fusion(bf16[16,16,12,128]{3,1,2,0:T(8,128)(2,1)S(1)} %multiply_convert_fusion.2, bf16[3,128,128]{2,1,0:T(8,128)(2,1)S(1)} %broadcast_select_fusion.8, f32[16,16,12,128]{3,1,2,0:T(8,128)S(1)} %fusion.50, f32[16,16,12,128]{3,1,2,0:T(8,128)S(1)} %fusion.52), kind=kOutput, calls=%fused_computation.21 | convolution fusion | flops 94994432 | bytes 5668864 | tf_op jit(solution)/shard_map/dot_general | solution.py:196
  21.9 3.7 %collective-permute-start.4 = (bf16[1,3,32,128]{3,2,1,0:T(8,128)(2,1)S(1)}, bf16[1,3,32,128]{3,2,1,0:T(8,128)(2,1)S(1)}, u32[]{:S(2)}, u32[]{:S(2)}) collective-permute-start(bf16[1,3,32,128]{3,2,1,0:T(8,128)(2,1)S(1)} %bitcast.153), channel_id=1, source_target_pairs={{0,8},{8,0},{16,24},{24,16},{32,40},{40,32},{48,56},{56,48},{64,72... | collective-permute-start | bytes 73736 | tf_op jit(solution)/shard_map/ppermute | solution.py:26
  27.5 3.9 %collective-permute-start.7 = (bf16[5,1,32,128]{3,2,1,0:T(8,128)(2,1)S(1)}, bf16[5,1,32,128]{3,2,1,0:T(8,128)(2,1)S(1)}, u32[]{:S(2)}, u32[]{:S(2)}) collective-permute-start(bf16[5,1,32,128]{3,2,1,0:T(8,128)(2,1)S(1)} %get-tuple-element.49), channel_id=1, source_target_pairs={{1,2},{2,1},{3,4},{4,3},{5,6},{6,5},{9,10},{10,9},{11,12},{12,11},... | collective-permute-start | bytes 122888 | tf_op jit(solution)/shard_map/ppermute | solution.py:27
  31.5 1.6 %collective-permute-done.7 = bf16[5,1,32,128]{3,2,1,0:T(8,128)(2,1)S(1)} collective-permute-done((bf16[5,1,32,128]{3,2,1,0:T(8,128)(2,1)S(1)}, bf16[5,1,32,128]{3,2,1,0:T(8,128)(2,1)S(1)}, u32[]{:S(2)}, u32[]{:S(2)}) %collective-permute-start.7) | collective-permute-done | bytes 40992 | tf_op jit(solution)/shard_map/ppermute | solution.py:27
  34.2 6.4 %collective-permute-start.8 = (bf16[1,1,32,128]{3,2,1,0:T(8,128)(2,1)S(1)}, bf16[1,1,32,128]{3,2,1,0:T(8,128)(2,1)S(1)}, u32[]{:S(2)}, u32[]{:S(2)}) collective-permute-start(bf16[1,1,32,128]{3,2,1,0:T(8,128)(2,1)S(1)} %fusion.54), channel_id=1, source_target_pairs={{0,8},{8,0},{16,24},{24,16},{32,40},{40,32},{48,56},{56,48},{64,72... | collective-permute-start | bytes 24584 | tf_op jit(solution)/shard_map/ppermute | solution.py:26
  41.8 4.6 %collective-permute-start.11 = (bf16[3,1,32,128]{3,2,1,0:T(8,128)(2,1)S(1)}, bf16[3,1,32,128]{3,2,1,0:T(8,128)(2,1)S(1)}, u32[]{:S(2)}, u32[]{:S(2)}) collective-permute-start(bf16[3,1,32,128]{3,2,1,0:T(8,128)(2,1)S(1)} %pad_maximum_fusion.17), channel_id=1, source_target_pairs={{1,2},{2,1},{3,4},{4,3},{5,6},{6,5},{9,10},{10,9},{11,12},{12,11},... | collective-permute-start | bytes 73736 | tf_op jit(solution)/shard_map/ppermute | solution.py:27
  46.8 0.9 collective-permute-done.11
  48.1 2.0 %multiply_convert_fusion.1 = bf16[16,16,12,128]{3,1,2,0:T(8,128)(2,1)S(1)} fusion(f32[16,16,12,128]{3,1,2,0:T(8,128)} %get-tuple-element.65, f32[16,16,128]{2,1,0:T(8,128)S(1)} %bitcast.147), kind=kLoop, calls=%fused_computation.20 | loop fusion | flops 3538944 | bytes 2490368 | tf_op jit(solution)/shard_map/convert_element_type | solution.py:257
  52.1 1.1 multiply_convert_fusion
  53.4 2.6 %fusion.20 = f32[3,3,64,128]{3,2,1,0:T(8,128)S(1)} fusion(bf16[18,18,12,64]{3,2,1,0:T(8,128)(2,1)S(1)} %copy-done.3, bf16[16,16,12,128]{3,1,2,0:T(8,128)(2,1)S(1)} %multiply_convert_fusion), kind=kOutput, calls=%fused_computation.34 | convolution fusion | flops 452984832 | bytes 1579008 | tf_op jit(solution)/shard_map/conv_general_dilated | solution.py:281
  57.0 4.1 %collective-permute-start.15 = (bf16[16,1,1536]{2,1,0:T(2,128)(2,1)S(1)}, bf16[16,1,1536]{2,1,0:T(2,128)(2,1)S(1)}, u32[]{:S(2)}, u32[]{:S(2)}) collective-permute-start(bf16[16,1,1536]{2,1,0:T(2,128)(2,1)S(1)} %get-tuple-element.32), channel_id=1, source_target_pairs={{1,2},{2,1},{3,4},{4,3},{5,6},{6,5},{9,10},{10,9},{11,12},{12,11},... | collective-permute-start | bytes 147464 | tf_op jit(solution)/shard_map/ppermute | solution.py:61
  61.2 1.4 %collective-permute-start.13 = (f32[320,128]{1,0:T(8,128)S(1)}, f32[320,128]{1,0:T(8,128)S(1)}, u32[]{:S(2)}, u32[]{:S(2)}) collective-permute-start(f32[320,128]{1,0:T(8,128)S(1)} %slice_add_fusion.1), channel_id=1, source_target_pairs={{0,2},{1,3},{2,0},{3,1},{4,6},{5,7},{6,4},{7,5},{8,10},{9,11},{10,... | collective-permute-start | bytes 491528 | tf_op jit(solution)/shard_map/ppermute | solution.py:40
  63.6 3.3 %collective-permute-done.13 = f32[320,128]{1,0:T(8,128)S(1)} collective-permute-done((f32[320,128]{1,0:T(8,128)S(1)}, f32[320,128]{1,0:T(8,128)S(1)}, u32[]{:S(2)}, u32[]{:S(2)}) %collective-permute-start.13) | collective-permute-done | bytes 163872 | tf_op jit(solution)/shard_map/ppermute | solution.py:40
  66.9 2.9 %collective-permute-start.14 = (f32[320,128]{1,0:T(8,128)S(1)}, f32[320,128]{1,0:T(8,128)S(1)}, u32[]{:S(2)}, u32[]{:S(2)}) collective-permute-start(f32[320,128]{1,0:T(8,128)S(1)} %add.126), channel_id=1, source_target_pairs={{0,4},{1,5},{2,6},{3,7},{4,0},{5,1},{6,2},{7,3},{8,12},{9,13},{10,... | collective-permute-start | bytes 491528 | tf_op jit(solution)/shard_map/ppermute | solution.py:40
  69.9 3.9 %collective-permute-done.14 = f32[320,128]{1,0:T(8,128)S(1)} collective-permute-done((f32[320,128]{1,0:T(8,128)S(1)}, f32[320,128]{1,0:T(8,128)S(1)}, u32[]{:S(2)}, u32[]{:S(2)}) %collective-permute-start.14) | collective-permute-done | bytes 163872 | tf_op jit(solution)/shard_map/ppermute | solution.py:40
  73.8 5.8 %collective-permute-start.16 = (f32[536,128]{1,0:T(8,128)S(1)}, f32[536,128]{1,0:T(8,128)S(1)}, u32[]{:S(2)}, u32[]{:S(2)}) collective-permute-start(f32[536,128]{1,0:T(8,128)S(1)} %pad_maximum_fusion.2), channel_id=1, source_target_pairs={{0,8},{8,0},{16,24},{24,16},{32,40},{40,32},{48,56},{56,48},{64,72... | collective-permute-start | bytes 823304 | tf_op jit(solution)/shard_map/ppermute | solution.py:40
  80.3 4.9 %collective-permute-done.16 = f32[536,128]{1,0:T(8,128)S(1)} collective-permute-done((f32[536,128]{1,0:T(8,128)S(1)}, f32[536,128]{1,0:T(8,128)S(1)}, u32[]{:S(2)}, u32[]{:S(2)}) %collective-permute-start.16) | collective-permute-done | bytes 274464 | tf_op jit(solution)/shard_map/ppermute | solution.py:40
  85.3 4.2 %collective-permute-start.18 = (f32[320,128]{1,0:T(8,128)S(1)}, f32[320,128]{1,0:T(8,128)S(1)}, u32[]{:S(2)}, u32[]{:S(2)}) collective-permute-start(f32[320,128]{1,0:T(8,128)S(1)} %slice_add_fusion), channel_id=1, source_target_pairs={{0,16},{8,24},{16,0},{24,8},{32,48},{40,56},{48,32},{56,40},{64,80... | collective-permute-start | bytes 491528 | tf_op jit(solution)/shard_map/ppermute | solution.py:40
  91.0 2.8 %fusion.72 = (bf16[16,16,12,128]{3,2,1,0:T(8,128)(2,1)S(1)}, bf16[16,16,12,128]{3,2,1,0:T(8,128)(2,1)S(1)}, bf16[16,16,12,128]{3,2,1,0:T(8,128)(2,1)S(1)}, bf16[...) fusion(bf16[18,18,12,128]{3,2,1,0:T(8,128)(2,1)S(1)} %reshape.224), kind=kLoop, calls=%fused_computation.181 | loop fusion | bytes 14155776 | tf_op jit(solution)/shard_map/slice | solution.py:149
  95.8 1.7 %collective-permute-start.19 = (f32[320,128]{1,0:T(8,128)S(1)}, f32[320,128]{1,0:T(8,128)S(1)}, u32[]{:S(2)}, u32[]{:S(2)}) collective-permute-start(f32[320,128]{1,0:T(8,128)S(1)} %add.131), channel_id=1, source_target_pairs={{0,32},{8,40},{16,48},{24,56},{32,0},{40,8},{48,16},{56,24},{64,96... | collective-permute-start | bytes 491528 | tf_op jit(solution)/shard_map/ppermute | solution.py:40
  98.3 1.9 %collective-permute-done.19 = f32[320,128]{1,0:T(8,128)S(1)} collective-permute-done((f32[320,128]{1,0:T(8,128)S(1)}, f32[320,128]{1,0:T(8,128)S(1)}, u32[]{:S(2)}, u32[]{:S(2)}) %collective-permute-start.19) | collective-permute-done | bytes 163872 | tf_op jit(solution)/shard_map/ppermute | solution.py:40
  100.3 3.5 %collective-permute-start.20 = (f32[320,128]{1,0:T(8,128)S(1)}, f32[320,128]{1,0:T(8,128)S(1)}, u32[]{:S(2)}, u32[]{:S(2)}) collective-permute-start(f32[320,128]{1,0:T(8,128)S(1)} %add.132), channel_id=1, source_target_pairs={{0,64},{8,72},{16,80},{24,88},{32,96},{40,104},{48,112},{56,120},{... | collective-permute-start | bytes 491528 | tf_op jit(solution)/shard_map/ppermute | solution.py:40
  104.5 2.1 %collective-permute-done.20 = f32[320,128]{1,0:T(8,128)S(1)} collective-permute-done((f32[320,128]{1,0:T(8,128)S(1)}, f32[320,128]{1,0:T(8,128)S(1)}, u32[]{:S(2)}, u32[]{:S(2)}) %collective-permute-start.20) | collective-permute-done | bytes 163872 | tf_op jit(solution)/shard_map/ppermute | solution.py:40
  106.7 4.1 %collective-permute-start.21 = (f32[320,128]{1,0:T(8,128)S(1)}, f32[320,128]{1,0:T(8,128)S(1)}, u32[]{:S(2)}, u32[]{:S(2)}) collective-permute-start(f32[320,128]{1,0:T(8,128)S(1)} %add.133), channel_id=1, source_target_pairs={{0,1},{1,0},{2,3},{3,2},{4,5},{5,4},{6,7},{7,6},{8,9},{9,8},{10,11... | collective-permute-start | bytes 491528 | tf_op jit(solution)/shard_map/ppermute | solution.py:40
  111.9 1.4 %reshape.225 = bf16[16,16,768]{2,1,0:T(8,128)(2,1)} reshape(bf16[16,16,12,64]{3,2,1,0:T(8,128)(2,1)S(1)} %copy.92) | data formatting | bytes 786432 | tf_op jit(solution)/shard_map/reshape | solution.py:310
  (135 shorter events, 24.2 us)
Async XLA Ops:
  0.6 32.9 %copy-start = (bf16[128,20]{0,1:T(8,128)(2,1)S(1)}, bf16[128,20]{0,1:T(8,128)(2,1)}, u32[]{:S(2)}) copy-start(bf16[128,20]{0,1:T(8,128)(2,1)} %param.11) | copy-start | bytes 15364
  0.6 12.9 %copy-start.1 = (bf16[16,16,768]{2,1,0:T(8,128)(2,1)S(1)}, bf16[16,16,768]{2,1,0:T(8,128)(2,1)}, u32[]{:S(2)}) copy-start(bf16[16,16,768]{2,1,0:T(8,128)(2,1)} %param.8) | copy-start | bytes 1179652
  0.7 11.1 %copy-start.5 = (s32[16,16]{1,0:T(8,128)S(1)}, s32[16,16]{1,0:T(8,128)}, u32[]{:S(2)}) copy-start(s32[16,16]{1,0:T(8,128)} %param.12) | copy-start | bytes 3076
  1.5 4.8 %collective-permute-start = (bf16[1,16,768]{2,1,0:T(8,128)(2,1)S(1)}, bf16[1,16,768]{2,1,0:T(8,128)(2,1)S(1)}, u32[]{:S(2)}, u32[]{:S(2)}) collective-permute-start(bf16[1,16,768]{2,1,0:T(8,128)(2,1)S(1)} %get-tuple-element.33), channel_id=1, source_target_pairs={{0,8},{8,0},{16,24},{24,16},{32,40},{40,32},{48,56},{56,48},{64,72... | collective-permute-start | bytes 73736 | tf_op jit(solution)/shard_map/ppermute | solution.py:26
  3.5 2.7 %collective-permute-start.1 = (bf16[1,16,768]{2,1,0:T(8,128)(2,1)S(1)}, bf16[1,16,768]{2,1,0:T(8,128)(2,1)S(1)}, u32[]{:S(2)}, u32[]{:S(2)}) collective-permute-start(bf16[1,16,768]{2,1,0:T(8,128)(2,1)S(1)} %get-tuple-element.34), channel_id=1, source_target_pairs={{8,16},{16,8},{24,32},{32,24},{40,48},{48,40},{56,64},{64,56},{72,... | collective-permute-start | bytes 73736 | tf_op jit(solution)/shard_map/ppermute | solution.py:27
  7.5 5.9 %collective-permute-start.3 = (bf16[18,1,768]{2,1,0:T(2,128)(2,1)S(1)}, bf16[18,1,768]{2,1,0:T(2,128)(2,1)S(1)}, u32[]{:S(2)}, u32[]{:S(2)}) collective-permute-start(bf16[18,1,768]{2,1,0:T(2,128)(2,1)S(1)} %broadcast_select_fusion.6), channel_id=1, source_target_pairs={{1,2},{2,1},{3,4},{4,3},{5,6},{6,5},{9,10},{10,9},{11,12},{12,11},... | collective-permute-start | bytes 82952 | tf_op jit(solution)/shard_map/ppermute | solution.py:27
  11.6 1.8 %collective-permute-start.2 = (bf16[18,1,768]{2,1,0:T(2,128)(2,1)S(1)}, bf16[18,1,768]{2,1,0:T(2,128)(2,1)S(1)}, u32[]{:S(2)}, u32[]{:S(2)}) collective-permute-start(bf16[18,1,768]{2,1,0:T(2,128)(2,1)S(1)} %get-tuple-element.19), channel_id=1, source_target_pairs={{0,1},{1,0},{2,3},{3,2},{4,5},{5,4},{6,7},{7,6},{8,9},{9,8},{10,11... | collective-permute-start | bytes 82952 | tf_op jit(solution)/shard_map/ppermute | solution.py:26
  14.7 1.1 copy-start.2
  21.5 12.3 %copy-start.6 = (s32[1,1,32]{2,1,0:T(1,128)S(1)}, s32[1,1,32]{2,1,0:T(1,128)}, u32[]{:S(2)}) copy-start(s32[1,1,32]{2,1,0:T(1,128)} %param.15) | copy-start | bytes 388
  21.9 5.1 %collective-permute-start.4 = (bf16[1,3,32,128]{3,2,1,0:T(8,128)(2,1)S(1)}, bf16[1,3,32,128]{3,2,1,0:T(8,128)(2,1)S(1)}, u32[]{:S(2)}, u32[]{:S(2)}) collective-permute-start(bf16[1,3,32,128]{3,2,1,0:T(8,128)(2,1)S(1)} %bitcast.153), channel_id=1, source_target_pairs={{0,8},{8,0},{16,24},{24,16},{32,40},{40,32},{48,56},{56,48},{64,72... | collective-permute-start | bytes 73736 | tf_op jit(solution)/shard_map/ppermute | solution.py:26
  25.6 1.4 %collective-permute-start.5 = (bf16[1,3,32,128]{3,2,1,0:T(8,128)(2,1)S(1)}, bf16[1,3,32,128]{3,2,1,0:T(8,128)(2,1)S(1)}, u32[]{:S(2)}, u32[]{:S(2)}) collective-permute-start(bf16[1,3,32,128]{3,2,1,0:T(8,128)(2,1)S(1)} %bitcast.152), channel_id=1, source_target_pairs={{8,16},{16,8},{24,32},{32,24},{40,48},{48,40},{56,64},{64,56},{72,... | collective-permute-start | bytes 73736 | tf_op jit(solution)/shard_map/ppermute | solution.py:27
  27.1 4.4 %collective-permute-start.6 = (bf16[5,1,32,128]{3,2,1,0:T(8,128)(2,1)S(1)}, bf16[5,1,32,128]{3,2,1,0:T(8,128)(2,1)S(1)}, u32[]{:S(2)}, u32[]{:S(2)}) collective-permute-start(bf16[5,1,32,128]{3,2,1,0:T(8,128)(2,1)S(1)} %get-tuple-element.48), channel_id=1, source_target_pairs={{0,1},{1,0},{2,3},{3,2},{4,5},{5,4},{6,7},{7,6},{8,9},{9,8},{10,11... | collective-permute-start | bytes 122888 | tf_op jit(solution)/shard_map/ppermute | solution.py:26
  27.5 5.6 %collective-permute-start.7 = (bf16[5,1,32,128]{3,2,1,0:T(8,128)(2,1)S(1)}, bf16[5,1,32,128]{3,2,1,0:T(8,128)(2,1)S(1)}, u32[]{:S(2)}, u32[]{:S(2)}) collective-permute-start(bf16[5,1,32,128]{3,2,1,0:T(8,128)(2,1)S(1)} %get-tuple-element.49), channel_id=1, source_target_pairs={{1,2},{2,1},{3,4},{4,3},{5,6},{6,5},{9,10},{10,9},{11,12},{12,11},... | collective-permute-start | bytes 122888 | tf_op jit(solution)/shard_map/ppermute | solution.py:27
  34.2 7.5 %collective-permute-start.8 = (bf16[1,1,32,128]{3,2,1,0:T(8,128)(2,1)S(1)}, bf16[1,1,32,128]{3,2,1,0:T(8,128)(2,1)S(1)}, u32[]{:S(2)}, u32[]{:S(2)}) collective-permute-start(bf16[1,1,32,128]{3,2,1,0:T(8,128)(2,1)S(1)} %fusion.54), channel_id=1, source_target_pairs={{0,8},{8,0},{16,24},{24,16},{32,40},{40,32},{48,56},{56,48},{64,72... | collective-permute-start | bytes 24584 | tf_op jit(solution)/shard_map/ppermute | solution.py:26
  40.6 1.0 collective-permute-start.9
  41.7 5.1 %collective-permute-start.10 = (bf16[3,1,32,128]{3,2,1,0:T(8,128)(2,1)S(1)}, bf16[3,1,32,128]{3,2,1,0:T(8,128)(2,1)S(1)}, u32[]{:S(2)}, u32[]{:S(2)}) collective-permute-start(bf16[3,1,32,128]{3,2,1,0:T(8,128)(2,1)S(1)} %pad_maximum_fusion.17), channel_id=1, source_target_pairs={{0,1},{1,0},{2,3},{3,2},{4,5},{5,4},{6,7},{7,6},{8,9},{9,8},{10,11... | collective-permute-start | bytes 73736 | tf_op jit(solution)/shard_map/ppermute | solution.py:26
  41.8 5.9 %collective-permute-start.11 = (bf16[3,1,32,128]{3,2,1,0:T(8,128)(2,1)S(1)}, bf16[3,1,32,128]{3,2,1,0:T(8,128)(2,1)S(1)}, u32[]{:S(2)}, u32[]{:S(2)}) collective-permute-start(bf16[3,1,32,128]{3,2,1,0:T(8,128)(2,1)S(1)} %pad_maximum_fusion.17), channel_id=1, source_target_pairs={{1,2},{2,1},{3,4},{4,3},{5,6},{6,5},{9,10},{10,9},{11,12},{12,11},... | collective-permute-start | bytes 73736 | tf_op jit(solution)/shard_map/ppermute | solution.py:27
  52.1 1.3 %copy-start.3 = (bf16[18,18,12,64]{3,2,1,0:T(8,128)(2,1)S(1)}, bf16[18,18,12,64]{3,2,1,0:T(8,128)(2,1)}, u32[]{:S(2)}) copy-start(bf16[18,18,12,64]{3,2,1,0:T(8,128)(2,1)} %copy-done.2) | copy-start | bytes 1492996
  56.0 0.9 copy-start.4
  56.8 4.2 %collective-permute-start.12 = (f32[512,128]{1,0:T(8,128)S(1)}, f32[512,128]{1,0:T(8,128)S(1)}, u32[]{:S(2)}, u32[]{:S(2)}) collective-permute-start(f32[512,128]{1,0:T(8,128)S(1)} %pad_maximum_fusion.3), channel_id=1, source_target_pairs={{0,1},{1,0},{2,3},{3,2},{4,5},{5,4},{6,7},{7,6},{8,9},{9,8},{10,11... | collective-permute-start | bytes 786440 | tf_op jit(solution)/shard_map/ppermute | solution.py:40
  57.0 6.4 %collective-permute-start.15 = (bf16[16,1,1536]{2,1,0:T(2,128)(2,1)S(1)}, bf16[16,1,1536]{2,1,0:T(2,128)(2,1)S(1)}, u32[]{:S(2)}, u32[]{:S(2)}) collective-permute-start(bf16[16,1,1536]{2,1,0:T(2,128)(2,1)S(1)} %get-tuple-element.32), channel_id=1, source_target_pairs={{1,2},{2,1},{3,4},{4,3},{5,6},{6,5},{9,10},{10,9},{11,12},{12,11},... | collective-permute-start | bytes 147464 | tf_op jit(solution)/shard_map/ppermute | solution.py:61
  61.2 5.7 %collective-permute-start.13 = (f32[320,128]{1,0:T(8,128)S(1)}, f32[320,128]{1,0:T(8,128)S(1)}, u32[]{:S(2)}, u32[]{:S(2)}) collective-permute-start(f32[320,128]{1,0:T(8,128)S(1)} %slice_add_fusion.1), channel_id=1, source_target_pairs={{0,2},{1,3},{2,0},{3,1},{4,6},{5,7},{6,4},{7,5},{8,10},{9,11},{10,... | collective-permute-start | bytes 491528 | tf_op jit(solution)/shard_map/ppermute | solution.py:40
  66.9 6.9 %collective-permute-start.14 = (f32[320,128]{1,0:T(8,128)S(1)}, f32[320,128]{1,0:T(8,128)S(1)}, u32[]{:S(2)}, u32[]{:S(2)}) collective-permute-start(f32[320,128]{1,0:T(8,128)S(1)} %add.126), channel_id=1, source_target_pairs={{0,4},{1,5},{2,6},{3,7},{4,0},{5,1},{6,2},{7,3},{8,12},{9,13},{10,... | collective-permute-start | bytes 491528 | tf_op jit(solution)/shard_map/ppermute | solution.py:40
  73.8 11.4 %collective-permute-start.16 = (f32[536,128]{1,0:T(8,128)S(1)}, f32[536,128]{1,0:T(8,128)S(1)}, u32[]{:S(2)}, u32[]{:S(2)}) collective-permute-start(f32[536,128]{1,0:T(8,128)S(1)} %pad_maximum_fusion.2), channel_id=1, source_target_pairs={{0,8},{8,0},{16,24},{24,16},{32,40},{40,32},{48,56},{56,48},{64,72... | collective-permute-start | bytes 823304 | tf_op jit(solution)/shard_map/ppermute | solution.py:40
  79.7 10.0 %collective-permute-start.17 = (bf16[1,18,1536]{2,1,0:T(8,128)(2,1)S(1)}, bf16[1,18,1536]{2,1,0:T(8,128)(2,1)S(1)}, u32[]{:S(2)}, u32[]{:S(2)}) collective-permute-start(bf16[1,18,1536]{2,1,0:T(8,128)(2,1)S(1)} %broadcast_select_fusion.11), channel_id=1, source_target_pairs={{8,16},{16,8},{24,32},{32,24},{40,48},{48,40},{56,64},{64,56},{72,... | collective-permute-start | bytes 165896 | tf_op jit(solution)/shard_map/ppermute | solution.py:61
  85.3 10.5 %collective-permute-start.18 = (f32[320,128]{1,0:T(8,128)S(1)}, f32[320,128]{1,0:T(8,128)S(1)}, u32[]{:S(2)}, u32[]{:S(2)}) collective-permute-start(f32[320,128]{1,0:T(8,128)S(1)} %slice_add_fusion), channel_id=1, source_target_pairs={{0,16},{8,24},{16,0},{24,8},{32,48},{40,56},{48,32},{56,40},{64,80... | collective-permute-start | bytes 491528 | tf_op jit(solution)/shard_map/ppermute | solution.py:40
  95.8 4.5 %collective-permute-start.19 = (f32[320,128]{1,0:T(8,128)S(1)}, f32[320,128]{1,0:T(8,128)S(1)}, u32[]{:S(2)}, u32[]{:S(2)}) collective-permute-start(f32[320,128]{1,0:T(8,128)S(1)} %add.131), channel_id=1, source_target_pairs={{0,32},{8,40},{16,48},{24,56},{32,0},{40,8},{48,16},{56,24},{64,96... | collective-permute-start | bytes 491528 | tf_op jit(solution)/shard_map/ppermute | solution.py:40
  100.3 6.4 %collective-permute-start.20 = (f32[320,128]{1,0:T(8,128)S(1)}, f32[320,128]{1,0:T(8,128)S(1)}, u32[]{:S(2)}, u32[]{:S(2)}) collective-permute-start(f32[320,128]{1,0:T(8,128)S(1)} %add.132), channel_id=1, source_target_pairs={{0,64},{8,72},{16,80},{24,88},{32,96},{40,104},{48,112},{56,120},{... | collective-permute-start | bytes 491528 | tf_op jit(solution)/shard_map/ppermute | solution.py:40
  106.7 6.6 %collective-permute-start.21 = (f32[320,128]{1,0:T(8,128)S(1)}, f32[320,128]{1,0:T(8,128)S(1)}, u32[]{:S(2)}, u32[]{:S(2)}) collective-permute-start(f32[320,128]{1,0:T(8,128)S(1)} %add.133), channel_id=1, source_target_pairs={{0,1},{1,0},{2,3},{3,2},{4,5},{5,4},{6,7},{7,6},{8,9},{9,8},{10,11... | collective-permute-start | bytes 491528 | tf_op jit(solution)/shard_map/ppermute | solution.py:40

commit v14 on v9

--- a/solution.py
+++ b/solution.py
@@ -90,7 +90,11 @@
         else:
             got = exchange(give, axis, bit)
         flat = keep + got
-    for axis, bit in steps[halvings:]:
+    middle = steps[halvings:]
+    middle = [step for step in middle if step == ("row", 1)] + [
+        step for step in middle if step != ("row", 1)
+    ]
+    for axis, bit in middle:
         if (axis, bit) == ("row", 1):
             odd, inner_piece, outer_piece = halo_ends(cells, "row", 0)
             outer = outer_swap(outer_piece, "row")

time: 111 us -> 112 us (level)
  waiting for transfers between devices: 14.4 us -> 16.8 us
  starting transfers between devices: 59.8 us -> 58.4 us
    ppermute x9, waiting for transfers between devices: 8.14 us -> 10.5 us  [exchange(): return lax.ppermute(value, axis, [(i, i ^ bit) for i in range(size)])]
    ppermute x9, starting transfers between devices: 28 us -> 26.7 us  [exchange(): return lax.ppermute(value, axis, [(i, i ^ bit) for i in range(size)])]
where the time goes in v14:
time: 112 us
  starting transfers between devices  58.4 us (52%)
  waiting for transfers between devices  16.8 us (15%)
  local copies, waits for them, and re-layouts  16 us (14%)
  matrix products  12.6 us (11%)
  other arithmetic  6.67 us (6%)
  between operations  1.48 us (1%)
    ppermute x9, starting transfers between devices, exchange(): return lax.ppermute(value, axis, [(i, i ^ bit) for i in range(size)])  26.7 us
    ppermute x6, starting transfers between devices, with_halo(): lax.ppermute(jnp.where(odd, tail, head), axis, [pair for k in range(1, co...  13.8 us
    ppermute x6, starting transfers between devices, with_halo(): lax.ppermute(jnp.where(odd, head, tail), axis, [(i, i ^ 1) for i in range...  13.2 us
    ppermute x9, waiting for transfers between devices, exchange(): return lax.ppermute(value, axis, [(i, i ^ bit) for i in range(size)])  10.5 us
    unnamed x30, local copies, waits for them, and re-layouts  8.06 us
    ppermute x6, waiting for transfers between devices, with_halo(): lax.ppermute(jnp.where(odd, tail, head), axis, [pair for k in range(1, co...  4.74 us
    ppermute x2, starting transfers between devices, outer_swap(): lax.ppermute(piece, axis, [pair for k in range(1, count - 1, 2) for pair...  4.72 us
    slice x1, local copies, waits for them, and re-layouts, transposed_conv(): padded_grad[2 - row_tap:2 - row_tap + out_rows, 2 - col_tap:2 - col_tap +...  2.81 us
  transfers between devices with their start and end apart: 23, of which 12 were waited for; matrix products, arithmetic and copies ran while one was open for 12% of the time, Pallas kernels for 0%

profile of v14, /device:TPU:1, one launch (start us, length us, event | category | flops | bytes accessed | tf_op | source)
XLA Modules:
  0.0 111.9 jit_solution(10676103158301992321)
XLA Ops:
  1.5 2.0 %collective-permute-start = (bf16[1,16,768]{2,1,0:T(8,128)(2,1)S(1)}, bf16[1,16,768]{2,1,0:T(8,128)(2,1)S(1)}, u32[]{:S(2)}, u32[]{:S(2)}) collective-permute-start(bf16[1,16,768]{2,1,0:T(8,128)(2,1)S(1)} %get-tuple-element.33), channel_id=1, source_target_pairs={{0,8},{8,0},{16,24},{24,16},{32,40},{40,32},{48,56},{56,48},{64,72... | collective-permute-start | bytes 73736 | tf_op jit(solution)/shard_map/ppermute | solution.py:26
  4.2 0.9 copy.68
  6.3 1.1 %broadcast_select_fusion.7 = (bf16[18,1,768]{2,1,0:T(2,128)(2,1)S(1)}, bf16[18,1,768]{2,1,0:T(2,128)(2,1)S(1)}, bf16[18,1,768]{2,1,0:T(2,128)(2,1)S(1)}) fusion(pred[]{:T(512)S(6)} %eq.104, bf16[1,16,768]{2,1,0:T(8,128)(2,1)S(1)} %get-tuple-element.61, bf16[16,16,768]{2,1,0:T(8,128)(2,1)} %param.8, bf16[1,16,768]{2,1,0:T(8,128)(2,1)S(1)} %get-tuple-element.60), kind=kLoop, calls=%fused_computation.66 | loop fusion | flops 179712 | bytes 525313 | tf_op jit(solution)/shard_map/jit(_where)/select_n | solution.py:26
  7.4 1.0 collective-permute-start.2
  8.5 3.1 %collective-permute-start.3 = (bf16[18,1,768]{2,1,0:T(2,128)(2,1)S(1)}, bf16[18,1,768]{2,1,0:T(2,128)(2,1)S(1)}, u32[]{:S(2)}, u32[]{:S(2)}) collective-permute-start(bf16[18,1,768]{2,1,0:T(2,128)(2,1)S(1)} %broadcast_select_fusion.6), channel_id=1, source_target_pairs={{1,2},{2,1},{3,4},{4,3},{5,6},{6,5},{9,10},{10,9},{11,12},{12,11},... | collective-permute-start | bytes 82952 | tf_op jit(solution)/shard_map/ppermute | solution.py:27
  11.8 2.2 %collective-permute-done.3 = bf16[18,1,768]{2,1,0:T(2,128)(2,1)S(1)} collective-permute-done((bf16[18,1,768]{2,1,0:T(2,128)(2,1)S(1)}, bf16[18,1,768]{2,1,0:T(2,128)(2,1)S(1)}, u32[]{:S(2)}, u32[]{:S(2)}) %collective-permute-start.3) | collective-permute-done | bytes 27680 | tf_op jit(solution)/shard_map/ppermute | solution.py:27
  15.3 1.1 copy-done.4
  16.4 1.6 %fusion.74 = f32[16,16,12,128]{3,2,1,0:T(8,128)S(1)} fusion(bf16[18,18,12,64]{3,2,1,0:T(8,128)(2,1)S(1)} %reshape.214, bf16[3,3,64,128]{3,2,1,0:T(8,128)(2,1)S(1)} %copy-done.6), kind=kOutput, calls=%fused_computation.186 | convolution fusion | flops 452984832 | bytes 2217984 | tf_op jit(solution)/shard_map/conv_general_dilated | solution.py:138
  20.8 3.7 %collective-permute-start.4 = (bf16[1,3,32,128]{3,2,1,0:T(8,128)(2,1)S(1)}, bf16[1,3,32,128]{3,2,1,0:T(8,128)(2,1)S(1)}, u32[]{:S(2)}, u32[]{:S(2)}) collective-permute-start(bf16[1,3,32,128]{3,2,1,0:T(8,128)(2,1)S(1)} %bitcast.153), channel_id=1, source_target_pairs={{0,8},{8,0},{16,24},{24,16},{32,40},{40,32},{48,56},{56,48},{64,72... | collective-permute-start | bytes 73736 | tf_op jit(solution)/shard_map/ppermute | solution.py:26
  25.9 4.0 %collective-permute-start.7 = (bf16[5,1,32,128]{3,2,1,0:T(8,128)(2,1)S(1)}, bf16[5,1,32,128]{3,2,1,0:T(8,128)(2,1)S(1)}, u32[]{:S(2)}, u32[]{:S(2)}) collective-permute-start(bf16[5,1,32,128]{3,2,1,0:T(8,128)(2,1)S(1)} %get-tuple-element.49), channel_id=1, source_target_pairs={{1,2},{2,1},{3,4},{4,3},{5,6},{6,5},{9,10},{10,9},{11,12},{12,11},... | collective-permute-start | bytes 122888 | tf_op jit(solution)/shard_map/ppermute | solution.py:27
  29.9 1.6 %collective-permute-done.7 = bf16[5,1,32,128]{3,2,1,0:T(8,128)(2,1)S(1)} collective-permute-done((bf16[5,1,32,128]{3,2,1,0:T(8,128)(2,1)S(1)}, bf16[5,1,32,128]{3,2,1,0:T(8,128)(2,1)S(1)}, u32[]{:S(2)}, u32[]{:S(2)}) %collective-permute-start.7) | collective-permute-done | bytes 40992 | tf_op jit(solution)/shard_map/ppermute | solution.py:27
  32.6 6.3 %collective-permute-start.8 = (bf16[1,1,32,128]{3,2,1,0:T(8,128)(2,1)S(1)}, bf16[1,1,32,128]{3,2,1,0:T(8,128)(2,1)S(1)}, u32[]{:S(2)}, u32[]{:S(2)}) collective-permute-start(bf16[1,1,32,128]{3,2,1,0:T(8,128)(2,1)S(1)} %fusion.54), channel_id=1, source_target_pairs={{0,8},{8,0},{16,24},{24,16},{32,40},{40,32},{48,56},{56,48},{64,72... | collective-permute-start | bytes 24584 | tf_op jit(solution)/shard_map/ppermute | solution.py:26
  40.1 4.7 %collective-permute-start.11 = (bf16[3,1,32,128]{3,2,1,0:T(8,128)(2,1)S(1)}, bf16[3,1,32,128]{3,2,1,0:T(8,128)(2,1)S(1)}, u32[]{:S(2)}, u32[]{:S(2)}) collective-permute-start(bf16[3,1,32,128]{3,2,1,0:T(8,128)(2,1)S(1)} %pad_maximum_fusion.17), channel_id=1, source_target_pairs={{1,2},{2,1},{3,4},{4,3},{5,6},{6,5},{9,10},{10,9},{11,12},{12,11},... | collective-permute-start | bytes 73736 | tf_op jit(solution)/shard_map/ppermute | solution.py:27
  47.8 1.2 %copy-done.2 = f32[16,16,12,128]{3,2,1,0:T(8,128)S(1)} copy-done((f32[16,16,12,128]{3,2,1,0:T(8,128)S(1)}, f32[16,16,12,128]{3,2,1,0:T(8,128)}, u32[]{:S(2)}) %copy-start.2) | copy-done | bytes 1572888
  49.0 1.0 multiply_convert_fusion
  50.1 1.3 %copy-done.5 = bf16[18,18,12,64]{3,2,1,0:T(8,128)(2,1)S(1)} copy-done((bf16[18,18,12,64]{3,2,1,0:T(8,128)(2,1)S(1)}, bf16[18,18,12,64]{3,2,1,0:T(8,128)(2,1)}, u32[]{:S(2)}) %copy-start.5) | copy-done | bytes 497688
  51.4 2.6 %fusion.20 = f32[3,3,64,128]{3,2,1,0:T(8,128)S(1)} fusion(bf16[18,18,12,64]{3,2,1,0:T(8,128)(2,1)S(1)} %copy-done.5, bf16[16,16,12,128]{3,1,2,0:T(8,128)(2,1)S(1)} %multiply_convert_fusion), kind=kOutput, calls=%fused_computation.34 | convolution fusion | flops 452984832 | bytes 1579008 | tf_op jit(solution)/shard_map/conv_general_dilated | solution.py:285
  56.1 4.1 %collective-permute-start.14 = (bf16[16,1,1536]{2,1,0:T(2,128)(2,1)S(1)}, bf16[16,1,1536]{2,1,0:T(2,128)(2,1)S(1)}, u32[]{:S(2)}, u32[]{:S(2)}) collective-permute-start(bf16[16,1,1536]{2,1,0:T(2,128)(2,1)S(1)} %get-tuple-element.32), channel_id=1, source_target_pairs={{1,2},{2,1},{3,4},{4,3},{5,6},{6,5},{9,10},{10,9},{11,12},{12,11},... | collective-permute-start | bytes 147464 | tf_op jit(solution)/shard_map/ppermute | solution.py:61
  60.4 1.4 %collective-permute-start.13 = (f32[160,128]{1,0:T(8,128)S(1)}, f32[160,128]{1,0:T(8,128)S(1)}, u32[]{:S(2)}, u32[]{:S(2)}) collective-permute-start(f32[160,128]{1,0:T(8,128)S(1)} %slice_select_fusion.1), channel_id=1, source_target_pairs={{0,2},{1,3},{2,0},{3,1},{4,6},{5,7},{6,4},{7,5},{8,10},{9,11},{10,... | collective-permute-start | bytes 245768 | tf_op jit(solution)/shard_map/ppermute | solution.py:40
  62.8 1.4 %collective-permute-done.13 = f32[160,128]{1,0:T(8,128)S(1)} collective-permute-done((f32[160,128]{1,0:T(8,128)S(1)}, f32[160,128]{1,0:T(8,128)S(1)}, u32[]{:S(2)}, u32[]{:S(2)}) %collective-permute-start.13) | collective-permute-done | bytes 81952 | tf_op jit(solution)/shard_map/ppermute | solution.py:40
  64.3 5.8 %collective-permute-start.15 = (f32[376,128]{1,0:T(8,128)S(1)}, f32[376,128]{1,0:T(8,128)S(1)}, u32[]{:S(2)}, u32[]{:S(2)}) collective-permute-start(f32[376,128]{1,0:T(8,128)S(1)} %pad_maximum_fusion.4), channel_id=1, source_target_pairs={{0,8},{8,0},{16,24},{24,16},{32,40},{40,32},{48,56},{56,48},{64,72... | collective-permute-start | bytes 577544 | tf_op jit(solution)/shard_map/ppermute | solution.py:40
  70.8 4.2 %collective-permute-done.15 = f32[376,128]{1,0:T(8,128)S(1)} collective-permute-done((f32[376,128]{1,0:T(8,128)S(1)}, f32[376,128]{1,0:T(8,128)S(1)}, u32[]{:S(2)}, u32[]{:S(2)}) %collective-permute-start.15) | collective-permute-done | bytes 192544 | tf_op jit(solution)/shard_map/ppermute | solution.py:40
  75.1 2.4 %collective-permute-start.17 = (f32[160,128]{1,0:T(8,128)S(1)}, f32[160,128]{1,0:T(8,128)S(1)}, u32[]{:S(2)}, u32[]{:S(2)}) collective-permute-start(f32[160,128]{1,0:T(8,128)S(1)} %slice_add_fusion.1), channel_id=1, source_target_pairs={{0,4},{1,5},{2,6},{3,7},{4,0},{5,1},{6,2},{7,3},{8,12},{9,13},{10,... | collective-permute-start | bytes 245768 | tf_op jit(solution)/shard_map/ppermute | solution.py:40
  77.6 2.4 %collective-permute-done.17 = f32[160,128]{1,0:T(8,128)S(1)} collective-permute-done((f32[160,128]{1,0:T(8,128)S(1)}, f32[160,128]{1,0:T(8,128)S(1)}, u32[]{:S(2)}, u32[]{:S(2)}) %collective-permute-start.17) | collective-permute-done | bytes 81952 | tf_op jit(solution)/shard_map/ppermute | solution.py:40
  80.0 4.0 %collective-permute-start.18 = (f32[160,128]{1,0:T(8,128)S(1)}, f32[160,128]{1,0:T(8,128)S(1)}, u32[]{:S(2)}, u32[]{:S(2)}) collective-permute-start(f32[160,128]{1,0:T(8,128)S(1)} %add.136), channel_id=1, source_target_pairs={{0,16},{8,24},{16,0},{24,8},{32,48},{40,56},{48,32},{56,40},{64,80... | collective-permute-start | bytes 245768 | tf_op jit(solution)/shard_map/ppermute | solution.py:40
  85.9 2.9 %collective-permute-start.19 = (f32[160,128]{1,0:T(8,128)S(1)}, f32[160,128]{1,0:T(8,128)S(1)}, u32[]{:S(2)}, u32[]{:S(2)}) collective-permute-start(f32[160,128]{1,0:T(8,128)S(1)} %add.137), channel_id=1, source_target_pairs={{0,32},{8,40},{16,48},{24,56},{32,0},{40,8},{48,16},{56,24},{64,96... | collective-permute-start | bytes 245768 | tf_op jit(solution)/shard_map/ppermute | solution.py:40
  88.7 2.8 %fusion.72 = (bf16[16,16,12,128]{3,2,1,0:T(8,128)(2,1)S(1)}, bf16[16,16,12,128]{3,2,1,0:T(8,128)(2,1)S(1)}, bf16[16,16,12,128]{3,2,1,0:T(8,128)(2,1)S(1)}, bf16[...) fusion(bf16[18,18,12,128]{3,2,1,0:T(8,128)(2,1)S(1)} %reshape.224), kind=kLoop, calls=%fused_computation.184 | loop fusion | bytes 14155776 | tf_op jit(solution)/shard_map/slice | solution.py:153
  92.2 3.6 %collective-permute-start.20 = (f32[160,128]{1,0:T(8,128)S(1)}, f32[160,128]{1,0:T(8,128)S(1)}, u32[]{:S(2)}, u32[]{:S(2)}) collective-permute-start(f32[160,128]{1,0:T(8,128)S(1)} %add.138), channel_id=1, source_target_pairs={{0,64},{8,72},{16,80},{24,88},{32,96},{40,104},{48,112},{56,120},{... | collective-permute-start | bytes 245768 | tf_op jit(solution)/shard_map/ppermute | solution.py:40
  97.2 1.2 %collective-permute-done.20 = f32[160,128]{1,0:T(8,128)S(1)} collective-permute-done((f32[160,128]{1,0:T(8,128)S(1)}, f32[160,128]{1,0:T(8,128)S(1)}, u32[]{:S(2)}, u32[]{:S(2)}) %collective-permute-start.20) | collective-permute-done | bytes 81952 | tf_op jit(solution)/shard_map/ppermute | solution.py:40
  98.4 1.5 %collective-permute-start.21 = (f32[160,128]{1,0:T(8,128)S(1)}, f32[160,128]{1,0:T(8,128)S(1)}, u32[]{:S(2)}, u32[]{:S(2)}) collective-permute-start(f32[160,128]{1,0:T(8,128)S(1)} %add.139), channel_id=1, source_target_pairs={{0,2},{1,3},{2,0},{3,1},{4,6},{5,7},{6,4},{7,5},{8,10},{9,11},{10,... | collective-permute-start | bytes 245768 | tf_op jit(solution)/shard_map/ppermute | solution.py:40
  102.0 5.0 %collective-permute-start.22 = (f32[320,128]{1,0:T(8,128)S(1)}, f32[320,128]{1,0:T(8,128)S(1)}, u32[]{:S(2)}, u32[]{:S(2)}) collective-permute-start(f32[320,128]{1,0:T(8,128)S(1)} %maximum_select_fusion.3), channel_id=1, source_target_pairs={{0,1},{1,0},{2,3},{3,2},{4,5},{5,4},{6,7},{7,6},{8,9},{9,8},{10,11... | collective-permute-start | bytes 491528 | tf_op jit(solution)/shard_map/ppermute | solution.py:40
  108.1 1.4 %reshape.225 = bf16[16,16,768]{2,1,0:T(8,128)(2,1)} reshape(bf16[16,16,12,64]{3,2,1,0:T(8,128)(2,1)S(1)} %copy.92) | data formatting | bytes 786432 | tf_op jit(solution)/shard_map/reshape | solution.py:314
  (143 shorter events, 26.8 us)
Async XLA Ops:
  0.6 31.3 %copy-start = (bf16[128,20]{0,1:T(8,128)(2,1)S(1)}, bf16[128,20]{0,1:T(8,128)(2,1)}, u32[]{:S(2)}) copy-start(bf16[128,20]{0,1:T(8,128)(2,1)} %param.11) | copy-start | bytes 15364
  0.6 13.5 %copy-start.3 = (bf16[16,16,768]{2,1,0:T(8,128)(2,1)S(1)}, bf16[16,16,768]{2,1,0:T(8,128)(2,1)}, u32[]{:S(2)}) copy-start(bf16[16,16,768]{2,1,0:T(8,128)(2,1)} %param.8) | copy-start | bytes 1179652
  0.7 11.1 %copy-start.7 = (s32[16,16]{1,0:T(8,128)S(1)}, s32[16,16]{1,0:T(8,128)}, u32[]{:S(2)}) copy-start(s32[16,16]{1,0:T(8,128)} %param.12) | copy-start | bytes 3076
  1.5 4.8 %collective-permute-start = (bf16[1,16,768]{2,1,0:T(8,128)(2,1)S(1)}, bf16[1,16,768]{2,1,0:T(8,128)(2,1)S(1)}, u32[]{:S(2)}, u32[]{:S(2)}) collective-permute-start(bf16[1,16,768]{2,1,0:T(8,128)(2,1)S(1)} %get-tuple-element.33), channel_id=1, source_target_pairs={{0,8},{8,0},{16,24},{24,16},{32,40},{40,32},{48,56},{56,48},{64,72... | collective-permute-start | bytes 73736 | tf_op jit(solution)/shard_map/ppermute | solution.py:26
  3.5 2.7 %collective-permute-start.1 = (bf16[1,16,768]{2,1,0:T(8,128)(2,1)S(1)}, bf16[1,16,768]{2,1,0:T(8,128)(2,1)S(1)}, u32[]{:S(2)}, u32[]{:S(2)}) collective-permute-start(bf16[1,16,768]{2,1,0:T(8,128)(2,1)S(1)} %get-tuple-element.34), channel_id=1, source_target_pairs={{8,16},{16,8},{24,32},{32,24},{40,48},{48,40},{56,64},{64,56},{72,... | collective-permute-start | bytes 73736 | tf_op jit(solution)/shard_map/ppermute | solution.py:27
  7.4 4.4 %collective-permute-start.2 = (bf16[18,1,768]{2,1,0:T(2,128)(2,1)S(1)}, bf16[18,1,768]{2,1,0:T(2,128)(2,1)S(1)}, u32[]{:S(2)}, u32[]{:S(2)}) collective-permute-start(bf16[18,1,768]{2,1,0:T(2,128)(2,1)S(1)} %get-tuple-element.19), channel_id=1, source_target_pairs={{0,1},{1,0},{2,3},{3,2},{4,5},{5,4},{6,7},{7,6},{8,9},{9,8},{10,11... | collective-permute-start | bytes 82952 | tf_op jit(solution)/shard_map/ppermute | solution.py:26
  8.5 5.5 %collective-permute-start.3 = (bf16[18,1,768]{2,1,0:T(2,128)(2,1)S(1)}, bf16[18,1,768]{2,1,0:T(2,128)(2,1)S(1)}, u32[]{:S(2)}, u32[]{:S(2)}) collective-permute-start(bf16[18,1,768]{2,1,0:T(2,128)(2,1)S(1)} %broadcast_select_fusion.6), channel_id=1, source_target_pairs={{1,2},{2,1},{3,4},{4,3},{5,6},{6,5},{9,10},{10,9},{11,12},{12,11},... | collective-permute-start | bytes 82952 | tf_op jit(solution)/shard_map/ppermute | solution.py:27
  14.2 2.2 %copy-start.6 = (bf16[3,3,64,128]{3,2,1,0:T(8,128)(2,1)S(1)}, bf16[3,3,64,128]{3,2,1,0:T(8,128)(2,1)}, u32[]{:S(2)}) copy-start(bf16[3,3,64,128]{3,2,1,0:T(8,128)(2,1)} %param.9) | copy-start | bytes 442372
  15.3 1.1 copy-start.4
  18.0 1.4 %copy-start.1 = (f32[16,16,12,128]{3,2,1,0:T(8,128)}, f32[16,16,12,128]{3,2,1,0:T(8,128)S(1)}, u32[]{:S(2)}) copy-start(f32[16,16,12,128]{3,2,1,0:T(8,128)S(1)} %fusion.74) | copy-start | bytes 4718596
  20.4 11.8 %copy-start.8 = (s32[1,1,32]{2,1,0:T(1,128)S(1)}, s32[1,1,32]{2,1,0:T(1,128)}, u32[]{:S(2)}) copy-start(s32[1,1,32]{2,1,0:T(1,128)} %param.15) | copy-start | bytes 388
  20.8 5.0 %collective-permute-start.4 = (bf16[1,3,32,128]{3,2,1,0:T(8,128)(2,1)S(1)}, bf16[1,3,32,128]{3,2,1,0:T(8,128)(2,1)S(1)}, u32[]{:S(2)}, u32[]{:S(2)}) collective-permute-start(bf16[1,3,32,128]{3,2,1,0:T(8,128)(2,1)S(1)} %bitcast.153), channel_id=1, source_target_pairs={{0,8},{8,0},{16,24},{24,16},{32,40},{40,32},{48,56},{56,48},{64,72... | collective-permute-start | bytes 73736 | tf_op jit(solution)/shard_map/ppermute | solution.py:26
  24.5 1.2 %collective-permute-start.5 = (bf16[1,3,32,128]{3,2,1,0:T(8,128)(2,1)S(1)}, bf16[1,3,32,128]{3,2,1,0:T(8,128)(2,1)S(1)}, u32[]{:S(2)}, u32[]{:S(2)}) collective-permute-start(bf16[1,3,32,128]{3,2,1,0:T(8,128)(2,1)S(1)} %bitcast.152), channel_id=1, source_target_pairs={{8,16},{16,8},{24,32},{32,24},{40,48},{48,40},{56,64},{64,56},{72,... | collective-permute-start | bytes 73736 | tf_op jit(solution)/shard_map/ppermute | solution.py:27
  25.8 4.2 %collective-permute-start.6 = (bf16[5,1,32,128]{3,2,1,0:T(8,128)(2,1)S(1)}, bf16[5,1,32,128]{3,2,1,0:T(8,128)(2,1)S(1)}, u32[]{:S(2)}, u32[]{:S(2)}) collective-permute-start(bf16[5,1,32,128]{3,2,1,0:T(8,128)(2,1)S(1)} %get-tuple-element.48), channel_id=1, source_target_pairs={{0,1},{1,0},{2,3},{3,2},{4,5},{5,4},{6,7},{7,6},{8,9},{9,8},{10,11... | collective-permute-start | bytes 122888 | tf_op jit(solution)/shard_map/ppermute | solution.py:26
  25.9 5.7 %collective-permute-start.7 = (bf16[5,1,32,128]{3,2,1,0:T(8,128)(2,1)S(1)}, bf16[5,1,32,128]{3,2,1,0:T(8,128)(2,1)S(1)}, u32[]{:S(2)}, u32[]{:S(2)}) collective-permute-start(bf16[5,1,32,128]{3,2,1,0:T(8,128)(2,1)S(1)} %get-tuple-element.49), channel_id=1, source_target_pairs={{1,2},{2,1},{3,4},{4,3},{5,6},{6,5},{9,10},{10,9},{11,12},{12,11},... | collective-permute-start | bytes 122888 | tf_op jit(solution)/shard_map/ppermute | solution.py:27
  32.6 7.3 %collective-permute-start.8 = (bf16[1,1,32,128]{3,2,1,0:T(8,128)(2,1)S(1)}, bf16[1,1,32,128]{3,2,1,0:T(8,128)(2,1)S(1)}, u32[]{:S(2)}, u32[]{:S(2)}) collective-permute-start(bf16[1,1,32,128]{3,2,1,0:T(8,128)(2,1)S(1)} %fusion.54), channel_id=1, source_target_pairs={{0,8},{8,0},{16,24},{24,16},{32,40},{40,32},{48,56},{56,48},{64,72... | collective-permute-start | bytes 24584 | tf_op jit(solution)/shard_map/ppermute | solution.py:26
  38.9 1.0 collective-permute-start.9
  40.0 5.2 %collective-permute-start.10 = (bf16[3,1,32,128]{3,2,1,0:T(8,128)(2,1)S(1)}, bf16[3,1,32,128]{3,2,1,0:T(8,128)(2,1)S(1)}, u32[]{:S(2)}, u32[]{:S(2)}) collective-permute-start(bf16[3,1,32,128]{3,2,1,0:T(8,128)(2,1)S(1)} %pad_maximum_fusion.17), channel_id=1, source_target_pairs={{0,1},{1,0},{2,3},{3,2},{4,5},{5,4},{6,7},{7,6},{8,9},{9,8},{10,11... | collective-permute-start | bytes 73736 | tf_op jit(solution)/shard_map/ppermute | solution.py:26
  40.1 6.0 %collective-permute-start.11 = (bf16[3,1,32,128]{3,2,1,0:T(8,128)(2,1)S(1)}, bf16[3,1,32,128]{3,2,1,0:T(8,128)(2,1)S(1)}, u32[]{:S(2)}, u32[]{:S(2)}) collective-permute-start(bf16[3,1,32,128]{3,2,1,0:T(8,128)(2,1)S(1)} %pad_maximum_fusion.17), channel_id=1, source_target_pairs={{1,2},{2,1},{3,4},{4,3},{5,6},{6,5},{9,10},{10,9},{11,12},{12,11},... | collective-permute-start | bytes 73736 | tf_op jit(solution)/shard_map/ppermute | solution.py:27
  47.5 1.6 %copy-start.2 = (f32[16,16,12,128]{3,2,1,0:T(8,128)S(1)}, f32[16,16,12,128]{3,2,1,0:T(8,128)}, u32[]{:S(2)}) copy-start(f32[16,16,12,128]{3,2,1,0:T(8,128)} %copy-done.1) | copy-start | bytes 4718596
  50.0 1.3 %copy-start.5 = (bf16[18,18,12,64]{3,2,1,0:T(8,128)(2,1)S(1)}, bf16[18,18,12,64]{3,2,1,0:T(8,128)(2,1)}, u32[]{:S(2)}) copy-start(bf16[18,18,12,64]{3,2,1,0:T(8,128)(2,1)} %copy-done.4) | copy-start | bytes 1492996
  56.0 4.2 %collective-permute-start.12 = (f32[512,128]{1,0:T(8,128)S(1)}, f32[512,128]{1,0:T(8,128)S(1)}, u32[]{:S(2)}, u32[]{:S(2)}) collective-permute-start(f32[512,128]{1,0:T(8,128)S(1)} %pad_maximum_fusion.2), channel_id=1, source_target_pairs={{0,1},{1,0},{2,3},{3,2},{4,5},{5,4},{6,7},{7,6},{8,9},{9,8},{10,11... | collective-permute-start | bytes 786440 | tf_op jit(solution)/shard_map/ppermute | solution.py:40
  56.1 6.4 %collective-permute-start.14 = (bf16[16,1,1536]{2,1,0:T(2,128)(2,1)S(1)}, bf16[16,1,1536]{2,1,0:T(2,128)(2,1)S(1)}, u32[]{:S(2)}, u32[]{:S(2)}) collective-permute-start(bf16[16,1,1536]{2,1,0:T(2,128)(2,1)S(1)} %get-tuple-element.32), channel_id=1, source_target_pairs={{1,2},{2,1},{3,4},{4,3},{5,6},{6,5},{9,10},{10,9},{11,12},{12,11},... | collective-permute-start | bytes 147464 | tf_op jit(solution)/shard_map/ppermute | solution.py:61
  60.4 3.9 %collective-permute-start.13 = (f32[160,128]{1,0:T(8,128)S(1)}, f32[160,128]{1,0:T(8,128)S(1)}, u32[]{:S(2)}, u32[]{:S(2)}) collective-permute-start(f32[160,128]{1,0:T(8,128)S(1)} %slice_select_fusion.1), channel_id=1, source_target_pairs={{0,2},{1,3},{2,0},{3,1},{4,6},{5,7},{6,4},{7,5},{8,10},{9,11},{10,... | collective-permute-start | bytes 245768 | tf_op jit(solution)/shard_map/ppermute | solution.py:40
  64.3 10.7 %collective-permute-start.15 = (f32[376,128]{1,0:T(8,128)S(1)}, f32[376,128]{1,0:T(8,128)S(1)}, u32[]{:S(2)}, u32[]{:S(2)}) collective-permute-start(f32[376,128]{1,0:T(8,128)S(1)} %pad_maximum_fusion.4), channel_id=1, source_target_pairs={{0,8},{8,0},{16,24},{24,16},{32,40},{40,32},{48,56},{56,48},{64,72... | collective-permute-start | bytes 577544 | tf_op jit(solution)/shard_map/ppermute | solution.py:40
  70.1 7.4 %collective-permute-start.16 = (bf16[1,18,1536]{2,1,0:T(8,128)(2,1)S(1)}, bf16[1,18,1536]{2,1,0:T(8,128)(2,1)S(1)}, u32[]{:S(2)}, u32[]{:S(2)}) collective-permute-start(bf16[1,18,1536]{2,1,0:T(8,128)(2,1)S(1)} %broadcast_select_fusion.11), channel_id=1, source_target_pairs={{8,16},{16,8},{24,32},{32,24},{40,48},{48,40},{56,64},{64,56},{72,... | collective-permute-start | bytes 165896 | tf_op jit(solution)/shard_map/ppermute | solution.py:61
  75.1 4.9 %collective-permute-start.17 = (f32[160,128]{1,0:T(8,128)S(1)}, f32[160,128]{1,0:T(8,128)S(1)}, u32[]{:S(2)}, u32[]{:S(2)}) collective-permute-start(f32[160,128]{1,0:T(8,128)S(1)} %slice_add_fusion.1), channel_id=1, source_target_pairs={{0,4},{1,5},{2,6},{3,7},{4,0},{5,1},{6,2},{7,3},{8,12},{9,13},{10,... | collective-permute-start | bytes 245768 | tf_op jit(solution)/shard_map/ppermute | solution.py:40
  80.0 5.8 %collective-permute-start.18 = (f32[160,128]{1,0:T(8,128)S(1)}, f32[160,128]{1,0:T(8,128)S(1)}, u32[]{:S(2)}, u32[]{:S(2)}) collective-permute-start(f32[160,128]{1,0:T(8,128)S(1)} %add.136), channel_id=1, source_target_pairs={{0,16},{8,24},{16,0},{24,8},{32,48},{40,56},{48,32},{56,40},{64,80... | collective-permute-start | bytes 245768 | tf_op jit(solution)/shard_map/ppermute | solution.py:40
  85.9 6.3 %collective-permute-start.19 = (f32[160,128]{1,0:T(8,128)S(1)}, f32[160,128]{1,0:T(8,128)S(1)}, u32[]{:S(2)}, u32[]{:S(2)}) collective-permute-start(f32[160,128]{1,0:T(8,128)S(1)} %add.137), channel_id=1, source_target_pairs={{0,32},{8,40},{16,48},{24,56},{32,0},{40,8},{48,16},{56,24},{64,96... | collective-permute-start | bytes 245768 | tf_op jit(solution)/shard_map/ppermute | solution.py:40
  92.2 6.2 %collective-permute-start.20 = (f32[160,128]{1,0:T(8,128)S(1)}, f32[160,128]{1,0:T(8,128)S(1)}, u32[]{:S(2)}, u32[]{:S(2)}) collective-permute-start(f32[160,128]{1,0:T(8,128)S(1)} %add.138), channel_id=1, source_target_pairs={{0,64},{8,72},{16,80},{24,88},{32,96},{40,104},{48,112},{56,120},{... | collective-permute-start | bytes 245768 | tf_op jit(solution)/shard_map/ppermute | solution.py:40
  98.4 3.6 %collective-permute-start.21 = (f32[160,128]{1,0:T(8,128)S(1)}, f32[160,128]{1,0:T(8,128)S(1)}, u32[]{:S(2)}, u32[]{:S(2)}) collective-permute-start(f32[160,128]{1,0:T(8,128)S(1)} %add.139), channel_id=1, source_target_pairs={{0,2},{1,3},{2,0},{3,1},{4,6},{5,7},{6,4},{7,5},{8,10},{9,11},{10,... | collective-permute-start | bytes 245768 | tf_op jit(solution)/shard_map/ppermute | solution.py:40
  102.0 7.4 %collective-permute-start.22 = (f32[320,128]{1,0:T(8,128)S(1)}, f32[320,128]{1,0:T(8,128)S(1)}, u32[]{:S(2)}, u32[]{:S(2)}) collective-permute-start(f32[320,128]{1,0:T(8,128)S(1)} %maximum_select_fusion.3), channel_id=1, source_target_pairs={{0,1},{1,0},{2,3},{3,2},{4,5},{5,4},{6,7},{7,6},{8,9},{9,8},{10,11... | collective-permute-start | bytes 491528 | tf_op jit(solution)/shard_map/ppermute | solution.py:40

commit v15 on v9

--- a/solution.py
+++ b/solution.py
@@ -85,7 +85,7 @@
         if (axis, bit) == ("col", 1):
             odd, inner_piece, outer_piece = halo_ends(cells, "col", 1)
             outer = outer_swap(outer_piece, "col")
-            got, inner = swap_with(give, axis, bit, inner_piece)
+            got, inner = exchange(give, axis, bit), exchange(inner_piece, axis, bit)
             cells = halo_join(cells, odd, inner, outer, 1)
         else:
             got = exchange(give, axis, bit)
@@ -94,7 +94,7 @@
         if (axis, bit) == ("row", 1):
             odd, inner_piece, outer_piece = halo_ends(cells, "row", 0)
             outer = outer_swap(outer_piece, "row")
-            got, inner = swap_with(flat, axis, bit, inner_piece)
+            got, inner = exchange(flat, axis, bit), exchange(inner_piece, axis, bit)
             cells = halo_join(cells, odd, inner, outer, 0)
         else:
             got = exchange(flat, axis, bit)

time: 111 us -> 117 us (1.054)
  other arithmetic: 6.67 us -> 8.99 us
  matrix products: 12.6 us -> 14.8 us
  local copies, waits for them, and re-layouts: 16 us -> 13.9 us
  waiting for transfers between devices: 14.4 us -> 16.1 us
  starting transfers between devices: 59.8 us -> 61.3 us
    unnamed x30 -> x42, local copies, waits for them, and re-layouts: 8.06 us -> 5.52 us
    convert_element_type x1, other arithmetic: 0.59 us -> 2.01 us  [per_device(): ((pixel_grad / DATES)[:, :, None, :] * silu_slope(mixed_time)).astype(jnp...]
    ppermute x2, waiting for transfers between devices: 0.71 us -> 2.06 us  [outer_swap(): lax.ppermute(piece, axis, [pair for k in range(1, count - 1, 2) for pair...]
    ppermute x9 -> x11, starting transfers between devices: 28 us -> 29.2 us  [exchange(): return lax.ppermute(value, axis, [(i, i ^ bit) for i in range(size)])]
    ppermute x9 -> x11, waiting for transfers between devices: 8.14 us -> 8.85 us  [exchange(): return lax.ppermute(value, axis, [(i, i ^ bit) for i in range(size)])]
  transfers between devices with their start and end apart: 23 -> 25, of which waited for: 12 -> 11; matrix products, arithmetic and copies ran while one was open for 12% -> 12% of each run, Pallas kernels for 0% -> 0%
where the time goes in v15:
time: 117 us
  starting transfers between devices  61.3 us (52%)
  waiting for transfers between devices  16.1 us (14%)
  matrix products  14.8 us (13%)
  local copies, waits for them, and re-layouts  13.9 us (12%)
  other arithmetic  8.99 us (8%)
  between operations  1.5 us (1%)
    ppermute x11, starting transfers between devices, exchange(): return lax.ppermute(value, axis, [(i, i ^ bit) for i in range(size)])  29.2 us
    ppermute x6, starting transfers between devices, with_halo(): lax.ppermute(jnp.where(odd, tail, head), axis, [pair for k in range(1, co...  14.5 us
    ppermute x6, starting transfers between devices, with_halo(): lax.ppermute(jnp.where(odd, head, tail), axis, [(i, i ^ 1) for i in range...  12.8 us
    ppermute x11, waiting for transfers between devices, exchange(): return lax.ppermute(value, axis, [(i, i ^ bit) for i in range(size)])  8.85 us
    unnamed x42, local copies, waits for them, and re-layouts  5.52 us
    ppermute x2, starting transfers between devices, outer_swap(): lax.ppermute(piece, axis, [pair for k in range(1, count - 1, 2) for pair...  4.76 us
    ppermute x6, waiting for transfers between devices, with_halo(): lax.ppermute(jnp.where(odd, tail, head), axis, [pair for k in range(1, co...  4.12 us
    slice x1, local copies, waits for them, and re-layouts, transposed_conv(): padded_grad[2 - row_tap:2 - row_tap + out_rows, 2 - col_tap:2 - col_tap +...  2.78 us
  transfers between devices with their start and end apart: 25, of which 11 were waited for; matrix products, arithmetic and copies ran while one was open for 12% of the time, Pallas kernels for 0%

profile of v15, /device:TPU:1, one launch (start us, length us, event | category | flops | bytes accessed | tf_op | source)
XLA Modules:
  0.0 116.6 jit_solution(13872923982651503010)
XLA Ops:
  1.5 2.0 %collective-permute-start = (bf16[1,16,768]{2,1,0:T(8,128)(2,1)S(1)}, bf16[1,16,768]{2,1,0:T(8,128)(2,1)S(1)}, u32[]{:S(2)}, u32[]{:S(2)}) collective-permute-start(bf16[1,16,768]{2,1,0:T(8,128)(2,1)S(1)} %get-tuple-element.33), channel_id=1, source_target_pairs={{0,8},{8,0},{16,24},{24,16},{32,40},{40,32},{48,56},{56,48},{64,72... | collective-permute-start | bytes 73736 | tf_op jit(solution)/shard_map/ppermute | solution.py:26
  4.2 0.9 copy.66
  6.3 1.1 broadcast_select_fusion.7
  7.5 4.0 %collective-permute-start.3 = (bf16[18,1,768]{2,1,0:T(2,128)(2,1)S(1)}, bf16[18,1,768]{2,1,0:T(2,128)(2,1)S(1)}, u32[]{:S(2)}, u32[]{:S(2)}) collective-permute-start(bf16[18,1,768]{2,1,0:T(2,128)(2,1)S(1)} %broadcast_select_fusion.6), channel_id=1, source_target_pairs={{1,2},{2,1},{3,4},{4,3},{5,6},{6,5},{9,10},{10,9},{11,12},{12,11},... | collective-permute-start | bytes 82952 | tf_op jit(solution)/shard_map/ppermute | solution.py:27
  11.8 1.6 %collective-permute-done.3 = bf16[18,1,768]{2,1,0:T(2,128)(2,1)S(1)} collective-permute-done((bf16[18,1,768]{2,1,0:T(2,128)(2,1)S(1)}, bf16[18,1,768]{2,1,0:T(2,128)(2,1)S(1)}, u32[]{:S(2)}, u32[]{:S(2)}) %collective-permute-start.3) | collective-permute-done | bytes 27680 | tf_op jit(solution)/shard_map/ppermute | solution.py:27
  14.7 1.1 copy-done.2
  15.7 2.5 %fusion.73 = f32[16,16,12,128]{3,2,1,0:T(8,128)S(1)} fusion(bf16[18,18,12,64]{3,2,1,0:T(8,128)(2,1)S(1)} %reshape.174, bf16[3,3,64,128]{3,2,1,0:T(8,128)(2,1)} %param.9), kind=kOutput, calls=%fused_computation.180 | convolution fusion | flops 452984832 | bytes 2217984 | tf_op jit(solution)/shard_map/conv_general_dilated | solution.py:134
  19.7 1.8 %multiply_reduce_fusion = (f32[16,16,128]{2,1,0:T(8,128)S(1)}, f32[16,16,12,128]{3,1,2,0:T(8,128)}) fusion(bf16[16,16,12,128]{3,1,2,0:T(8,128)(2,1)S(1)} %multiply_convert_fusion.2, bf16[3,128,128]{2,1,0:T(8,128)(2,1)S(1)} %broadcast_select_fusion.8, f32[16,16,12,128]{3,1,2,0:T(8,128)S(1)} %fusion.49, f32[16,16,12,128]{3,1,2,0:T(8,128)S(1)} %fusion.51), kind=kOutput, calls=%fused_computation.21 | convolution fusion | flops 94994432 | bytes 5668864 | tf_op jit(solution)/shard_map/dot_general | solution.py:196
  21.9 3.7 %collective-permute-start.4 = (bf16[1,3,32,128]{3,2,1,0:T(8,128)(2,1)S(1)}, bf16[1,3,32,128]{3,2,1,0:T(8,128)(2,1)S(1)}, u32[]{:S(2)}, u32[]{:S(2)}) collective-permute-start(bf16[1,3,32,128]{3,2,1,0:T(8,128)(2,1)S(1)} %bitcast.151), channel_id=1, source_target_pairs={{0,8},{8,0},{16,24},{24,16},{32,40},{40,32},{48,56},{56,48},{64,72... | collective-permute-start | bytes 73736 | tf_op jit(solution)/shard_map/ppermute | solution.py:26
  27.6 3.9 %collective-permute-start.7 = (bf16[5,1,32,128]{3,2,1,0:T(8,128)(2,1)S(1)}, bf16[5,1,32,128]{3,2,1,0:T(8,128)(2,1)S(1)}, u32[]{:S(2)}, u32[]{:S(2)}) collective-permute-start(bf16[5,1,32,128]{3,2,1,0:T(8,128)(2,1)S(1)} %get-tuple-element.49), channel_id=1, source_target_pairs={{1,2},{2,1},{3,4},{4,3},{5,6},{6,5},{9,10},{10,9},{11,12},{12,11},... | collective-permute-start | bytes 122888 | tf_op jit(solution)/shard_map/ppermute | solution.py:27
  31.5 1.6 %collective-permute-done.7 = bf16[5,1,32,128]{3,2,1,0:T(8,128)(2,1)S(1)} collective-permute-done((bf16[5,1,32,128]{3,2,1,0:T(8,128)(2,1)S(1)}, bf16[5,1,32,128]{3,2,1,0:T(8,128)(2,1)S(1)}, u32[]{:S(2)}, u32[]{:S(2)}) %collective-permute-start.7) | collective-permute-done | bytes 40992 | tf_op jit(solution)/shard_map/ppermute | solution.py:27
  34.2 6.4 %collective-permute-start.8 = (bf16[1,1,32,128]{3,2,1,0:T(8,128)(2,1)S(1)}, bf16[1,1,32,128]{3,2,1,0:T(8,128)(2,1)S(1)}, u32[]{:S(2)}, u32[]{:S(2)}) collective-permute-start(bf16[1,1,32,128]{3,2,1,0:T(8,128)(2,1)S(1)} %fusion.53), channel_id=1, source_target_pairs={{0,8},{8,0},{16,24},{24,16},{32,40},{40,32},{48,56},{56,48},{64,72... | collective-permute-start | bytes 24584 | tf_op jit(solution)/shard_map/ppermute | solution.py:26
  41.8 4.6 %collective-permute-start.11 = (bf16[3,1,32,128]{3,2,1,0:T(8,128)(2,1)S(1)}, bf16[3,1,32,128]{3,2,1,0:T(8,128)(2,1)S(1)}, u32[]{:S(2)}, u32[]{:S(2)}) collective-permute-start(bf16[3,1,32,128]{3,2,1,0:T(8,128)(2,1)S(1)} %pad_maximum_fusion.15), channel_id=1, source_target_pairs={{1,2},{2,1},{3,4},{4,3},{5,6},{6,5},{9,10},{10,9},{11,12},{12,11},... | collective-permute-start | bytes 73736 | tf_op jit(solution)/shard_map/ppermute | solution.py:27
  46.8 0.9 collective-permute-done.11
  48.1 2.0 %multiply_convert_fusion.1 = bf16[16,16,12,128]{3,1,2,0:T(8,128)(2,1)S(1)} fusion(f32[16,16,12,128]{3,1,2,0:T(8,128)} %get-tuple-element.65, f32[16,16,128]{2,1,0:T(8,128)S(1)} %bitcast.146), kind=kLoop, calls=%fused_computation.20 | loop fusion | flops 3538944 | bytes 2490368 | tf_op jit(solution)/shard_map/convert_element_type | solution.py:257
  52.1 1.1 multiply_convert_fusion
  53.4 2.6 %fusion.20 = f32[3,3,64,128]{3,2,1,0:T(8,128)S(1)} fusion(bf16[18,18,12,64]{3,2,1,0:T(8,128)(2,1)S(1)} %copy-done.3, bf16[16,16,12,128]{3,1,2,0:T(8,128)(2,1)S(1)} %multiply_convert_fusion), kind=kOutput, calls=%fused_computation.34 | convolution fusion | flops 452984832 | bytes 1579008 | tf_op jit(solution)/shard_map/conv_general_dilated | solution.py:281
  56.8 4.1 %collective-permute-start.13 = (bf16[16,1,1536]{2,1,0:T(2,128)(2,1)S(1)}, bf16[16,1,1536]{2,1,0:T(2,128)(2,1)S(1)}, u32[]{:S(2)}, u32[]{:S(2)}) collective-permute-start(bf16[16,1,1536]{2,1,0:T(2,128)(2,1)S(1)} %get-tuple-element.32), channel_id=1, source_target_pairs={{1,2},{2,1},{3,4},{4,3},{5,6},{6,5},{9,10},{10,9},{11,12},{12,11},... | collective-permute-start | bytes 147464 | tf_op jit(solution)/shard_map/ppermute | solution.py:61
  61.1 2.1 %collective-permute-done.13 = bf16[16,1,1536]{2,1,0:T(2,128)(2,1)S(1)} collective-permute-done((bf16[16,1,1536]{2,1,0:T(2,128)(2,1)S(1)}, bf16[16,1,1536]{2,1,0:T(2,128)(2,1)S(1)}, u32[]{:S(2)}, u32[]{:S(2)}) %collective-permute-start.13) | collective-permute-done | bytes 49184 | tf_op jit(solution)/shard_map/ppermute | solution.py:61
  63.6 1.5 %collective-permute-start.17 = (f32[160,128]{1,0:T(8,128)S(1)}, f32[160,128]{1,0:T(8,128)S(1)}, u32[]{:S(2)}, u32[]{:S(2)}) collective-permute-start(f32[160,128]{1,0:T(8,128)S(1)} %slice_select_fusion.1), channel_id=1, source_target_pairs={{0,2},{1,3},{2,0},{3,1},{4,6},{5,7},{6,4},{7,5},{8,10},{9,11},{10,... | collective-permute-start | bytes 245768 | tf_op jit(solution)/shard_map/ppermute | solution.py:40
  65.8 8.8 %collective-permute-start.14 = (bf16[1,18,1536]{2,1,0:T(8,128)(2,1)S(1)}, bf16[1,18,1536]{2,1,0:T(8,128)(2,1)S(1)}, u32[]{:S(2)}, u32[]{:S(2)}) collective-permute-start(bf16[1,18,1536]{2,1,0:T(8,128)(2,1)S(1)} %get-tuple-element.16), channel_id=1, source_target_pairs={{0,8},{8,0},{16,24},{24,16},{32,40},{40,32},{48,56},{56,48},{64,72... | collective-permute-start | bytes 165896 | tf_op jit(solution)/shard_map/ppermute | solution.py:40
  74.7 1.7 %collective-permute-start.18 = (f32[160,128]{1,0:T(8,128)S(1)}, f32[160,128]{1,0:T(8,128)S(1)}, u32[]{:S(2)}, u32[]{:S(2)}) collective-permute-start(f32[160,128]{1,0:T(8,128)S(1)} %select_add_fusion.1), channel_id=1, source_target_pairs={{0,4},{1,5},{2,6},{3,7},{4,0},{5,1},{6,2},{7,3},{8,12},{9,13},{10,... | collective-permute-start | bytes 245768 | tf_op jit(solution)/shard_map/ppermute | solution.py:40
  77.0 2.5 %collective-permute-done.18 = f32[160,128]{1,0:T(8,128)S(1)} collective-permute-done((f32[160,128]{1,0:T(8,128)S(1)}, f32[160,128]{1,0:T(8,128)S(1)}, u32[]{:S(2)}, u32[]{:S(2)}) %collective-permute-start.18) | collective-permute-done | bytes 81952 | tf_op jit(solution)/shard_map/ppermute | solution.py:40
  79.7 3.2 %collective-permute-done.19 = f32[160,128]{1,0:T(8,128)S(1)} collective-permute-done((f32[160,128]{1,0:T(8,128)S(1)}, f32[160,128]{1,0:T(8,128)S(1)}, u32[]{:S(2)}, u32[]{:S(2)}) %collective-permute-start.19) | collective-permute-done | bytes 81952 | tf_op jit(solution)/shard_map/ppermute | solution.py:40
  82.9 4.5 %collective-permute-start.20 = (f32[160,128]{1,0:T(8,128)S(1)}, f32[160,128]{1,0:T(8,128)}, u32[]{:S(2)}, u32[]{:S(2)}) collective-permute-start(f32[160,128]{1,0:T(8,128)S(1)} %add.136), channel_id=1, source_target_pairs={{0,16},{8,24},{16,0},{24,8},{32,48},{40,56},{48,32},{56,40},{64,80... | collective-permute-start | bytes 245768 | tf_op jit(solution)/shard_map/ppermute | solution.py:40
  89.4 0.9 add.137
  90.3 1.7 %collective-permute-start.21 = (f32[160,128]{1,0:T(8,128)S(1)}, f32[160,128]{1,0:T(8,128)S(1)}, u32[]{:S(2)}, u32[]{:S(2)}) collective-permute-start(f32[160,128]{1,0:T(8,128)S(1)} %add.137), channel_id=1, source_target_pairs={{0,32},{8,40},{16,48},{24,56},{32,0},{40,8},{48,16},{56,24},{64,96... | collective-permute-start | bytes 245768 | tf_op jit(solution)/shard_map/ppermute | solution.py:40
  92.0 2.8 %fusion.71 = (bf16[16,16,12,128]{3,2,1,0:T(8,128)(2,1)S(1)}, bf16[16,16,12,128]{3,2,1,0:T(8,128)(2,1)S(1)}, bf16[16,16,12,128]{3,2,1,0:T(8,128)(2,1)S(1)}, bf16[...) fusion(bf16[18,18,12,128]{3,2,1,0:T(8,128)(2,1)S(1)} %reshape.178), kind=kLoop, calls=%fused_computation.178 | loop fusion | bytes 14155776 | tf_op jit(solution)/shard_map/slice | solution.py:149
  95.5 3.0 %collective-permute-start.22 = (f32[160,128]{1,0:T(8,128)S(1)}, f32[160,128]{1,0:T(8,128)S(1)}, u32[]{:S(2)}, u32[]{:S(2)}) collective-permute-start(f32[160,128]{1,0:T(8,128)S(1)} %add.138), channel_id=1, source_target_pairs={{0,64},{8,72},{16,80},{24,88},{32,96},{40,104},{48,112},{56,120},{... | collective-permute-start | bytes 245768 | tf_op jit(solution)/shard_map/ppermute | solution.py:40
  102.2 1.8 %collective-permute-done.23 = f32[160,128]{1,0:T(8,128)S(1)} collective-permute-done((f32[160,128]{1,0:T(8,128)S(1)}, f32[160,128]{1,0:T(8,128)S(1)}, u32[]{:S(2)}, u32[]{:S(2)}) %collective-permute-start.23) | collective-permute-done | bytes 81952 | tf_op jit(solution)/shard_map/ppermute | solution.py:40
  104.1 7.6 %collective-permute-start.24 = (f32[320,128]{1,0:T(8,128)S(1)}, f32[320,128]{1,0:T(8,128)S(1)}, u32[]{:S(2)}, u32[]{:S(2)}) collective-permute-start(f32[320,128]{1,0:T(8,128)S(1)} %maximum_select_fusion.3), channel_id=1, source_target_pairs={{0,1},{1,0},{2,3},{3,2},{4,5},{5,4},{6,7},{7,6},{8,9},{9,8},{10,11... | collective-permute-start | bytes 491528 | tf_op jit(solution)/shard_map/ppermute | solution.py:40
  112.7 1.4 %reshape.179 = bf16[16,16,768]{2,1,0:T(8,128)(2,1)} reshape(bf16[16,16,12,64]{3,2,1,0:T(8,128)(2,1)S(1)} %copy.79) | data formatting | bytes 786432 | tf_op jit(solution)/shard_map/reshape | solution.py:310
  (152 shorter events, 25.4 us)
Async XLA Ops:
  0.6 32.9 %copy-start = (bf16[128,20]{0,1:T(8,128)(2,1)S(1)}, bf16[128,20]{0,1:T(8,128)(2,1)}, u32[]{:S(2)}) copy-start(bf16[128,20]{0,1:T(8,128)(2,1)} %param.11) | copy-start | bytes 15364
  0.6 12.9 %copy-start.1 = (bf16[16,16,768]{2,1,0:T(8,128)(2,1)S(1)}, bf16[16,16,768]{2,1,0:T(8,128)(2,1)}, u32[]{:S(2)}) copy-start(bf16[16,16,768]{2,1,0:T(8,128)(2,1)} %param.8) | copy-start | bytes 1179652
  0.7 11.1 %copy-start.13 = (s32[16,16]{1,0:T(8,128)S(1)}, s32[16,16]{1,0:T(8,128)}, u32[]{:S(2)}) copy-start(s32[16,16]{1,0:T(8,128)} %param.12) | copy-start | bytes 3076
  1.5 4.8 %collective-permute-start = (bf16[1,16,768]{2,1,0:T(8,128)(2,1)S(1)}, bf16[1,16,768]{2,1,0:T(8,128)(2,1)S(1)}, u32[]{:S(2)}, u32[]{:S(2)}) collective-permute-start(bf16[1,16,768]{2,1,0:T(8,128)(2,1)S(1)} %get-tuple-element.33), channel_id=1, source_target_pairs={{0,8},{8,0},{16,24},{24,16},{32,40},{40,32},{48,56},{56,48},{64,72... | collective-permute-start | bytes 73736 | tf_op jit(solution)/shard_map/ppermute | solution.py:26
  3.5 2.7 %collective-permute-start.1 = (bf16[1,16,768]{2,1,0:T(8,128)(2,1)S(1)}, bf16[1,16,768]{2,1,0:T(8,128)(2,1)S(1)}, u32[]{:S(2)}, u32[]{:S(2)}) collective-permute-start(bf16[1,16,768]{2,1,0:T(8,128)(2,1)S(1)} %get-tuple-element.34), channel_id=1, source_target_pairs={{8,16},{16,8},{24,32},{32,24},{40,48},{48,40},{56,64},{64,56},{72,... | collective-permute-start | bytes 73736 | tf_op jit(solution)/shard_map/ppermute | solution.py:27
  7.5 5.9 %collective-permute-start.3 = (bf16[18,1,768]{2,1,0:T(2,128)(2,1)S(1)}, bf16[18,1,768]{2,1,0:T(2,128)(2,1)S(1)}, u32[]{:S(2)}, u32[]{:S(2)}) collective-permute-start(bf16[18,1,768]{2,1,0:T(2,128)(2,1)S(1)} %broadcast_select_fusion.6), channel_id=1, source_target_pairs={{1,2},{2,1},{3,4},{4,3},{5,6},{6,5},{9,10},{10,9},{11,12},{12,11},... | collective-permute-start | bytes 82952 | tf_op jit(solution)/shard_map/ppermute | solution.py:27
  11.6 1.8 %collective-permute-start.2 = (bf16[18,1,768]{2,1,0:T(2,128)(2,1)S(1)}, bf16[18,1,768]{2,1,0:T(2,128)(2,1)S(1)}, u32[]{:S(2)}, u32[]{:S(2)}) collective-permute-start(bf16[18,1,768]{2,1,0:T(2,128)(2,1)S(1)} %get-tuple-element.19), channel_id=1, source_target_pairs={{0,1},{1,0},{2,3},{3,2},{4,5},{5,4},{6,7},{7,6},{8,9},{9,8},{10,11... | collective-permute-start | bytes 82952 | tf_op jit(solution)/shard_map/ppermute | solution.py:26
  21.5 12.3 %copy-start.14 = (s32[1,1,32]{2,1,0:T(1,128)S(1)}, s32[1,1,32]{2,1,0:T(1,128)}, u32[]{:S(2)}) copy-start(s32[1,1,32]{2,1,0:T(1,128)} %param.15) | copy-start | bytes 388
  21.9 5.2 %collective-permute-start.4 = (bf16[1,3,32,128]{3,2,1,0:T(8,128)(2,1)S(1)}, bf16[1,3,32,128]{3,2,1,0:T(8,128)(2,1)S(1)}, u32[]{:S(2)}, u32[]{:S(2)}) collective-permute-start(bf16[1,3,32,128]{3,2,1,0:T(8,128)(2,1)S(1)} %bitcast.151), channel_id=1, source_target_pairs={{0,8},{8,0},{16,24},{24,16},{32,40},{40,32},{48,56},{56,48},{64,72... | collective-permute-start | bytes 73736 | tf_op jit(solution)/shard_map/ppermute | solution.py:26
  25.6 1.4 %collective-permute-start.5 = (bf16[1,3,32,128]{3,2,1,0:T(8,128)(2,1)S(1)}, bf16[1,3,32,128]{3,2,1,0:T(8,128)(2,1)S(1)}, u32[]{:S(2)}, u32[]{:S(2)}) collective-permute-start(bf16[1,3,32,128]{3,2,1,0:T(8,128)(2,1)S(1)} %bitcast.150), channel_id=1, source_target_pairs={{8,16},{16,8},{24,32},{32,24},{40,48},{48,40},{56,64},{64,56},{72,... | collective-permute-start | bytes 73736 | tf_op jit(solution)/shard_map/ppermute | solution.py:27
  27.1 4.4 %collective-permute-start.6 = (bf16[5,1,32,128]{3,2,1,0:T(8,128)(2,1)S(1)}, bf16[5,1,32,128]{3,2,1,0:T(8,128)(2,1)S(1)}, u32[]{:S(2)}, u32[]{:S(2)}) collective-permute-start(bf16[5,1,32,128]{3,2,1,0:T(8,128)(2,1)S(1)} %get-tuple-element.48), channel_id=1, source_target_pairs={{0,1},{1,0},{2,3},{3,2},{4,5},{5,4},{6,7},{7,6},{8,9},{9,8},{10,11... | collective-permute-start | bytes 122888 | tf_op jit(solution)/shard_map/ppermute | solution.py:26
  27.6 5.6 %collective-permute-start.7 = (bf16[5,1,32,128]{3,2,1,0:T(8,128)(2,1)S(1)}, bf16[5,1,32,128]{3,2,1,0:T(8,128)(2,1)S(1)}, u32[]{:S(2)}, u32[]{:S(2)}) collective-permute-start(bf16[5,1,32,128]{3,2,1,0:T(8,128)(2,1)S(1)} %get-tuple-element.49), channel_id=1, source_target_pairs={{1,2},{2,1},{3,4},{4,3},{5,6},{6,5},{9,10},{10,9},{11,12},{12,11},... | collective-permute-start | bytes 122888 | tf_op jit(solution)/shard_map/ppermute | solution.py:27
  34.2 7.4 %collective-permute-start.8 = (bf16[1,1,32,128]{3,2,1,0:T(8,128)(2,1)S(1)}, bf16[1,1,32,128]{3,2,1,0:T(8,128)(2,1)S(1)}, u32[]{:S(2)}, u32[]{:S(2)}) collective-permute-start(bf16[1,1,32,128]{3,2,1,0:T(8,128)(2,1)S(1)} %fusion.53), channel_id=1, source_target_pairs={{0,8},{8,0},{16,24},{24,16},{32,40},{40,32},{48,56},{56,48},{64,72... | collective-permute-start | bytes 24584 | tf_op jit(solution)/shard_map/ppermute | solution.py:26
  40.6 1.0 collective-permute-start.9
  41.7 5.1 %collective-permute-start.10 = (bf16[3,1,32,128]{3,2,1,0:T(8,128)(2,1)S(1)}, bf16[3,1,32,128]{3,2,1,0:T(8,128)(2,1)S(1)}, u32[]{:S(2)}, u32[]{:S(2)}) collective-permute-start(bf16[3,1,32,128]{3,2,1,0:T(8,128)(2,1)S(1)} %pad_maximum_fusion.15), channel_id=1, source_target_pairs={{0,1},{1,0},{2,3},{3,2},{4,5},{5,4},{6,7},{7,6},{8,9},{9,8},{10,11... | collective-permute-start | bytes 73736 | tf_op jit(solution)/shard_map/ppermute | solution.py:26
  41.8 5.9 %collective-permute-start.11 = (bf16[3,1,32,128]{3,2,1,0:T(8,128)(2,1)S(1)}, bf16[3,1,32,128]{3,2,1,0:T(8,128)(2,1)S(1)}, u32[]{:S(2)}, u32[]{:S(2)}) collective-permute-start(bf16[3,1,32,128]{3,2,1,0:T(8,128)(2,1)S(1)} %pad_maximum_fusion.15), channel_id=1, source_target_pairs={{1,2},{2,1},{3,4},{4,3},{5,6},{6,5},{9,10},{10,9},{11,12},{12,11},... | collective-permute-start | bytes 73736 | tf_op jit(solution)/shard_map/ppermute | solution.py:27
  56.7 4.4 %collective-permute-start.12 = (bf16[16,1,1536]{2,1,0:T(2,128)(2,1)S(1)}, bf16[16,1,1536]{2,1,0:T(2,128)(2,1)S(1)}, u32[]{:S(2)}, u32[]{:S(2)}) collective-permute-start(bf16[16,1,1536]{2,1,0:T(2,128)(2,1)S(1)} %get-tuple-element.31), channel_id=1, source_target_pairs={{0,1},{1,0},{2,3},{3,2},{4,5},{5,4},{6,7},{7,6},{8,9},{9,8},{10,11... | collective-permute-start | bytes 147464 | tf_op jit(solution)/shard_map/ppermute | solution.py:40
  56.8 6.4 %collective-permute-start.13 = (bf16[16,1,1536]{2,1,0:T(2,128)(2,1)S(1)}, bf16[16,1,1536]{2,1,0:T(2,128)(2,1)S(1)}, u32[]{:S(2)}, u32[]{:S(2)}) collective-permute-start(bf16[16,1,1536]{2,1,0:T(2,128)(2,1)S(1)} %get-tuple-element.32), channel_id=1, source_target_pairs={{1,2},{2,1},{3,4},{4,3},{5,6},{6,5},{9,10},{10,9},{11,12},{12,11},... | collective-permute-start | bytes 147464 | tf_op jit(solution)/shard_map/ppermute | solution.py:61
  61.0 15.4 %copy-start.4 = (bf16[3,3,64,128]{3,2,1,0:T(8,128)(2,1)S(1)}, bf16[3,3,64,128]{3,2,1,0:T(8,128)(2,1)}, u32[]{:S(2)}) copy-start(bf16[3,3,64,128]{3,2,1,0:T(8,128)(2,1)} %param.9) | copy-start | bytes 442372
  61.0 2.5 %collective-permute-start.16 = (f32[320,128]{1,0:T(8,128)S(1)}, f32[320,128]{1,0:T(8,128)S(1)}, u32[]{:S(2)}, u32[]{:S(2)}) collective-permute-start(f32[320,128]{1,0:T(8,128)S(1)} %slice_select_fusion), channel_id=1, source_target_pairs={{0,1},{1,0},{2,3},{3,2},{4,5},{5,4},{6,7},{7,6},{8,9},{9,8},{10,11... | collective-permute-start | bytes 491528 | tf_op jit(solution)/shard_map/ppermute | solution.py:40
  63.6 11.0 %collective-permute-start.17 = (f32[160,128]{1,0:T(8,128)S(1)}, f32[160,128]{1,0:T(8,128)S(1)}, u32[]{:S(2)}, u32[]{:S(2)}) collective-permute-start(f32[160,128]{1,0:T(8,128)S(1)} %slice_select_fusion.1), channel_id=1, source_target_pairs={{0,2},{1,3},{2,0},{3,1},{4,6},{5,7},{6,4},{7,5},{8,10},{9,11},{10,... | collective-permute-start | bytes 245768 | tf_op jit(solution)/shard_map/ppermute | solution.py:40
  65.2 14.5 %collective-permute-start.15 = (bf16[1,18,1536]{2,1,0:T(8,128)(2,1)S(1)}, bf16[1,18,1536]{2,1,0:T(8,128)(2,1)S(1)}, u32[]{:S(2)}, u32[]{:S(2)}) collective-permute-start(bf16[1,18,1536]{2,1,0:T(8,128)(2,1)S(1)} %broadcast_select_fusion.11), channel_id=1, source_target_pairs={{8,16},{16,8},{24,32},{32,24},{40,48},{48,40},{56,64},{64,56},{72,... | collective-permute-start | bytes 165896 | tf_op jit(solution)/shard_map/ppermute | solution.py:61
  65.8 13.8 %collective-permute-start.14 = (bf16[1,18,1536]{2,1,0:T(8,128)(2,1)S(1)}, bf16[1,18,1536]{2,1,0:T(8,128)(2,1)S(1)}, u32[]{:S(2)}, u32[]{:S(2)}) collective-permute-start(bf16[1,18,1536]{2,1,0:T(8,128)(2,1)S(1)} %get-tuple-element.16), channel_id=1, source_target_pairs={{0,8},{8,0},{16,24},{24,16},{32,40},{40,32},{48,56},{56,48},{64,72... | collective-permute-start | bytes 165896 | tf_op jit(solution)/shard_map/ppermute | solution.py:40
  74.7 4.9 %collective-permute-start.18 = (f32[160,128]{1,0:T(8,128)S(1)}, f32[160,128]{1,0:T(8,128)S(1)}, u32[]{:S(2)}, u32[]{:S(2)}) collective-permute-start(f32[160,128]{1,0:T(8,128)S(1)} %select_add_fusion.1), channel_id=1, source_target_pairs={{0,4},{1,5},{2,6},{3,7},{4,0},{5,1},{6,2},{7,3},{8,12},{9,13},{10,... | collective-permute-start | bytes 245768 | tf_op jit(solution)/shard_map/ppermute | solution.py:40
  79.6 3.4 %collective-permute-start.19 = (f32[160,128]{1,0:T(8,128)S(1)}, f32[160,128]{1,0:T(8,128)S(1)}, u32[]{:S(2)}, u32[]{:S(2)}) collective-permute-start(f32[160,128]{1,0:T(8,128)S(1)} %add.135), channel_id=1, source_target_pairs={{0,8},{8,0},{16,24},{24,16},{32,40},{40,32},{48,56},{56,48},{64,72... | collective-permute-start | bytes 245768 | tf_op jit(solution)/shard_map/ppermute | solution.py:40
  82.9 6.5 %collective-permute-start.20 = (f32[160,128]{1,0:T(8,128)S(1)}, f32[160,128]{1,0:T(8,128)}, u32[]{:S(2)}, u32[]{:S(2)}) collective-permute-start(f32[160,128]{1,0:T(8,128)S(1)} %add.136), channel_id=1, source_target_pairs={{0,16},{8,24},{16,0},{24,8},{32,48},{40,56},{48,32},{56,40},{64,80... | collective-permute-start | bytes 245768 | tf_op jit(solution)/shard_map/ppermute | solution.py:40
  90.3 5.2 %collective-permute-start.21 = (f32[160,128]{1,0:T(8,128)S(1)}, f32[160,128]{1,0:T(8,128)S(1)}, u32[]{:S(2)}, u32[]{:S(2)}) collective-permute-start(f32[160,128]{1,0:T(8,128)S(1)} %add.137), channel_id=1, source_target_pairs={{0,32},{8,40},{16,48},{24,56},{32,0},{40,8},{48,16},{56,24},{64,96... | collective-permute-start | bytes 245768 | tf_op jit(solution)/shard_map/ppermute | solution.py:40
  95.5 5.1 %collective-permute-start.22 = (f32[160,128]{1,0:T(8,128)S(1)}, f32[160,128]{1,0:T(8,128)S(1)}, u32[]{:S(2)}, u32[]{:S(2)}) collective-permute-start(f32[160,128]{1,0:T(8,128)S(1)} %add.138), channel_id=1, source_target_pairs={{0,64},{8,72},{16,80},{24,88},{32,96},{40,104},{48,112},{56,120},{... | collective-permute-start | bytes 245768 | tf_op jit(solution)/shard_map/ppermute | solution.py:40
  100.7 3.4 %collective-permute-start.23 = (f32[160,128]{1,0:T(8,128)S(1)}, f32[160,128]{1,0:T(8,128)S(1)}, u32[]{:S(2)}, u32[]{:S(2)}) collective-permute-start(f32[160,128]{1,0:T(8,128)S(1)} %add.139), channel_id=1, source_target_pairs={{0,2},{1,3},{2,0},{3,1},{4,6},{5,7},{6,4},{7,5},{8,10},{9,11},{10,... | collective-permute-start | bytes 245768 | tf_op jit(solution)/shard_map/ppermute | solution.py:40
  101.8 9.8 %copy-start.5 = (bf16[128,64]{0,1:T(8,128)(2,1)S(1)}, bf16[128,64]{0,1:T(8,128)(2,1)}, u32[]{:S(2)}) copy-start(bf16[128,64]{0,1:T(8,128)(2,1)} %get-tuple-element.44) | copy-start | bytes 49156
  101.8 9.8 %copy-start.6 = (bf16[128,64]{0,1:T(8,128)(2,1)S(1)}, bf16[128,64]{0,1:T(8,128)(2,1)}, u32[]{:S(2)}) copy-start(bf16[128,64]{0,1:T(8,128)(2,1)} %get-tuple-element.45) | copy-start | bytes 49156
  104.1 10.0 %collective-permute-start.24 = (f32[320,128]{1,0:T(8,128)S(1)}, f32[320,128]{1,0:T(8,128)S(1)}, u32[]{:S(2)}, u32[]{:S(2)}) collective-permute-start(f32[320,128]{1,0:T(8,128)S(1)} %maximum_select_fusion.3), channel_id=1, source_target_pairs={{0,1},{1,0},{2,3},{3,2},{4,5},{5,4},{6,7},{7,6},{8,9},{9,8},{10,11... | collective-permute-start | bytes 491528 | tf_op jit(solution)/shard_map/ppermute | solution.py:40
  (8 other events, 16.6 us)

commit v16 on v9

--- a/solution.py
+++ b/solution.py
@@ -35,8 +35,16 @@
     return cells
 
 
+def ring_partner(i, bit):
+    low = i % (bit * 4) // bit
+    other = (low + 1) % 4 if low % 2 else (low - 1) % 4
+    return i + (other - low) * bit
+
+
 def exchange(value, axis, bit):
     size = lax.axis_size(axis)
+    if axis == "row" and bit in (2, 8):
+        return lax.ppermute(value, axis, [(i, ring_partner(i, bit // 2)) for i in range(size)])
     return lax.ppermute(value, axis, [(i, i ^ bit) for i in range(size)])
 
 

time: 111 us -> 110 us (level)
    ppermute x9 -> x7, starting transfers between devices: 28 us -> 20.4 us  [exchange(): return lax.ppermute(value, axis, [(i, i ^ bit) for i in range(size)])]
    ppermute x0 -> x2, starting transfers between devices: none -> 6.45 us  [exchange(): lax.ppermute(value, axis, [(i, ring_partner(i, bit // 2)) for i in range(...]
    ppermute x0 -> x2, waiting for transfers between devices: none -> 1.3 us  [exchange(): lax.ppermute(value, axis, [(i, ring_partner(i, bit // 2)) for i in range(...]
    ppermute x9 -> x7, waiting for transfers between devices: 8.14 us -> 6.99 us  [exchange(): return lax.ppermute(value, axis, [(i, i ^ bit) for i in range(size)])]
where the time goes in v16:
time: 110 us
  starting transfers between devices  58.7 us (53%)
  local copies, waits for them, and re-layouts  16 us (15%)
  waiting for transfers between devices  14.6 us (13%)
  matrix products  12.6 us (11%)
  other arithmetic  6.67 us (6%)
  between operations  1.47 us (1%)
    ppermute x7, starting transfers between devices, exchange(): return lax.ppermute(value, axis, [(i, i ^ bit) for i in range(size)])  20.4 us
    ppermute x6, starting transfers between devices, with_halo(): lax.ppermute(jnp.where(odd, tail, head), axis, [pair for k in range(1, co...  13.8 us
    ppermute x6, starting transfers between devices, with_halo(): lax.ppermute(jnp.where(odd, head, tail), axis, [(i, i ^ 1) for i in range...  13.2 us
    unnamed x30, local copies, waits for them, and re-layouts  8.06 us
    ppermute x7, waiting for transfers between devices, exchange(): return lax.ppermute(value, axis, [(i, i ^ bit) for i in range(size)])  6.99 us
    ppermute x2, starting transfers between devices, exchange(): lax.ppermute(value, axis, [(i, ring_partner(i, bit // 2)) for i in range(...  6.45 us
    ppermute x6, waiting for transfers between devices, with_halo(): lax.ppermute(jnp.where(odd, tail, head), axis, [pair for k in range(1, co...  4.74 us
    ppermute x2, starting transfers between devices, outer_swap(): lax.ppermute(piece, axis, [pair for k in range(1, count - 1, 2) for pair...  4.72 us
  transfers between devices with their start and end apart: 23, of which 12 were waited for; matrix products, arithmetic and copies ran while one was open for 12% of the time, Pallas kernels for 0%

profile of v16, /device:TPU:1, one launch (start us, length us, event | category | flops | bytes accessed | tf_op | source)
XLA Modules:
  0.0 110.0 jit_solution(5811132448717366557)
XLA Ops:
  1.5 2.0 %collective-permute-start = (bf16[1,16,768]{2,1,0:T(8,128)(2,1)S(1)}, bf16[1,16,768]{2,1,0:T(8,128)(2,1)S(1)}, u32[]{:S(2)}, u32[]{:S(2)}) collective-permute-start(bf16[1,16,768]{2,1,0:T(8,128)(2,1)S(1)} %get-tuple-element.33), channel_id=1, source_target_pairs={{0,8},{8,0},{16,24},{24,16},{32,40},{40,32},{48,56},{56,48},{64,72... | collective-permute-start | bytes 73736 | tf_op jit(solution)/shard_map/ppermute | solution.py:26
  4.2 0.9 copy.68
  6.3 1.1 %broadcast_select_fusion.7 = (bf16[18,1,768]{2,1,0:T(2,128)(2,1)S(1)}, bf16[18,1,768]{2,1,0:T(2,128)(2,1)S(1)}, bf16[18,1,768]{2,1,0:T(2,128)(2,1)S(1)}) fusion(pred[]{:T(512)S(6)} %eq.104, bf16[1,16,768]{2,1,0:T(8,128)(2,1)S(1)} %get-tuple-element.61, bf16[16,16,768]{2,1,0:T(8,128)(2,1)} %param.8, bf16[1,16,768]{2,1,0:T(8,128)(2,1)S(1)} %get-tuple-element.60), kind=kLoop, calls=%fused_computation.66 | loop fusion | flops 179712 | bytes 525313 | tf_op jit(solution)/shard_map/jit(_where)/select_n | solution.py:26
  7.4 1.0 collective-permute-start.2
  8.5 3.1 %collective-permute-start.3 = (bf16[18,1,768]{2,1,0:T(2,128)(2,1)S(1)}, bf16[18,1,768]{2,1,0:T(2,128)(2,1)S(1)}, u32[]{:S(2)}, u32[]{:S(2)}) collective-permute-start(bf16[18,1,768]{2,1,0:T(2,128)(2,1)S(1)} %broadcast_select_fusion.6), channel_id=1, source_target_pairs={{1,2},{2,1},{3,4},{4,3},{5,6},{6,5},{9,10},{10,9},{11,12},{12,11},... | collective-permute-start | bytes 82952 | tf_op jit(solution)/shard_map/ppermute | solution.py:27
  11.8 2.2 %collective-permute-done.3 = bf16[18,1,768]{2,1,0:T(2,128)(2,1)S(1)} collective-permute-done((bf16[18,1,768]{2,1,0:T(2,128)(2,1)S(1)}, bf16[18,1,768]{2,1,0:T(2,128)(2,1)S(1)}, u32[]{:S(2)}, u32[]{:S(2)}) %collective-permute-start.3) | collective-permute-done | bytes 27680 | tf_op jit(solution)/shard_map/ppermute | solution.py:27
  15.3 1.1 copy-done.4
  16.4 1.6 %fusion.74 = f32[16,16,12,128]{3,2,1,0:T(8,128)S(1)} fusion(bf16[18,18,12,64]{3,2,1,0:T(8,128)(2,1)S(1)} %reshape.214, bf16[3,3,64,128]{3,2,1,0:T(8,128)(2,1)S(1)} %copy-done.6), kind=kOutput, calls=%fused_computation.186 | convolution fusion | flops 452984832 | bytes 2217984 | tf_op jit(solution)/shard_map/conv_general_dilated | solution.py:142
  20.8 3.7 %collective-permute-start.4 = (bf16[1,3,32,128]{3,2,1,0:T(8,128)(2,1)S(1)}, bf16[1,3,32,128]{3,2,1,0:T(8,128)(2,1)S(1)}, u32[]{:S(2)}, u32[]{:S(2)}) collective-permute-start(bf16[1,3,32,128]{3,2,1,0:T(8,128)(2,1)S(1)} %bitcast.153), channel_id=1, source_target_pairs={{0,8},{8,0},{16,24},{24,16},{32,40},{40,32},{48,56},{56,48},{64,72... | collective-permute-start | bytes 73736 | tf_op jit(solution)/shard_map/ppermute | solution.py:26
  25.9 4.0 %collective-permute-start.7 = (bf16[5,1,32,128]{3,2,1,0:T(8,128)(2,1)S(1)}, bf16[5,1,32,128]{3,2,1,0:T(8,128)(2,1)S(1)}, u32[]{:S(2)}, u32[]{:S(2)}) collective-permute-start(bf16[5,1,32,128]{3,2,1,0:T(8,128)(2,1)S(1)} %get-tuple-element.49), channel_id=1, source_target_pairs={{1,2},{2,1},{3,4},{4,3},{5,6},{6,5},{9,10},{10,9},{11,12},{12,11},... | collective-permute-start | bytes 122888 | tf_op jit(solution)/shard_map/ppermute | solution.py:27
  29.9 1.6 %collective-permute-done.7 = bf16[5,1,32,128]{3,2,1,0:T(8,128)(2,1)S(1)} collective-permute-done((bf16[5,1,32,128]{3,2,1,0:T(8,128)(2,1)S(1)}, bf16[5,1,32,128]{3,2,1,0:T(8,128)(2,1)S(1)}, u32[]{:S(2)}, u32[]{:S(2)}) %collective-permute-start.7) | collective-permute-done | bytes 40992 | tf_op jit(solution)/shard_map/ppermute | solution.py:27
  32.6 6.3 %collective-permute-start.8 = (bf16[1,1,32,128]{3,2,1,0:T(8,128)(2,1)S(1)}, bf16[1,1,32,128]{3,2,1,0:T(8,128)(2,1)S(1)}, u32[]{:S(2)}, u32[]{:S(2)}) collective-permute-start(bf16[1,1,32,128]{3,2,1,0:T(8,128)(2,1)S(1)} %fusion.54), channel_id=1, source_target_pairs={{0,8},{8,0},{16,24},{24,16},{32,40},{40,32},{48,56},{56,48},{64,72... | collective-permute-start | bytes 24584 | tf_op jit(solution)/shard_map/ppermute | solution.py:26
  40.1 4.7 %collective-permute-start.11 = (bf16[3,1,32,128]{3,2,1,0:T(8,128)(2,1)S(1)}, bf16[3,1,32,128]{3,2,1,0:T(8,128)(2,1)S(1)}, u32[]{:S(2)}, u32[]{:S(2)}) collective-permute-start(bf16[3,1,32,128]{3,2,1,0:T(8,128)(2,1)S(1)} %pad_maximum_fusion.17), channel_id=1, source_target_pairs={{1,2},{2,1},{3,4},{4,3},{5,6},{6,5},{9,10},{10,9},{11,12},{12,11},... | collective-permute-start | bytes 73736 | tf_op jit(solution)/shard_map/ppermute | solution.py:27
  45.2 0.9 collective-permute-done.11
  47.8 1.2 %copy-done.2 = f32[16,16,12,128]{3,2,1,0:T(8,128)S(1)} copy-done((f32[16,16,12,128]{3,2,1,0:T(8,128)S(1)}, f32[16,16,12,128]{3,2,1,0:T(8,128)}, u32[]{:S(2)}) %copy-start.2) | copy-done | bytes 1572888
  49.0 1.0 multiply_convert_fusion
  50.1 1.3 %copy-done.5 = bf16[18,18,12,64]{3,2,1,0:T(8,128)(2,1)S(1)} copy-done((bf16[18,18,12,64]{3,2,1,0:T(8,128)(2,1)S(1)}, bf16[18,18,12,64]{3,2,1,0:T(8,128)(2,1)}, u32[]{:S(2)}) %copy-start.5) | copy-done | bytes 497688
  51.4 2.6 %fusion.20 = f32[3,3,64,128]{3,2,1,0:T(8,128)S(1)} fusion(bf16[18,18,12,64]{3,2,1,0:T(8,128)(2,1)S(1)} %copy-done.5, bf16[16,16,12,128]{3,1,2,0:T(8,128)(2,1)S(1)} %multiply_convert_fusion), kind=kOutput, calls=%fused_computation.34 | convolution fusion | flops 452984832 | bytes 1579008 | tf_op jit(solution)/shard_map/conv_general_dilated | solution.py:289
  56.1 4.1 %collective-permute-start.15 = (bf16[16,1,1536]{2,1,0:T(2,128)(2,1)S(1)}, bf16[16,1,1536]{2,1,0:T(2,128)(2,1)S(1)}, u32[]{:S(2)}, u32[]{:S(2)}) collective-permute-start(bf16[16,1,1536]{2,1,0:T(2,128)(2,1)S(1)} %get-tuple-element.32), channel_id=1, source_target_pairs={{1,2},{2,1},{3,4},{4,3},{5,6},{6,5},{9,10},{10,9},{11,12},{12,11},... | collective-permute-start | bytes 147464 | tf_op jit(solution)/shard_map/ppermute | solution.py:69
  60.4 1.4 %collective-permute-start.13 = (f32[160,128]{1,0:T(8,128)S(1)}, f32[160,128]{1,0:T(8,128)S(1)}, u32[]{:S(2)}, u32[]{:S(2)}) collective-permute-start(f32[160,128]{1,0:T(8,128)S(1)} %slice_select_fusion.1), channel_id=1, source_target_pairs={{0,2},{1,3},{2,0},{3,1},{4,6},{5,7},{6,4},{7,5},{8,10},{9,11},{10,... | collective-permute-start | bytes 245768 | tf_op jit(solution)/shard_map/ppermute | solution.py:48
  62.7 1.5 %collective-permute-done.13 = f32[160,128]{1,0:T(8,128)S(1)} collective-permute-done((f32[160,128]{1,0:T(8,128)S(1)}, f32[160,128]{1,0:T(8,128)S(1)}, u32[]{:S(2)}, u32[]{:S(2)}) %collective-permute-start.13) | collective-permute-done | bytes 81952 | tf_op jit(solution)/shard_map/ppermute | solution.py:48
  64.2 3.0 %collective-permute-start.14 = (f32[160,128]{1,0:T(8,128)S(1)}, f32[160,128]{1,0:T(8,128)S(1)}, u32[]{:S(2)}, u32[]{:S(2)}) collective-permute-start(f32[160,128]{1,0:T(8,128)S(1)} %select_add_fusion), channel_id=1, source_target_pairs={{0,4},{1,5},{2,6},{3,7},{4,0},{5,1},{6,2},{7,3},{8,12},{9,13},{10,... | collective-permute-start | bytes 245768 | tf_op jit(solution)/shard_map/ppermute | solution.py:48
  67.3 1.8 %collective-permute-done.14 = f32[160,128]{1,0:T(8,128)S(1)} collective-permute-done((f32[160,128]{1,0:T(8,128)S(1)}, f32[160,128]{1,0:T(8,128)S(1)}, u32[]{:S(2)}, u32[]{:S(2)}) %collective-permute-start.14) | collective-permute-done | bytes 81952 | tf_op jit(solution)/shard_map/ppermute | solution.py:48
  69.1 5.8 %collective-permute-start.16 = (f32[376,128]{1,0:T(8,128)S(1)}, f32[376,128]{1,0:T(8,128)S(1)}, u32[]{:S(2)}, u32[]{:S(2)}) collective-permute-start(f32[376,128]{1,0:T(8,128)S(1)} %pad_maximum_fusion.4), channel_id=1, source_target_pairs={{0,8},{8,0},{16,24},{24,16},{32,40},{40,32},{48,56},{56,48},{64,72... | collective-permute-start | bytes 577544 | tf_op jit(solution)/shard_map/ppermute | solution.py:48
  75.7 2.9 %collective-permute-done.16 = f32[376,128]{1,0:T(8,128)S(1)} collective-permute-done((f32[376,128]{1,0:T(8,128)S(1)}, f32[376,128]{1,0:T(8,128)S(1)}, u32[]{:S(2)}, u32[]{:S(2)}) %collective-permute-start.16) | collective-permute-done | bytes 192544 | tf_op jit(solution)/shard_map/ppermute | solution.py:48
  78.7 3.7 %collective-permute-start.18 = (f32[160,128]{1,0:T(8,128)S(1)}, f32[160,128]{1,0:T(8,128)S(1)}, u32[]{:S(2)}, u32[]{:S(2)}) collective-permute-start(f32[160,128]{1,0:T(8,128)S(1)} %slice_add_fusion.1), channel_id=1, source_target_pairs={{0,24},{8,16},{16,8},{24,0},{32,56},{40,48},{48,40},{56,32},{64,88... | collective-permute-start | bytes 245768 | tf_op jit(solution)/shard_map/ppermute | solution.py:47
  84.5 2.8 %collective-permute-start.19 = (f32[160,128]{1,0:T(8,128)S(1)}, f32[160,128]{1,0:T(8,128)S(1)}, u32[]{:S(2)}, u32[]{:S(2)}) collective-permute-start(f32[160,128]{1,0:T(8,128)S(1)} %add.137), channel_id=1, source_target_pairs={{0,32},{8,40},{16,48},{24,56},{32,0},{40,8},{48,16},{56,24},{64,96... | collective-permute-start | bytes 245768 | tf_op jit(solution)/shard_map/ppermute | solution.py:48
  87.2 2.8 %fusion.72 = (bf16[16,16,12,128]{3,2,1,0:T(8,128)(2,1)S(1)}, bf16[16,16,12,128]{3,2,1,0:T(8,128)(2,1)S(1)}, bf16[16,16,12,128]{3,2,1,0:T(8,128)(2,1)S(1)}, bf16[...) fusion(bf16[18,18,12,128]{3,2,1,0:T(8,128)(2,1)S(1)} %reshape.224), kind=kLoop, calls=%fused_computation.184 | loop fusion | bytes 14155776 | tf_op jit(solution)/shard_map/slice | solution.py:157
  90.7 2.8 %collective-permute-start.20 = (f32[160,128]{1,0:T(8,128)S(1)}, f32[160,128]{1,0:T(8,128)S(1)}, u32[]{:S(2)}, u32[]{:S(2)}) collective-permute-start(f32[160,128]{1,0:T(8,128)S(1)} %add.138), channel_id=1, source_target_pairs={{0,96},{8,104},{16,112},{24,120},{32,64},{40,72},{48,80},{56,88},{... | collective-permute-start | bytes 245768 | tf_op jit(solution)/shard_map/ppermute | solution.py:47
  95.5 2.3 %collective-permute-start.21 = (f32[160,128]{1,0:T(8,128)S(1)}, f32[160,128]{1,0:T(8,128)S(1)}, u32[]{:S(2)}, u32[]{:S(2)}) collective-permute-start(f32[160,128]{1,0:T(8,128)S(1)} %add.139), channel_id=1, source_target_pairs={{0,2},{1,3},{2,0},{3,1},{4,6},{5,7},{6,4},{7,5},{8,10},{9,11},{10,... | collective-permute-start | bytes 245768 | tf_op jit(solution)/shard_map/ppermute | solution.py:48
  100.0 5.1 %collective-permute-start.22 = (f32[320,128]{1,0:T(8,128)S(1)}, f32[320,128]{1,0:T(8,128)S(1)}, u32[]{:S(2)}, u32[]{:S(2)}) collective-permute-start(f32[320,128]{1,0:T(8,128)S(1)} %maximum_select_fusion.3), channel_id=1, source_target_pairs={{0,1},{1,0},{2,3},{3,2},{4,5},{5,4},{6,7},{7,6},{8,9},{9,8},{10,11... | collective-permute-start | bytes 491528 | tf_op jit(solution)/shard_map/ppermute | solution.py:48
  106.1 1.4 %reshape.225 = bf16[16,16,768]{2,1,0:T(8,128)(2,1)} reshape(bf16[16,16,12,64]{3,2,1,0:T(8,128)(2,1)S(1)} %copy.92) | data formatting | bytes 786432 | tf_op jit(solution)/shard_map/reshape | solution.py:318
  (143 shorter events, 26.8 us)
Async XLA Ops:
  0.6 31.3 %copy-start = (bf16[128,20]{0,1:T(8,128)(2,1)S(1)}, bf16[128,20]{0,1:T(8,128)(2,1)}, u32[]{:S(2)}) copy-start(bf16[128,20]{0,1:T(8,128)(2,1)} %param.11) | copy-start | bytes 15364
  0.6 13.5 %copy-start.3 = (bf16[16,16,768]{2,1,0:T(8,128)(2,1)S(1)}, bf16[16,16,768]{2,1,0:T(8,128)(2,1)}, u32[]{:S(2)}) copy-start(bf16[16,16,768]{2,1,0:T(8,128)(2,1)} %param.8) | copy-start | bytes 1179652
  0.7 11.1 %copy-start.7 = (s32[16,16]{1,0:T(8,128)S(1)}, s32[16,16]{1,0:T(8,128)}, u32[]{:S(2)}) copy-start(s32[16,16]{1,0:T(8,128)} %param.12) | copy-start | bytes 3076
  1.5 4.8 %collective-permute-start = (bf16[1,16,768]{2,1,0:T(8,128)(2,1)S(1)}, bf16[1,16,768]{2,1,0:T(8,128)(2,1)S(1)}, u32[]{:S(2)}, u32[]{:S(2)}) collective-permute-start(bf16[1,16,768]{2,1,0:T(8,128)(2,1)S(1)} %get-tuple-element.33), channel_id=1, source_target_pairs={{0,8},{8,0},{16,24},{24,16},{32,40},{40,32},{48,56},{56,48},{64,72... | collective-permute-start | bytes 73736 | tf_op jit(solution)/shard_map/ppermute | solution.py:26
  3.5 2.7 %collective-permute-start.1 = (bf16[1,16,768]{2,1,0:T(8,128)(2,1)S(1)}, bf16[1,16,768]{2,1,0:T(8,128)(2,1)S(1)}, u32[]{:S(2)}, u32[]{:S(2)}) collective-permute-start(bf16[1,16,768]{2,1,0:T(8,128)(2,1)S(1)} %get-tuple-element.34), channel_id=1, source_target_pairs={{8,16},{16,8},{24,32},{32,24},{40,48},{48,40},{56,64},{64,56},{72,... | collective-permute-start | bytes 73736 | tf_op jit(solution)/shard_map/ppermute | solution.py:27
  7.4 4.4 %collective-permute-start.2 = (bf16[18,1,768]{2,1,0:T(2,128)(2,1)S(1)}, bf16[18,1,768]{2,1,0:T(2,128)(2,1)S(1)}, u32[]{:S(2)}, u32[]{:S(2)}) collective-permute-start(bf16[18,1,768]{2,1,0:T(2,128)(2,1)S(1)} %get-tuple-element.19), channel_id=1, source_target_pairs={{0,1},{1,0},{2,3},{3,2},{4,5},{5,4},{6,7},{7,6},{8,9},{9,8},{10,11... | collective-permute-start | bytes 82952 | tf_op jit(solution)/shard_map/ppermute | solution.py:26
  8.5 5.5 %collective-permute-start.3 = (bf16[18,1,768]{2,1,0:T(2,128)(2,1)S(1)}, bf16[18,1,768]{2,1,0:T(2,128)(2,1)S(1)}, u32[]{:S(2)}, u32[]{:S(2)}) collective-permute-start(bf16[18,1,768]{2,1,0:T(2,128)(2,1)S(1)} %broadcast_select_fusion.6), channel_id=1, source_target_pairs={{1,2},{2,1},{3,4},{4,3},{5,6},{6,5},{9,10},{10,9},{11,12},{12,11},... | collective-permute-start | bytes 82952 | tf_op jit(solution)/shard_map/ppermute | solution.py:27
  14.2 2.2 %copy-start.6 = (bf16[3,3,64,128]{3,2,1,0:T(8,128)(2,1)S(1)}, bf16[3,3,64,128]{3,2,1,0:T(8,128)(2,1)}, u32[]{:S(2)}) copy-start(bf16[3,3,64,128]{3,2,1,0:T(8,128)(2,1)} %param.9) | copy-start | bytes 442372
  15.3 1.1 copy-start.4
  18.0 1.4 %copy-start.1 = (f32[16,16,12,128]{3,2,1,0:T(8,128)}, f32[16,16,12,128]{3,2,1,0:T(8,128)S(1)}, u32[]{:S(2)}) copy-start(f32[16,16,12,128]{3,2,1,0:T(8,128)S(1)} %fusion.74) | copy-start | bytes 4718596
  20.4 11.8 %copy-start.8 = (s32[1,1,32]{2,1,0:T(1,128)S(1)}, s32[1,1,32]{2,1,0:T(1,128)}, u32[]{:S(2)}) copy-start(s32[1,1,32]{2,1,0:T(1,128)} %param.15) | copy-start | bytes 388
  20.8 5.0 %collective-permute-start.4 = (bf16[1,3,32,128]{3,2,1,0:T(8,128)(2,1)S(1)}, bf16[1,3,32,128]{3,2,1,0:T(8,128)(2,1)S(1)}, u32[]{:S(2)}, u32[]{:S(2)}) collective-permute-start(bf16[1,3,32,128]{3,2,1,0:T(8,128)(2,1)S(1)} %bitcast.153), channel_id=1, source_target_pairs={{0,8},{8,0},{16,24},{24,16},{32,40},{40,32},{48,56},{56,48},{64,72... | collective-permute-start | bytes 73736 | tf_op jit(solution)/shard_map/ppermute | solution.py:26
  24.5 1.2 %collective-permute-start.5 = (bf16[1,3,32,128]{3,2,1,0:T(8,128)(2,1)S(1)}, bf16[1,3,32,128]{3,2,1,0:T(8,128)(2,1)S(1)}, u32[]{:S(2)}, u32[]{:S(2)}) collective-permute-start(bf16[1,3,32,128]{3,2,1,0:T(8,128)(2,1)S(1)} %bitcast.152), channel_id=1, source_target_pairs={{8,16},{16,8},{24,32},{32,24},{40,48},{48,40},{56,64},{64,56},{72,... | collective-permute-start | bytes 73736 | tf_op jit(solution)/shard_map/ppermute | solution.py:27
  25.8 4.2 %collective-permute-start.6 = (bf16[5,1,32,128]{3,2,1,0:T(8,128)(2,1)S(1)}, bf16[5,1,32,128]{3,2,1,0:T(8,128)(2,1)S(1)}, u32[]{:S(2)}, u32[]{:S(2)}) collective-permute-start(bf16[5,1,32,128]{3,2,1,0:T(8,128)(2,1)S(1)} %get-tuple-element.48), channel_id=1, source_target_pairs={{0,1},{1,0},{2,3},{3,2},{4,5},{5,4},{6,7},{7,6},{8,9},{9,8},{10,11... | collective-permute-start | bytes 122888 | tf_op jit(solution)/shard_map/ppermute | solution.py:26
  25.9 5.7 %collective-permute-start.7 = (bf16[5,1,32,128]{3,2,1,0:T(8,128)(2,1)S(1)}, bf16[5,1,32,128]{3,2,1,0:T(8,128)(2,1)S(1)}, u32[]{:S(2)}, u32[]{:S(2)}) collective-permute-start(bf16[5,1,32,128]{3,2,1,0:T(8,128)(2,1)S(1)} %get-tuple-element.49), channel_id=1, source_target_pairs={{1,2},{2,1},{3,4},{4,3},{5,6},{6,5},{9,10},{10,9},{11,12},{12,11},... | collective-permute-start | bytes 122888 | tf_op jit(solution)/shard_map/ppermute | solution.py:27
  32.6 7.3 %collective-permute-start.8 = (bf16[1,1,32,128]{3,2,1,0:T(8,128)(2,1)S(1)}, bf16[1,1,32,128]{3,2,1,0:T(8,128)(2,1)S(1)}, u32[]{:S(2)}, u32[]{:S(2)}) collective-permute-start(bf16[1,1,32,128]{3,2,1,0:T(8,128)(2,1)S(1)} %fusion.54), channel_id=1, source_target_pairs={{0,8},{8,0},{16,24},{24,16},{32,40},{40,32},{48,56},{56,48},{64,72... | collective-permute-start | bytes 24584 | tf_op jit(solution)/shard_map/ppermute | solution.py:26
  38.9 1.0 collective-permute-start.9
  40.0 5.2 %collective-permute-start.10 = (bf16[3,1,32,128]{3,2,1,0:T(8,128)(2,1)S(1)}, bf16[3,1,32,128]{3,2,1,0:T(8,128)(2,1)S(1)}, u32[]{:S(2)}, u32[]{:S(2)}) collective-permute-start(bf16[3,1,32,128]{3,2,1,0:T(8,128)(2,1)S(1)} %pad_maximum_fusion.17), channel_id=1, source_target_pairs={{0,1},{1,0},{2,3},{3,2},{4,5},{5,4},{6,7},{7,6},{8,9},{9,8},{10,11... | collective-permute-start | bytes 73736 | tf_op jit(solution)/shard_map/ppermute | solution.py:26
  40.1 6.0 %collective-permute-start.11 = (bf16[3,1,32,128]{3,2,1,0:T(8,128)(2,1)S(1)}, bf16[3,1,32,128]{3,2,1,0:T(8,128)(2,1)S(1)}, u32[]{:S(2)}, u32[]{:S(2)}) collective-permute-start(bf16[3,1,32,128]{3,2,1,0:T(8,128)(2,1)S(1)} %pad_maximum_fusion.17), channel_id=1, source_target_pairs={{1,2},{2,1},{3,4},{4,3},{5,6},{6,5},{9,10},{10,9},{11,12},{12,11},... | collective-permute-start | bytes 73736 | tf_op jit(solution)/shard_map/ppermute | solution.py:27
  47.5 1.6 %copy-start.2 = (f32[16,16,12,128]{3,2,1,0:T(8,128)S(1)}, f32[16,16,12,128]{3,2,1,0:T(8,128)}, u32[]{:S(2)}) copy-start(f32[16,16,12,128]{3,2,1,0:T(8,128)} %copy-done.1) | copy-start | bytes 4718596
  50.0 1.3 %copy-start.5 = (bf16[18,18,12,64]{3,2,1,0:T(8,128)(2,1)S(1)}, bf16[18,18,12,64]{3,2,1,0:T(8,128)(2,1)}, u32[]{:S(2)}) copy-start(bf16[18,18,12,64]{3,2,1,0:T(8,128)(2,1)} %copy-done.4) | copy-start | bytes 1492996
  56.0 4.2 %collective-permute-start.12 = (f32[512,128]{1,0:T(8,128)S(1)}, f32[512,128]{1,0:T(8,128)S(1)}, u32[]{:S(2)}, u32[]{:S(2)}) collective-permute-start(f32[512,128]{1,0:T(8,128)S(1)} %pad_maximum_fusion.2), channel_id=1, source_target_pairs={{0,1},{1,0},{2,3},{3,2},{4,5},{5,4},{6,7},{7,6},{8,9},{9,8},{10,11... | collective-permute-start | bytes 786440 | tf_op jit(solution)/shard_map/ppermute | solution.py:48
  56.1 6.4 %collective-permute-start.15 = (bf16[16,1,1536]{2,1,0:T(2,128)(2,1)S(1)}, bf16[16,1,1536]{2,1,0:T(2,128)(2,1)S(1)}, u32[]{:S(2)}, u32[]{:S(2)}) collective-permute-start(bf16[16,1,1536]{2,1,0:T(2,128)(2,1)S(1)} %get-tuple-element.32), channel_id=1, source_target_pairs={{1,2},{2,1},{3,4},{4,3},{5,6},{6,5},{9,10},{10,9},{11,12},{12,11},... | collective-permute-start | bytes 147464 | tf_op jit(solution)/shard_map/ppermute | solution.py:69
  60.4 3.9 %collective-permute-start.13 = (f32[160,128]{1,0:T(8,128)S(1)}, f32[160,128]{1,0:T(8,128)S(1)}, u32[]{:S(2)}, u32[]{:S(2)}) collective-permute-start(f32[160,128]{1,0:T(8,128)S(1)} %slice_select_fusion.1), channel_id=1, source_target_pairs={{0,2},{1,3},{2,0},{3,1},{4,6},{5,7},{6,4},{7,5},{8,10},{9,11},{10,... | collective-permute-start | bytes 245768 | tf_op jit(solution)/shard_map/ppermute | solution.py:48
  64.2 4.9 %collective-permute-start.14 = (f32[160,128]{1,0:T(8,128)S(1)}, f32[160,128]{1,0:T(8,128)S(1)}, u32[]{:S(2)}, u32[]{:S(2)}) collective-permute-start(f32[160,128]{1,0:T(8,128)S(1)} %select_add_fusion), channel_id=1, source_target_pairs={{0,4},{1,5},{2,6},{3,7},{4,0},{5,1},{6,2},{7,3},{8,12},{9,13},{10,... | collective-permute-start | bytes 245768 | tf_op jit(solution)/shard_map/ppermute | solution.py:48
  69.1 9.4 %collective-permute-start.16 = (f32[376,128]{1,0:T(8,128)S(1)}, f32[376,128]{1,0:T(8,128)S(1)}, u32[]{:S(2)}, u32[]{:S(2)}) collective-permute-start(f32[376,128]{1,0:T(8,128)S(1)} %pad_maximum_fusion.4), channel_id=1, source_target_pairs={{0,8},{8,0},{16,24},{24,16},{32,40},{40,32},{48,56},{56,48},{64,72... | collective-permute-start | bytes 577544 | tf_op jit(solution)/shard_map/ppermute | solution.py:48
  75.0 7.4 %collective-permute-start.17 = (bf16[1,18,1536]{2,1,0:T(8,128)(2,1)S(1)}, bf16[1,18,1536]{2,1,0:T(8,128)(2,1)S(1)}, u32[]{:S(2)}, u32[]{:S(2)}) collective-permute-start(bf16[1,18,1536]{2,1,0:T(8,128)(2,1)S(1)} %broadcast_select_fusion.11), channel_id=1, source_target_pairs={{8,16},{16,8},{24,32},{32,24},{40,48},{48,40},{56,64},{64,56},{72,... | collective-permute-start | bytes 165896 | tf_op jit(solution)/shard_map/ppermute | solution.py:69
  78.7 5.8 %collective-permute-start.18 = (f32[160,128]{1,0:T(8,128)S(1)}, f32[160,128]{1,0:T(8,128)S(1)}, u32[]{:S(2)}, u32[]{:S(2)}) collective-permute-start(f32[160,128]{1,0:T(8,128)S(1)} %slice_add_fusion.1), channel_id=1, source_target_pairs={{0,24},{8,16},{16,8},{24,0},{32,56},{40,48},{48,40},{56,32},{64,88... | collective-permute-start | bytes 245768 | tf_op jit(solution)/shard_map/ppermute | solution.py:47
  84.5 6.2 %collective-permute-start.19 = (f32[160,128]{1,0:T(8,128)S(1)}, f32[160,128]{1,0:T(8,128)S(1)}, u32[]{:S(2)}, u32[]{:S(2)}) collective-permute-start(f32[160,128]{1,0:T(8,128)S(1)} %add.137), channel_id=1, source_target_pairs={{0,32},{8,40},{16,48},{24,56},{32,0},{40,8},{48,16},{56,24},{64,96... | collective-permute-start | bytes 245768 | tf_op jit(solution)/shard_map/ppermute | solution.py:48
  90.7 4.8 %collective-permute-start.20 = (f32[160,128]{1,0:T(8,128)S(1)}, f32[160,128]{1,0:T(8,128)S(1)}, u32[]{:S(2)}, u32[]{:S(2)}) collective-permute-start(f32[160,128]{1,0:T(8,128)S(1)} %add.138), channel_id=1, source_target_pairs={{0,96},{8,104},{16,112},{24,120},{32,64},{40,72},{48,80},{56,88},{... | collective-permute-start | bytes 245768 | tf_op jit(solution)/shard_map/ppermute | solution.py:47
  95.5 4.4 %collective-permute-start.21 = (f32[160,128]{1,0:T(8,128)S(1)}, f32[160,128]{1,0:T(8,128)S(1)}, u32[]{:S(2)}, u32[]{:S(2)}) collective-permute-start(f32[160,128]{1,0:T(8,128)S(1)} %add.139), channel_id=1, source_target_pairs={{0,2},{1,3},{2,0},{3,1},{4,6},{5,7},{6,4},{7,5},{8,10},{9,11},{10,... | collective-permute-start | bytes 245768 | tf_op jit(solution)/shard_map/ppermute | solution.py:48
  100.0 7.5 %collective-permute-start.22 = (f32[320,128]{1,0:T(8,128)S(1)}, f32[320,128]{1,0:T(8,128)S(1)}, u32[]{:S(2)}, u32[]{:S(2)}) collective-permute-start(f32[320,128]{1,0:T(8,128)S(1)} %maximum_select_fusion.3), channel_id=1, source_target_pairs={{0,1},{1,0},{2,3},{3,2},{4,5},{5,4},{6,7},{7,6},{8,9},{9,8},{10,11... | collective-permute-start | bytes 491528 | tf_op jit(solution)/shard_map/ppermute | solution.py:48
